TPU v7x, 32 devices: a whole 2x2x4 slice. The times are simulated.
32 devices in a mesh: dp: 16 (over z, y, core), head: 2 (over x).
Axes of the slice: x: 2, y: 2, z: 4, core: 2. Of those that a mesh axis runs over, the one named last changes fastest.
Arguments:
- layer_input: bfloat16 [16, 256, 768], P('dp', 'head'), may hold values from -6 to 6
- pair_input: bfloat16 [16, 256, 256, 256], P('dp', 'head'), may hold values from -6 to 6
- time_cond: float32 [16, 256], P('dp'), may hold values from -6 to 6
- chain_lengths: int32 [16], P('dp'), may hold values from 128 to 256, as said below
- residue_mask: int32 [16, 256], P('dp'), may hold values from 0 to 1, as said below
- mod_weight: bfloat16 [256, 4608], replicated, may hold values from -0.375 to 0.375
- mod_bias: float32 [4608], replicated, may hold values from -3 to 3
- qkv_weight: bfloat16 [768, 3, 768], P(None, None, 'head'), may hold values from -0.21875 to 0.21875
- pair_gain: float32 [256], replicated, may hold values from 0.25 to 1.75
- pair_weight: bfloat16 [256, 12], replicated, may hold values from -0.375 to 0.375
- out_weight: bfloat16 [768, 768], P('head'), may hold values from -0.625 to 0.625
- out_bias: float32 [768], replicated, may hold values from -3 to 3
- gate_up_weight: bfloat16 [768, 2, 3072], P(None, None, 'head'), may hold values from -0.21875 to 0.21875
- down_weight: bfloat16 [3072, 768], P('head'), may hold values from -0.21875 to 0.21875
- output_grad: bfloat16 [16, 256, 768], P('dp', 'head'), may hold values from -6 to 6
Outputs:
- layer_output: bfloat16 [16, 256, 768], P('dp', 'head')
- input_grad: float32 [16, 256, 768], P('dp', 'head')
- pair_grad: bfloat16 [16, 256, 256, 256], P('dp', 'head')
- cond_grad: float32 [16, 256], P('dp')
- mod_weight_grad: float32 [256, 4608], replicated
- mod_bias_grad: float32 [4608], replicated
- qkv_weight_grad: float32 [768, 3, 768], P('dp', None, 'head')
- pair_gain_grad: float32 [256], replicated
- pair_weight_grad: float32 [256, 12], replicated
- out_weight_grad: float32 [768, 768], P('head', 'dp')
- out_bias_grad: float32 [768], replicated
- gate_up_grad: float32 [768, 2, 3072], P('dp', None, 'head')
- down_grad: float32 [3072, 768], P('head', 'dp')
Inputs may be any that keep to these rules, and one draw needn't show every extreme that they name: `chain_lengths`: each chain has 128 to 256 residues in use; the first chain has all 256. `residue_mask`: the first residue of every chain is resolved.
All inputs are finite; a program needn't handle non-finite values.
Results may differ from a plain program's by a relative error of at most 0.014.
The roundings to bfloat16 on the way count: a program that leaves them out, or rounds other values in their place, can miss the bound.
Values may be sent and summed in bfloat16 or wider, within the bound.
No kernel may reach another device: no remote copies, remote signals or barrier semaphores. Data moves between devices by JAX's collectives and lax.ppermute only.
A program may use at most 256 MiB of HBM per device.

v0:
```python
import jax
import jax.numpy as jnp
from jax import lax
from jax.experimental import pallas as pl
from jax.experimental.pallas import tpu as pltpu
from jax.sharding import PartitionSpec as P

DH = 64


epsilon = 1e-05
masked_score = -1000000000.0
precise = lax.Precision.HIGHEST
LANES = 128
PAIR_TILE = 2048
HEAD_PAD = 16


def pair_stats(x):
    centred = x - jnp.mean(x, axis=-1, keepdims=True)
    inv_std = lax.rsqrt(jnp.mean(centred * centred, axis=-1, keepdims=True) + epsilon)
    return centred * inv_std, inv_std


def pair_forward_kernel(x_ref, gain_ref, wt_ref, bias_ref):
    normed, _ = pair_stats(x_ref[...].astype(jnp.float32))
    scaled = (normed * gain_ref[...]).astype(jnp.bfloat16)
    bias = lax.dot_general(
        wt_ref[...], scaled, (((1,), (1,)), ((), ())), preferred_element_type=jnp.float32
    )
    bias_ref[...] = bias[: bias_ref.shape[0]].astype(bias_ref.dtype)


def pair_forward(flat, gain, wt, heads):
    m, width = flat.shape
    tile = min(PAIR_TILE, m)
    return pl.pallas_call(
        pair_forward_kernel,
        grid=(m // tile,),
        in_specs=[
            pl.BlockSpec((tile, width), lambda i: (i, 0)),
            pl.BlockSpec((1, width), lambda i: (0, 0)),
            pl.BlockSpec(wt.shape, lambda i: (0, 0)),
        ],
        out_specs=pl.BlockSpec((heads, tile), lambda i: (0, i)),
        out_shape=jax.ShapeDtypeStruct((heads, m), jnp.bfloat16),
        cost_estimate=pl.CostEstimate(
            flops=m * width * (2 * HEAD_PAD + 10),
            transcendentals=m,
            bytes_accessed=m * width * 2 + heads * m * 2,
        ),
    )(flat, gain, wt)


def pair_backward_kernel(x_ref, ds_ref, gain_ref, wt_ref, grad_ref, wg_ref, gg_ref):
    step = pl.program_id(0)
    normed, inv_std = pair_stats(x_ref[...].astype(jnp.float32))
    gain = gain_ref[...]
    scaled = (normed * gain).astype(jnp.bfloat16)
    ds = ds_ref[...]
    d_scaled = lax.dot_general(
        ds, wt_ref[...], (((0,), (0,)), ((), ())), preferred_element_type=jnp.float32
    )
    wg = lax.dot_general(ds, scaled, (((1,), (0,)), ((), ())), preferred_element_type=jnp.float32)
    gg = jnp.sum(d_scaled * normed, axis=0, keepdims=True)
    d_normed = d_scaled * gain
    mean_grad = jnp.mean(d_normed, axis=-1, keepdims=True)
    mean_proj = jnp.mean(d_normed * normed, axis=-1, keepdims=True)
    grad_ref[...] = (inv_std * (d_normed - mean_grad - normed * mean_proj)).astype(grad_ref.dtype)

    @pl.when(step == 0)
    def _():
        wg_ref[...] = jnp.zeros_like(wg_ref)
        gg_ref[...] = jnp.zeros_like(gg_ref)

    wg_ref[...] += wg
    gg_ref[...] += gg


def pair_backward(flat, ds, gain, wt):
    m, width = flat.shape
    tile = min(PAIR_TILE, m)
    pad = ds.shape[0]
    return pl.pallas_call(
        pair_backward_kernel,
        grid=(m // tile,),
        in_specs=[
            pl.BlockSpec((tile, width), lambda i: (i, 0)),
            pl.BlockSpec((pad, tile), lambda i: (0, i)),
            pl.BlockSpec((1, width), lambda i: (0, 0)),
            pl.BlockSpec(wt.shape, lambda i: (0, 0)),
        ],
        out_specs=[
            pl.BlockSpec((tile, width), lambda i: (i, 0)),
            pl.BlockSpec((pad, width), lambda i: (0, 0)),
            pl.BlockSpec((1, width), lambda i: (0, 0)),
        ],
        out_shape=[
            jax.ShapeDtypeStruct((m, width), jnp.bfloat16),
            jax.ShapeDtypeStruct((pad, width), jnp.float32),
            jax.ShapeDtypeStruct((1, width), jnp.float32),
        ],
        compiler_params=pltpu.CompilerParams(dimension_semantics=("arbitrary",)),
        cost_estimate=pl.CostEstimate(
            flops=m * width * (4 * HEAD_PAD + 20),
            transcendentals=m,
            bytes_accessed=2 * m * width * 2 + pad * m * 2,
        ),
    )(flat, ds, gain, wt)


def layer_norm(values):
    centred = values - jnp.mean(values, axis=-1, keepdims=True)
    inv_std = lax.rsqrt(jnp.mean(centred * centred, axis=-1, keepdims=True) + epsilon)
    return (centred * inv_std, inv_std)


def norm_back(normed, inv_std, grad):
    mean_grad = jnp.mean(grad, axis=-1, keepdims=True)
    mean_proj = jnp.mean(grad * normed, axis=-1, keepdims=True)
    return inv_std * (grad - mean_grad - normed * mean_proj)


def silu_slope(values):
    sigma = jax.nn.sigmoid(values)
    return sigma * (1.0 + values * (1.0 - sigma))


def head_split(values):
    return values.reshape(values.shape[:-1] + (values.shape[-1] // DH, DH))


def swap_heads(values):
    return lax.ppermute(values, "head", [(0, 1), (1, 0)])


def whole_rows(own, first):
    other = swap_heads(own)
    return jnp.where(
        first,
        jnp.concatenate([own, other], axis=0),
        jnp.concatenate([other, own], axis=0),
    )


def own_rows(values, head, rows):
    return lax.dynamic_slice_in_dim(values, head * rows, rows, 1)


def head_sum(part):
    return part + swap_heads(part)


def attn_scores(queries, keys, biases, valid):
    scores = jnp.einsum("cqhe,ckhe->chqk", queries, keys, preferred_element_type=jnp.float32)
    scores = scores * DH ** (-0.5) + biases.astype(jnp.float32)
    return jnp.where(valid[:, None, None, :], scores, masked_score)


def to_chunks(values, parts):
    return values.reshape(parts, -1, LANES)


def shards(
    layer_input,
    pair_input,
    time_cond,
    chain_lengths,
    residue_mask,
    mod_weight,
    mod_bias,
    qkv_weight,
    pair_gain,
    pair_weight,
    out_weight,
    out_bias,
    gate_up_weight,
    down_weight,
    output_grad,
):
    assert layer_input.shape[0] == 1
    rows = layer_input.shape[1]
    width = layer_input.shape[2]
    length = residue_mask.shape[1]
    head = lax.axis_index("head")
    first = head == 0
    data_count = lax.axis_size("dp")
    proj = qkv_weight.shape[2]
    ffn = gate_up_weight.shape[2]
    qkv_w = qkv_weight.reshape(width, 3 * proj)
    gate_up_w = gate_up_weight.reshape(width, 2 * ffn)

    x_rows = whole_rows(layer_input[0], first)
    g_rows = whole_rows(output_grad[0], first)

    positions = jnp.arange(length, dtype=jnp.int32)
    valid = (positions < chain_lengths[0]) & ((residue_mask[0] == 1) | (positions == 0))
    silu_cond = jax.nn.silu(time_cond).astype(jnp.bfloat16)
    modulation = jnp.dot(silu_cond, mod_weight, preferred_element_type=jnp.float32) + mod_bias
    scale_a, shift_a, gate_a, scale_t, shift_t, gate_t = [
        modulation[:, section * width : (section + 1) * width] for section in range(6)
    ]

    heads_all = pair_weight.shape[1]
    pair_width = pair_input.shape[-1]
    pair_flat = pair_input.reshape(-1, pair_width)
    pair_wt = jnp.zeros((HEAD_PAD, pair_width), jnp.bfloat16).at[:heads_all].set(pair_weight.T)
    pair_gain_row = pair_gain.reshape(1, pair_width)
    bias_flat = pair_forward(pair_flat, pair_gain_row, pair_wt, heads_all)
    bias_rows = bias_flat.reshape(heads_all, rows, length)
    biases = lax.all_to_all(bias_rows, "head", split_axis=0, concat_axis=1, tiled=True)

    residues = x_rows.astype(jnp.float32)
    norm_in, inv_in = layer_norm(residues)
    normed_a = (norm_in * (1.0 + scale_a) + shift_a).astype(jnp.bfloat16)
    projected = jnp.dot(normed_a, qkv_w, preferred_element_type=jnp.float32).astype(jnp.bfloat16)
    queries = head_split(projected[:, :proj])
    keys = head_split(projected[:, proj : 2 * proj])
    values = head_split(projected[:, 2 * proj :])
    scores = jnp.einsum("qhe,khe->hqk", queries, keys, preferred_element_type=jnp.float32)
    scores = scores * DH ** (-0.5) + biases.astype(jnp.float32)
    scores = jnp.where(valid[None, None, :], scores, masked_score)
    row_max = jnp.max(scores, axis=-1, keepdims=True)
    exp_scores = jnp.exp(scores - row_max)
    row_total = jnp.sum(exp_scores, axis=-1, keepdims=True)
    attn_probs = exp_scores / row_total
    probs_low = attn_probs.astype(jnp.bfloat16)
    mixed = jnp.einsum("hqk,khe->qhe", probs_low, values, preferred_element_type=jnp.float32)
    mixed = mixed.reshape(length, proj).astype(jnp.bfloat16)
    attn_part = jnp.dot(mixed, out_weight, preferred_element_type=jnp.float32)
    attn_branch = head_sum(attn_part) + out_bias
    sig_a = jax.nn.sigmoid(gate_a)
    middle = residues + sig_a * attn_branch

    norm_mid, inv_mid = layer_norm(middle)
    normed_t = (norm_mid * (1.0 + scale_t) + shift_t).astype(jnp.bfloat16)
    gate_up = jnp.dot(normed_t, gate_up_w, preferred_element_type=jnp.float32)
    gate_pre = gate_up[:, :ffn]
    up_pre = gate_up[:, ffn:]
    hidden = (jax.nn.silu(gate_pre) * up_pre).astype(jnp.bfloat16)
    ffn_part = jnp.dot(hidden, down_weight, preferred_element_type=jnp.float32).astype(jnp.bfloat16)
    ffn_branch = ffn_part.astype(jnp.float32) + swap_heads(ffn_part).astype(jnp.float32)
    sig_t = jax.nn.sigmoid(gate_t)
    layer_output = own_rows((middle + sig_t * ffn_branch).astype(jnp.bfloat16)[None], head, rows)

    grad_out = g_rows.astype(jnp.float32)
    d_ffn = (grad_out * sig_t).astype(jnp.bfloat16)
    d_gate_t = jnp.sum(grad_out * ffn_branch * sig_t * (1.0 - sig_t), axis=0, keepdims=True)
    down_grad_t = lax.dot_general(
        d_ffn, hidden, (((0,), (0,)), ((), ())), preferred_element_type=jnp.float32
    )
    d_hidden = lax.dot_general(
        d_ffn, down_weight, (((1,), (1,)), ((), ())), preferred_element_type=jnp.float32
    )
    d_gate = d_hidden * up_pre * silu_slope(gate_pre)
    d_up = d_hidden * jax.nn.silu(gate_pre)
    d_gate_up = jnp.concatenate([d_gate, d_up], axis=1).astype(jnp.bfloat16)
    gate_up_grad = lax.dot_general(
        normed_t, d_gate_up, (((0,), (0,)), ((), ())), preferred_element_type=jnp.float32
    )
    ffn_in_part = lax.dot_general(
        d_gate_up, gate_up_w, (((1,), (1,)), ((), ())), preferred_element_type=jnp.float32
    )
    d_normed_t = head_sum(ffn_in_part)
    d_middle = grad_out + norm_back(norm_mid, inv_mid, d_normed_t * (1.0 + scale_t))
    d_scale_t = jnp.sum(d_normed_t * norm_mid, axis=0, keepdims=True)
    d_shift_t = jnp.sum(d_normed_t, axis=0, keepdims=True)
    d_attn = d_middle * sig_a
    d_gate_a = jnp.sum(d_middle * attn_branch * sig_a * (1.0 - sig_a), axis=0, keepdims=True)
    d_out_bias = jnp.sum(d_attn, axis=0, keepdims=True)
    d_attn_low = d_attn.astype(jnp.bfloat16)

    out_weight_grad_t = lax.dot_general(
        d_attn_low, mixed, (((0,), (0,)), ((), ())), preferred_element_type=jnp.float32
    )
    d_mixed = head_split(
        lax.dot_general(
            d_attn_low, out_weight, (((1,), (1,)), ((), ())), preferred_element_type=jnp.float32
        ).astype(jnp.bfloat16)
    )
    d_values = jnp.einsum("hqk,qhe->khe", probs_low, d_mixed, preferred_element_type=jnp.float32)
    d_probs = jnp.einsum("qhe,khe->hqk", d_mixed, values, preferred_element_type=jnp.float32)
    d_scores = (
        attn_probs * (d_probs - jnp.sum(d_probs * attn_probs, axis=-1, keepdims=True))
    ).astype(jnp.bfloat16)
    d_queries = jnp.einsum(
        "hqk,khe->qhe", d_scores, keys, preferred_element_type=jnp.float32
    ) * DH ** (-0.5)
    d_keys = jnp.einsum(
        "hqk,qhe->khe", d_scores, queries, preferred_element_type=jnp.float32
    ) * DH ** (-0.5)
    d_qkv = jnp.concatenate(
        [d_queries.reshape(length, proj), d_keys.reshape(length, proj), d_values.reshape(length, proj)],
        axis=1,
    ).astype(jnp.bfloat16)
    qkv_grad = lax.dot_general(
        normed_a, d_qkv, (((0,), (0,)), ((), ())), preferred_element_type=jnp.float32
    )

    packed = jnp.concatenate(
        [
            qkv_grad.astype(jnp.bfloat16),
            out_weight_grad_t.astype(jnp.bfloat16),
            gate_up_grad.astype(jnp.bfloat16),
            down_grad_t.astype(jnp.bfloat16),
        ],
        axis=1,
    )
    reduced = lax.psum_scatter(packed, "dp", scatter_dimension=0, tiled=True).astype(jnp.float32)

    attn_in_part = lax.dot_general(
        d_qkv, qkv_w, (((1,), (1,)), ((), ())), preferred_element_type=jnp.float32
    ).astype(jnp.bfloat16)
    d_normed_a = attn_in_part.astype(jnp.float32) + swap_heads(attn_in_part).astype(jnp.float32)
    input_grad = own_rows(
        (d_middle + norm_back(norm_in, inv_in, d_normed_a * (1.0 + scale_a)))[None], head, rows
    )
    d_scale_a = jnp.sum(d_normed_a * norm_in, axis=0, keepdims=True)
    d_shift_a = jnp.sum(d_normed_a, axis=0, keepdims=True)
    d_modulation = jnp.concatenate(
        [d_scale_a, d_shift_a, d_gate_a, d_scale_t, d_shift_t, d_gate_t], axis=-1
    )

    d_bias_rows = lax.all_to_all(d_scores, "head", split_axis=1, concat_axis=0, tiled=True)
    d_bias_flat = jnp.pad(d_bias_rows.reshape(heads_all, -1), ((0, HEAD_PAD - heads_all), (0, 0)))
    pair_grad, pair_wg, pair_gg = pair_backward(pair_flat, d_bias_flat, pair_gain_row, pair_wt)
    pair_grad = pair_grad.reshape(pair_input.shape)
    pair_weight_grad = pair_wg[:heads_all].T
    pair_gain_grad = pair_gg[0]

    pair_small = head_sum(
        jnp.concatenate([pair_weight_grad.reshape(-1), pair_gain_grad])[None]
    )
    small = jnp.concatenate([d_modulation, time_cond, pair_small, d_out_bias], axis=-1)
    small_rows = lax.all_gather(small, "dp", axis=0, tiled=True)
    mod_size = d_modulation.shape[-1]
    cond_size = time_cond.shape[-1]
    pw_size = pair_weight.size
    pg_size = pair_gain.size
    mod_chain = small_rows[:, :mod_size]
    cond_chain = small_rows[:, mod_size : mod_size + cond_size]
    rest = jnp.sum(small_rows[:, mod_size + cond_size :], axis=0)
    pair_weight_grad = rest[:pw_size].reshape(pair_weight.shape)
    pair_gain_grad = rest[pw_size : pw_size + pg_size]
    out_bias_grad = rest[pw_size + pg_size :]
    cond_act = lax.optimization_barrier(jax.nn.silu(cond_chain).astype(jnp.bfloat16)).astype(
        jnp.float32
    )
    mod_weight_grad = jnp.dot(cond_act.T, mod_chain, precision=precise)
    mod_bias_grad = jnp.sum(mod_chain, axis=0)
    cond_grad = jnp.dot(
        d_modulation, mod_weight.astype(jnp.float32).T, precision=precise
    ) * silu_slope(time_cond)

    cuts = [0, 3 * proj, 4 * proj, 4 * proj + 2 * ffn, 4 * proj + 3 * ffn]
    pieces = [reduced[:, cuts[i] : cuts[i + 1]] for i in range(4)]
    qkv_grad = pieces[0].reshape(-1, 3, proj)
    out_weight_grad = pieces[1].T
    gate_up_grad = pieces[2].reshape(-1, 2, ffn)
    down_grad = pieces[3].T
    return (
        layer_output,
        input_grad,
        pair_grad,
        cond_grad,
        mod_weight_grad,
        mod_bias_grad,
        qkv_grad,
        pair_gain_grad,
        pair_weight_grad,
        out_weight_grad,
        out_bias_grad,
        gate_up_grad,
        down_grad,
    )


def solution(mesh):
    placed = (
        P("dp", "head", None),
        P("dp", "head", None, None),
        P("dp", None),
        P("dp"),
        P("dp", None),
        P(),
        P(),
        P(None, None, "head"),
        P(),
        P(),
        P("head", None),
        P(),
        P(None, None, "head"),
        P("head", None),
        P("dp", "head", None),
    )
    return jax.shard_map(
        shards,
        mesh=mesh,
        in_specs=placed,
        out_specs=(
            P("dp", "head", None),
            P("dp", "head", None),
            P("dp", "head", None, None),
            P("dp", None),
            P(),
            P(),
            P("dp", None, "head"),
            P(),
            P(),
            P("head", "dp"),
            P(),
            P("dp", None, "head"),
            P("head", "dp"),
        ),
        check_vma=False,
    )
```

profile of v0, /device:TPU:0, one launch (start us, length us, event | category | flops | bytes accessed | tf_op | source)
XLA Modules:
  0.0 261.7 jit_solution(1071598494341606046)
XLA Ops:
  7.2 3.0 %collective-permute-start = (bf16[128,768]{1,0:T(8,128)(2,1)}, bf16[128,768]{1,0:T(8,128)(2,1)S(1)}, u32[]{:S(2)}, u32[]{:S(2)}) collective-permute-start(bf16[128,768]{1,0:T(8,128)(2,1)} %bitcast.110), channel_id=1, source_target_pairs={{0,1},{1,0},{2,3},{3,2},{4,5},{5,4},{6,7},{7,6},{8,9},{9,8},{10,11... | collective-permute-start | bytes 589832 | tf_op jit(solution)/shard_map/ppermute | solution.py:134
  11.5 18.9 %shard_map.246 = bf16[12,32768]{1,0:T(8,128)(2,1)} custom-call(bf16[32768,256]{1,0:T(8,128)(2,1)} %bitcast.95, f32[1,256]{1,0:T(1,128)} %bitcast.143, bf16[16,256]{1,0:T(8,128)(2,1)} %scatter.4.wt_ref), custom_call_target="tpu_custom_call" | custom-call | flops 352321536 | bytes 17563648 | tf_op jit(solution)/shard_map/pallas_call | solution.py:37
  32.8 3.5 %all-to-all-start = ((bf16[12,128,256]{2,1,0:T(8,128)(2,1)}), bf16[12,128,256]{2,1,0:T(8,128)(2,1)S(1)}, u32[]{:S(2)}, u32[]{:S(2)}) async-start(bf16[12,128,256]{2,1,0:T(8,128)(2,1)} %slice.125), calls=%async_computation | async-start | bytes 1572864 | tf_op jit(solution)/shard_map/all_to_all | solution.py:211
  37.6 2.1 convolution_reduce_fusion
  40.4 3.9 %copy.59 = bf16[768,3,384]{0,2,1:T(8,128)(2,1)} copy(bf16[768,3,384]{2,0,1:T(8,128)(2,1)} %param.24) | data formatting | bytes 3538944 | tf_op args[7]
  45.9 2.3 convolution_convert_fusion.3
  56.1 3.4 %reshape.206 = f32[6,256,256]{1,2,0:T(8,128)} reshape(f32[6,2,128,256]{2,1,3,0:T(2,128)} %bitcast.97) | data formatting | bytes 3145728 | tf_op jit(solution)/shard_map/convert_element_type | solution.py:221
  63.0 2.5 convolution_convert_fusion.9
  65.9 2.0 collective-permute-start.1
  68.5 3.6 %copy.82 = bf16[96,8,2,1536]{3,1,2,0:T(8,128)(2,1)S(1)} copy(bf16[96,8,2,1536]{3,2,1,0:T(2,128)(2,1)} %bitcast.98) | data formatting | bytes 9437184
  72.7 13.7 %collective-permute-done.1 = f32[256,768]{1,0:T(8,128)S(1)} collective-permute-done((f32[256,768]{1,0:T(8,128)S(1)}, f32[256,768]{1,0:T(8,128)S(1)}, u32[]{:S(2)}, u32[]{:S(2)}) %collective-permute-start.1) | collective-permute-done | bytes 786464 | tf_op jit(solution)/shard_map/ppermute | solution.py:134
  93.6 2.2 convolution_convert_fusion.1
  95.8 3.8 %convolution_convert_fusion = bf16[768,3072]{1,0:T(8,128)(2,1)} fusion(bf16[256,1536]{1,0:T(8,128)(2,1)S(1)} %get-tuple-element.94, bf16[256,1536]{1,0:T(8,128)(2,1)S(1)} %get-tuple-element.93, f32[256,768]{1,0:T(8,128)S(1)} %get-tuple-element.92, f32[768]{0:T(1024)S(1)} %get-tuple-element.81, f32[768]{0:T(1024)S(1)} %get-tuple-element.80, ...), kind=kOutput, calls=%fused_computation.2 | convolution fusion | flops 1214447616 | bytes 7086080 | tf_op jit(solution)/shard_map/dot_general | solution.py:258
  99.6 10.5 %collective-permute-done.4 = f32[256,768]{1,0:T(8,128)S(1)} collective-permute-done((f32[256,768]{1,0:T(8,128)S(1)}, f32[256,768]{1,0:T(8,128)S(1)}, u32[]{:S(2)}, u32[]{:S(2)}) %collective-permute-start.4) | collective-permute-done | bytes 786464 | tf_op jit(solution)/shard_map/ppermute | solution.py:134
  116.3 3.1 %convolution_convert_fusion.7 = bf16[6,64,256]{2,1,0:T(8,128)(2,1)} fusion(bf16[256,6,64]{0,2,1:T(8,128)(2,1)} %bitcast.139, f32[6,256]{1,0:T(8,128)S(1)} %copy-done.23, f32[6,256,256]{1,2,0:T(8,128)} %copy-done.5), kind=kOutput, calls=%fused_computation.30 | convolution fusion | flops 51611392 | bytes 1972224 | tf_op jit(solution)/shard_map/hqk,qhe->khe/dot_general | solution.py:281
  119.4 2.1 multiply_reduce_fusion
  124.5 2.3 copy.72
  126.9 2.1 convolution_convert_fusion.2
  129.0 8.5 %pad_maximum_fusion = bf16[768,6144]{1,0:T(8,128)(2,1)} fusion(bf16[768,1536]{1,0:T(8,128)(2,1)S(1)} %copy-done.8, bf16[768,3072]{1,0:T(8,128)(2,1)} %convolution_convert_fusion, bf16[768,384]{1,0:T(8,128)(2,1)S(1)} %copy-done.9, bf16[768,1152]{1,0:T(8,128)(2,1)S(1)} %convolution_convert_fusion.2), kind=kLoop, calls=%fused_computation.1 | loop fusion | flops 37748736 | bytes 18874368 | tf_op jit(solution)/shard_map/concatenate | solution.py:300
  137.6 2.7 %convolution_convert_fusion.6 = bf16[256,768]{1,0:T(8,128)(2,1)} fusion(bf16[256,1536]{1,0:T(8,128)(2,1)} %copy-done.47, bf16[1536,768]{1,0:T(8,128)(2,1)S(1)} %copy-done), kind=kOutput, calls=%fused_computation.19 | convolution fusion | flops 604176384 | bytes 3538944 | tf_op jit(solution)/shard_map/dot_general | solution.py:241
  142.3 2.6 copy.69
  144.9 4.4 %all-to-all-start.1 = ((bf16[6,256,256]{2,0,1:T(8,128)(2,1)}), bf16[6,256,256]{2,0,1:T(8,128)(2,1)}, u32[]{:S(2)}, u32[]{:S(2)}) async-start(bf16[6,256,256]{2,0,1:T(8,128)(2,1)} %copy.69), calls=%async_computation.1 | async-start | bytes 2097152 | tf_op jit(solution)/shard_map/all_to_all | solution.py:324
  149.4 3.6 %convolution_convert_fusion.5 = bf16[256,768]{1,0:T(8,128)(2,1)} fusion(bf16[768,1152]{0,1:T(8,128)(2,1)} %bitcast.119, bf16[256,384]{0,1:T(8,128)(2,1)} %bitcast.148, bf16[256,384]{0,1:T(8,128)(2,1)} %bitcast.134, bf16[256,384]{0,1:T(8,128)(2,1)} %bitcast.136), kind=kOutput, calls=%fused_computation.18 | convolution fusion | flops 454950912 | bytes 2752512 | tf_op jit(solution)/shard_map/dot_general | solution.py:311
  153.0 2.0 collective-permute-start.5
  157.2 7.3 %all-to-all-done.1 = bf16[6,256,256]{2,0,1:T(8,128)(2,1)} async-done(((bf16[6,256,256]{2,0,1:T(8,128)(2,1)}), bf16[6,256,256]{2,0,1:T(8,128)(2,1)}, u32[]{:S(2)}, u32[]{:S(2)}) %all-to-all-start.1) | async-done | bytes 786464 | tf_op jit(solution)/shard_map/all_to_all | solution.py:324
  169.2 3.3 %fusion.14 = (f32[768]{0:T(1024)S(1)}, f32[768]{0:T(1024)}, f32[256]{0:T(256)S(1)}, f32[256]{0:T(256)S(1)}, f32[256,768]{1,0:T(8,128)}, /*index=5*/f32[256,768]{1,0:T(8,128)}) fusion(bf16[256,768]{1,0:T(8,128)(2,1)} %collective-permute-done.5, bf16[256,768]{1,0:T(8,128)(2,1)} %convolution_convert_fusion.5, f32[256]{0:T(256)S(1)} %copy-done.42, ...), kind=kLoop, calls=%fused_computation.58 | loop fusion | flops 4323328 | bytes 2765825 | tf_op jit(solution)/shard_map/reduce_sum | solution.py:319
  172.7 34.1 %shard_map.247 = (bf16[32768,256]{1,0:T(8,128)(2,1)}, f32[16,256]{1,0:T(8,128)}, f32[1,256]{1,0:T(1,128)}) custom-call(bf16[32768,256]{1,0:T(8,128)(2,1)} %bitcast.96, bf16[16,32768]{1,0:T(8,128)(2,1)} %pad.7.ds_ref, f32[1,256]{1,0:T(1,128)} %bitcast.144, bf16[16,256]{1,0:T(8,128)(2,1)} %scatter.4.wt_ref), custom_call_target="tpu_custom_call" | custom-call | flops 704643072 | bytes 34603008 | tf_op jit(solution)/shard_map/pallas_call | solution.py:84
  209.6 2.0 fusion.16
  211.7 4.2 %convolution_multiply_fusion.2 = f32[1,256]{1,0:T(1,128)} fusion(bf16[256,4608]{1,0:T(8,128)(2,1)} %param.22, f32[1,4608]{1,0:T(1,128)S(1)} %get-tuple-element.108, f32[1,256]{1,0:T(1,128)S(1)} %copy-done.36), kind=kOutput, calls=%fused_computation.34 | convolution fusion | flops 14157824 | bytes 2379776 | tf_op jit(solution)/shard_map/dot_general | solution.py:351
  215.9 25.0 %all-gather = f32[16,1,8960]{2,1,0:T(1,128)S(1)} all-gather(f32[1,1,8960]{2,1,0:T(1,128)S(1)} %bitcast.141), channel_id=1, replica_groups=mesh['dp'=16,'head'=2] {'dp'}, dimensions={0}, use_global_device_ids=true | all-gather | bytes 609280 | tf_op jit(solution)/shard_map/all_gather | solution.py:335
  243.7 4.2 %fusion.25 = f32[256,4608]{1,0:T(8,128)} fusion(bf16[16,256]{1,0:T(8,128)(2,1)S(1)} %multiply_convert_fusion.7, f32[16,8960]{1,0:T(8,128)S(1)} %bitcast.107), kind=kOutput, calls=%fused_computation.79 | convolution fusion | flops 226492416 | bytes 5021696 | tf_op jit(solution)/shard_map/dot_general | solution.py:349
  247.9 2.2 reduce-scatter.2.cloned.1.call-done
  (187 shorter events, 55.2 us)
Async XLA Ops:
  7.2 82.0 %copy-start = (bf16[1536,768]{1,0:T(8,128)(2,1)S(1)}, bf16[1536,768]{1,0:T(8,128)(2,1)}, u32[]{:S(2)}) copy-start(bf16[1536,768]{1,0:T(8,128)(2,1)} %param.30) | copy-start | bytes 7077892
  7.2 38.2 %collective-permute-start = (bf16[128,768]{1,0:T(8,128)(2,1)}, bf16[128,768]{1,0:T(8,128)(2,1)S(1)}, u32[]{:S(2)}, u32[]{:S(2)}) collective-permute-start(bf16[128,768]{1,0:T(8,128)(2,1)} %bitcast.110), channel_id=1, source_target_pairs={{0,1},{1,0},{2,3},{3,2},{4,5},{5,4},{6,7},{7,6},{8,9},{9,8},{10,11... | collective-permute-start | bytes 589832 | tf_op jit(solution)/shard_map/ppermute | solution.py:134
  31.8 5.2 %copy-start.46 = (s32[1,256]{1,0:T(1,128)S(1)}, s32[1,256]{1,0:T(1,128)}, u32[]{:S(2)}) copy-start(s32[1,256]{1,0:T(1,128)} %param.21) | copy-start | bytes 3076
  31.9 5.7 %copy-start.35 = (f32[1,256]{1,0:T(1,128)S(1)}, f32[1,256]{1,0:T(1,128)}, u32[]{:S(2)}) copy-start(f32[1,256]{1,0:T(1,128)} %param.19) | copy-start | bytes 3076
  32.8 21.4 %all-to-all-start = ((bf16[12,128,256]{2,1,0:T(8,128)(2,1)}), bf16[12,128,256]{2,1,0:T(8,128)(2,1)S(1)}, u32[]{:S(2)}, u32[]{:S(2)}) async-start(bf16[12,128,256]{2,1,0:T(8,128)(2,1)} %slice.125), calls=%async_computation | async-start | bytes 1572864 | tf_op jit(solution)/shard_map/all_to_all | solution.py:211
  36.4 213.8 %reduce-scatter.2.cloned.1.call-start = ((), (), s32[]{:S(2)}) async-start(), calls=%async_computation.3 | async-start | bytes 10027008 | tf_op jit(solution)/shard_map/reduce_scatter | solution.py:309
  40.4 5.5 %copy-start.25 = (f32[768]{0:T(1024)}, f32[768]{0:T(1024)S(1)}, u32[]{:S(2)}) copy-start(f32[768]{0:T(1024)S(1)} %get-tuple-element.83) | copy-start | bytes 9220
  40.4 5.5 %copy-start.43 = (f32[768]{0:T(1024)}, f32[768]{0:T(1024)S(1)}, u32[]{:S(2)}) copy-start(f32[768]{0:T(1024)S(1)} %get-tuple-element.82) | copy-start | bytes 9220
  40.4 5.1 %copy-start.7 = (bf16[1,128,768]{2,1,0:T(8,128)(2,1)S(1)}, bf16[1,128,768]{2,1,0:T(8,128)(2,1)}, u32[]{:S(2)}) copy-start(bf16[1,128,768]{2,1,0:T(8,128)(2,1)} %param.17) | copy-start | bytes 589828
  65.5 6.5 %copy-start.16 = (bf16[6,64,256]{2,1,0:T(8,128)(2,1)}, bf16[6,64,256]{2,1,0:T(8,128)(2,1)S(1)}, u32[]{:S(2)}) copy-start(bf16[6,64,256]{2,1,0:T(8,128)(2,1)S(1)} %convolution_convert_fusion.9) | copy-start | bytes 589828
  65.9 20.5 %collective-permute-start.1 = (f32[256,768]{1,0:T(8,128)S(1)}, f32[256,768]{1,0:T(8,128)S(1)}, u32[]{:S(2)}, u32[]{:S(2)}) collective-permute-start(f32[256,768]{1,0:T(8,128)S(1)} %fusion.52), channel_id=1, source_target_pairs={{0,1},{1,0},{2,3},{3,2},{4,5},{5,4},{6,7},{7,6},{8,9},{9,8},{10,11... | collective-permute-start | bytes 2359304 | tf_op jit(solution)/shard_map/ppermute | solution.py:134
  67.9 21.2 %collective-permute-start.3 = (bf16[128,768]{1,0:T(8,128)(2,1)S(1)}, bf16[128,768]{1,0:T(8,128)(2,1)S(1)}, u32[]{:S(2)}, u32[]{:S(2)}) collective-permute-start(bf16[128,768]{1,0:T(8,128)(2,1)S(1)} %bitcast.127), channel_id=1, source_target_pairs={{0,1},{1,0},{2,3},{3,2},{4,5},{5,4},{6,7},{7,6},{8,9},{9,8},{10,11... | collective-permute-start | bytes 589832 | tf_op jit(solution)/shard_map/ppermute | solution.py:134
  68.4 17.9 %copy-start.30 = (f32[768]{0:T(1024)S(1)}, f32[768]{0:T(1024)}, u32[]{:S(2)}) copy-start(f32[768]{0:T(1024)} %param.28) | copy-start | bytes 9220
  89.2 21.9 %copy-start.20 = (bf16[128,768]{1,0:T(8,128)(2,1)}, bf16[128,768]{1,0:T(8,128)(2,1)S(1)}, u32[]{:S(2)}) copy-start(bf16[128,768]{1,0:T(8,128)(2,1)S(1)} %collective-permute-done.3) | copy-start | bytes 589828
  91.9 18.2 %collective-permute-start.4 = (f32[256,768]{1,0:T(8,128)S(1)}, f32[256,768]{1,0:T(8,128)S(1)}, u32[]{:S(2)}, u32[]{:S(2)}) collective-permute-start(f32[256,768]{1,0:T(8,128)S(1)} %fusion.6), channel_id=1, source_target_pairs={{0,1},{1,0},{2,3},{3,2},{4,5},{5,4},{6,7},{7,6},{8,9},{9,8},{10,11... | collective-permute-start | bytes 2359304 | tf_op jit(solution)/shard_map/ppermute | solution.py:134
  122.5 4.3 %copy-start.26 = (f32[768]{0:T(1024)S(1)}, f32[768]{0:T(1024)}, u32[]{:S(2)}) copy-start(f32[768]{0:T(1024)} %copy-done.25) | copy-start | bytes 9220
  122.5 4.3 %copy-start.38 = (f32[256]{0:T(256)S(1)}, f32[256]{0:T(256)}, u32[]{:S(2)}) copy-start(f32[256]{0:T(256)} %copy-done.37) | copy-start | bytes 3076
  137.6 4.1 %copy-start.41 = (f32[256]{0:T(256)S(1)}, f32[256]{0:T(256)}, u32[]{:S(2)}) copy-start(f32[256]{0:T(256)} %copy-done.40) | copy-start | bytes 3076
  140.3 14.7 %collective-permute-start.2 = (bf16[256,768]{1,0:T(8,128)(2,1)}, bf16[256,768]{1,0:T(8,128)(2,1)}, u32[]{:S(2)}, u32[]{:S(2)}) collective-permute-start(bf16[256,768]{1,0:T(8,128)(2,1)} %convolution_convert_fusion.6), channel_id=1, source_target_pairs={{0,1},{1,0},{2,3},{3,2},{4,5},{5,4},{6,7},{7,6},{8,9},{9,8},{10,11... | collective-permute-start | bytes 1179656 | tf_op jit(solution)/shard_map/ppermute | solution.py:134
  144.9 19.5 %all-to-all-start.1 = ((bf16[6,256,256]{2,0,1:T(8,128)(2,1)}), bf16[6,256,256]{2,0,1:T(8,128)(2,1)}, u32[]{:S(2)}, u32[]{:S(2)}) async-start(bf16[6,256,256]{2,0,1:T(8,128)(2,1)} %copy.69), calls=%async_computation.1 | async-start | bytes 2097152 | tf_op jit(solution)/shard_map/all_to_all | solution.py:324
  149.3 5.6 %copy-start.19 = (bf16[1,128,768]{2,1,0:T(8,128)(2,1)S(1)}, bf16[1,128,768]{2,1,0:T(8,128)(2,1)}, u32[]{:S(2)}) copy-start(bf16[1,128,768]{2,1,0:T(8,128)(2,1)} %param.31) | copy-start | bytes 589828
  149.4 5.6 %copy-start.21 = (bf16[128,768]{1,0:T(8,128)(2,1)S(1)}, bf16[128,768]{1,0:T(8,128)(2,1)}, u32[]{:S(2)}) copy-start(bf16[128,768]{1,0:T(8,128)(2,1)} %copy-done.20) | copy-start | bytes 589828
  149.4 5.6 %copy-start.29 = (f32[768]{0:T(1024)S(1)}, f32[768]{0:T(1024)}, u32[]{:S(2)}) copy-start(f32[768]{0:T(1024)} %get-tuple-element.84) | copy-start | bytes 9220
  153.0 16.2 %collective-permute-start.5 = (bf16[256,768]{1,0:T(8,128)(2,1)}, bf16[256,768]{1,0:T(8,128)(2,1)}, u32[]{:S(2)}, u32[]{:S(2)}) collective-permute-start(bf16[256,768]{1,0:T(8,128)(2,1)} %convolution_convert_fusion.5), channel_id=1, source_target_pairs={{0,1},{1,0},{2,3},{3,2},{4,5},{5,4},{6,7},{7,6},{8,9},{9,8},{10,11... | collective-permute-start | bytes 1179656 | tf_op jit(solution)/shard_map/ppermute | solution.py:134
  172.6 36.9 %copy-start.28 = (f32[768]{0:T(1024)S(1)}, f32[768]{0:T(1024)}, u32[]{:S(2)}) copy-start(f32[768]{0:T(1024)} %get-tuple-element.77) | copy-start | bytes 9220
  172.6 36.9 %copy-start.32 = (f32[768]{0:T(1024)S(1)}, f32[768]{0:T(1024)}, u32[]{:S(2)}) copy-start(f32[768]{0:T(1024)} %get-tuple-element.74) | copy-start | bytes 9220
  172.6 36.9 %copy-start.27 = (f32[768]{0:T(1024)S(1)}, f32[768]{0:T(1024)}, u32[]{:S(2)}) copy-start(f32[768]{0:T(1024)} %get-tuple-element.70) | copy-start | bytes 9220
  172.6 37.0 %copy-start.3 = (f32[256,768]{1,0:T(8,128)S(1)}, f32[256,768]{1,0:T(8,128)}, u32[]{:S(2)}) copy-start(f32[256,768]{1,0:T(8,128)} %copy-done.2) | copy-start | bytes 2359300
  172.7 37.0 %copy-start.44 = (f32[128]{0:T(128)S(1)}, f32[128]{0:T(128)}, u32[]{:S(2)}) copy-start(f32[128]{0:T(128)} %dynamic-slice.22) | copy-start | bytes 1540
  206.7 4.9 %copy-start.36 = (f32[1,256]{1,0:T(1,128)S(1)}, f32[1,256]{1,0:T(1,128)}, u32[]{:S(2)}) copy-start(f32[1,256]{1,0:T(1,128)} %param.19) | copy-start | bytes 3076
  208.4 7.4 %collective-permute-start.6 = (f32[1,3328]{1,0:T(1,128)S(1)}, f32[1,3328]{1,0:T(1,128)S(1)}, u32[]{:S(2)}, u32[]{:S(2)}) collective-permute-start(f32[1,3328]{1,0:T(1,128)S(1)} %broadcast_in_dim.61), channel_id=1, source_target_pairs={{0,1},{1,0},{2,3},{3,2},{4,5},{5,4},{6,7},{7,6},{8,9},{9,8},{10,11... | collective-permute-start | bytes 39944 | tf_op jit(solution)/shard_map/ppermute | solution.py:134
  211.7 4.2 %copy-start.31 = (f32[768]{0:T(1024)S(1)}, f32[768]{0:T(1024)}, u32[]{:S(2)}) copy-start(f32[768]{0:T(1024)} %get-tuple-element.73) | copy-start | bytes 9220
  (26 other events, 63.5 us)
Sparse Core Ops, SparseCore 0:
  137.7 112.3 reduce-scatter.1
where the time goes:
time: 264 us; the launch traced here: 262 us
  Pallas kernels  53 us (20%)
  matrix products  45.4 us (17%)
  local copies, waits for them, and re-layouts  40.5 us (15%)
  waiting for transfers between devices  36.1 us (14%)
  other arithmetic  26.7 us (10%)
  blocking collectives  25 us (9%)
  starting transfers between devices  19.8 us (8%)
  between operations  15.3 us (6%)
    pallas_call x1, Pallas kernels, pair_backward(): pl.pallas_call(pair_backward_kernel, grid=(m // tile,), in_specs=[pl.Bloc...  34.1 us
    ppermute x7, waiting for transfers between devices, swap_heads(): return lax.ppermute(values, 'head', [(0, 1), (1, 0)])  26.5 us
    all_gather x1, blocking collectives, shards(): small_rows = lax.all_gather(small, 'dp', axis=0, tiled=True)  25 us
    pallas_call x1, Pallas kernels, pair_forward(): pl.pallas_call(pair_forward_kernel, grid=(m // tile,), in_specs=[pl.Block...  18.9 us
    ppermute x7, starting transfers between devices, swap_heads(): return lax.ppermute(values, 'head', [(0, 1), (1, 0)])  11.8 us
    unnamed x110, local copies, waits for them, and re-layouts  11.2 us
    concatenate x1, other arithmetic, shards(): jnp.concatenate([qkv_grad.astype(jnp.bfloat16), out_weight_grad_t.astype(...  8.54 us
    all_to_all x1, waiting for transfers between devices, shards(): lax.all_to_all(d_scores, 'head', split_axis=1, concat_axis=0, tiled=True)  7.28 us
  transfers between devices with their start and end apart: 10, of which 6 were waited for; matrix products, arithmetic and copies ran while one was open for 25% of the time, Pallas kernels for 20%

commit v1 on v0

--- a/solution.py
+++ b/solution.py
@@ -12,7 +12,8 @@
 masked_score = -1000000000.0
 precise = lax.Precision.HIGHEST
 LANES = 128
-PAIR_TILE = 2048
+PAIR_TILE = 4096
+PAIR_BACK_TILE = 2048
 HEAD_PAD = 16
 
 
@@ -79,7 +80,7 @@
 
 def pair_backward(flat, ds, gain, wt):
     m, width = flat.shape
-    tile = min(PAIR_TILE, m)
+    tile = min(PAIR_BACK_TILE, m)
     pad = ds.shape[0]
     return pl.pallas_call(
         pair_backward_kernel,
@@ -149,6 +150,16 @@
 
 def head_sum(part):
     return part + swap_heads(part)
+
+
+def trade_blocks(values, head, size, axis, mine_axis):
+    mine = lax.dynamic_slice_in_dim(values, head * size, size, axis)
+    theirs = swap_heads(lax.dynamic_slice_in_dim(values, (1 - head) * size, size, axis))
+    return jnp.where(
+        head == 0,
+        jnp.concatenate([mine, theirs], axis=mine_axis),
+        jnp.concatenate([theirs, mine], axis=mine_axis),
+    )
 
 
 def attn_scores(queries, keys, biases, valid):
@@ -204,11 +215,12 @@
     heads_all = pair_weight.shape[1]
     pair_width = pair_input.shape[-1]
     pair_flat = pair_input.reshape(-1, pair_width)
-    pair_wt = jnp.zeros((HEAD_PAD, pair_width), jnp.bfloat16).at[:heads_all].set(pair_weight.T)
+    pair_wt = jnp.pad(pair_weight.T, ((0, HEAD_PAD - heads_all), (0, 0)))
     pair_gain_row = pair_gain.reshape(1, pair_width)
     bias_flat = pair_forward(pair_flat, pair_gain_row, pair_wt, heads_all)
     bias_rows = bias_flat.reshape(heads_all, rows, length)
-    biases = lax.all_to_all(bias_rows, "head", split_axis=0, concat_axis=1, tiled=True)
+    heads_own = proj // DH
+    biases = trade_blocks(bias_rows, head, heads_own, 0, 1)
 
     residues = x_rows.astype(jnp.float32)
     norm_in, inv_in = layer_norm(residues)
@@ -321,7 +333,7 @@
         [d_scale_a, d_shift_a, d_gate_a, d_scale_t, d_shift_t, d_gate_t], axis=-1
     )
 
-    d_bias_rows = lax.all_to_all(d_scores, "head", split_axis=1, concat_axis=0, tiled=True)
+    d_bias_rows = trade_blocks(d_scores, head, rows, 1, 0)
     d_bias_flat = jnp.pad(d_bias_rows.reshape(heads_all, -1), ((0, HEAD_PAD - heads_all), (0, 0)))
     pair_grad, pair_wg, pair_gg = pair_backward(pair_flat, d_bias_flat, pair_gain_row, pair_wt)
     pair_grad = pair_grad.reshape(pair_input.shape)

time: 264 us -> 244 us (0.924)
  starting transfers between devices: 19.8 us -> 11.5 us
  local copies, waits for them, and re-layouts: 40.5 us -> 35 us
  Pallas kernels: 53 us -> 49.3 us
    ppermute x7 -> x9, waiting for transfers between devices: 26.5 us -> 34.9 us  [swap_heads(): return lax.ppermute(values, 'head', [(0, 1), (1, 0)])]
    all_to_all x2 -> x0, starting transfers between devices: 7.98 us -> none  [the longest x1 4.44 us: shards(): lax.all_to_all(d_scores, 'head', split_axis=1, concat_axis=0, tiled=True)]
    convert_element_type x3 -> x0, local copies, waits for them, and re-layouts: 7.87 us -> none  [the longest x2 5.28 us: shards(): scores = scores * DH ** (-0.5) + biases.astype(jnp.float32)]
    all_to_all x2 -> x0, waiting for transfers between devices: 7.28 us -> none  [the longest x1 7.28 us: shards(): lax.all_to_all(d_scores, 'head', split_axis=1, concat_axis=0, tiled=True)]
    unnamed x110 -> x102, local copies, waits for them, and re-layouts: 11.2 us -> 15.9 us
    dynamic_slice x0 -> x3, local copies, waits for them, and re-layouts: none -> 3.9 us  [trade_blocks(): mine = lax.dynamic_slice_in_dim(values, head * size, size, axis)]
    pallas_call x1, Pallas kernels: 18.9 us -> 15.2 us  [pair_forward(): pl.pallas_call(pair_forward_kernel, grid=(m // tile,), in_specs=[pl.Block...]
    sub x0 -> x1, matrix products: none -> 3.39 us  [shards(): exp_scores = jnp.exp(scores - row_max)]
  transfers between devices with their start and end apart: 10 -> 10, of which waited for: 6 -> 6; matrix products, arithmetic and copies ran while one was open for 25% -> 27% of each run, Pallas kernels for 20% -> 20%
where the time goes in v1:
time: 244 us; the launch traced here: 242 us
  Pallas kernels  49.3 us (20%)
  matrix products  44.2 us (18%)
  waiting for transfers between devices  37.2 us (15%)
  local copies, waits for them, and re-layouts  35 us (14%)
  blocking collectives  25.2 us (10%)
  other arithmetic  24.8 us (10%)
  between operations  15.3 us (6%)
  starting transfers between devices  11.5 us (5%)
    ppermute x9, waiting for transfers between devices, swap_heads(): return lax.ppermute(values, 'head', [(0, 1), (1, 0)])  34.9 us
    pallas_call x1, Pallas kernels, pair_backward(): pl.pallas_call(pair_backward_kernel, grid=(m // tile,), in_specs=[pl.Bloc...  34.1 us
    all_gather x1, blocking collectives, shards(): small_rows = lax.all_gather(small, 'dp', axis=0, tiled=True)  25.2 us
    unnamed x102, local copies, waits for them, and re-layouts  15.9 us
    pallas_call x1, Pallas kernels, pair_forward(): pl.pallas_call(pair_forward_kernel, grid=(m // tile,), in_specs=[pl.Block...  15.2 us
    ppermute x9, starting transfers between devices, swap_heads(): return lax.ppermute(values, 'head', [(0, 1), (1, 0)])  11.5 us
    concatenate x1, other arithmetic, shards(): jnp.concatenate([qkv_grad.astype(jnp.bfloat16), out_weight_grad_t.astype(...  8.54 us
  transfers between devices with their start and end apart: 10, of which 6 were waited for; matrix products, arithmetic and copies ran while one was open for 27% of the time, Pallas kernels for 20%

profile of v1, /device:TPU:0, one launch (start us, length us, event | category | flops | bytes accessed | tf_op | source)
XLA Modules:
  0.0 242.4 jit_solution(6628873479936494993)
XLA Ops:
  7.2 3.0 %collective-permute-start = (bf16[128,768]{1,0:T(8,128)(2,1)}, bf16[128,768]{1,0:T(8,128)(2,1)S(1)}, u32[]{:S(2)}, u32[]{:S(2)}) collective-permute-start(bf16[128,768]{1,0:T(8,128)(2,1)} %bitcast.96), channel_id=1, source_target_pairs={{0,1},{1,0},{2,3},{3,2},{4,5},{5,4},{6,7},{7,6},{8,9},{9,8},{10,11... | collective-permute-start | bytes 589832 | tf_op jit(solution)/shard_map/ppermute | solution.py:135
  11.6 15.2 %shard_map.246 = bf16[12,32768]{1,0:T(8,128)(2,1)} custom-call(bf16[32768,256]{1,0:T(8,128)(2,1)} %bitcast.85, f32[1,256]{1,0:T(1,128)} %bitcast.132, bf16[16,256]{1,0:T(8,128)(2,1)} %pad.8.wt_ref), custom_call_target="tpu_custom_call" | custom-call | flops 352321536 | bytes 17563648 | tf_op jit(solution)/shard_map/pallas_call | solution.py:38
  29.3 2.0 copy.86
  32.1 2.1 convolution_reduce_fusion
  35.8 3.9 %copy.63 = bf16[768,3,384]{0,2,1:T(8,128)(2,1)} copy(bf16[768,3,384]{2,0,1:T(8,128)(2,1)} %param.22) | data formatting | bytes 3538944 | tf_op args[7]
  40.6 2.3 convolution_convert_fusion.3
  43.5 3.4 %fusion.60 = (f32[6,256]{1,0:T(8,128)S(1)}, f32[6,256,256]{1,2,0:T(8,128)}) fusion(pred[256]{0:T(512)(128)(4,1)} %or_and_fusion, bf16[256,6,64]{0,2,1:T(8,128)(2,1)S(1)} %bitcast.114, bf16[256,6,64]{0,2,1:T(8,128)(2,1)S(1)} %bitcast.112, bf16[6,128,256]{1,2,0:T(8,128)(2,1)} %copy.85, bf16[6,128,256]{1,2,0:T(8,128)(2,1)} %collective-permute-done.1, pred[]{:T(512)S(6)} %eq.28), kind=kOutput, calls=%fused_computation.156 | convolution fusion | flops 56230144 | bytes 2758913 | tf_op jit(solution)/shard_map/sub | solution.py:236
  49.1 1.9 collective-permute-start.2
  51.5 3.6 %copy.89 = bf16[96,8,2,1536]{3,1,2,0:T(8,128)(2,1)S(1)} copy(bf16[96,8,2,1536]{3,2,1,0:T(2,128)(2,1)} %bitcast.87) | data formatting | bytes 9437184
  55.7 13.9 %collective-permute-done.2 = f32[256,768]{1,0:T(8,128)S(1)} collective-permute-done((f32[256,768]{1,0:T(8,128)S(1)}, f32[256,768]{1,0:T(8,128)S(1)}, u32[]{:S(2)}, u32[]{:S(2)}) %collective-permute-start.2) | collective-permute-done | bytes 786464 | tf_op jit(solution)/shard_map/ppermute | solution.py:135
  76.7 2.2 convolution_convert_fusion.1
  78.9 3.8 %convolution_convert_fusion = bf16[768,3072]{1,0:T(8,128)(2,1)} fusion(bf16[256,1536]{1,0:T(8,128)(2,1)S(1)} %get-tuple-element.82, bf16[256,1536]{1,0:T(8,128)(2,1)S(1)} %get-tuple-element.81, f32[256,768]{1,0:T(8,128)S(1)} %get-tuple-element.80, f32[768]{0:T(1024)S(1)} %get-tuple-element.69, f32[768]{0:T(1024)S(1)} %get-tuple-element.68, ...), kind=kOutput, calls=%fused_computation.2 | convolution fusion | flops 1214447616 | bytes 7086080 | tf_op jit(solution)/shard_map/dot_general | solution.py:270
  82.7 10.6 %collective-permute-done.5 = f32[256,768]{1,0:T(8,128)S(1)} collective-permute-done((f32[256,768]{1,0:T(8,128)S(1)}, f32[256,768]{1,0:T(8,128)S(1)}, u32[]{:S(2)}, u32[]{:S(2)}) %collective-permute-start.5) | collective-permute-done | bytes 786464 | tf_op jit(solution)/shard_map/ppermute | solution.py:135
  97.7 1.7 copy.70
  99.4 2.6 %convolution_convert_fusion.7 = bf16[6,64,256]{2,1,0:T(8,128)(2,1)} fusion(bf16[256,6,64]{0,2,1:T(8,128)(2,1)} %bitcast.128, f32[6,256,256]{1,2,0:T(8,128)} %get-tuple-element.112, f32[6,256]{1,0:T(8,128)} %copy-done.34), kind=kOutput, calls=%fused_computation.30 | convolution fusion | flops 51216384 | bytes 1972224 | tf_op jit(solution)/shard_map/hqk,qhe->khe/dot_general | solution.py:293
  105.6 2.1 copy.77
  107.7 2.1 convolution_convert_fusion.2
  109.9 8.5 %pad_maximum_fusion = bf16[768,6144]{1,0:T(8,128)(2,1)} fusion(bf16[768,1536]{1,0:T(8,128)(2,1)S(1)} %copy-done.7, bf16[768,3072]{1,0:T(8,128)(2,1)} %convolution_convert_fusion, bf16[768,384]{1,0:T(8,128)(2,1)S(1)} %copy-done.8, bf16[768,1152]{1,0:T(8,128)(2,1)S(1)} %convolution_convert_fusion.2), kind=kLoop, calls=%fused_computation.1 | loop fusion | flops 37748736 | bytes 18874368 | tf_op jit(solution)/shard_map/concatenate | solution.py:312
  118.5 2.7 %convolution_convert_fusion.6 = bf16[256,768]{1,0:T(8,128)(2,1)} fusion(bf16[256,1536]{1,0:T(8,128)(2,1)} %copy-done.42, bf16[1536,768]{1,0:T(8,128)(2,1)S(1)} %copy-done), kind=kOutput, calls=%fused_computation.19 | convolution fusion | flops 604176384 | bytes 3538944 | tf_op jit(solution)/shard_map/dot_general | solution.py:253
  123.1 7.2 %collective-permute-done.3 = bf16[256,768]{1,0:T(8,128)(2,1)} collective-permute-done((bf16[256,768]{1,0:T(8,128)(2,1)}, bf16[256,768]{1,0:T(8,128)(2,1)}, u32[]{:S(2)}, u32[]{:S(2)}) %collective-permute-start.3) | collective-permute-done | bytes 393248 | tf_op jit(solution)/shard_map/ppermute | solution.py:135
  130.3 1.8 fusion.14
  134.9 1.9 copy.74
  138.1 3.5 %convolution_convert_fusion.5 = bf16[256,768]{1,0:T(8,128)(2,1)} fusion(bf16[768,1152]{0,1:T(8,128)(2,1)} %bitcast.106, bf16[256,384]{0,1:T(8,128)(2,1)} %bitcast.137, bf16[256,384]{0,1:T(8,128)(2,1)} %bitcast.123, bf16[256,384]{0,1:T(8,128)(2,1)} %bitcast.125), kind=kOutput, calls=%fused_computation.18 | convolution fusion | flops 454950912 | bytes 2752512 | tf_op jit(solution)/shard_map/dot_general | solution.py:323
  142.7 1.9 copy.75
  147.6 2.4 collective-permute-done.6
  150.0 3.3 %fusion.18 = (f32[768]{0:T(1024)S(1)}, f32[768]{0:T(1024)}, f32[256]{0:T(256)S(1)}, f32[256]{0:T(256)S(1)}, f32[256,768]{1,0:T(8,128)}, /*index=5*/f32[256,768]{1,0:T(8,128)}) fusion(bf16[256,768]{1,0:T(8,128)(2,1)} %collective-permute-done.6, bf16[256,768]{1,0:T(8,128)(2,1)} %convolution_convert_fusion.5, f32[256]{0:T(256)S(1)} %copy-done.38, ...), kind=kLoop, calls=%fused_computation.64 | loop fusion | flops 4323328 | bytes 2765825 | tf_op jit(solution)/shard_map/reduce_sum | solution.py:331
  153.5 34.1 %shard_map.247 = (bf16[32768,256]{1,0:T(8,128)(2,1)}, f32[16,256]{1,0:T(8,128)}, f32[1,256]{1,0:T(1,128)}) custom-call(bf16[32768,256]{1,0:T(8,128)(2,1)} %bitcast.86, bf16[16,32768]{1,0:T(8,128)(2,1)} %pad.9.ds_ref, f32[1,256]{1,0:T(1,128)} %bitcast.133, bf16[16,256]{1,0:T(8,128)(2,1)} %pad.8.wt_ref), custom_call_target="tpu_custom_call" | custom-call | flops 704643072 | bytes 34603008 | tf_op jit(solution)/shard_map/pallas_call | solution.py:85
  190.3 2.0 fusion.20
  192.3 4.2 %convolution_multiply_fusion.2 = f32[1,256]{1,0:T(1,128)} fusion(bf16[256,4608]{1,0:T(8,128)(2,1)} %param.20, f32[1,4608]{1,0:T(1,128)S(1)} %get-tuple-element.100, f32[1,256]{1,0:T(1,128)S(1)} %copy-done.30), kind=kOutput, calls=%fused_computation.34 | convolution fusion | flops 14157824 | bytes 2379776 | tf_op jit(solution)/shard_map/dot_general | solution.py:363
  196.5 25.2 %all-gather = f32[16,1,8960]{2,1,0:T(1,128)S(1)} all-gather(f32[1,1,8960]{2,1,0:T(1,128)S(1)} %bitcast.130), channel_id=1, replica_groups=mesh['dp'=16,'head'=2] {'dp'}, dimensions={0}, use_global_device_ids=true | all-gather | bytes 609280 | tf_op jit(solution)/shard_map/all_gather | solution.py:347
  224.4 4.2 %fusion.29 = f32[256,4608]{1,0:T(8,128)} fusion(bf16[16,256]{1,0:T(8,128)(2,1)S(1)} %multiply_convert_fusion.7, f32[16,8960]{1,0:T(8,128)S(1)} %bitcast.94), kind=kOutput, calls=%fused_computation.85 | convolution fusion | flops 226492416 | bytes 5021696 | tf_op jit(solution)/shard_map/dot_general | solution.py:361
  228.7 2.3 reduce-scatter.2.cloned.1.call-done
  (179 shorter events, 45.5 us)
Async XLA Ops:
  7.2 65.2 %copy-start = (bf16[1536,768]{1,0:T(8,128)(2,1)S(1)}, bf16[1536,768]{1,0:T(8,128)(2,1)}, u32[]{:S(2)}) copy-start(bf16[1536,768]{1,0:T(8,128)(2,1)} %param.28) | copy-start | bytes 7077892
  7.2 223.7 %reduce-scatter.2.cloned.1.call-start = ((), (), s32[]{:S(2)}) async-start(), calls=%async_computation.1 | async-start | bytes 10027008 | tf_op jit(solution)/shard_map/reduce_scatter | solution.py:321
  7.2 32.9 %collective-permute-start = (bf16[128,768]{1,0:T(8,128)(2,1)}, bf16[128,768]{1,0:T(8,128)(2,1)S(1)}, u32[]{:S(2)}, u32[]{:S(2)}) collective-permute-start(bf16[128,768]{1,0:T(8,128)(2,1)} %bitcast.96), channel_id=1, source_target_pairs={{0,1},{1,0},{2,3},{3,2},{4,5},{5,4},{6,7},{7,6},{8,9},{9,8},{10,11... | collective-permute-start | bytes 589832 | tf_op jit(solution)/shard_map/ppermute | solution.py:135
  28.3 3.7 %copy-start.41 = (s32[1,256]{1,0:T(1,128)S(1)}, s32[1,256]{1,0:T(1,128)}, u32[]{:S(2)}) copy-start(s32[1,256]{1,0:T(1,128)} %param.19) | copy-start | bytes 3076
  28.3 3.8 %copy-start.29 = (f32[1,256]{1,0:T(1,128)S(1)}, f32[1,256]{1,0:T(1,128)}, u32[]{:S(2)}) copy-start(f32[1,256]{1,0:T(1,128)} %param.17) | copy-start | bytes 3076
  29.3 4.9 %copy-start.21 = (f32[4608]{0:T(1024)S(1)}, f32[4608]{0:T(1024)}, u32[]{:S(2)}) copy-start(f32[4608]{0:T(1024)} %param.21) | copy-start | bytes 55300
  29.3 5.6 %copy-start.10 = (bf16[6,128,256]{2,1,0:T(8,128)(2,1)S(1)}, bf16[6,128,256]{2,1,0:T(8,128)(2,1)}, u32[]{:S(2)}) copy-start(bf16[6,128,256]{2,1,0:T(8,128)(2,1)} %get-tuple-element.91) | copy-start | bytes 1179652
  31.2 12.2 %collective-permute-start.1 = (bf16[6,128,256]{1,2,0:T(8,128)(2,1)}, bf16[6,128,256]{1,2,0:T(8,128)(2,1)}, u32[]{:S(2)}, u32[]{:S(2)}) collective-permute-start(bf16[6,128,256]{1,2,0:T(8,128)(2,1)} %copy.86), channel_id=1, source_target_pairs={{0,1},{1,0},{2,3},{3,2},{4,5},{5,4},{6,7},{7,6},{8,9},{9,8},{10,11... | collective-permute-start | bytes 1179656 | tf_op jit(solution)/shard_map/ppermute | solution.py:135
  34.8 5.8 %copy-start.39 = (f32[768]{0:T(1024)}, f32[768]{0:T(1024)S(1)}, u32[]{:S(2)}) copy-start(f32[768]{0:T(1024)S(1)} %get-tuple-element.70) | copy-start | bytes 9220
  35.8 4.4 %copy-start.6 = (bf16[1,128,768]{2,1,0:T(8,128)(2,1)S(1)}, bf16[1,128,768]{2,1,0:T(8,128)(2,1)}, u32[]{:S(2)}) copy-start(bf16[1,128,768]{2,1,0:T(8,128)(2,1)} %param.15) | copy-start | bytes 589828
  43.1 3.7 %copy-start.12 = (bf16[256,384]{0,1:T(8,128)(2,1)}, bf16[256,384]{0,1:T(8,128)(2,1)S(1)}, u32[]{:S(2)}) copy-start(bf16[256,384]{0,1:T(8,128)(2,1)S(1)} %copy.66) | copy-start | bytes 589828
  43.3 3.6 %copy-start.14 = (bf16[256,384]{0,1:T(8,128)(2,1)}, bf16[256,384]{0,1:T(8,128)(2,1)S(1)}, u32[]{:S(2)}) copy-start(bf16[256,384]{0,1:T(8,128)(2,1)S(1)} %copy.65) | copy-start | bytes 589828
  49.1 20.5 %collective-permute-start.2 = (f32[256,768]{1,0:T(8,128)S(1)}, f32[256,768]{1,0:T(8,128)S(1)}, u32[]{:S(2)}, u32[]{:S(2)}) collective-permute-start(f32[256,768]{1,0:T(8,128)S(1)} %fusion.61), channel_id=1, source_target_pairs={{0,1},{1,0},{2,3},{3,2},{4,5},{5,4},{6,7},{7,6},{8,9},{9,8},{10,11... | collective-permute-start | bytes 2359304 | tf_op jit(solution)/shard_map/ppermute | solution.py:135
  51.0 21.3 %collective-permute-start.4 = (bf16[128,768]{1,0:T(8,128)(2,1)S(1)}, bf16[128,768]{1,0:T(8,128)(2,1)S(1)}, u32[]{:S(2)}, u32[]{:S(2)}) collective-permute-start(bf16[128,768]{1,0:T(8,128)(2,1)S(1)} %bitcast.117), channel_id=1, source_target_pairs={{0,1},{1,0},{2,3},{3,2},{4,5},{5,4},{6,7},{7,6},{8,9},{9,8},{10,11... | collective-permute-start | bytes 589832 | tf_op jit(solution)/shard_map/ppermute | solution.py:135
  51.5 3.6 %copy-start.28 = (f32[1,768]{1,0:T(1,128)S(1)}, f32[1,768]{1,0:T(1,128)}, u32[]{:S(2)}) copy-start(f32[1,768]{1,0:T(1,128)} %get-tuple-element.98) | copy-start | bytes 9220
  51.5 18.1 %copy-start.24 = (f32[768]{0:T(1024)S(1)}, f32[768]{0:T(1024)}, u32[]{:S(2)}) copy-start(f32[768]{0:T(1024)} %param.26) | copy-start | bytes 9220
  72.4 21.9 %copy-start.17 = (bf16[128,768]{1,0:T(8,128)(2,1)}, bf16[128,768]{1,0:T(8,128)(2,1)S(1)}, u32[]{:S(2)}) copy-start(bf16[128,768]{1,0:T(8,128)(2,1)S(1)} %collective-permute-done.4) | copy-start | bytes 589828
  75.1 18.2 %collective-permute-start.5 = (f32[256,768]{1,0:T(8,128)S(1)}, f32[256,768]{1,0:T(8,128)S(1)}, u32[]{:S(2)}, u32[]{:S(2)}) collective-permute-start(f32[256,768]{1,0:T(8,128)S(1)} %fusion.6), channel_id=1, source_target_pairs={{0,1},{1,0},{2,3},{3,2},{4,5},{5,4},{6,7},{7,6},{8,9},{9,8},{10,11... | collective-permute-start | bytes 2359304 | tf_op jit(solution)/shard_map/ppermute | solution.py:135
  103.6 4.1 %copy-start.32 = (f32[256]{0:T(256)S(1)}, f32[256]{0:T(256)}, u32[]{:S(2)}) copy-start(f32[256]{0:T(256)} %copy-done.31) | copy-start | bytes 3076
  118.5 4.0 %copy-start.37 = (f32[256]{0:T(256)S(1)}, f32[256]{0:T(256)}, u32[]{:S(2)}) copy-start(f32[256]{0:T(256)} %copy-done.36) | copy-start | bytes 3076
  121.1 9.2 %collective-permute-start.3 = (bf16[256,768]{1,0:T(8,128)(2,1)}, bf16[256,768]{1,0:T(8,128)(2,1)}, u32[]{:S(2)}, u32[]{:S(2)}) collective-permute-start(bf16[256,768]{1,0:T(8,128)(2,1)} %convolution_convert_fusion.6), channel_id=1, source_target_pairs={{0,1},{1,0},{2,3},{3,2},{4,5},{5,4},{6,7},{7,6},{8,9},{9,8},{10,11... | collective-permute-start | bytes 1179656 | tf_op jit(solution)/shard_map/ppermute | solution.py:135
  122.4 9.7 %copy-start.2 = (bf16[6,256,256]{1,2,0:T(8,128)(2,1)S(1)}, bf16[6,256,256]{1,2,0:T(8,128)(2,1)}, u32[]{:S(2)}) copy-start(bf16[6,256,256]{1,2,0:T(8,128)(2,1)} %copy-done.1) | copy-start | bytes 2359300
  133.2 9.5 %collective-permute-start.7 = (bf16[6,128,256]{1,2,0:T(8,128)(2,1)}, bf16[6,128,256]{1,2,0:T(8,128)(2,1)}, u32[]{:S(2)}, u32[]{:S(2)}) collective-permute-start(bf16[6,128,256]{1,2,0:T(8,128)(2,1)} %get-tuple-element.90), channel_id=1, source_target_pairs={{0,1},{1,0},{2,3},{3,2},{4,5},{5,4},{6,7},{7,6},{8,9},{9,8},{10,11... | collective-permute-start | bytes 1179656 | tf_op jit(solution)/shard_map/ppermute | solution.py:135
  141.6 8.4 %collective-permute-start.6 = (bf16[256,768]{1,0:T(8,128)(2,1)}, bf16[256,768]{1,0:T(8,128)(2,1)}, u32[]{:S(2)}, u32[]{:S(2)}) collective-permute-start(bf16[256,768]{1,0:T(8,128)(2,1)} %convolution_convert_fusion.5), channel_id=1, source_target_pairs={{0,1},{1,0},{2,3},{3,2},{4,5},{5,4},{6,7},{7,6},{8,9},{9,8},{10,11... | collective-permute-start | bytes 1179656 | tf_op jit(solution)/shard_map/ppermute | solution.py:135
  153.5 36.7 %copy-start.23 = (f32[768]{0:T(1024)S(1)}, f32[768]{0:T(1024)}, u32[]{:S(2)}) copy-start(f32[768]{0:T(1024)} %get-tuple-element.65) | copy-start | bytes 9220
  153.5 36.7 %copy-start.26 = (f32[768]{0:T(1024)S(1)}, f32[768]{0:T(1024)}, u32[]{:S(2)}) copy-start(f32[768]{0:T(1024)} %get-tuple-element.62) | copy-start | bytes 9220
  153.5 36.7 %copy-start.22 = (f32[768]{0:T(1024)S(1)}, f32[768]{0:T(1024)}, u32[]{:S(2)}) copy-start(f32[768]{0:T(1024)} %get-tuple-element.58) | copy-start | bytes 9220
  153.5 36.8 %copy-start.4 = (f32[256,768]{1,0:T(8,128)S(1)}, f32[256,768]{1,0:T(8,128)}, u32[]{:S(2)}) copy-start(f32[256,768]{1,0:T(8,128)} %copy-done.3) | copy-start | bytes 2359300
  153.5 36.8 %copy-start.40 = (f32[128]{0:T(128)S(1)}, f32[128]{0:T(128)}, u32[]{:S(2)}) copy-start(f32[128]{0:T(128)} %dynamic-slice.14) | copy-start | bytes 1540
  187.6 4.7 %copy-start.30 = (f32[1,256]{1,0:T(1,128)S(1)}, f32[1,256]{1,0:T(1,128)}, u32[]{:S(2)}) copy-start(f32[1,256]{1,0:T(1,128)} %param.17) | copy-start | bytes 3076
  189.2 7.2 %collective-permute-start.8 = (f32[1,3328]{1,0:T(1,128)S(1)}, f32[1,3328]{1,0:T(1,128)S(1)}, u32[]{:S(2)}, u32[]{:S(2)}) collective-permute-start(f32[1,3328]{1,0:T(1,128)S(1)} %broadcast_in_dim.60), channel_id=1, source_target_pairs={{0,1},{1,0},{2,3},{3,2},{4,5},{5,4},{6,7},{7,6},{8,9},{9,8},{10,11... | collective-permute-start | bytes 39944 | tf_op jit(solution)/shard_map/ppermute | solution.py:135
  192.3 4.2 %copy-start.25 = (f32[768]{0:T(1024)S(1)}, f32[768]{0:T(1024)}, u32[]{:S(2)}) copy-start(f32[768]{0:T(1024)} %get-tuple-element.61) | copy-start | bytes 9220
  (21 other events, 50.1 us)
Sparse Core Ops, SparseCore 0:
  118.6 112.2 reduce-scatter.1

commit v2 on v1

--- a/solution.py
+++ b/solution.py
@@ -144,6 +144,33 @@
     )
 
 
+def dp_gather(values):
+    count = lax.axis_size("dp")
+    index = lax.axis_index("dp")
+    block = values
+    step = 1
+    while step < count:
+        other = lax.ppermute(block, "dp", [(i, i ^ step) for i in range(count)])
+        block = jnp.where(
+            (index & step) == 0,
+            jnp.concatenate([block, other], axis=0),
+            jnp.concatenate([other, block], axis=0),
+        )
+        step *= 2
+    return block
+
+
+def dp_sum(values):
+    count = lax.axis_size("dp")
+    index = lax.axis_index("dp")
+    step = 1
+    while step < count:
+        other = lax.ppermute(values, "dp", [(i, i ^ step) for i in range(count)])
+        values = jnp.where((index & step) == 0, values + other, other + values)
+        step *= 2
+    return values
+
+
 def own_rows(values, head, rows):
     return lax.dynamic_slice_in_dim(values, head * rows, rows, 1)
 
@@ -309,15 +336,13 @@
         normed_a, d_qkv, (((0,), (0,)), ((), ())), preferred_element_type=jnp.float32
     )
 
-    packed = jnp.concatenate(
-        [
-            qkv_grad.astype(jnp.bfloat16),
-            out_weight_grad_t.astype(jnp.bfloat16),
-            gate_up_grad.astype(jnp.bfloat16),
-            down_grad_t.astype(jnp.bfloat16),
-        ],
-        axis=1,
-    )
+    packed = jnp.zeros((width, 4 * proj + 3 * ffn), jnp.bfloat16)
+    packed = lax.dynamic_update_slice(packed, gate_up_grad.astype(jnp.bfloat16), (0, 4 * proj))
+    packed = lax.dynamic_update_slice(
+        packed, down_grad_t.astype(jnp.bfloat16), (0, 4 * proj + 2 * ffn)
+    )
+    packed = lax.dynamic_update_slice(packed, out_weight_grad_t.astype(jnp.bfloat16), (0, 3 * proj))
+    packed = lax.dynamic_update_slice(packed, qkv_grad.astype(jnp.bfloat16), (0, 0))
     reduced = lax.psum_scatter(packed, "dp", scatter_dimension=0, tiled=True).astype(jnp.float32)
 
     attn_in_part = lax.dot_general(
@@ -343,18 +368,17 @@
     pair_small = head_sum(
         jnp.concatenate([pair_weight_grad.reshape(-1), pair_gain_grad])[None]
     )
-    small = jnp.concatenate([d_modulation, time_cond, pair_small, d_out_bias], axis=-1)
-    small_rows = lax.all_gather(small, "dp", axis=0, tiled=True)
+    small = jnp.concatenate([d_modulation, time_cond, d_out_bias], axis=-1)
+    small_rows = dp_gather(small)
     mod_size = d_modulation.shape[-1]
     cond_size = time_cond.shape[-1]
     pw_size = pair_weight.size
-    pg_size = pair_gain.size
     mod_chain = small_rows[:, :mod_size]
     cond_chain = small_rows[:, mod_size : mod_size + cond_size]
-    rest = jnp.sum(small_rows[:, mod_size + cond_size :], axis=0)
-    pair_weight_grad = rest[:pw_size].reshape(pair_weight.shape)
-    pair_gain_grad = rest[pw_size : pw_size + pg_size]
-    out_bias_grad = rest[pw_size + pg_size :]
+    out_bias_grad = jnp.sum(small_rows[:, mod_size + cond_size :], axis=0)
+    pair_total = dp_sum(pair_small)[0]
+    pair_weight_grad = pair_total[:pw_size].reshape(pair_weight.shape)
+    pair_gain_grad = pair_total[pw_size:]
     cond_act = lax.optimization_barrier(jax.nn.silu(cond_chain).astype(jnp.bfloat16)).astype(
         jnp.float32
     )

time: 244 us -> 238 us (0.975)
  blocking collectives: 25.2 us -> 0 us
  waiting for transfers between devices: 37.2 us -> 49 us
  starting transfers between devices: 11.5 us -> 21.4 us
  other arithmetic: 24.8 us -> 15.3 us
  local copies, waits for them, and re-layouts: 35 us -> 42.8 us
    all_gather x1 -> x0, blocking collectives: 25.2 us -> none  [shards(): small_rows = lax.all_gather(small, 'dp', axis=0, tiled=True)]
    reduce_scatter x1, waiting for transfers between devices: 2.27 us -> 14.5 us  [shards(): lax.psum_scatter(packed, 'dp', scatter_dimension=0, tiled=True)]
    ppermute x9, waiting for transfers between devices: 34.9 us -> 23.7 us  [swap_heads(): return lax.ppermute(values, 'head', [(0, 1), (1, 0)])]
    ppermute x0 -> x8, waiting for transfers between devices: none -> 10.7 us  [the longest x4 5.66 us: dp_gather(): other = lax.ppermute(block, 'dp', [(i, i ^ step) for i in range(count)])]
    ppermute x0 -> x8, starting transfers between devices: none -> 9.98 us  [the longest x4 5.18 us: dp_sum(): other = lax.ppermute(values, 'dp', [(i, i ^ step) for i in range(count)])]
    concatenate x1 -> x0, other arithmetic: 8.54 us -> none  [shards(): jnp.concatenate([qkv_grad.astype(jnp.bfloat16), out_weight_grad_t.astype(...]
    dynamic_update_slice x0 -> x1, local copies, waits for them, and re-layouts: none -> 7.16 us  [shards(): lax.dynamic_update_slice(packed, gate_up_grad.astype(jnp.bfloat16), (0, 4...]
    unnamed x102 -> x127, local copies, waits for them, and re-layouts: 15.9 us -> 19.2 us
  transfers between devices with their start and end apart: 10 -> 18, of which waited for: 6 -> 10; matrix products, arithmetic and copies ran while one was open for 27% -> 30% of each run, Pallas kernels for 20% -> 21%
where the time goes in v2:
time: 238 us; the launch traced here: 236 us
  Pallas kernels  49.2 us (21%)
  waiting for transfers between devices  49 us (21%)
  matrix products  43.1 us (18%)
  local copies, waits for them, and re-layouts  42.8 us (18%)
  starting transfers between devices  21.4 us (9%)
  between operations  15.4 us (6%)
  other arithmetic  15.3 us (6%)
    pallas_call x1, Pallas kernels, pair_backward(): pl.pallas_call(pair_backward_kernel, grid=(m // tile,), in_specs=[pl.Bloc...  34 us
    ppermute x9, waiting for transfers between devices, swap_heads(): return lax.ppermute(values, 'head', [(0, 1), (1, 0)])  23.7 us
    unnamed x127, local copies, waits for them, and re-layouts  19.2 us
    pallas_call x1, Pallas kernels, pair_forward(): pl.pallas_call(pair_forward_kernel, grid=(m // tile,), in_specs=[pl.Block...  15.2 us
    reduce_scatter x1, waiting for transfers between devices, shards(): lax.psum_scatter(packed, 'dp', scatter_dimension=0, tiled=True)  14.5 us
    ppermute x9, starting transfers between devices, swap_heads(): return lax.ppermute(values, 'head', [(0, 1), (1, 0)])  11.4 us
    dynamic_update_slice x1, local copies, waits for them, and re-layouts, shards(): lax.dynamic_update_slice(packed, gate_up_grad.astype(jnp.bfloat16), (0, 4...  7.16 us
    ppermute x4, waiting for transfers between devices, dp_gather(): other = lax.ppermute(block, 'dp', [(i, i ^ step) for i in range(count)])  5.66 us
  transfers between devices with their start and end apart: 18, of which 10 were waited for; matrix products, arithmetic and copies ran while one was open for 30% of the time, Pallas kernels for 21%

profile of v2, /device:TPU:0, one launch (start us, length us, event | category | flops | bytes accessed | tf_op | source)
XLA Modules:
  0.0 236.2 jit_solution(6801133010114641512)
XLA Ops:
  7.2 3.0 %collective-permute-start = (bf16[128,768]{1,0:T(8,128)(2,1)}, bf16[128,768]{1,0:T(8,128)(2,1)S(1)}, u32[]{:S(2)}, u32[]{:S(2)}) collective-permute-start(bf16[128,768]{1,0:T(8,128)(2,1)} %bitcast.89), channel_id=1, source_target_pairs={{0,1},{1,0},{2,3},{3,2},{4,5},{5,4},{6,7},{7,6},{8,9},{9,8},{10,11... | collective-permute-start | bytes 589832 | tf_op jit(solution)/shard_map/ppermute | solution.py:135
  11.6 15.2 %shard_map.246 = bf16[12,32768]{1,0:T(8,128)(2,1)} custom-call(bf16[32768,256]{1,0:T(8,128)(2,1)} %bitcast.82, f32[1,256]{1,0:T(1,128)} %bitcast.124, bf16[16,256]{1,0:T(8,128)(2,1)} %pad.9.wt_ref), custom_call_target="tpu_custom_call" | custom-call | flops 352321536 | bytes 17563648 | tf_op jit(solution)/shard_map/pallas_call | solution.py:38
  29.3 2.0 copy.82
  32.1 2.1 convolution_reduce_fusion
  35.8 3.9 %copy.61 = bf16[768,3,384]{0,2,1:T(8,128)(2,1)} copy(bf16[768,3,384]{2,0,1:T(8,128)(2,1)} %param.22) | data formatting | bytes 3538944 | tf_op args[7]
  40.6 2.3 convolution_convert_fusion.3
  43.5 3.4 %fusion.63 = (f32[6,256]{1,0:T(8,128)S(1)}, f32[6,256,256]{1,2,0:T(8,128)}) fusion(pred[256]{0:T(512)(128)(4,1)S(1)} %or_and_fusion, bf16[256,6,64]{0,2,1:T(8,128)(2,1)S(1)} %bitcast.107, bf16[256,6,64]{0,2,1:T(8,128)(2,1)S(1)} %bitcast.105, bf16[6,128,256]{1,2,0:T(8,128)(2,1)} %copy.81, bf16[6,128,256]{1,2,0:T(8,128)(2,1)} %collective-permute-done.1, ...), kind=kOutput, calls=%fused_computation.161 | convolution fusion | flops 56230144 | bytes 2758913 | tf_op jit(solution)/shard_map/sub | solution.py:263
  49.7 1.9 collective-permute-start.2
  51.8 3.6 %copy.85 = bf16[96,8,2,1536]{3,1,2,0:T(8,128)(2,1)S(1)} copy(bf16[96,8,2,1536]{3,2,1,0:T(2,128)(2,1)} %bitcast.84) | data formatting | bytes 9437184
  56.0 14.2 %collective-permute-done.2 = f32[256,768]{1,0:T(8,128)S(1)} collective-permute-done((f32[256,768]{1,0:T(8,128)S(1)}, f32[256,768]{1,0:T(8,128)S(1)}, u32[]{:S(2)}, u32[]{:S(2)}) %collective-permute-start.2) | collective-permute-done | bytes 786464 | tf_op jit(solution)/shard_map/ppermute | solution.py:135
  73.0 2.2 multiply_convert_fusion.2
  78.2 3.8 %convolution_convert_fusion = bf16[768,3072]{1,0:T(8,128)(2,1)} fusion(bf16[256,1536]{1,0:T(8,128)(2,1)S(1)} %get-tuple-element.82, bf16[256,1536]{1,0:T(8,128)(2,1)S(1)} %get-tuple-element.81, f32[256,768]{1,0:T(8,128)S(1)} %get-tuple-element.80, f32[768]{0:T(1024)S(1)} %get-tuple-element.69, f32[768]{0:T(1024)S(1)} %get-tuple-element.68, ...), kind=kOutput, calls=%fused_computation.1 | convolution fusion | flops 1214447616 | bytes 7086080 | tf_op jit(solution)/shard_map/dot_general | solution.py:297
  82.0 7.2 %dynamic_update_slice.12 = bf16[768,6144]{1,0:T(8,128)(2,1)} pad(bf16[768,3072]{1,0:T(8,128)(2,1)} %convolution_convert_fusion, bf16[]{:T(256)} %constant.16.clone.1), padding=0_0x1536_1536 | pad | bytes 14155778 | tf_op jit(solution)/shard_map/dynamic_update_slice | solution.py:340
  89.2 3.8 %fusion.1 = bf16[768,6144]{1,0:T(8,128)(2,1)} fusion(bf16[768,6144]{1,0:T(8,128)(2,1)} %dynamic_update_slice.12, bf16[256,1536]{1,0:T(8,128)(2,1)} %get-tuple-element.83, f32[768]{0:T(1024)S(1)} %get-tuple-element.73, bf16[128,768]{1,0:T(8,128)(2,1)} %copy-done.23, bf16[128,768]{1,0:T(8,128)(2,1)} %bitcast.109, pred[]{:T(512)S(6)} %eq.44), kind=kOutput, calls=%fused_computation.4 | convolution fusion | flops 607518720 | bytes 3542017 | tf_op jit(solution)/shard_map/dot_general | solution.py:288
  93.0 1.9 collective-permute-done.5
  94.9 2.2 multiply_reduce_fusion.1
  102.3 1.9 convolution_convert_fusion.7
  108.5 2.2 fusion.2
  110.8 2.7 %convolution_convert_fusion.6 = bf16[256,768]{1,0:T(8,128)(2,1)} fusion(bf16[256,1536]{1,0:T(8,128)(2,1)} %get-tuple-element.83, bf16[1536,768]{1,0:T(8,128)(2,1)S(1)} %copy-done), kind=kOutput, calls=%fused_computation.21 | convolution fusion | flops 604176384 | bytes 3538944 | tf_op jit(solution)/shard_map/dot_general | solution.py:280
  115.3 7.3 %collective-permute-done.3 = bf16[256,768]{1,0:T(8,128)(2,1)} collective-permute-done((bf16[256,768]{1,0:T(8,128)(2,1)}, bf16[256,768]{1,0:T(8,128)(2,1)}, u32[]{:S(2)}, u32[]{:S(2)}) %collective-permute-start.3) | collective-permute-done | bytes 393248 | tf_op jit(solution)/shard_map/ppermute | solution.py:135
  122.6 1.8 fusion.17
  127.2 1.9 copy.72
  130.4 3.5 %convolution_convert_fusion.5 = bf16[256,768]{1,0:T(8,128)(2,1)} fusion(bf16[768,1152]{0,1:T(8,128)(2,1)} %bitcast.99, bf16[256,384]{0,1:T(8,128)(2,1)} %bitcast.130, bf16[256,384]{0,1:T(8,128)(2,1)} %bitcast.116, bf16[256,384]{0,1:T(8,128)(2,1)} %bitcast.118), kind=kOutput, calls=%fused_computation.20 | convolution fusion | flops 454950912 | bytes 2752512 | tf_op jit(solution)/shard_map/dot_general | solution.py:348
  135.0 1.9 copy.73
  139.8 34.0 %shard_map.247 = (bf16[32768,256]{1,0:T(8,128)(2,1)}, f32[16,256]{1,0:T(8,128)}, f32[1,256]{1,0:T(1,128)}) custom-call(bf16[32768,256]{1,0:T(8,128)(2,1)} %bitcast.83, bf16[16,32768]{1,0:T(8,128)(2,1)} %pad.10.ds_ref, f32[1,256]{1,0:T(1,128)} %bitcast.125, bf16[16,256]{1,0:T(8,128)(2,1)} %pad.9.wt_ref), custom_call_target="tpu_custom_call" | custom-call | flops 704643072 | bytes 34603008 | tf_op jit(solution)/shard_map/pallas_call | solution.py:85
  178.6 2.5 %convolution_multiply_fusion.2 = f32[1,256]{1,0:T(1,128)} fusion(bf16[256,4608]{1,0:T(8,128)(2,1)S(1)} %copy-done.6, f32[1,4608]{1,0:T(1,128)S(1)} %get-tuple-element.100, f32[1,256]{1,0:T(1,128)S(1)} %copy-done.41), kind=kOutput, calls=%fused_computation.36 | convolution fusion | flops 14157824 | bytes 2379776 | tf_op jit(solution)/shard_map/dot_general | solution.py:387
  184.6 3.5 %collective-permute-done.14 = f32[1,3328]{1,0:T(1,128)S(1)} collective-permute-done((f32[1,3328]{1,0:T(1,128)S(1)}, f32[1,3328]{1,0:T(1,128)S(1)}, u32[]{:S(2)}, u32[]{:S(2)}) %collective-permute-start.14) | collective-permute-done | bytes 13344 | tf_op jit(solution)/shard_map/ppermute | solution.py:168
  192.0 2.4 %collective-permute-start.16 = (f32[1,3328]{1,0:T(1,128)S(1)}, f32[1,3328]{1,0:T(1,128)S(1)}, u32[]{:S(2)}, u32[]{:S(2)}) collective-permute-start(f32[1,3328]{1,0:T(1,128)S(1)} %add.190), channel_id=1, source_target_pairs={{0,16},{2,18},{4,20},{6,22},{8,24},{10,26},{12,28},{14,30},{16,0},... | collective-permute-start | bytes 39944 | tf_op jit(solution)/shard_map/ppermute | solution.py:168
  194.6 2.7 %collective-permute-start.11 = (f32[8,5632]{1,0:T(8,128)S(1)}, f32[8,5632]{1,0:T(8,128)S(1)}, u32[]{:S(2)}, u32[]{:S(2)}) collective-permute-start(f32[8,5632]{1,0:T(8,128)S(1)} %maximum_select_fusion.5), channel_id=1, source_target_pairs={{0,16},{2,18},{4,20},{6,22},{8,24},{10,26},{12,28},{14,30},{16,0},... | collective-permute-start | bytes 540680 | tf_op jit(solution)/shard_map/ppermute | solution.py:153
  199.7 4.9 %collective-permute-done.11 = f32[8,5632]{1,0:T(8,128)S(1)} collective-permute-done((f32[8,5632]{1,0:T(8,128)S(1)}, f32[8,5632]{1,0:T(8,128)S(1)}, u32[]{:S(2)}, u32[]{:S(2)}) %collective-permute-start.11) | collective-permute-done | bytes 180256 | tf_op jit(solution)/shard_map/ppermute | solution.py:153
  205.9 4.2 %fusion.32 = f32[256,4608]{1,0:T(8,128)} fusion(bf16[16,256]{1,0:T(8,128)(2,1)S(1)} %multiply_convert_fusion.7, f32[16,5632]{1,0:T(8,128)S(1)} %maximum_select_fusion.4), kind=kOutput, calls=%fused_computation.87 | convolution fusion | flops 226492416 | bytes 5021696 | tf_op jit(solution)/shard_map/dot_general | solution.py:385
  210.2 14.5 %reduce-scatter.2.cloned.1.call-done = bf16[48,6144]{1,0:T(8,128)(2,1)} async-done(((bf16[768,6144]{1,0:T(8,128)(2,1)}), bf16[48,6144]{1,0:T(8,128)(2,1)}) %reduce-scatter.2.cloned.1.call-update) | async-done | bytes 589840 | tf_op jit(solution)/shard_map/reduce_scatter | solution.py:346
  (225 shorter events, 56.3 us)
Async XLA Ops:
  7.2 65.8 %copy-start = (bf16[1536,768]{1,0:T(8,128)(2,1)S(1)}, bf16[1536,768]{1,0:T(8,128)(2,1)}, u32[]{:S(2)}) copy-start(bf16[1536,768]{1,0:T(8,128)(2,1)} %param.28) | copy-start | bytes 7077892
  7.2 217.5 %reduce-scatter.2.cloned.1.call-start = ((), (), s32[]{:S(2)}) async-start(), calls=%async_computation.1 | async-start | bytes 10027008 | tf_op jit(solution)/shard_map/reduce_scatter | solution.py:346
  7.2 32.4 %collective-permute-start = (bf16[128,768]{1,0:T(8,128)(2,1)}, bf16[128,768]{1,0:T(8,128)(2,1)S(1)}, u32[]{:S(2)}, u32[]{:S(2)}) collective-permute-start(bf16[128,768]{1,0:T(8,128)(2,1)} %bitcast.89), channel_id=1, source_target_pairs={{0,1},{1,0},{2,3},{3,2},{4,5},{5,4},{6,7},{7,6},{8,9},{9,8},{10,11... | collective-permute-start | bytes 589832 | tf_op jit(solution)/shard_map/ppermute | solution.py:135
  29.3 4.9 %copy-start.30 = (f32[4608]{0:T(1024)S(1)}, f32[4608]{0:T(1024)}, u32[]{:S(2)}) copy-start(f32[4608]{0:T(1024)} %param.21) | copy-start | bytes 55300
  29.3 5.6 %copy-start.13 = (bf16[6,128,256]{2,1,0:T(8,128)(2,1)S(1)}, bf16[6,128,256]{2,1,0:T(8,128)(2,1)}, u32[]{:S(2)}) copy-start(bf16[6,128,256]{2,1,0:T(8,128)(2,1)} %get-tuple-element.91) | copy-start | bytes 1179652
  31.2 12.2 %collective-permute-start.1 = (bf16[6,128,256]{1,2,0:T(8,128)(2,1)}, bf16[6,128,256]{1,2,0:T(8,128)(2,1)}, u32[]{:S(2)}, u32[]{:S(2)}) collective-permute-start(bf16[6,128,256]{1,2,0:T(8,128)(2,1)} %copy.82), channel_id=1, source_target_pairs={{0,1},{1,0},{2,3},{3,2},{4,5},{5,4},{6,7},{7,6},{8,9},{9,8},{10,11... | collective-permute-start | bytes 1179656 | tf_op jit(solution)/shard_map/ppermute | solution.py:135
  34.8 5.3 %copy-start.31 = (f32[768]{0:T(1024)}, f32[768]{0:T(1024)S(1)}, u32[]{:S(2)}) copy-start(f32[768]{0:T(1024)S(1)} %get-tuple-element.71) | copy-start | bytes 9220
  34.8 5.3 %copy-start.51 = (f32[768]{0:T(1024)}, f32[768]{0:T(1024)S(1)}, u32[]{:S(2)}) copy-start(f32[768]{0:T(1024)S(1)} %get-tuple-element.70) | copy-start | bytes 9220
  49.7 20.5 %collective-permute-start.2 = (f32[256,768]{1,0:T(8,128)S(1)}, f32[256,768]{1,0:T(8,128)S(1)}, u32[]{:S(2)}, u32[]{:S(2)}) collective-permute-start(f32[256,768]{1,0:T(8,128)S(1)} %fusion.64), channel_id=1, source_target_pairs={{0,1},{1,0},{2,3},{3,2},{4,5},{5,4},{6,7},{7,6},{8,9},{9,8},{10,11... | collective-permute-start | bytes 2359304 | tf_op jit(solution)/shard_map/ppermute | solution.py:135
  51.6 21.3 %collective-permute-start.4 = (bf16[128,768]{1,0:T(8,128)(2,1)S(1)}, bf16[128,768]{1,0:T(8,128)(2,1)S(1)}, u32[]{:S(2)}, u32[]{:S(2)}) collective-permute-start(bf16[128,768]{1,0:T(8,128)(2,1)S(1)} %bitcast.111), channel_id=1, source_target_pairs={{0,1},{1,0},{2,3},{3,2},{4,5},{5,4},{6,7},{7,6},{8,9},{9,8},{10,11... | collective-permute-start | bytes 589832 | tf_op jit(solution)/shard_map/ppermute | solution.py:135
  51.8 18.4 %copy-start.34 = (f32[768]{0:T(1024)S(1)}, f32[768]{0:T(1024)}, u32[]{:S(2)}) copy-start(f32[768]{0:T(1024)} %param.26) | copy-start | bytes 9220
  76.6 18.3 %collective-permute-start.5 = (f32[256,768]{1,0:T(8,128)S(1)}, f32[256,768]{1,0:T(8,128)}, u32[]{:S(2)}, u32[]{:S(2)}) collective-permute-start(f32[256,768]{1,0:T(8,128)S(1)} %fusion.9), channel_id=1, source_target_pairs={{0,1},{1,0},{2,3},{3,2},{4,5},{5,4},{6,7},{7,6},{8,9},{9,8},{10,11... | collective-permute-start | bytes 2359304 | tf_op jit(solution)/shard_map/ppermute | solution.py:135
  93.0 4.1 %copy-start.24 = (bf16[128,768]{1,0:T(8,128)(2,1)S(1)}, bf16[128,768]{1,0:T(8,128)(2,1)}, u32[]{:S(2)}) copy-start(bf16[128,768]{1,0:T(8,128)(2,1)} %copy-done.23) | copy-start | bytes 589828
  93.0 4.1 %copy-start.37 = (f32[768]{0:T(1024)S(1)}, f32[768]{0:T(1024)}, u32[]{:S(2)}) copy-start(f32[768]{0:T(1024)} %get-tuple-element.116) | copy-start | bytes 9220
  104.3 4.2 %copy-start.55 = (bf16[6,64,256]{2,1,0:T(8,128)(2,1)}, bf16[6,64,256]{2,1,0:T(8,128)(2,1)S(1)}, u32[]{:S(2)}) copy-start(bf16[6,64,256]{2,1,0:T(8,128)(2,1)S(1)} %convolution_convert_fusion.7) | copy-start | bytes 589828
  113.4 9.2 %collective-permute-start.3 = (bf16[256,768]{1,0:T(8,128)(2,1)}, bf16[256,768]{1,0:T(8,128)(2,1)}, u32[]{:S(2)}, u32[]{:S(2)}) collective-permute-start(bf16[256,768]{1,0:T(8,128)(2,1)} %convolution_convert_fusion.6), channel_id=1, source_target_pairs={{0,1},{1,0},{2,3},{3,2},{4,5},{5,4},{6,7},{7,6},{8,9},{9,8},{10,11... | collective-permute-start | bytes 1179656 | tf_op jit(solution)/shard_map/ppermute | solution.py:135
  114.7 9.7 %copy-start.2 = (bf16[6,256,256]{1,2,0:T(8,128)(2,1)S(1)}, bf16[6,256,256]{1,2,0:T(8,128)(2,1)}, u32[]{:S(2)}) copy-start(bf16[6,256,256]{1,2,0:T(8,128)(2,1)} %copy-done.1) | copy-start | bytes 2359300
  125.4 9.5 %collective-permute-start.7 = (bf16[6,128,256]{1,2,0:T(8,128)(2,1)}, bf16[6,128,256]{1,2,0:T(8,128)(2,1)}, u32[]{:S(2)}, u32[]{:S(2)}) collective-permute-start(bf16[6,128,256]{1,2,0:T(8,128)(2,1)} %get-tuple-element.90), channel_id=1, source_target_pairs={{0,1},{1,0},{2,3},{3,2},{4,5},{5,4},{6,7},{7,6},{8,9},{9,8},{10,11... | collective-permute-start | bytes 1179656 | tf_op jit(solution)/shard_map/ppermute | solution.py:135
  133.9 42.8 %collective-permute-start.6 = (bf16[256,768]{1,0:T(8,128)(2,1)}, bf16[256,768]{1,0:T(8,128)(2,1)}, u32[]{:S(2)}, u32[]{:S(2)}) collective-permute-start(bf16[256,768]{1,0:T(8,128)(2,1)} %convolution_convert_fusion.5), channel_id=1, source_target_pairs={{0,1},{1,0},{2,3},{3,2},{4,5},{5,4},{6,7},{7,6},{8,9},{9,8},{10,11... | collective-permute-start | bytes 1179656 | tf_op jit(solution)/shard_map/ppermute | solution.py:135
  139.8 36.9 %copy-start.44 = (f32[256]{0:T(256)S(1)}, f32[256]{0:T(256)}, u32[]{:S(2)}) copy-start(f32[256]{0:T(256)} %copy-done.42) | copy-start | bytes 3076
  139.8 36.9 %copy-start.50 = (f32[256]{0:T(256)S(1)}, f32[256]{0:T(256)}, u32[]{:S(2)}) copy-start(f32[256]{0:T(256)} %copy-done.47) | copy-start | bytes 3076
  175.7 5.5 %collective-permute-start.12 = (f32[1,3328]{1,0:T(1,128)S(1)}, f32[1,3328]{1,0:T(1,128)S(1)}, u32[]{:S(2)}, u32[]{:S(2)}) collective-permute-start(f32[1,3328]{1,0:T(1,128)S(1)} %broadcast_in_dim.62), channel_id=1, source_target_pairs={{0,1},{1,0},{2,3},{3,2},{4,5},{5,4},{6,7},{7,6},{8,9},{9,8},{10,11... | collective-permute-start | bytes 39944 | tf_op jit(solution)/shard_map/ppermute | solution.py:135
  178.6 18.7 %copy-start.5 = (f32[256,768]{1,0:T(8,128)S(1)}, f32[256,768]{1,0:T(8,128)}, u32[]{:S(2)}) copy-start(f32[256,768]{1,0:T(8,128)} %copy-done.3) | copy-start | bytes 2359300
  178.6 18.7 %copy-start.53 = (f32[128]{0:T(128)S(1)}, f32[128]{0:T(128)}, u32[]{:S(2)}) copy-start(f32[128]{0:T(128)} %dynamic-slice.14) | copy-start | bytes 1540
  181.1 1.2 collective-permute-start.8
  181.2 2.8 %collective-permute-start.13 = (f32[1,3328]{1,0:T(1,128)S(1)}, f32[1,3328]{1,0:T(1,128)S(1)}, u32[]{:S(2)}, u32[]{:S(2)}) collective-permute-start(f32[1,3328]{1,0:T(1,128)S(1)} %reshape_add_fusion), channel_id=1, source_target_pairs={{0,2},{2,0},{4,6},{6,4},{8,10},{10,8},{12,14},{14,12},{16,18},{18,... | collective-permute-start | bytes 39944 | tf_op jit(solution)/shard_map/ppermute | solution.py:168
  182.4 7.4 %collective-permute-start.9 = (f32[2,5632]{1,0:T(2,128)S(1)}, f32[2,5632]{1,0:T(2,128)S(1)}, u32[]{:S(2)}, u32[]{:S(2)}) collective-permute-start(f32[2,5632]{1,0:T(2,128)S(1)} %maximum_select_fusion.8), channel_id=1, source_target_pairs={{0,4},{2,6},{4,0},{6,2},{8,12},{10,14},{12,8},{14,10},{16,20},{18,... | collective-permute-start | bytes 135176 | tf_op jit(solution)/shard_map/ppermute | solution.py:153
  184.0 4.1 %collective-permute-start.14 = (f32[1,3328]{1,0:T(1,128)S(1)}, f32[1,3328]{1,0:T(1,128)S(1)}, u32[]{:S(2)}, u32[]{:S(2)}) collective-permute-start(f32[1,3328]{1,0:T(1,128)S(1)} %add.188), channel_id=1, source_target_pairs={{0,4},{2,6},{4,0},{6,2},{8,12},{10,14},{12,8},{14,10},{16,20},{18,... | collective-permute-start | bytes 39944 | tf_op jit(solution)/shard_map/ppermute | solution.py:168
  188.1 3.9 %collective-permute-start.15 = (f32[1,3328]{1,0:T(1,128)S(1)}, f32[1,3328]{1,0:T(1,128)S(1)}, u32[]{:S(2)}, u32[]{:S(2)}) collective-permute-start(f32[1,3328]{1,0:T(1,128)S(1)} %add.189), channel_id=1, source_target_pairs={{0,8},{2,10},{4,12},{6,14},{8,0},{10,2},{12,4},{14,6},{16,24},{18,... | collective-permute-start | bytes 39944 | tf_op jit(solution)/shard_map/ppermute | solution.py:168
  189.8 4.7 %collective-permute-start.10 = (f32[4,5632]{1,0:T(4,128)S(1)}, f32[4,5632]{1,0:T(4,128)S(1)}, u32[]{:S(2)}, u32[]{:S(2)}) collective-permute-start(f32[4,5632]{1,0:T(4,128)S(1)} %maximum_select_fusion.7), channel_id=1, source_target_pairs={{0,8},{2,10},{4,12},{6,14},{8,0},{10,2},{12,4},{14,6},{16,24},{18,... | collective-permute-start | bytes 270344 | tf_op jit(solution)/shard_map/ppermute | solution.py:153
  192.0 6.2 %collective-permute-start.16 = (f32[1,3328]{1,0:T(1,128)S(1)}, f32[1,3328]{1,0:T(1,128)S(1)}, u32[]{:S(2)}, u32[]{:S(2)}) collective-permute-start(f32[1,3328]{1,0:T(1,128)S(1)} %add.190), channel_id=1, source_target_pairs={{0,16},{2,18},{4,20},{6,22},{8,24},{10,26},{12,28},{14,30},{16,0},... | collective-permute-start | bytes 39944 | tf_op jit(solution)/shard_map/ppermute | solution.py:168
  194.6 10.0 %collective-permute-start.11 = (f32[8,5632]{1,0:T(8,128)S(1)}, f32[8,5632]{1,0:T(8,128)S(1)}, u32[]{:S(2)}, u32[]{:S(2)}) collective-permute-start(f32[8,5632]{1,0:T(8,128)S(1)} %maximum_select_fusion.5), channel_id=1, source_target_pairs={{0,16},{2,18},{4,20},{6,22},{8,24},{10,26},{12,28},{14,30},{16,0},... | collective-permute-start | bytes 540680 | tf_op jit(solution)/shard_map/ppermute | solution.py:153
  (42 other events, 107.0 us)
Sparse Core Ops, SparseCore 0:
  110.9 113.7 reduce-scatter.1

commit v3 on v2

--- a/solution.py
+++ b/solution.py
@@ -230,6 +230,7 @@
 
     x_rows = whole_rows(layer_input[0], first)
     g_rows = whole_rows(output_grad[0], first)
+    out_weight_all = whole_rows(out_weight, first)
 
     positions = jnp.arange(length, dtype=jnp.int32)
     valid = (positions < chain_lengths[0]) & ((residue_mask[0] == 1) | (positions == 0))
@@ -266,8 +267,12 @@
     probs_low = attn_probs.astype(jnp.bfloat16)
     mixed = jnp.einsum("hqk,khe->qhe", probs_low, values, preferred_element_type=jnp.float32)
     mixed = mixed.reshape(length, proj).astype(jnp.bfloat16)
-    attn_part = jnp.dot(mixed, out_weight, preferred_element_type=jnp.float32)
-    attn_branch = head_sum(attn_part) + out_bias
+    mixed_all = jnp.where(
+        first,
+        jnp.concatenate([mixed, swap_heads(mixed)], axis=1),
+        jnp.concatenate([swap_heads(mixed), mixed], axis=1),
+    )
+    attn_branch = jnp.dot(mixed_all, out_weight_all, preferred_element_type=jnp.float32) + out_bias
     sig_a = jax.nn.sigmoid(gate_a)
     middle = residues + sig_a * attn_branch
 
@@ -336,7 +341,7 @@
         normed_a, d_qkv, (((0,), (0,)), ((), ())), preferred_element_type=jnp.float32
     )
 
-    packed = jnp.zeros((width, 4 * proj + 3 * ffn), jnp.bfloat16)
+    packed = lax.optimization_barrier(jnp.zeros((width, 4 * proj + 3 * ffn), jnp.bfloat16))
     packed = lax.dynamic_update_slice(packed, gate_up_grad.astype(jnp.bfloat16), (0, 4 * proj))
     packed = lax.dynamic_update_slice(
         packed, down_grad_t.astype(jnp.bfloat16), (0, 4 * proj + 2 * ffn)

time: 238 us -> 221 us (0.929)
  waiting for transfers between devices: 49 us -> 41.1 us
  local copies, waits for them, and re-layouts: 42.8 us -> 38 us
    ppermute x9 -> x10, waiting for transfers between devices: 23.7 us -> 15.7 us  [swap_heads(): return lax.ppermute(values, 'head', [(0, 1), (1, 0)])]
    dynamic_update_slice x1 -> x0, local copies, waits for them, and re-layouts: 7.16 us -> none  [shards(): lax.dynamic_update_slice(packed, gate_up_grad.astype(jnp.bfloat16), (0, 4...]
    broadcast_in_dim x0 -> x1, local copies, waits for them, and re-layouts: none -> 4.79 us  [shards(): jnp.zeros((width, 4 * proj + 3 * ffn), jnp.bfloat16)]
    ppermute x9 -> x10, starting transfers between devices: 11.4 us -> 9.68 us  [swap_heads(): return lax.ppermute(values, 'head', [(0, 1), (1, 0)])]
    unnamed x127 -> x117, local copies, waits for them, and re-layouts: 19.2 us -> 17.6 us
  transfers between devices with their start and end apart: 18 -> 19, of which waited for: 10 -> 10; matrix products, arithmetic and copies ran while one was open for 30% -> 34% of each run, Pallas kernels for 21% -> 22%
where the time goes in v3:
time: 221 us; the launch traced here: 220 us
  Pallas kernels  49.2 us (22%)
  matrix products  41.8 us (19%)
  waiting for transfers between devices  41.1 us (19%)
  local copies, waits for them, and re-layouts  38 us (17%)
  starting transfers between devices  19.7 us (9%)
  between operations  15.5 us (7%)
  other arithmetic  14.9 us (7%)
    pallas_call x1, Pallas kernels, pair_backward(): pl.pallas_call(pair_backward_kernel, grid=(m // tile,), in_specs=[pl.Bloc...  34 us
    unnamed x117, local copies, waits for them, and re-layouts  17.6 us
    ppermute x10, waiting for transfers between devices, swap_heads(): return lax.ppermute(values, 'head', [(0, 1), (1, 0)])  15.7 us
    pallas_call x1, Pallas kernels, pair_forward(): pl.pallas_call(pair_forward_kernel, grid=(m // tile,), in_specs=[pl.Block...  15.2 us
    reduce_scatter x1, waiting for transfers between devices, shards(): lax.psum_scatter(packed, 'dp', scatter_dimension=0, tiled=True)  14.4 us
    ppermute x10, starting transfers between devices, swap_heads(): return lax.ppermute(values, 'head', [(0, 1), (1, 0)])  9.68 us
    ppermute x4, waiting for transfers between devices, dp_gather(): other = lax.ppermute(block, 'dp', [(i, i ^ step) for i in range(count)])  5.86 us
    ppermute x4, waiting for transfers between devices, dp_sum(): other = lax.ppermute(values, 'dp', [(i, i ^ step) for i in range(count)])  5.18 us
  transfers between devices with their start and end apart: 19, of which 10 were waited for; matrix products, arithmetic and copies ran while one was open for 34% of the time, Pallas kernels for 22%

profile of v3, /device:TPU:0, one launch (start us, length us, event | category | flops | bytes accessed | tf_op | source)
XLA Modules:
  0.0 220.1 jit_solution(17844440199340061627)
XLA Ops:
  7.2 3.0 %collective-permute-start = (bf16[128,768]{1,0:T(8,128)(2,1)}, bf16[128,768]{1,0:T(8,128)(2,1)S(1)}, u32[]{:S(2)}, u32[]{:S(2)}) collective-permute-start(bf16[128,768]{1,0:T(8,128)(2,1)} %bitcast.91), channel_id=1, source_target_pairs={{0,1},{1,0},{2,3},{3,2},{4,5},{5,4},{6,7},{7,6},{8,9},{9,8},{10,11... | collective-permute-start | bytes 589832 | tf_op jit(solution)/shard_map/ppermute | solution.py:135
  11.7 15.2 %shard_map.246 = bf16[12,32768]{1,0:T(8,128)(2,1)} custom-call(bf16[32768,256]{1,0:T(8,128)(2,1)} %bitcast.80, f32[1,256]{1,0:T(1,128)} %bitcast.122, bf16[16,256]{1,0:T(8,128)(2,1)} %pad.8.wt_ref), custom_call_target="tpu_custom_call" | custom-call | flops 352321536 | bytes 17563648 | tf_op jit(solution)/shard_map/pallas_call | solution.py:38
  29.3 2.0 copy.90
  31.3 1.9 collective-permute-start.1
  33.9 2.1 convolution_reduce_fusion
  38.2 3.9 %copy.66 = bf16[768,3,384]{0,2,1:T(8,128)(2,1)} copy(bf16[768,3,384]{2,0,1:T(8,128)(2,1)} %param.22) | data formatting | bytes 3538944 | tf_op args[7]
  43.1 2.3 %convolution_convert_fusion.3 = bf16[256,1152]{1,0:T(8,128)(2,1)S(1)} fusion(bf16[768,1152]{0,1:T(8,128)(2,1)} %bitcast.89, f32[768]{0:T(1024)S(1)} %get-tuple-element.57, f32[768]{0:T(1024)S(1)} %get-tuple-element.58, f32[256]{0:T(256)S(1)} %add_rsqrt_fusion.1, f32[256]{0:T(256)S(1)} %broadcast_multiply_fusion.5, bf16[128,768]{1,0:T(8,128)(2,1)S(1)} %bitcast.94, ...), kind=kOutput, calls=%fused_computation.7 | convolution fusion | flops 456228864 | bytes 2760705 | tf_op jit(solution)/shard_map/dot_general | solution.py:256
  45.9 3.3 %fusion.77 = (f32[6,256]{1,0:T(8,128)S(1)}, f32[6,256,256]{1,2,0:T(8,128)}) fusion(pred[256]{0:T(512)(128)(4,1)} %or_and_fusion, bf16[256,6,64]{0,2,1:T(8,128)(2,1)S(1)} %bitcast.103, bf16[256,6,64]{0,2,1:T(8,128)(2,1)S(1)} %bitcast.101, bf16[6,128,256]{1,2,0:T(8,128)(2,1)} %copy.89, bf16[6,128,256]{1,2,0:T(8,128)(2,1)} %collective-permute-done.1, pred[]{:T(512)S(6)} %eq.44), kind=kOutput, calls=%fused_computation.177 | convolution fusion | flops 56230144 | bytes 2758913 | tf_op jit(solution)/shard_map/sub | solution.py:264
  51.9 1.9 collective-permute-start.5
  53.8 3.6 %copy.93 = bf16[96,8,2,1536]{3,1,2,0:T(8,128)(2,1)S(1)} copy(bf16[96,8,2,1536]{3,2,1,0:T(2,128)(2,1)} %bitcast.82) | data formatting | bytes 9437184
  58.1 1.7 collective-permute-done.2
  59.8 2.2 %fusion.75 = (f32[256]{0:T(256)S(1)}, f32[256,768]{1,0:T(8,128)S(1)}, f32[256,768]{1,0:T(8,128)S(1)}) fusion(f32[768]{0:T(1024)S(1)} %get-tuple-element.103, bf16[128,768]{1,0:T(8,128)(2,1)S(1)} %bitcast.95, bf16[128,768]{1,0:T(8,128)(2,1)S(1)} %collective-permute-done, pred[]{:T(512)S(6)} %eq.44, f32[768]{0:T(1024)S(1)} %copy-done.47, ...), kind=kOutput, calls=%fused_computation.175 | convolution fusion | flops 311820032 | bytes 3546113 | tf_op jit(solution)/shard_map/dot_general | solution.py:275
  66.6 4.8 %broadcast_in_dim.64 = bf16[768,6144]{1,0:T(8,128)(2,1)} broadcast(bf16[]{:T(256)} %constant.30.clone.1), dimensions={} | broadcast | bytes 9437186 | tf_op jit(solution)/shard_map/broadcast_in_dim | solution.py:344
  71.4 3.9 %fusion.1 = bf16[768,6144]{1,0:T(8,128)(2,1)} fusion(bf16[768,6144]{1,0:T(8,128)(2,1)} %broadcast_in_dim.64, bf16[256,1536]{1,0:T(8,128)(2,1)S(1)} %get-tuple-element.69, bf16[256,1536]{1,0:T(8,128)(2,1)S(1)} %get-tuple-element.68, f32[256,768]{1,0:T(8,128)S(1)} %get-tuple-element.67, f32[768]{0:T(1024)S(1)} %copy-done.45, f32[768]{0:T(1024)S(1)} %get-tuple-element.55, ...), kind=kOutput, calls=%fused_computation.2 | convolution fusion | flops 1214447616 | bytes 7086080 | tf_op jit(solution)/shard_map/dot_general | solution.py:302
  75.3 2.3 %fusion.2 = bf16[768,6144]{1,0:T(8,128)(2,1)} fusion(bf16[768,6144]{1,0:T(8,128)(2,1)} %fusion.1, bf16[256,1536]{1,0:T(8,128)(2,1)S(1)} %get-tuple-element.70, f32[768]{0:T(1024)S(1)} %get-tuple-element.60, bf16[128,768]{1,0:T(8,128)(2,1)S(1)} %collective-permute-done.5, bf16[128,768]{1,0:T(8,128)(2,1)S(1)} %bitcast.110, pred[]{:T(512)S(6)} %eq.44), kind=kOutput, calls=%fused_computation.5 | convolution fusion | flops 607518720 | bytes 3542017 | tf_op jit(solution)/shard_map/dot_general | solution.py:293
  77.6 5.2 %collective-permute-done.6 = f32[256,768]{1,0:T(8,128)S(1)} collective-permute-done((f32[256,768]{1,0:T(8,128)S(1)}, f32[256,768]{1,0:T(8,128)S(1)}, u32[]{:S(2)}, u32[]{:S(2)}) %collective-permute-start.6) | collective-permute-done | bytes 786464 | tf_op jit(solution)/shard_map/ppermute | solution.py:135
  86.6 1.9 convolution_convert_fusion.7
  92.7 2.2 fusion.3
  94.9 2.7 %convolution_convert_fusion.6 = bf16[256,768]{1,0:T(8,128)(2,1)} fusion(bf16[256,1536]{1,0:T(8,128)(2,1)} %copy-done.50, bf16[1536,768]{1,0:T(8,128)(2,1)S(1)} %copy-done), kind=kOutput, calls=%fused_computation.23 | convolution fusion | flops 604176384 | bytes 3538944 | tf_op jit(solution)/shard_map/dot_general | solution.py:285
  98.6 7.1 %collective-permute-done.4 = bf16[256,768]{1,0:T(8,128)(2,1)} collective-permute-done((bf16[256,768]{1,0:T(8,128)(2,1)}, bf16[256,768]{1,0:T(8,128)(2,1)}, u32[]{:S(2)}, u32[]{:S(2)}) %collective-permute-start.4) | collective-permute-done | bytes 393248 | tf_op jit(solution)/shard_map/ppermute | solution.py:135
  105.7 1.9 fusion.24
  109.7 1.9 copy.80
  112.9 3.4 %convolution_convert_fusion.5 = bf16[256,768]{1,0:T(8,128)(2,1)} fusion(bf16[768,1152]{0,1:T(8,128)(2,1)} %bitcast.90, bf16[256,384]{0,1:T(8,128)(2,1)} %bitcast.128, bf16[256,384]{0,1:T(8,128)(2,1)S(1)} %bitcast.114, bf16[256,384]{0,1:T(8,128)(2,1)} %bitcast.116), kind=kOutput, calls=%fused_computation.22 | convolution fusion | flops 454950912 | bytes 2752512 | tf_op jit(solution)/shard_map/dot_general | solution.py:353
  119.6 1.9 copy.81
  124.5 34.0 %shard_map.247 = (bf16[32768,256]{1,0:T(8,128)(2,1)}, f32[16,256]{1,0:T(8,128)}, f32[1,256]{1,0:T(1,128)}) custom-call(bf16[32768,256]{1,0:T(8,128)(2,1)} %bitcast.81, bf16[16,32768]{1,0:T(8,128)(2,1)} %pad.9.ds_ref, f32[1,256]{1,0:T(1,128)} %bitcast.123, bf16[16,256]{1,0:T(8,128)(2,1)} %pad.8.wt_ref), custom_call_target="tpu_custom_call" | custom-call | flops 704643072 | bytes 34603008 | tf_op jit(solution)/shard_map/pallas_call | solution.py:85
  162.3 2.5 %convolution_multiply_fusion.2 = f32[1,256]{1,0:T(1,128)} fusion(bf16[256,4608]{1,0:T(8,128)(2,1)S(1)} %copy-done.6, f32[1,4608]{1,0:T(1,128)S(1)} %get-tuple-element.87, f32[1,256]{1,0:T(1,128)S(1)} %copy-done.32), kind=kOutput, calls=%fused_computation.45 | convolution fusion | flops 14157824 | bytes 2379776 | tf_op jit(solution)/shard_map/dot_general | solution.py:392
  168.3 3.6 %collective-permute-done.15 = f32[1,3328]{1,0:T(1,128)S(1)} collective-permute-done((f32[1,3328]{1,0:T(1,128)S(1)}, f32[1,3328]{1,0:T(1,128)S(1)}, u32[]{:S(2)}, u32[]{:S(2)}) %collective-permute-start.15) | collective-permute-done | bytes 13344 | tf_op jit(solution)/shard_map/ppermute | solution.py:168
  175.9 2.3 %collective-permute-start.17 = (f32[1,3328]{1,0:T(1,128)S(1)}, f32[1,3328]{1,0:T(1,128)S(1)}, u32[]{:S(2)}, u32[]{:S(2)}) collective-permute-start(f32[1,3328]{1,0:T(1,128)S(1)} %add.184), channel_id=1, source_target_pairs={{0,16},{2,18},{4,20},{6,22},{8,24},{10,26},{12,28},{14,30},{16,0},... | collective-permute-start | bytes 39944 | tf_op jit(solution)/shard_map/ppermute | solution.py:168
  178.4 2.7 %collective-permute-start.12 = (f32[8,5632]{1,0:T(8,128)S(1)}, f32[8,5632]{1,0:T(8,128)S(1)}, u32[]{:S(2)}, u32[]{:S(2)}) collective-permute-start(f32[8,5632]{1,0:T(8,128)S(1)} %maximum_select_fusion.9), channel_id=1, source_target_pairs={{0,16},{2,18},{4,20},{6,22},{8,24},{10,26},{12,28},{14,30},{16,0},... | collective-permute-start | bytes 540680 | tf_op jit(solution)/shard_map/ppermute | solution.py:153
  183.4 5.2 %collective-permute-done.12 = f32[8,5632]{1,0:T(8,128)S(1)} collective-permute-done((f32[8,5632]{1,0:T(8,128)S(1)}, f32[8,5632]{1,0:T(8,128)S(1)}, u32[]{:S(2)}, u32[]{:S(2)}) %collective-permute-start.12) | collective-permute-done | bytes 180256 | tf_op jit(solution)/shard_map/ppermute | solution.py:153
  189.9 4.2 %fusion.45 = f32[256,4608]{1,0:T(8,128)} fusion(bf16[16,256]{1,0:T(8,128)(2,1)S(1)} %multiply_convert_fusion.7, f32[16,5632]{1,0:T(8,128)S(1)} %maximum_select_fusion.8), kind=kOutput, calls=%fused_computation.102 | convolution fusion | flops 226492416 | bytes 5021696 | tf_op jit(solution)/shard_map/dot_general | solution.py:390
  194.1 14.4 %reduce-scatter.2.cloned.1.call-done = bf16[48,6144]{1,0:T(8,128)(2,1)} async-done(((bf16[768,6144]{1,0:T(8,128)(2,1)}), bf16[48,6144]{1,0:T(8,128)(2,1)}) %reduce-scatter.2.cloned.1.call-update) | async-done | bytes 589840 | tf_op jit(solution)/shard_map/reduce_scatter | solution.py:351
  (217 shorter events, 53.3 us)
Async XLA Ops:
  7.2 56.6 %copy-start = (bf16[1536,768]{1,0:T(8,128)(2,1)S(1)}, bf16[1536,768]{1,0:T(8,128)(2,1)}, u32[]{:S(2)}) copy-start(bf16[1536,768]{1,0:T(8,128)(2,1)} %param.28) | copy-start | bytes 7077892
  7.2 201.3 %reduce-scatter.2.cloned.1.call-start = ((), (), s32[]{:S(2)}) async-start(), calls=%async_computation.1 | async-start | bytes 10027008 | tf_op jit(solution)/shard_map/reduce_scatter | solution.py:351
  7.2 35.4 %collective-permute-start = (bf16[128,768]{1,0:T(8,128)(2,1)}, bf16[128,768]{1,0:T(8,128)(2,1)S(1)}, u32[]{:S(2)}, u32[]{:S(2)}) collective-permute-start(bf16[128,768]{1,0:T(8,128)(2,1)} %bitcast.91), channel_id=1, source_target_pairs={{0,1},{1,0},{2,3},{3,2},{4,5},{5,4},{6,7},{7,6},{8,9},{9,8},{10,11... | collective-permute-start | bytes 589832 | tf_op jit(solution)/shard_map/ppermute | solution.py:135
  10.3 47.8 %collective-permute-start.3 = (bf16[384,768]{1,0:T(8,128)(2,1)}, bf16[384,768]{1,0:T(8,128)(2,1)}, u32[]{:S(2)}, u32[]{:S(2)}) collective-permute-start(bf16[384,768]{1,0:T(8,128)(2,1)} %param.25), channel_id=1, source_target_pairs={{0,1},{1,0},{2,3},{3,2},{4,5},{5,4},{6,7},{7,6},{8,9},{9,8},{10,11... | collective-permute-start | bytes 1769480 | tf_op jit(solution)/shard_map/ppermute | solution.py:135
  29.3 6.7 %copy-start.23 = (f32[4608]{0:T(1024)S(1)}, f32[4608]{0:T(1024)}, u32[]{:S(2)}) copy-start(f32[4608]{0:T(1024)} %param.21) | copy-start | bytes 55300
  29.3 8.0 %copy-start.9 = (bf16[6,128,256]{2,1,0:T(8,128)(2,1)S(1)}, bf16[6,128,256]{2,1,0:T(8,128)(2,1)}, u32[]{:S(2)}) copy-start(bf16[6,128,256]{2,1,0:T(8,128)(2,1)} %get-tuple-element.78) | copy-start | bytes 1179652
  31.3 14.6 %collective-permute-start.1 = (bf16[6,128,256]{1,2,0:T(8,128)(2,1)}, bf16[6,128,256]{1,2,0:T(8,128)(2,1)}, u32[]{:S(2)}, u32[]{:S(2)}) collective-permute-start(bf16[6,128,256]{1,2,0:T(8,128)(2,1)} %copy.90), channel_id=1, source_target_pairs={{0,1},{1,0},{2,3},{3,2},{4,5},{5,4},{6,7},{7,6},{8,9},{9,8},{10,11... | collective-permute-start | bytes 1179656 | tf_op jit(solution)/shard_map/ppermute | solution.py:135
  51.0 6.5 %copy-start.15 = (bf16[6,64,256]{2,1,0:T(8,128)(2,1)}, bf16[6,64,256]{2,1,0:T(8,128)(2,1)S(1)}, u32[]{:S(2)}) copy-start(bf16[6,64,256]{2,1,0:T(8,128)(2,1)S(1)} %convolution_convert_fusion.9) | copy-start | bytes 589828
  51.8 8.0 %collective-permute-start.2 = (bf16[256,384]{1,0:T(8,128)(2,1)}, bf16[256,384]{1,0:T(8,128)(2,1)S(1)}, u32[]{:S(2)}, u32[]{:S(2)}) collective-permute-start(bf16[256,384]{1,0:T(8,128)(2,1)} %copy.74), channel_id=1, source_target_pairs={{0,1},{1,0},{2,3},{3,2},{4,5},{5,4},{6,7},{7,6},{8,9},{9,8},{10,11... | collective-permute-start | bytes 589832 | tf_op jit(solution)/shard_map/ppermute | solution.py:135
  51.9 11.9 %collective-permute-start.5 = (bf16[128,768]{1,0:T(8,128)(2,1)S(1)}, bf16[128,768]{1,0:T(8,128)(2,1)S(1)}, u32[]{:S(2)}, u32[]{:S(2)}) collective-permute-start(bf16[128,768]{1,0:T(8,128)(2,1)S(1)} %bitcast.108), channel_id=1, source_target_pairs={{0,1},{1,0},{2,3},{3,2},{4,5},{5,4},{6,7},{7,6},{8,9},{9,8},{10,11... | collective-permute-start | bytes 589832 | tf_op jit(solution)/shard_map/ppermute | solution.py:135
  53.8 6.0 %copy-start.47 = (f32[768]{0:T(1024)S(1)}, f32[768]{0:T(1024)}, u32[]{:S(2)}) copy-start(f32[768]{0:T(1024)} %param.26) | copy-start | bytes 9220
  62.0 21.7 %copy-start.4 = (f32[256,768]{1,0:T(8,128)}, f32[256,768]{1,0:T(8,128)S(1)}, u32[]{:S(2)}) copy-start(f32[256,768]{1,0:T(8,128)S(1)} %get-tuple-element.67) | copy-start | bytes 2359300
  63.8 20.0 %copy-start.18 = (bf16[128,768]{1,0:T(8,128)(2,1)}, bf16[128,768]{1,0:T(8,128)(2,1)S(1)}, u32[]{:S(2)}) copy-start(bf16[128,768]{1,0:T(8,128)(2,1)S(1)} %collective-permute-done.5) | copy-start | bytes 589828
  65.1 10.3 %copy-start.50 = (bf16[256,1536]{1,0:T(8,128)(2,1)}, bf16[256,1536]{1,0:T(8,128)(2,1)S(1)}, u32[]{:S(2)}) copy-start(bf16[256,1536]{1,0:T(8,128)(2,1)S(1)} %get-tuple-element.70) | copy-start | bytes 2359300
  66.5 16.2 %collective-permute-start.6 = (f32[256,768]{1,0:T(8,128)S(1)}, f32[256,768]{1,0:T(8,128)S(1)}, u32[]{:S(2)}, u32[]{:S(2)}) collective-permute-start(f32[256,768]{1,0:T(8,128)S(1)} %fusion.16), channel_id=1, source_target_pairs={{0,1},{1,0},{2,3},{3,2},{4,5},{5,4},{6,7},{7,6},{8,9},{9,8},{10,11... | collective-permute-start | bytes 2359304 | tf_op jit(solution)/shard_map/ppermute | solution.py:135
  94.9 10.8 %copy-start.26 = (f32[768]{0:T(1024)S(1)}, f32[768]{0:T(1024)}, u32[]{:S(2)}) copy-start(f32[768]{0:T(1024)} %get-tuple-element.59) | copy-start | bytes 9220
  97.6 8.1 %collective-permute-start.4 = (bf16[256,768]{1,0:T(8,128)(2,1)}, bf16[256,768]{1,0:T(8,128)(2,1)}, u32[]{:S(2)}, u32[]{:S(2)}) collective-permute-start(bf16[256,768]{1,0:T(8,128)(2,1)} %convolution_convert_fusion.6), channel_id=1, source_target_pairs={{0,1},{1,0},{2,3},{3,2},{4,5},{5,4},{6,7},{7,6},{8,9},{9,8},{10,11... | collective-permute-start | bytes 1179656 | tf_op jit(solution)/shard_map/ppermute | solution.py:135
  108.6 11.0 %collective-permute-start.8 = (bf16[6,128,256]{1,2,0:T(8,128)(2,1)}, bf16[6,128,256]{1,2,0:T(8,128)(2,1)}, u32[]{:S(2)}, u32[]{:S(2)}) collective-permute-start(bf16[6,128,256]{1,2,0:T(8,128)(2,1)} %get-tuple-element.77), channel_id=1, source_target_pairs={{0,1},{1,0},{2,3},{3,2},{4,5},{5,4},{6,7},{7,6},{8,9},{9,8},{10,11... | collective-permute-start | bytes 1179656 | tf_op jit(solution)/shard_map/ppermute | solution.py:135
  116.3 44.1 %collective-permute-start.7 = (bf16[256,768]{1,0:T(8,128)(2,1)}, bf16[256,768]{1,0:T(8,128)(2,1)}, u32[]{:S(2)}, u32[]{:S(2)}) collective-permute-start(bf16[256,768]{1,0:T(8,128)(2,1)} %convolution_convert_fusion.5), channel_id=1, source_target_pairs={{0,1},{1,0},{2,3},{3,2},{4,5},{5,4},{6,7},{7,6},{8,9},{9,8},{10,11... | collective-permute-start | bytes 1179656 | tf_op jit(solution)/shard_map/ppermute | solution.py:135
  124.5 35.9 %copy-start.35 = (f32[256]{0:T(256)S(1)}, f32[256]{0:T(256)}, u32[]{:S(2)}) copy-start(f32[256]{0:T(256)} %copy-done.33) | copy-start | bytes 3076
  124.5 36.0 %copy-start.42 = (f32[256]{0:T(256)S(1)}, f32[256]{0:T(256)}, u32[]{:S(2)}) copy-start(f32[256]{0:T(256)} %copy-done.39) | copy-start | bytes 3076
  160.3 4.5 %collective-permute-start.13 = (f32[1,3328]{1,0:T(1,128)S(1)}, f32[1,3328]{1,0:T(1,128)S(1)}, u32[]{:S(2)}, u32[]{:S(2)}) collective-permute-start(f32[1,3328]{1,0:T(1,128)S(1)} %broadcast_in_dim.65), channel_id=1, source_target_pairs={{0,1},{1,0},{2,3},{3,2},{4,5},{5,4},{6,7},{7,6},{8,9},{9,8},{10,11... | collective-permute-start | bytes 39944 | tf_op jit(solution)/shard_map/ppermute | solution.py:135
  162.3 18.8 %copy-start.3 = (f32[256,768]{1,0:T(8,128)S(1)}, f32[256,768]{1,0:T(8,128)}, u32[]{:S(2)}) copy-start(f32[256,768]{1,0:T(8,128)} %copy-done.1) | copy-start | bytes 2359300
  162.3 18.8 %copy-start.46 = (f32[128]{0:T(128)S(1)}, f32[128]{0:T(128)}, u32[]{:S(2)}) copy-start(f32[128]{0:T(128)} %dynamic-slice.14) | copy-start | bytes 1540
  164.8 1.2 collective-permute-start.9
  164.9 2.9 %collective-permute-start.14 = (f32[1,3328]{1,0:T(1,128)S(1)}, f32[1,3328]{1,0:T(1,128)S(1)}, u32[]{:S(2)}, u32[]{:S(2)}) collective-permute-start(f32[1,3328]{1,0:T(1,128)S(1)} %reshape_add_fusion), channel_id=1, source_target_pairs={{0,2},{2,0},{4,6},{6,4},{8,10},{10,8},{12,14},{14,12},{16,18},{18,... | collective-permute-start | bytes 39944 | tf_op jit(solution)/shard_map/ppermute | solution.py:168
  166.1 7.4 %collective-permute-start.10 = (f32[2,5632]{1,0:T(2,128)S(1)}, f32[2,5632]{1,0:T(2,128)S(1)}, u32[]{:S(2)}, u32[]{:S(2)}) collective-permute-start(f32[2,5632]{1,0:T(2,128)S(1)} %maximum_select_fusion.12), channel_id=1, source_target_pairs={{0,4},{2,6},{4,0},{6,2},{8,12},{10,14},{12,8},{14,10},{16,20},{18,... | collective-permute-start | bytes 135176 | tf_op jit(solution)/shard_map/ppermute | solution.py:153
  167.7 4.2 %collective-permute-start.15 = (f32[1,3328]{1,0:T(1,128)S(1)}, f32[1,3328]{1,0:T(1,128)S(1)}, u32[]{:S(2)}, u32[]{:S(2)}) collective-permute-start(f32[1,3328]{1,0:T(1,128)S(1)} %add.182), channel_id=1, source_target_pairs={{0,4},{2,6},{4,0},{6,2},{8,12},{10,14},{12,8},{14,10},{16,20},{18,... | collective-permute-start | bytes 39944 | tf_op jit(solution)/shard_map/ppermute | solution.py:168
  171.9 3.9 %collective-permute-start.16 = (f32[1,3328]{1,0:T(1,128)S(1)}, f32[1,3328]{1,0:T(1,128)S(1)}, u32[]{:S(2)}, u32[]{:S(2)}) collective-permute-start(f32[1,3328]{1,0:T(1,128)S(1)} %add.183), channel_id=1, source_target_pairs={{0,8},{2,10},{4,12},{6,14},{8,0},{10,2},{12,4},{14,6},{16,24},{18,... | collective-permute-start | bytes 39944 | tf_op jit(solution)/shard_map/ppermute | solution.py:168
  173.6 4.7 %collective-permute-start.11 = (f32[4,5632]{1,0:T(4,128)S(1)}, f32[4,5632]{1,0:T(4,128)S(1)}, u32[]{:S(2)}, u32[]{:S(2)}) collective-permute-start(f32[4,5632]{1,0:T(4,128)S(1)} %maximum_select_fusion.11), channel_id=1, source_target_pairs={{0,8},{2,10},{4,12},{6,14},{8,0},{10,2},{12,4},{14,6},{16,24},{18,... | collective-permute-start | bytes 270344 | tf_op jit(solution)/shard_map/ppermute | solution.py:153
  175.9 6.1 %collective-permute-start.17 = (f32[1,3328]{1,0:T(1,128)S(1)}, f32[1,3328]{1,0:T(1,128)S(1)}, u32[]{:S(2)}, u32[]{:S(2)}) collective-permute-start(f32[1,3328]{1,0:T(1,128)S(1)} %add.184), channel_id=1, source_target_pairs={{0,16},{2,18},{4,20},{6,22},{8,24},{10,26},{12,28},{14,30},{16,0},... | collective-permute-start | bytes 39944 | tf_op jit(solution)/shard_map/ppermute | solution.py:168
  178.4 10.3 %collective-permute-start.12 = (f32[8,5632]{1,0:T(8,128)S(1)}, f32[8,5632]{1,0:T(8,128)S(1)}, u32[]{:S(2)}, u32[]{:S(2)}) collective-permute-start(f32[8,5632]{1,0:T(8,128)S(1)} %maximum_select_fusion.9), channel_id=1, source_target_pairs={{0,16},{2,18},{4,20},{6,22},{8,24},{10,26},{12,28},{14,30},{16,0},... | collective-permute-start | bytes 540680 | tf_op jit(solution)/shard_map/ppermute | solution.py:153
  (38 other events, 107.8 us)
Sparse Core Ops, SparseCore 0:
  95.0 113.4 reduce-scatter.1

commit v4 on v3

--- a/solution.py
+++ b/solution.py
@@ -15,6 +15,18 @@
 PAIR_TILE = 4096
 PAIR_BACK_TILE = 2048
 HEAD_PAD = 16
+
+
+def blank_kernel(out_ref):
+    del out_ref
+
+
+def blank(shape, dtype):
+    return pl.pallas_call(
+        blank_kernel,
+        out_shape=jax.ShapeDtypeStruct(shape, dtype),
+        out_specs=pl.BlockSpec(memory_space=pl.ANY),
+    )()
 
 
 def pair_stats(x):
@@ -341,7 +353,7 @@
         normed_a, d_qkv, (((0,), (0,)), ((), ())), preferred_element_type=jnp.float32
     )
 
-    packed = lax.optimization_barrier(jnp.zeros((width, 4 * proj + 3 * ffn), jnp.bfloat16))
+    packed = blank((width, 4 * proj + 3 * ffn), jnp.bfloat16)
     packed = lax.dynamic_update_slice(packed, gate_up_grad.astype(jnp.bfloat16), (0, 4 * proj))
     packed = lax.dynamic_update_slice(
         packed, down_grad_t.astype(jnp.bfloat16), (0, 4 * proj + 2 * ffn)

time: 221 us -> 227 us (1.027)
  matrix products: 41.8 us -> 47.9 us
  local copies, waits for them, and re-layouts: 38 us -> 32.8 us
  waiting for transfers between devices: 41.1 us -> 43.6 us
  other arithmetic: 14.9 us -> 17.4 us
    broadcast_in_dim x1 -> x0, local copies, waits for them, and re-layouts: 4.79 us -> none  [shards(): jnp.zeros((width, 4 * proj + 3 * ffn), jnp.bfloat16)]
    unnamed x117 -> x141, local copies, waits for them, and re-layouts: 17.6 us -> 17.6 us
  transfers between devices with their start and end apart: 19 -> 19, of which waited for: 10 -> 10; matrix products, arithmetic and copies ran while one was open for 34% -> 32% of each run, Pallas kernels for 22% -> 22%
where the time goes in v4:
time: 227 us; the launch traced here: 226 us
  Pallas kernels  49.2 us (22%)
  matrix products  47.9 us (21%)
  waiting for transfers between devices  43.6 us (19%)
  local copies, waits for them, and re-layouts  32.8 us (14%)
  starting transfers between devices  19.1 us (8%)
  other arithmetic  17.4 us (8%)
  between operations  15.5 us (7%)
    pallas_call x1, Pallas kernels, pair_backward(): pl.pallas_call(pair_backward_kernel, grid=(m // tile,), in_specs=[pl.Bloc...  34 us
    ppermute x10, waiting for transfers between devices, swap_heads(): return lax.ppermute(values, 'head', [(0, 1), (1, 0)])  17.8 us
    unnamed x141, local copies, waits for them, and re-layouts  17.6 us
    pallas_call x1, Pallas kernels, pair_forward(): pl.pallas_call(pair_forward_kernel, grid=(m // tile,), in_specs=[pl.Block...  15.2 us
    reduce_scatter x1, waiting for transfers between devices, shards(): lax.psum_scatter(packed, 'dp', scatter_dimension=0, tiled=True)  14.5 us
    ppermute x10, starting transfers between devices, swap_heads(): return lax.ppermute(values, 'head', [(0, 1), (1, 0)])  9.7 us
    ppermute x4, waiting for transfers between devices, dp_gather(): other = lax.ppermute(block, 'dp', [(i, i ^ step) for i in range(count)])  5.92 us
    dot_general x1, matrix products, shards(): lax.dot_general(normed_t, d_gate_up, (((0,), (0,)), ((), ())), preferred_...  5.38 us
  transfers between devices with their start and end apart: 19, of which 10 were waited for; matrix products, arithmetic and copies ran while one was open for 32% of the time, Pallas kernels for 22%

profile of v4, /device:TPU:0, one launch (start us, length us, event | category | flops | bytes accessed | tf_op | source)
XLA Modules:
  0.0 225.6 jit_solution(7588458100379921884)
XLA Ops:
  7.2 3.0 %collective-permute-start = (bf16[128,768]{1,0:T(8,128)(2,1)}, bf16[128,768]{1,0:T(8,128)(2,1)S(1)}, u32[]{:S(2)}, u32[]{:S(2)}) collective-permute-start(bf16[128,768]{1,0:T(8,128)(2,1)} %bitcast.91), channel_id=1, source_target_pairs={{0,1},{1,0},{2,3},{3,2},{4,5},{5,4},{6,7},{7,6},{8,9},{9,8},{10,11... | collective-permute-start | bytes 589832 | tf_op jit(solution)/shard_map/ppermute | solution.py:147
  11.7 15.2 %shard_map.246 = bf16[12,32768]{1,0:T(8,128)(2,1)} custom-call(bf16[32768,256]{1,0:T(8,128)(2,1)} %bitcast.80, f32[1,256]{1,0:T(1,128)} %bitcast.117, bf16[16,256]{1,0:T(8,128)(2,1)} %pad.8.wt_ref), custom_call_target="tpu_custom_call" | custom-call | flops 352321536 | bytes 17563648 | tf_op jit(solution)/shard_map/pallas_call | solution.py:50
  29.3 2.0 copy.91
  31.3 1.9 collective-permute-start.1
  33.9 2.1 convolution_reduce_fusion
  38.2 3.9 %copy.67 = bf16[768,3,384]{0,2,1:T(8,128)(2,1)} copy(bf16[768,3,384]{2,0,1:T(8,128)(2,1)} %param.22) | data formatting | bytes 3538944 | tf_op args[7]
  43.1 2.3 %convolution_convert_fusion.3 = bf16[256,1152]{1,0:T(8,128)(2,1)S(1)} fusion(bf16[768,1152]{0,1:T(8,128)(2,1)} %bitcast.89, f32[768]{0:T(1024)S(1)} %get-tuple-element.70, f32[768]{0:T(1024)S(1)} %get-tuple-element.71, f32[256]{0:T(256)S(1)} %add_rsqrt_fusion.1, f32[256]{0:T(256)S(1)} %broadcast_multiply_fusion.5, bf16[128,768]{1,0:T(8,128)(2,1)S(1)} %bitcast.94, ...), kind=kOutput, calls=%fused_computation.7 | convolution fusion | flops 456228864 | bytes 2760705 | tf_op jit(solution)/shard_map/dot_general | solution.py:268
  45.9 3.4 %fusion.77 = (f32[6,256]{1,0:T(8,128)S(1)}, f32[6,256,256]{1,2,0:T(8,128)}) fusion(pred[256]{0:T(512)(128)(4,1)} %or_and_fusion, bf16[256,6,64]{0,2,1:T(8,128)(2,1)S(1)} %bitcast.103, bf16[256,6,64]{0,2,1:T(8,128)(2,1)S(1)} %bitcast.101, bf16[6,128,256]{1,2,0:T(8,128)(2,1)} %copy.90, bf16[6,128,256]{1,2,0:T(8,128)(2,1)} %collective-permute-done.1, pred[]{:T(512)S(6)} %eq.44), kind=kOutput, calls=%fused_computation.177 | convolution fusion | flops 56230144 | bytes 2758913 | tf_op jit(solution)/shard_map/sub | solution.py:276
  51.3 1.9 collective-permute-start.5
  53.3 3.6 %copy.94 = bf16[96,8,2,1536]{3,1,2,0:T(8,128)(2,1)S(1)} copy(bf16[96,8,2,1536]{3,2,1,0:T(2,128)(2,1)} %bitcast.82) | data formatting | bytes 9437184
  59.0 3.1 %fusion.75 = (f32[256]{0:T(256)S(1)}, f32[256,768]{1,0:T(8,128)S(1)}, f32[256,768]{1,0:T(8,128)}) fusion(f32[768]{0:T(1024)S(1)} %get-tuple-element.116, bf16[128,768]{1,0:T(8,128)(2,1)S(1)} %bitcast.95, bf16[128,768]{1,0:T(8,128)(2,1)S(1)} %collective-permute-done, pred[]{:T(512)S(6)} %eq.44, f32[768]{0:T(1024)S(1)} %copy-done.57, ...), kind=kOutput, calls=%fused_computation.175 | convolution fusion | flops 311820032 | bytes 3546113 | tf_op jit(solution)/shard_map/dot_general | solution.py:287
  63.9 3.3 %multiply_convert_fusion.2 = (bf16[256,1536]{1,0:T(8,128)(2,1)S(1)}, bf16[256,1536]{1,0:T(8,128)(2,1)S(1)}, bf16[256,1536]{1,0:T(8,128)(2,1)}) fusion(f32[256,3072]{1,0:T(8,128)S(1)} %fusion.70, bf16[1536,768]{1,0:T(8,128)(2,1)S(1)} %copy-done, f32[768]{0:T(1024)S(1)} %get-tuple-element.73, bf16[128,768]{1,0:T(8,128)(2,1)} %bitcast.13, ...), kind=kOutput, calls=%fused_computation.13 | convolution fusion | flops 612237312 | bytes 8260609 | tf_op jit(solution)/shard_map/dot_general | solution.py:308
  67.2 2.3 %fusion.16 = f32[256,768]{1,0:T(8,128)} fusion(bf16[768,3072]{1,0:T(8,128)(2,1)S(1)} %bitcast.84, bf16[256,1536]{1,0:T(8,128)(2,1)S(1)} %get-tuple-element.82, bf16[256,1536]{1,0:T(8,128)(2,1)S(1)} %get-tuple-element.81), kind=kOutput, calls=%fused_computation.47 | convolution fusion | flops 1211105280 | bytes 7077888 | tf_op jit(solution)/shard_map/dot_general | solution.py:317
  69.6 5.4 %fusion.1 = bf16[768,6144]{1,0:T(8,128)(2,1)} fusion(bf16[768,6144]{1,0:T(8,128)(2,1)} %shard_map.248, bf16[256,1536]{1,0:T(8,128)(2,1)} %copy-done.62, bf16[256,1536]{1,0:T(8,128)(2,1)} %copy-done.61, f32[256,768]{1,0:T(8,128)S(1)} %get-tuple-element.80, f32[768]{0:T(1024)} %get-tuple-element.69, f32[768]{0:T(1024)S(1)} %get-tuple-element.68, ...), kind=kOutput, calls=%fused_computation.2 | convolution fusion | flops 1214447616 | bytes 7087104 | tf_op jit(solution)/shard_map/dot_general | solution.py:314
  75.0 3.4 %fusion.2 = bf16[768,6144]{1,0:T(8,128)(2,1)} fusion(bf16[768,6144]{1,0:T(8,128)(2,1)} %fusion.1, bf16[256,1536]{1,0:T(8,128)(2,1)S(1)} %copy-done.60, f32[768]{0:T(1024)S(1)} %get-tuple-element.73, bf16[128,768]{1,0:T(8,128)(2,1)S(1)} %copy-done.19, bf16[128,768]{1,0:T(8,128)(2,1)} %bitcast.13, pred[]{:T(512)S(6)} %eq.44), kind=kOutput, calls=%fused_computation.5 | convolution fusion | flops 607518720 | bytes 3542017 | tf_op jit(solution)/shard_map/dot_general | solution.py:305
  78.4 7.8 %collective-permute-done.6 = f32[256,768]{1,0:T(8,128)} collective-permute-done((f32[256,768]{1,0:T(8,128)}, f32[256,768]{1,0:T(8,128)}, u32[]{:S(2)}, u32[]{:S(2)}) %collective-permute-start.6) | collective-permute-done | bytes 786464 | tf_op jit(solution)/shard_map/ppermute | solution.py:147
  86.2 2.4 %multiply_reduce_fusion.1 = (f32[768]{0:T(1024)}, f32[256]{0:T(256)S(1)}, f32[256]{0:T(256)S(1)}, f32[768]{0:T(1024)}, f32[256,768]{1,0:T(8,128)S(1)}) fusion(f32[256,768]{1,0:T(8,128)S(1)} %get-tuple-element.80, f32[256]{0:T(256)S(1)} %copy-done.45, f32[256]{0:T(256)S(1)} %copy-done.36, f32[768]{0:T(1024)S(1)} %get-tuple-element.68, f32[256,768]{1,0:T(8,128)} %fusion.16, ...), kind=kLoop, calls=%fused_computation.57 | loop fusion | flops 1964032 | bytes 3159040 | tf_op jit(solution)/shard_map/reduce_sum | solution.py:322
  88.7 2.2 multiply_reduce_fusion.7
  98.7 2.2 fusion.3
  100.9 2.7 %convolution_convert_fusion.6 = bf16[256,768]{1,0:T(8,128)(2,1)} fusion(bf16[256,1536]{1,0:T(8,128)(2,1)} %get-tuple-element.83, bf16[1536,768]{1,0:T(8,128)(2,1)S(1)} %copy-done), kind=kOutput, calls=%fused_computation.23 | convolution fusion | flops 604176384 | bytes 3538944 | tf_op jit(solution)/shard_map/dot_general | solution.py:297
  104.6 7.1 %collective-permute-done.4 = bf16[256,768]{1,0:T(8,128)(2,1)} collective-permute-done((bf16[256,768]{1,0:T(8,128)(2,1)}, bf16[256,768]{1,0:T(8,128)(2,1)}, u32[]{:S(2)}, u32[]{:S(2)}) %collective-permute-start.4) | collective-permute-done | bytes 393248 | tf_op jit(solution)/shard_map/ppermute | solution.py:147
  115.7 1.9 copy.81
  118.9 3.4 %convolution_convert_fusion.5 = bf16[256,768]{1,0:T(8,128)(2,1)} fusion(bf16[768,1152]{0,1:T(8,128)(2,1)} %bitcast.90, bf16[256,384]{0,1:T(8,128)(2,1)} %bitcast.123, bf16[256,384]{0,1:T(8,128)(2,1)S(1)} %bitcast.109, bf16[256,384]{0,1:T(8,128)(2,1)} %bitcast.111), kind=kOutput, calls=%fused_computation.22 | convolution fusion | flops 454950912 | bytes 2752512 | tf_op jit(solution)/shard_map/dot_general | solution.py:365
  125.3 1.9 copy.82
  130.2 34.0 %shard_map.247 = (bf16[32768,256]{1,0:T(8,128)(2,1)}, f32[16,256]{1,0:T(8,128)}, f32[1,256]{1,0:T(1,128)}) custom-call(bf16[32768,256]{1,0:T(8,128)(2,1)} %bitcast.81, bf16[16,32768]{1,0:T(8,128)(2,1)} %pad.9.ds_ref, f32[1,256]{1,0:T(1,128)} %bitcast.118, bf16[16,256]{1,0:T(8,128)(2,1)} %pad.8.wt_ref), custom_call_target="tpu_custom_call" | custom-call | flops 704643072 | bytes 34603008 | tf_op jit(solution)/shard_map/pallas_call | solution.py:97
  168.0 2.5 %convolution_multiply_fusion.2 = f32[1,256]{1,0:T(1,128)} fusion(bf16[256,4608]{1,0:T(8,128)(2,1)S(1)} %copy-done.6, f32[1,4608]{1,0:T(1,128)S(1)} %get-tuple-element.100, f32[1,256]{1,0:T(1,128)S(1)} %copy-done.40), kind=kOutput, calls=%fused_computation.45 | convolution fusion | flops 14157824 | bytes 2379776 | tf_op jit(solution)/shard_map/dot_general | solution.py:404
  174.0 3.8 %collective-permute-done.15 = f32[1,3328]{1,0:T(1,128)S(1)} collective-permute-done((f32[1,3328]{1,0:T(1,128)S(1)}, f32[1,3328]{1,0:T(1,128)S(1)}, u32[]{:S(2)}, u32[]{:S(2)}) %collective-permute-start.15) | collective-permute-done | bytes 13344 | tf_op jit(solution)/shard_map/ppermute | solution.py:180
  181.8 2.0 collective-permute-start.17
  184.1 2.5 %collective-permute-start.12 = (f32[8,5632]{1,0:T(8,128)S(1)}, f32[8,5632]{1,0:T(8,128)S(1)}, u32[]{:S(2)}, u32[]{:S(2)}) collective-permute-start(f32[8,5632]{1,0:T(8,128)S(1)} %maximum_select_fusion.9), channel_id=1, source_target_pairs={{0,16},{2,18},{4,20},{6,22},{8,24},{10,26},{12,28},{14,30},{16,0},... | collective-permute-start | bytes 540680 | tf_op jit(solution)/shard_map/ppermute | solution.py:165
  189.0 5.0 %collective-permute-done.12 = f32[8,5632]{1,0:T(8,128)S(1)} collective-permute-done((f32[8,5632]{1,0:T(8,128)S(1)}, f32[8,5632]{1,0:T(8,128)S(1)}, u32[]{:S(2)}, u32[]{:S(2)}) %collective-permute-start.12) | collective-permute-done | bytes 180256 | tf_op jit(solution)/shard_map/ppermute | solution.py:165
  195.3 4.2 %fusion.45 = f32[256,4608]{1,0:T(8,128)} fusion(bf16[16,256]{1,0:T(8,128)(2,1)S(1)} %multiply_convert_fusion.7, f32[16,5632]{1,0:T(8,128)S(1)} %maximum_select_fusion.8), kind=kOutput, calls=%fused_computation.102 | convolution fusion | flops 226492416 | bytes 5021696 | tf_op jit(solution)/shard_map/dot_general | solution.py:402
  199.5 14.5 %reduce-scatter.2.cloned.1.call-done = bf16[48,6144]{1,0:T(8,128)(2,1)} async-done(((bf16[768,6144]{1,0:T(8,128)(2,1)}), bf16[48,6144]{1,0:T(8,128)(2,1)}) %reduce-scatter.2.cloned.1.call-update) | async-done | bytes 589840 | tf_op jit(solution)/shard_map/reduce_scatter | solution.py:363
  (241 shorter events, 53.1 us)
Async XLA Ops:
  7.2 56.7 %copy-start = (bf16[1536,768]{1,0:T(8,128)(2,1)S(1)}, bf16[1536,768]{1,0:T(8,128)(2,1)}, u32[]{:S(2)}) copy-start(bf16[1536,768]{1,0:T(8,128)(2,1)} %param.28) | copy-start | bytes 7077892
  7.2 206.9 %reduce-scatter.2.cloned.1.call-start = ((), (), s32[]{:S(2)}) async-start(), calls=%async_computation.1 | async-start | bytes 10027008 | tf_op jit(solution)/shard_map/reduce_scatter | solution.py:363
  7.2 35.4 %collective-permute-start = (bf16[128,768]{1,0:T(8,128)(2,1)}, bf16[128,768]{1,0:T(8,128)(2,1)S(1)}, u32[]{:S(2)}, u32[]{:S(2)}) collective-permute-start(bf16[128,768]{1,0:T(8,128)(2,1)} %bitcast.91), channel_id=1, source_target_pairs={{0,1},{1,0},{2,3},{3,2},{4,5},{5,4},{6,7},{7,6},{8,9},{9,8},{10,11... | collective-permute-start | bytes 589832 | tf_op jit(solution)/shard_map/ppermute | solution.py:147
  10.3 47.3 %collective-permute-start.3 = (bf16[384,768]{1,0:T(8,128)(2,1)}, bf16[384,768]{1,0:T(8,128)(2,1)}, u32[]{:S(2)}, u32[]{:S(2)}) collective-permute-start(bf16[384,768]{1,0:T(8,128)(2,1)} %param.25), channel_id=1, source_target_pairs={{0,1},{1,0},{2,3},{3,2},{4,5},{5,4},{6,7},{7,6},{8,9},{9,8},{10,11... | collective-permute-start | bytes 1769480 | tf_op jit(solution)/shard_map/ppermute | solution.py:147
  29.3 6.7 %copy-start.28 = (f32[4608]{0:T(1024)S(1)}, f32[4608]{0:T(1024)}, u32[]{:S(2)}) copy-start(f32[4608]{0:T(1024)} %param.21) | copy-start | bytes 55300
  29.3 8.0 %copy-start.9 = (bf16[6,128,256]{2,1,0:T(8,128)(2,1)S(1)}, bf16[6,128,256]{2,1,0:T(8,128)(2,1)}, u32[]{:S(2)}) copy-start(bf16[6,128,256]{2,1,0:T(8,128)(2,1)} %get-tuple-element.91) | copy-start | bytes 1179652
  31.3 14.6 %collective-permute-start.1 = (bf16[6,128,256]{1,2,0:T(8,128)(2,1)}, bf16[6,128,256]{1,2,0:T(8,128)(2,1)}, u32[]{:S(2)}, u32[]{:S(2)}) collective-permute-start(bf16[6,128,256]{1,2,0:T(8,128)(2,1)} %copy.91), channel_id=1, source_target_pairs={{0,1},{1,0},{2,3},{3,2},{4,5},{5,4},{6,7},{7,6},{8,9},{9,8},{10,11... | collective-permute-start | bytes 1179656 | tf_op jit(solution)/shard_map/ppermute | solution.py:147
  51.2 7.8 %collective-permute-start.2 = (bf16[256,384]{1,0:T(8,128)(2,1)S(1)}, bf16[256,384]{1,0:T(8,128)(2,1)S(1)}, u32[]{:S(2)}, u32[]{:S(2)}) collective-permute-start(bf16[256,384]{1,0:T(8,128)(2,1)S(1)} %copy.75), channel_id=1, source_target_pairs={{0,1},{1,0},{2,3},{3,2},{4,5},{5,4},{6,7},{7,6},{8,9},{9,8},{10,11... | collective-permute-start | bytes 589832 | tf_op jit(solution)/shard_map/ppermute | solution.py:147
  51.3 12.5 %collective-permute-start.5 = (bf16[128,768]{1,0:T(8,128)(2,1)}, bf16[128,768]{1,0:T(8,128)(2,1)S(1)}, u32[]{:S(2)}, u32[]{:S(2)}) collective-permute-start(bf16[128,768]{1,0:T(8,128)(2,1)} %bitcast.13), channel_id=1, source_target_pairs={{0,1},{1,0},{2,3},{3,2},{4,5},{5,4},{6,7},{7,6},{8,9},{9,8},{10,11... | collective-permute-start | bytes 589832 | tf_op jit(solution)/shard_map/ppermute | solution.py:147
  62.1 26.6 %copy-start.4 = (f32[256,768]{1,0:T(8,128)}, f32[256,768]{1,0:T(8,128)S(1)}, u32[]{:S(2)}) copy-start(f32[256,768]{1,0:T(8,128)S(1)} %get-tuple-element.80) | copy-start | bytes 2359300
  69.5 16.7 %collective-permute-start.6 = (f32[256,768]{1,0:T(8,128)}, f32[256,768]{1,0:T(8,128)}, u32[]{:S(2)}, u32[]{:S(2)}) collective-permute-start(f32[256,768]{1,0:T(8,128)} %fusion.16), channel_id=1, source_target_pairs={{0,1},{1,0},{2,3},{3,2},{4,5},{5,4},{6,7},{7,6},{8,9},{9,8},{10,11... | collective-permute-start | bytes 2359304 | tf_op jit(solution)/shard_map/ppermute | solution.py:147
  75.0 11.2 %copy-start.36 = (f32[256]{0:T(256)S(1)}, f32[256]{0:T(256)}, u32[]{:S(2)}) copy-start(f32[256]{0:T(256)} %copy-done.35) | copy-start | bytes 3076
  75.0 11.2 %copy-start.45 = (f32[256]{0:T(256)S(1)}, f32[256]{0:T(256)}, u32[]{:S(2)}) copy-start(f32[256]{0:T(256)} %copy-done.44) | copy-start | bytes 3076
  78.4 10.2 %copy-start.17 = (f32[256,768]{1,0:T(8,128)S(1)}, f32[256,768]{1,0:T(8,128)}, u32[]{:S(2)}) copy-start(f32[256,768]{1,0:T(8,128)} %get-tuple-element.113) | copy-start | bytes 2359300
  78.4 10.2 %copy-start.34 = (f32[768]{0:T(1024)S(1)}, f32[768]{0:T(1024)}, u32[]{:S(2)}) copy-start(f32[768]{0:T(1024)} %get-tuple-element.117) | copy-start | bytes 9220
  100.9 10.8 %copy-start.31 = (f32[768]{0:T(1024)S(1)}, f32[768]{0:T(1024)}, u32[]{:S(2)}) copy-start(f32[768]{0:T(1024)} %get-tuple-element.72) | copy-start | bytes 9220
  103.6 8.1 %collective-permute-start.4 = (bf16[256,768]{1,0:T(8,128)(2,1)}, bf16[256,768]{1,0:T(8,128)(2,1)}, u32[]{:S(2)}, u32[]{:S(2)}) collective-permute-start(bf16[256,768]{1,0:T(8,128)(2,1)} %convolution_convert_fusion.6), channel_id=1, source_target_pairs={{0,1},{1,0},{2,3},{3,2},{4,5},{5,4},{6,7},{7,6},{8,9},{9,8},{10,11... | collective-permute-start | bytes 1179656 | tf_op jit(solution)/shard_map/ppermute | solution.py:147
  114.6 10.8 %collective-permute-start.8 = (bf16[6,128,256]{1,2,0:T(8,128)(2,1)}, bf16[6,128,256]{1,2,0:T(8,128)(2,1)}, u32[]{:S(2)}, u32[]{:S(2)}) collective-permute-start(bf16[6,128,256]{1,2,0:T(8,128)(2,1)} %get-tuple-element.90), channel_id=1, source_target_pairs={{0,1},{1,0},{2,3},{3,2},{4,5},{5,4},{6,7},{7,6},{8,9},{9,8},{10,11... | collective-permute-start | bytes 1179656 | tf_op jit(solution)/shard_map/ppermute | solution.py:147
  122.3 43.8 %collective-permute-start.7 = (bf16[256,768]{1,0:T(8,128)(2,1)}, bf16[256,768]{1,0:T(8,128)(2,1)}, u32[]{:S(2)}, u32[]{:S(2)}) collective-permute-start(bf16[256,768]{1,0:T(8,128)(2,1)} %convolution_convert_fusion.5), channel_id=1, source_target_pairs={{0,1},{1,0},{2,3},{3,2},{4,5},{5,4},{6,7},{7,6},{8,9},{9,8},{10,11... | collective-permute-start | bytes 1179656 | tf_op jit(solution)/shard_map/ppermute | solution.py:147
  130.2 35.9 %copy-start.43 = (f32[256]{0:T(256)S(1)}, f32[256]{0:T(256)}, u32[]{:S(2)}) copy-start(f32[256]{0:T(256)} %copy-done.41) | copy-start | bytes 3076
  130.2 35.9 %copy-start.52 = (f32[256]{0:T(256)S(1)}, f32[256]{0:T(256)}, u32[]{:S(2)}) copy-start(f32[256]{0:T(256)} %copy-done.49) | copy-start | bytes 3076
  166.0 4.5 %collective-permute-start.13 = (f32[1,3328]{1,0:T(1,128)S(1)}, f32[1,3328]{1,0:T(1,128)S(1)}, u32[]{:S(2)}, u32[]{:S(2)}) collective-permute-start(f32[1,3328]{1,0:T(1,128)S(1)} %broadcast_in_dim.61), channel_id=1, source_target_pairs={{0,1},{1,0},{2,3},{3,2},{4,5},{5,4},{6,7},{7,6},{8,9},{9,8},{10,11... | collective-permute-start | bytes 39944 | tf_op jit(solution)/shard_map/ppermute | solution.py:147
  168.0 18.6 %copy-start.3 = (f32[256,768]{1,0:T(8,128)S(1)}, f32[256,768]{1,0:T(8,128)}, u32[]{:S(2)}) copy-start(f32[256,768]{1,0:T(8,128)} %copy-done.1) | copy-start | bytes 2359300
  168.0 18.6 %copy-start.56 = (f32[128]{0:T(128)S(1)}, f32[128]{0:T(128)}, u32[]{:S(2)}) copy-start(f32[128]{0:T(128)} %dynamic-slice.14) | copy-start | bytes 1540
  170.5 1.2 collective-permute-start.9
  170.6 3.0 %collective-permute-start.14 = (f32[1,3328]{1,0:T(1,128)S(1)}, f32[1,3328]{1,0:T(1,128)S(1)}, u32[]{:S(2)}, u32[]{:S(2)}) collective-permute-start(f32[1,3328]{1,0:T(1,128)S(1)} %reshape_add_fusion), channel_id=1, source_target_pairs={{0,2},{2,0},{4,6},{6,4},{8,10},{10,8},{12,14},{14,12},{16,18},{18,... | collective-permute-start | bytes 39944 | tf_op jit(solution)/shard_map/ppermute | solution.py:180
  171.8 7.5 %collective-permute-start.10 = (f32[2,5632]{1,0:T(2,128)S(1)}, f32[2,5632]{1,0:T(2,128)S(1)}, u32[]{:S(2)}, u32[]{:S(2)}) collective-permute-start(f32[2,5632]{1,0:T(2,128)S(1)} %maximum_select_fusion.12), channel_id=1, source_target_pairs={{0,4},{2,6},{4,0},{6,2},{8,12},{10,14},{12,8},{14,10},{16,20},{18,... | collective-permute-start | bytes 135176 | tf_op jit(solution)/shard_map/ppermute | solution.py:165
  173.6 4.2 %collective-permute-start.15 = (f32[1,3328]{1,0:T(1,128)S(1)}, f32[1,3328]{1,0:T(1,128)S(1)}, u32[]{:S(2)}, u32[]{:S(2)}) collective-permute-start(f32[1,3328]{1,0:T(1,128)S(1)} %add.182), channel_id=1, source_target_pairs={{0,4},{2,6},{4,0},{6,2},{8,12},{10,14},{12,8},{14,10},{16,20},{18,... | collective-permute-start | bytes 39944 | tf_op jit(solution)/shard_map/ppermute | solution.py:180
  177.8 3.9 %collective-permute-start.16 = (f32[1,3328]{1,0:T(1,128)S(1)}, f32[1,3328]{1,0:T(1,128)S(1)}, u32[]{:S(2)}, u32[]{:S(2)}) collective-permute-start(f32[1,3328]{1,0:T(1,128)S(1)} %add.183), channel_id=1, source_target_pairs={{0,8},{2,10},{4,12},{6,14},{8,0},{10,2},{12,4},{14,6},{16,24},{18,... | collective-permute-start | bytes 39944 | tf_op jit(solution)/shard_map/ppermute | solution.py:180
  179.3 4.7 %collective-permute-start.11 = (f32[4,5632]{1,0:T(4,128)S(1)}, f32[4,5632]{1,0:T(4,128)S(1)}, u32[]{:S(2)}, u32[]{:S(2)}) collective-permute-start(f32[4,5632]{1,0:T(4,128)S(1)} %maximum_select_fusion.11), channel_id=1, source_target_pairs={{0,8},{2,10},{4,12},{6,14},{8,0},{10,2},{12,4},{14,6},{16,24},{18,... | collective-permute-start | bytes 270344 | tf_op jit(solution)/shard_map/ppermute | solution.py:165
  181.8 5.8 %collective-permute-start.17 = (f32[1,3328]{1,0:T(1,128)S(1)}, f32[1,3328]{1,0:T(1,128)S(1)}, u32[]{:S(2)}, u32[]{:S(2)}) collective-permute-start(f32[1,3328]{1,0:T(1,128)S(1)} %add.184), channel_id=1, source_target_pairs={{0,16},{2,18},{4,20},{6,22},{8,24},{10,26},{12,28},{14,30},{16,0},... | collective-permute-start | bytes 39944 | tf_op jit(solution)/shard_map/ppermute | solution.py:180
  184.1 9.8 %collective-permute-start.12 = (f32[8,5632]{1,0:T(8,128)S(1)}, f32[8,5632]{1,0:T(8,128)S(1)}, u32[]{:S(2)}, u32[]{:S(2)}) collective-permute-start(f32[8,5632]{1,0:T(8,128)S(1)} %maximum_select_fusion.9), channel_id=1, source_target_pairs={{0,16},{2,18},{4,20},{6,22},{8,24},{10,26},{12,28},{14,30},{16,0},... | collective-permute-start | bytes 540680 | tf_op jit(solution)/shard_map/ppermute | solution.py:165
  (50 other events, 153.7 us)
Sparse Core Ops, SparseCore 0:
  101.0 112.9 reduce-scatter.1

commit v5 on v3

--- a/solution.py
+++ b/solution.py
@@ -373,17 +373,18 @@
     pair_small = head_sum(
         jnp.concatenate([pair_weight_grad.reshape(-1), pair_gain_grad])[None]
     )
-    small = jnp.concatenate([d_modulation, time_cond, d_out_bias], axis=-1)
+    small = jnp.concatenate([d_modulation, time_cond, pair_small, d_out_bias], axis=-1)
     small_rows = dp_gather(small)
     mod_size = d_modulation.shape[-1]
     cond_size = time_cond.shape[-1]
     pw_size = pair_weight.size
+    pg_size = pair_gain.size
     mod_chain = small_rows[:, :mod_size]
     cond_chain = small_rows[:, mod_size : mod_size + cond_size]
-    out_bias_grad = jnp.sum(small_rows[:, mod_size + cond_size :], axis=0)
-    pair_total = dp_sum(pair_small)[0]
-    pair_weight_grad = pair_total[:pw_size].reshape(pair_weight.shape)
-    pair_gain_grad = pair_total[pw_size:]
+    rest = jnp.sum(small_rows[:, mod_size + cond_size :], axis=0)
+    pair_weight_grad = rest[:pw_size].reshape(pair_weight.shape)
+    pair_gain_grad = rest[pw_size : pw_size + pg_size]
+    out_bias_grad = rest[pw_size + pg_size :]
     cond_act = lax.optimization_barrier(jax.nn.silu(cond_chain).astype(jnp.bfloat16)).astype(
         jnp.float32
     )

time: 221 us -> 224 us (1.014)
  waiting for transfers between devices: 41.1 us -> 45.4 us
  starting transfers between devices: 19.7 us -> 17.1 us
    ppermute x4, waiting for transfers between devices: 5.86 us -> 27.6 us  [dp_gather(): other = lax.ppermute(block, 'dp', [(i, i ^ step) for i in range(count)])]
    reduce_scatter x1, waiting for transfers between devices: 14.4 us -> 2.75 us  [shards(): lax.psum_scatter(packed, 'dp', scatter_dimension=0, tiled=True)]
    ppermute x4 -> x0, waiting for transfers between devices: 5.18 us -> none  [dp_sum(): other = lax.ppermute(values, 'dp', [(i, i ^ step) for i in range(count)])]
    ppermute x4 -> x0, starting transfers between devices: 4.97 us -> none  [dp_sum(): other = lax.ppermute(values, 'dp', [(i, i ^ step) for i in range(count)])]
    unnamed x117 -> x125, local copies, waits for them, and re-layouts: 17.6 us -> 17.6 us
  transfers between devices with their start and end apart: 19 -> 15, of which waited for: 10 -> 9; matrix products, arithmetic and copies ran while one was open for 34% -> 34% of each run, Pallas kernels for 22% -> 22%
where the time goes in v5:
time: 224 us; the launch traced here: 223 us
  Pallas kernels  49.2 us (22%)
  waiting for transfers between devices  45.4 us (20%)
  matrix products  41.8 us (19%)
  local copies, waits for them, and re-layouts  39.2 us (18%)
  starting transfers between devices  17.1 us (8%)
  between operations  15.5 us (7%)
  other arithmetic  14.9 us (7%)
    pallas_call x1, Pallas kernels, pair_backward(): pl.pallas_call(pair_backward_kernel, grid=(m // tile,), in_specs=[pl.Bloc...  34 us
    ppermute x4, waiting for transfers between devices, dp_gather(): other = lax.ppermute(block, 'dp', [(i, i ^ step) for i in range(count)])  27.6 us
    unnamed x125, local copies, waits for them, and re-layouts  17.6 us
    pallas_call x1, Pallas kernels, pair_forward(): pl.pallas_call(pair_forward_kernel, grid=(m // tile,), in_specs=[pl.Block...  15.2 us
    ppermute x10, waiting for transfers between devices, swap_heads(): return lax.ppermute(values, 'head', [(0, 1), (1, 0)])  15.1 us
    ppermute x10, starting transfers between devices, swap_heads(): return lax.ppermute(values, 'head', [(0, 1), (1, 0)])  11.4 us
    ppermute x4, starting transfers between devices, dp_gather(): other = lax.ppermute(block, 'dp', [(i, i ^ step) for i in range(count)])  5.72 us
    broadcast_in_dim x1, local copies, waits for them, and re-layouts, shards(): jnp.zeros((width, 4 * proj + 3 * ffn), jnp.bfloat16)  4.79 us
  transfers between devices with their start and end apart: 15, of which 9 were waited for; matrix products, arithmetic and copies ran while one was open for 34% of the time, Pallas kernels for 22%

profile of v5, /device:TPU:0, one launch (start us, length us, event | category | flops | bytes accessed | tf_op | source)
XLA Modules:
  0.0 223.1 jit_solution(6140620220861189197)
XLA Ops:
  7.2 3.0 %collective-permute-start = (bf16[128,768]{1,0:T(8,128)(2,1)}, bf16[128,768]{1,0:T(8,128)(2,1)S(1)}, u32[]{:S(2)}, u32[]{:S(2)}) collective-permute-start(bf16[128,768]{1,0:T(8,128)(2,1)} %bitcast.90), channel_id=1, source_target_pairs={{0,1},{1,0},{2,3},{3,2},{4,5},{5,4},{6,7},{7,6},{8,9},{9,8},{10,11... | collective-permute-start | bytes 589832 | tf_op jit(solution)/shard_map/ppermute | solution.py:135
  11.7 15.2 %shard_map.246 = bf16[12,32768]{1,0:T(8,128)(2,1)} custom-call(bf16[32768,256]{1,0:T(8,128)(2,1)} %bitcast.79, f32[1,256]{1,0:T(1,128)} %bitcast.121, bf16[16,256]{1,0:T(8,128)(2,1)} %pad.8.wt_ref), custom_call_target="tpu_custom_call" | custom-call | flops 352321536 | bytes 17563648 | tf_op jit(solution)/shard_map/pallas_call | solution.py:38
  29.3 2.0 copy.90
  31.3 1.9 collective-permute-start.1
  33.9 2.1 convolution_reduce_fusion
  38.2 3.9 %copy.66 = bf16[768,3,384]{0,2,1:T(8,128)(2,1)} copy(bf16[768,3,384]{2,0,1:T(8,128)(2,1)} %param.22) | data formatting | bytes 3538944 | tf_op args[7]
  42.6 2.3 %convolution_convert_fusion.3 = bf16[256,1152]{1,0:T(8,128)(2,1)S(1)} fusion(bf16[768,1152]{0,1:T(8,128)(2,1)} %bitcast.88, f32[768]{0:T(1024)S(1)} %get-tuple-element.57, f32[768]{0:T(1024)S(1)} %get-tuple-element.58, f32[256]{0:T(256)S(1)} %add_rsqrt_fusion.1, f32[256]{0:T(256)S(1)} %broadcast_multiply_fusion.5, bf16[128,768]{1,0:T(8,128)(2,1)S(1)} %bitcast.93, ...), kind=kOutput, calls=%fused_computation.7 | convolution fusion | flops 456228864 | bytes 2760705 | tf_op jit(solution)/shard_map/dot_general | solution.py:256
  45.4 3.3 %fusion.77 = (f32[6,256]{1,0:T(8,128)S(1)}, f32[6,256,256]{1,2,0:T(8,128)}) fusion(pred[256]{0:T(512)(128)(4,1)S(1)} %or_and_fusion, bf16[256,6,64]{0,2,1:T(8,128)(2,1)S(1)} %bitcast.102, bf16[256,6,64]{0,2,1:T(8,128)(2,1)S(1)} %bitcast.100, bf16[6,128,256]{1,2,0:T(8,128)(2,1)} %copy.89, bf16[6,128,256]{1,2,0:T(8,128)(2,1)} %collective-permute-done.1, ...), kind=kOutput, calls=%fused_computation.177 | convolution fusion | flops 56230144 | bytes 2758913 | tf_op jit(solution)/shard_map/sub | solution.py:264
  48.8 1.7 convolution_convert_fusion.9
  51.4 1.9 collective-permute-start.5
  53.4 3.6 %copy.93 = bf16[96,8,2,1536]{3,1,2,0:T(8,128)(2,1)S(1)} copy(bf16[96,8,2,1536]{3,2,1,0:T(2,128)(2,1)} %bitcast.81) | data formatting | bytes 9437184
  57.6 1.7 collective-permute-done.2
  59.3 2.2 %fusion.75 = (f32[256]{0:T(256)S(1)}, f32[256,768]{1,0:T(8,128)S(1)}, f32[256,768]{1,0:T(8,128)S(1)}) fusion(f32[768]{0:T(1024)S(1)} %get-tuple-element.103, bf16[128,768]{1,0:T(8,128)(2,1)S(1)} %bitcast.94, bf16[128,768]{1,0:T(8,128)(2,1)S(1)} %collective-permute-done, pred[]{:T(512)S(6)} %eq.40, f32[768]{0:T(1024)S(1)} %copy-done.51, ...), kind=kOutput, calls=%fused_computation.175 | convolution fusion | flops 311820032 | bytes 3546113 | tf_op jit(solution)/shard_map/dot_general | solution.py:275
  66.2 4.8 %broadcast_in_dim.65 = bf16[768,6144]{1,0:T(8,128)(2,1)} broadcast(bf16[]{:T(256)} %constant.30.clone.1), dimensions={} | broadcast | bytes 9437186 | tf_op jit(solution)/shard_map/broadcast_in_dim | solution.py:344
  71.0 3.9 %fusion.1 = bf16[768,6144]{1,0:T(8,128)(2,1)} fusion(bf16[768,6144]{1,0:T(8,128)(2,1)} %broadcast_in_dim.65, bf16[256,1536]{1,0:T(8,128)(2,1)S(1)} %get-tuple-element.69, bf16[256,1536]{1,0:T(8,128)(2,1)S(1)} %get-tuple-element.68, f32[256,768]{1,0:T(8,128)S(1)} %get-tuple-element.67, f32[768]{0:T(1024)S(1)} %copy-done.49, f32[768]{0:T(1024)S(1)} %get-tuple-element.55, ...), kind=kOutput, calls=%fused_computation.2 | convolution fusion | flops 1214447616 | bytes 7086080 | tf_op jit(solution)/shard_map/dot_general | solution.py:302
  74.9 2.3 %fusion.2 = bf16[768,6144]{1,0:T(8,128)(2,1)} fusion(bf16[768,6144]{1,0:T(8,128)(2,1)} %fusion.1, bf16[256,1536]{1,0:T(8,128)(2,1)S(1)} %get-tuple-element.70, f32[768]{0:T(1024)S(1)} %get-tuple-element.60, bf16[128,768]{1,0:T(8,128)(2,1)S(1)} %collective-permute-done.5, bf16[128,768]{1,0:T(8,128)(2,1)S(1)} %bitcast.108, pred[]{:T(512)S(6)} %eq.40), kind=kOutput, calls=%fused_computation.5 | convolution fusion | flops 607518720 | bytes 3542017 | tf_op jit(solution)/shard_map/dot_general | solution.py:293
  77.1 5.2 %collective-permute-done.6 = f32[256,768]{1,0:T(8,128)S(1)} collective-permute-done((f32[256,768]{1,0:T(8,128)S(1)}, f32[256,768]{1,0:T(8,128)S(1)}, u32[]{:S(2)}, u32[]{:S(2)}) %collective-permute-start.6) | collective-permute-done | bytes 786464 | tf_op jit(solution)/shard_map/ppermute | solution.py:135
  86.1 1.9 convolution_convert_fusion.7
  92.2 2.2 fusion.3
  94.5 2.7 %convolution_convert_fusion.6 = bf16[256,768]{1,0:T(8,128)(2,1)} fusion(bf16[256,1536]{1,0:T(8,128)(2,1)} %copy-done.54, bf16[1536,768]{1,0:T(8,128)(2,1)S(1)} %copy-done), kind=kOutput, calls=%fused_computation.23 | convolution fusion | flops 604176384 | bytes 3538944 | tf_op jit(solution)/shard_map/dot_general | solution.py:285
  100.8 7.7 %collective-permute-done.4 = bf16[256,768]{1,0:T(8,128)(2,1)} collective-permute-done((bf16[256,768]{1,0:T(8,128)(2,1)}, bf16[256,768]{1,0:T(8,128)(2,1)}, u32[]{:S(2)}, u32[]{:S(2)}) %collective-permute-start.4) | collective-permute-done | bytes 393248 | tf_op jit(solution)/shard_map/ppermute | solution.py:135
  108.6 3.0 %fusion.24 = (f32[768]{0:T(1024)}, f32[256,768]{1,0:T(8,128)}) fusion(f32[768]{0:T(1024)S(1)} %copy-done.32, f32[768]{0:T(1024)S(1)} %get-tuple-element.60, bf16[256,768]{1,0:T(8,128)(2,1)} %collective-permute-done.4, bf16[256,768]{1,0:T(8,128)(2,1)} %convolution_convert_fusion.6, bf16[128,768]{1,0:T(8,128)(2,1)S(1)} %bitcast.110, ...), kind=kLoop, calls=%fused_computation.55 | loop fusion | flops 3341568 | bytes 1975297 | tf_op jit(solution)/shard_map/reduce_sum | solution.py:292
  113.7 3.4 %convolution_convert_fusion.5 = bf16[256,768]{1,0:T(8,128)(2,1)} fusion(bf16[768,1152]{0,1:T(8,128)(2,1)} %bitcast.89, bf16[256,384]{0,1:T(8,128)(2,1)} %bitcast.126, bf16[256,384]{0,1:T(8,128)(2,1)S(1)} %bitcast.113, bf16[256,384]{0,1:T(8,128)(2,1)} %bitcast.115), kind=kOutput, calls=%fused_computation.22 | convolution fusion | flops 454950912 | bytes 2752512 | tf_op jit(solution)/shard_map/dot_general | solution.py:353
  117.8 1.9 copy.81
  122.6 34.0 %shard_map.247 = (bf16[32768,256]{1,0:T(8,128)(2,1)}, f32[16,256]{1,0:T(8,128)}, f32[1,256]{1,0:T(1,128)}) custom-call(bf16[32768,256]{1,0:T(8,128)(2,1)} %bitcast.80, bf16[16,32768]{1,0:T(8,128)(2,1)} %pad.9.ds_ref, f32[1,256]{1,0:T(1,128)} %bitcast.122, bf16[16,256]{1,0:T(8,128)(2,1)} %pad.8.wt_ref), custom_call_target="tpu_custom_call" | custom-call | flops 704643072 | bytes 34603008 | tf_op jit(solution)/shard_map/pallas_call | solution.py:85
  166.8 4.7 %collective-permute-done.11 = f32[2,8960]{1,0:T(2,128)S(1)} collective-permute-done((f32[2,8960]{1,0:T(2,128)S(1)}, f32[2,8960]{1,0:T(2,128)S(1)}, u32[]{:S(2)}, u32[]{:S(2)}) %collective-permute-start.11) | collective-permute-done | bytes 71712 | tf_op jit(solution)/shard_map/ppermute | solution.py:153
  173.2 3.6 %collective-permute-done.12 = f32[4,8960]{1,0:T(4,128)S(1)} collective-permute-done((f32[4,8960]{1,0:T(4,128)S(1)}, f32[4,8960]{1,0:T(4,128)S(1)}, u32[]{:S(2)}, u32[]{:S(2)}) %collective-permute-start.12) | collective-permute-done | bytes 143392 | tf_op jit(solution)/shard_map/ppermute | solution.py:153
  176.9 2.7 %collective-permute-start.13 = (f32[8,8960]{1,0:T(8,128)S(1)}, f32[8,8960]{1,0:T(8,128)S(1)}, u32[]{:S(2)}, u32[]{:S(2)}) collective-permute-start(f32[8,8960]{1,0:T(8,128)S(1)} %maximum_select_fusion.9), channel_id=1, source_target_pairs={{0,16},{2,18},{4,20},{6,22},{8,24},{10,26},{12,28},{14,30},{16,0},... | collective-permute-start | bytes 860168 | tf_op jit(solution)/shard_map/ppermute | solution.py:153
  180.5 2.5 %convolution_multiply_fusion.2 = f32[1,256]{1,0:T(1,128)} fusion(bf16[256,4608]{1,0:T(8,128)(2,1)S(1)} %copy-done.6, f32[1,4608]{1,0:T(1,128)S(1)} %get-tuple-element.87, f32[1,256]{1,0:T(1,128)S(1)} %copy-done.38), kind=kOutput, calls=%fused_computation.45 | convolution fusion | flops 14157824 | bytes 2379776 | tf_op jit(solution)/shard_map/dot_general | solution.py:393
  183.0 18.9 %collective-permute-done.13 = f32[8,8960]{1,0:T(8,128)S(1)} collective-permute-done((f32[8,8960]{1,0:T(8,128)S(1)}, f32[8,8960]{1,0:T(8,128)S(1)}, u32[]{:S(2)}, u32[]{:S(2)}) %collective-permute-start.13) | collective-permute-done | bytes 286752 | tf_op jit(solution)/shard_map/ppermute | solution.py:153
  204.6 4.2 %fusion.45 = f32[256,4608]{1,0:T(8,128)} fusion(bf16[16,256]{1,0:T(8,128)(2,1)S(1)} %multiply_convert_fusion.7, f32[16,8960]{1,0:T(8,128)S(1)} %maximum_select_fusion.4), kind=kOutput, calls=%fused_computation.103 | convolution fusion | flops 226492416 | bytes 5021696 | tf_op jit(solution)/shard_map/dot_general | solution.py:391
  208.9 2.7 %reduce-scatter.2.cloned.1.call-done = bf16[48,6144]{1,0:T(8,128)(2,1)} async-done(((bf16[768,6144]{1,0:T(8,128)(2,1)}), bf16[48,6144]{1,0:T(8,128)(2,1)}) %reduce-scatter.2.cloned.1.call-update) | async-done | bytes 589840 | tf_op jit(solution)/shard_map/reduce_scatter | solution.py:351
  (214 shorter events, 50.5 us)
Async XLA Ops:
  7.2 56.2 %copy-start = (bf16[1536,768]{1,0:T(8,128)(2,1)S(1)}, bf16[1536,768]{1,0:T(8,128)(2,1)}, u32[]{:S(2)}) copy-start(bf16[1536,768]{1,0:T(8,128)(2,1)} %param.28) | copy-start | bytes 7077892
  7.2 204.4 %reduce-scatter.2.cloned.1.call-start = ((), (), s32[]{:S(2)}) async-start(), calls=%async_computation.1 | async-start | bytes 10027008 | tf_op jit(solution)/shard_map/reduce_scatter | solution.py:351
  7.2 34.9 %collective-permute-start = (bf16[128,768]{1,0:T(8,128)(2,1)}, bf16[128,768]{1,0:T(8,128)(2,1)S(1)}, u32[]{:S(2)}, u32[]{:S(2)}) collective-permute-start(bf16[128,768]{1,0:T(8,128)(2,1)} %bitcast.90), channel_id=1, source_target_pairs={{0,1},{1,0},{2,3},{3,2},{4,5},{5,4},{6,7},{7,6},{8,9},{9,8},{10,11... | collective-permute-start | bytes 589832 | tf_op jit(solution)/shard_map/ppermute | solution.py:135
  10.3 47.3 %collective-permute-start.3 = (bf16[384,768]{1,0:T(8,128)(2,1)}, bf16[384,768]{1,0:T(8,128)(2,1)}, u32[]{:S(2)}, u32[]{:S(2)}) collective-permute-start(bf16[384,768]{1,0:T(8,128)(2,1)} %param.25), channel_id=1, source_target_pairs={{0,1},{1,0},{2,3},{3,2},{4,5},{5,4},{6,7},{7,6},{8,9},{9,8},{10,11... | collective-permute-start | bytes 1769480 | tf_op jit(solution)/shard_map/ppermute | solution.py:135
  29.3 6.7 %copy-start.27 = (f32[4608]{0:T(1024)S(1)}, f32[4608]{0:T(1024)}, u32[]{:S(2)}) copy-start(f32[4608]{0:T(1024)} %param.21) | copy-start | bytes 55300
  29.3 8.0 %copy-start.10 = (bf16[6,128,256]{2,1,0:T(8,128)(2,1)S(1)}, bf16[6,128,256]{2,1,0:T(8,128)(2,1)}, u32[]{:S(2)}) copy-start(bf16[6,128,256]{2,1,0:T(8,128)(2,1)} %get-tuple-element.78) | copy-start | bytes 1179652
  31.3 14.1 %collective-permute-start.1 = (bf16[6,128,256]{1,2,0:T(8,128)(2,1)}, bf16[6,128,256]{1,2,0:T(8,128)(2,1)}, u32[]{:S(2)}, u32[]{:S(2)}) collective-permute-start(bf16[6,128,256]{1,2,0:T(8,128)(2,1)} %copy.90), channel_id=1, source_target_pairs={{0,1},{1,0},{2,3},{3,2},{4,5},{5,4},{6,7},{7,6},{8,9},{9,8},{10,11... | collective-permute-start | bytes 1179656 | tf_op jit(solution)/shard_map/ppermute | solution.py:135
  37.3 54.9 %copy-start.28 = (f32[768]{0:T(1024)}, f32[768]{0:T(1024)S(1)}, u32[]{:S(2)}) copy-start(f32[768]{0:T(1024)S(1)} %get-tuple-element.58) | copy-start | bytes 9220
  50.5 6.5 %copy-start.17 = (bf16[6,64,256]{2,1,0:T(8,128)(2,1)}, bf16[6,64,256]{2,1,0:T(8,128)(2,1)S(1)}, u32[]{:S(2)}) copy-start(bf16[6,64,256]{2,1,0:T(8,128)(2,1)S(1)} %convolution_convert_fusion.9) | copy-start | bytes 589828
  51.3 8.0 %collective-permute-start.2 = (bf16[256,384]{1,0:T(8,128)(2,1)}, bf16[256,384]{1,0:T(8,128)(2,1)S(1)}, u32[]{:S(2)}, u32[]{:S(2)}) collective-permute-start(bf16[256,384]{1,0:T(8,128)(2,1)} %copy.74), channel_id=1, source_target_pairs={{0,1},{1,0},{2,3},{3,2},{4,5},{5,4},{6,7},{7,6},{8,9},{9,8},{10,11... | collective-permute-start | bytes 589832 | tf_op jit(solution)/shard_map/ppermute | solution.py:135
  51.4 11.9 %collective-permute-start.5 = (bf16[128,768]{1,0:T(8,128)(2,1)S(1)}, bf16[128,768]{1,0:T(8,128)(2,1)S(1)}, u32[]{:S(2)}, u32[]{:S(2)}) collective-permute-start(bf16[128,768]{1,0:T(8,128)(2,1)S(1)} %bitcast.106), channel_id=1, source_target_pairs={{0,1},{1,0},{2,3},{3,2},{4,5},{5,4},{6,7},{7,6},{8,9},{9,8},{10,11... | collective-permute-start | bytes 589832 | tf_op jit(solution)/shard_map/ppermute | solution.py:135
  53.4 6.0 %copy-start.23 = (bf16[384,768]{1,0:T(8,128)(2,1)S(1)}, bf16[384,768]{1,0:T(8,128)(2,1)}, u32[]{:S(2)}) copy-start(bf16[384,768]{1,0:T(8,128)(2,1)} %param.25) | copy-start | bytes 1769476
  53.4 6.0 %copy-start.51 = (f32[768]{0:T(1024)S(1)}, f32[768]{0:T(1024)}, u32[]{:S(2)}) copy-start(f32[768]{0:T(1024)} %param.26) | copy-start | bytes 9220
  61.6 21.7 %copy-start.1 = (f32[256,768]{1,0:T(8,128)}, f32[256,768]{1,0:T(8,128)S(1)}, u32[]{:S(2)}) copy-start(f32[256,768]{1,0:T(8,128)S(1)} %get-tuple-element.67) | copy-start | bytes 2359300
  63.3 20.0 %copy-start.21 = (bf16[128,768]{1,0:T(8,128)(2,1)}, bf16[128,768]{1,0:T(8,128)(2,1)S(1)}, u32[]{:S(2)}) copy-start(bf16[128,768]{1,0:T(8,128)(2,1)S(1)} %collective-permute-done.5) | copy-start | bytes 589828
  64.6 10.3 %copy-start.54 = (bf16[256,1536]{1,0:T(8,128)(2,1)}, bf16[256,1536]{1,0:T(8,128)(2,1)S(1)}, u32[]{:S(2)}) copy-start(bf16[256,1536]{1,0:T(8,128)(2,1)S(1)} %get-tuple-element.70) | copy-start | bytes 2359300
  66.0 16.2 %collective-permute-start.6 = (f32[256,768]{1,0:T(8,128)S(1)}, f32[256,768]{1,0:T(8,128)S(1)}, u32[]{:S(2)}, u32[]{:S(2)}) collective-permute-start(f32[256,768]{1,0:T(8,128)S(1)} %fusion.16), channel_id=1, source_target_pairs={{0,1},{1,0},{2,3},{3,2},{4,5},{5,4},{6,7},{7,6},{8,9},{9,8},{10,11... | collective-permute-start | bytes 2359304 | tf_op jit(solution)/shard_map/ppermute | solution.py:135
  97.1 11.4 %copy-start.32 = (f32[768]{0:T(1024)S(1)}, f32[768]{0:T(1024)}, u32[]{:S(2)}) copy-start(f32[768]{0:T(1024)} %get-tuple-element.59) | copy-start | bytes 9220
  97.1 11.4 %collective-permute-start.4 = (bf16[256,768]{1,0:T(8,128)(2,1)}, bf16[256,768]{1,0:T(8,128)(2,1)}, u32[]{:S(2)}, u32[]{:S(2)}) collective-permute-start(bf16[256,768]{1,0:T(8,128)(2,1)} %convolution_convert_fusion.6), channel_id=1, source_target_pairs={{0,1},{1,0},{2,3},{3,2},{4,5},{5,4},{6,7},{7,6},{8,9},{9,8},{10,11... | collective-permute-start | bytes 1179656 | tf_op jit(solution)/shard_map/ppermute | solution.py:135
  97.5 11.1 %copy-start.20 = (bf16[1,128,768]{2,1,0:T(8,128)(2,1)S(1)}, bf16[1,128,768]{2,1,0:T(8,128)(2,1)}, u32[]{:S(2)}) copy-start(bf16[1,128,768]{2,1,0:T(8,128)(2,1)} %param.29) | copy-start | bytes 589828
  97.5 11.1 %copy-start.22 = (bf16[128,768]{1,0:T(8,128)(2,1)S(1)}, bf16[128,768]{1,0:T(8,128)(2,1)}, u32[]{:S(2)}) copy-start(bf16[128,768]{1,0:T(8,128)(2,1)} %copy-done.21) | copy-start | bytes 589828
  99.1 12.4 %copy-start.11 = (bf16[6,128,256]{1,2,0:T(8,128)(2,1)S(1)}, bf16[6,128,256]{1,2,0:T(8,128)(2,1)}, u32[]{:S(2)}) copy-start(bf16[6,128,256]{1,2,0:T(8,128)(2,1)} %get-tuple-element.76) | copy-start | bytes 1179652
  99.1 18.6 %collective-permute-start.8 = (bf16[6,128,256]{1,2,0:T(8,128)(2,1)}, bf16[6,128,256]{1,2,0:T(8,128)(2,1)}, u32[]{:S(2)}, u32[]{:S(2)}) collective-permute-start(bf16[6,128,256]{1,2,0:T(8,128)(2,1)} %get-tuple-element.77), channel_id=1, source_target_pairs={{0,1},{1,0},{2,3},{3,2},{4,5},{5,4},{6,7},{7,6},{8,9},{9,8},{10,11... | collective-permute-start | bytes 1179656 | tf_op jit(solution)/shard_map/ppermute | solution.py:135
  117.2 44.4 %collective-permute-start.7 = (bf16[256,768]{1,0:T(8,128)(2,1)}, bf16[256,768]{1,0:T(8,128)(2,1)}, u32[]{:S(2)}, u32[]{:S(2)}) collective-permute-start(bf16[256,768]{1,0:T(8,128)(2,1)} %convolution_convert_fusion.5), channel_id=1, source_target_pairs={{0,1},{1,0},{2,3},{3,2},{4,5},{5,4},{6,7},{7,6},{8,9},{9,8},{10,11... | collective-permute-start | bytes 1179656 | tf_op jit(solution)/shard_map/ppermute | solution.py:135
  160.1 3.8 %collective-permute-start.9 = (f32[1,3328]{1,0:T(1,128)S(1)}, f32[1,3328]{1,0:T(1,128)S(1)}, u32[]{:S(2)}, u32[]{:S(2)}) collective-permute-start(f32[1,3328]{1,0:T(1,128)S(1)} %broadcast_in_dim.63), channel_id=1, source_target_pairs={{0,1},{1,0},{2,3},{3,2},{4,5},{5,4},{6,7},{7,6},{8,9},{9,8},{10,11... | collective-permute-start | bytes 39944 | tf_op jit(solution)/shard_map/ppermute | solution.py:135
  163.3 16.3 %copy-start.5 = (f32[256,768]{1,0:T(8,128)S(1)}, f32[256,768]{1,0:T(8,128)}, u32[]{:S(2)}) copy-start(f32[256,768]{1,0:T(8,128)} %copy-done.3) | copy-start | bytes 2359300
  163.3 16.3 %copy-start.50 = (f32[128]{0:T(128)S(1)}, f32[128]{0:T(128)}, u32[]{:S(2)}) copy-start(f32[128]{0:T(128)} %dynamic-slice.14) | copy-start | bytes 1540
  163.9 1.3 collective-permute-start.10
  164.0 16.5 %copy-start.6 = (bf16[256,4608]{1,0:T(8,128)(2,1)S(1)}, bf16[256,4608]{1,0:T(8,128)(2,1)}, u32[]{:S(2)}) copy-start(bf16[256,4608]{1,0:T(8,128)(2,1)} %param.20) | copy-start | bytes 7077892
  165.3 6.2 %collective-permute-start.11 = (f32[2,8960]{1,0:T(2,128)S(1)}, f32[2,8960]{1,0:T(2,128)S(1)}, u32[]{:S(2)}, u32[]{:S(2)}) collective-permute-start(f32[2,8960]{1,0:T(2,128)S(1)} %maximum_select_fusion.12), channel_id=1, source_target_pairs={{0,4},{2,6},{4,0},{6,2},{8,12},{10,14},{12,8},{14,10},{16,20},{18,... | collective-permute-start | bytes 215048 | tf_op jit(solution)/shard_map/ppermute | solution.py:153
  171.6 5.2 %collective-permute-start.12 = (f32[4,8960]{1,0:T(4,128)S(1)}, f32[4,8960]{1,0:T(4,128)S(1)}, u32[]{:S(2)}, u32[]{:S(2)}) collective-permute-start(f32[4,8960]{1,0:T(4,128)S(1)} %maximum_select_fusion.10), channel_id=1, source_target_pairs={{0,8},{2,10},{4,12},{6,14},{8,0},{10,2},{12,4},{14,6},{16,24},{18,... | collective-permute-start | bytes 430088 | tf_op jit(solution)/shard_map/ppermute | solution.py:153
  176.9 25.0 %collective-permute-start.13 = (f32[8,8960]{1,0:T(8,128)S(1)}, f32[8,8960]{1,0:T(8,128)S(1)}, u32[]{:S(2)}, u32[]{:S(2)}) collective-permute-start(f32[8,8960]{1,0:T(8,128)S(1)} %maximum_select_fusion.9), channel_id=1, source_target_pairs={{0,16},{2,18},{4,20},{6,22},{8,24},{10,26},{12,28},{14,30},{16,0},... | collective-permute-start | bytes 860168 | tf_op jit(solution)/shard_map/ppermute | solution.py:153
  (38 other events, 116.6 us)
Sparse Core Ops, SparseCore 0:
  94.6 117.0 reduce-scatter.1

commit v6 on v5

--- a/solution.py
+++ b/solution.py
@@ -144,31 +144,48 @@
     )
 
 
+def bit_reverse(value, bits):
+    out = 0
+    for bit in range(bits):
+        out |= ((value >> bit) & 1) << (bits - 1 - bit)
+    return out
+
+
 def dp_gather(values):
     count = lax.axis_size("dp")
     index = lax.axis_index("dp")
+    bits = count.bit_length() - 1
     block = values
-    step = 1
-    while step < count:
+    step = count // 2
+    while step >= 1:
         other = lax.ppermute(block, "dp", [(i, i ^ step) for i in range(count)])
         block = jnp.where(
             (index & step) == 0,
             jnp.concatenate([block, other], axis=0),
             jnp.concatenate([other, block], axis=0),
         )
+        step //= 2
+    order = [bit_reverse(i, bits) for i in range(count)]
+    return block[jnp.array(order)]
+
+
+def dp_reduce_rows(values):
+    count = lax.axis_size("dp")
+    index = lax.axis_index("dp")
+    rows_each = values.shape[0] // count
+    block = values.astype(jnp.float32)
+    step = 1
+    while step < count:
+        pairs = block.reshape(-1, 2, rows_each, block.shape[-1])
+        even = pairs[:, 0].reshape(-1, block.shape[-1])
+        odd = pairs[:, 1].reshape(-1, block.shape[-1])
+        upper = (index & step) != 0
+        keep = jnp.where(upper, odd, even)
+        send = jnp.where(upper, even, odd).astype(jnp.bfloat16)
+        got = lax.ppermute(send, "dp", [(i, i ^ step) for i in range(count)])
+        block = keep + got.astype(jnp.float32)
         step *= 2
     return block
-
-
-def dp_sum(values):
-    count = lax.axis_size("dp")
-    index = lax.axis_index("dp")
-    step = 1
-    while step < count:
-        other = lax.ppermute(values, "dp", [(i, i ^ step) for i in range(count)])
-        values = jnp.where((index & step) == 0, values + other, other + values)
-        step *= 2
-    return values
 
 
 def own_rows(values, head, rows):
@@ -317,6 +334,11 @@
     out_weight_grad_t = lax.dot_general(
         d_attn_low, mixed, (((0,), (0,)), ((), ())), preferred_element_type=jnp.float32
     )
+    packed = lax.optimization_barrier(jnp.zeros((width, proj + 3 * ffn), jnp.bfloat16))
+    packed = lax.dynamic_update_slice(packed, gate_up_grad.astype(jnp.bfloat16), (0, proj))
+    packed = lax.dynamic_update_slice(packed, down_grad_t.astype(jnp.bfloat16), (0, proj + 2 * ffn))
+    packed = lax.dynamic_update_slice(packed, out_weight_grad_t.astype(jnp.bfloat16), (0, 0))
+    reduced = lax.psum_scatter(packed, "dp", scatter_dimension=0, tiled=True).astype(jnp.float32)
     d_mixed = head_split(
         lax.dot_general(
             d_attn_low, out_weight, (((1,), (1,)), ((), ())), preferred_element_type=jnp.float32
@@ -341,14 +363,8 @@
         normed_a, d_qkv, (((0,), (0,)), ((), ())), preferred_element_type=jnp.float32
     )
 
-    packed = lax.optimization_barrier(jnp.zeros((width, 4 * proj + 3 * ffn), jnp.bfloat16))
-    packed = lax.dynamic_update_slice(packed, gate_up_grad.astype(jnp.bfloat16), (0, 4 * proj))
-    packed = lax.dynamic_update_slice(
-        packed, down_grad_t.astype(jnp.bfloat16), (0, 4 * proj + 2 * ffn)
-    )
-    packed = lax.dynamic_update_slice(packed, out_weight_grad_t.astype(jnp.bfloat16), (0, 3 * proj))
-    packed = lax.dynamic_update_slice(packed, qkv_grad.astype(jnp.bfloat16), (0, 0))
-    reduced = lax.psum_scatter(packed, "dp", scatter_dimension=0, tiled=True).astype(jnp.float32)
+
+    qkv_grad = dp_reduce_rows(qkv_grad.astype(jnp.bfloat16))
 
     attn_in_part = lax.dot_general(
         d_qkv, qkv_w, (((1,), (1,)), ((), ())), preferred_element_type=jnp.float32
@@ -394,12 +410,12 @@
         d_modulation, mod_weight.astype(jnp.float32).T, precision=precise
     ) * silu_slope(time_cond)
 
-    cuts = [0, 3 * proj, 4 * proj, 4 * proj + 2 * ffn, 4 * proj + 3 * ffn]
-    pieces = [reduced[:, cuts[i] : cuts[i + 1]] for i in range(4)]
-    qkv_grad = pieces[0].reshape(-1, 3, proj)
-    out_weight_grad = pieces[1].T
-    gate_up_grad = pieces[2].reshape(-1, 2, ffn)
-    down_grad = pieces[3].T
+    cuts = [0, proj, proj + 2 * ffn, proj + 3 * ffn]
+    pieces = [reduced[:, cuts[i] : cuts[i + 1]] for i in range(3)]
+    qkv_grad = qkv_grad.reshape(-1, 3, proj)
+    out_weight_grad = pieces[0].T
+    gate_up_grad = pieces[1].reshape(-1, 2, ffn)
+    down_grad = pieces[2].T
     return (
         layer_output,
         input_grad,

time: 224 us -> 242 us (1.080)
  waiting for transfers between devices: 45.4 us -> 54.7 us
  other arithmetic: 14.9 us -> 21.2 us
  starting transfers between devices: 17.1 us -> 21.5 us
  local copies, waits for them, and re-layouts: 39.2 us -> 36.7 us
    ppermute x0 -> x4, waiting for transfers between devices: none -> 25.6 us  [dp_reduce_rows(): got = lax.ppermute(send, 'dp', [(i, i ^ step) for i in range(count)])]
    ppermute x4, waiting for transfers between devices: 27.6 us -> 13.4 us  [dp_gather(): other = lax.ppermute(block, 'dp', [(i, i ^ step) for i in range(count)])]
    ppermute x0 -> x4, starting transfers between devices: none -> 4.15 us  [dp_reduce_rows(): got = lax.ppermute(send, 'dp', [(i, i ^ step) for i in range(count)])]
    reduce_scatter x1, waiting for transfers between devices: 2.75 us -> 0.01 us  [shards(): lax.psum_scatter(packed, 'dp', scatter_dimension=0, tiled=True)]
    dot_general x1, matrix products: 1.48 us -> 3.95 us  [shards(): gate_up = jnp.dot(normed_t, gate_up_w, preferred_element_type=jnp.float32)]
    unnamed x125 -> x103, local copies, waits for them, and re-layouts: 17.6 us -> 18 us
  transfers between devices with their start and end apart: 15 -> 19, of which waited for: 9 -> 11; matrix products, arithmetic and copies ran while one was open for 34% -> 34% of each run, Pallas kernels for 22% -> 21%
where the time goes in v6:
time: 242 us; the launch traced here: 241 us
  waiting for transfers between devices  54.7 us (23%)
  Pallas kernels  49.5 us (20%)
  matrix products  42.1 us (17%)
  local copies, waits for them, and re-layouts  36.7 us (15%)
  starting transfers between devices  21.5 us (9%)
  other arithmetic  21.2 us (9%)
  between operations  15.5 us (6%)
    pallas_call x1, Pallas kernels, pair_backward(): pl.pallas_call(pair_backward_kernel, grid=(m // tile,), in_specs=[pl.Bloc...  34.2 us
    ppermute x4, waiting for transfers between devices, dp_reduce_rows(): got = lax.ppermute(send, 'dp', [(i, i ^ step) for i in range(count)])  25.6 us
    unnamed x103, local copies, waits for them, and re-layouts  18 us
    ppermute x10, waiting for transfers between devices, swap_heads(): return lax.ppermute(values, 'head', [(0, 1), (1, 0)])  15.7 us
    pallas_call x1, Pallas kernels, pair_forward(): pl.pallas_call(pair_forward_kernel, grid=(m // tile,), in_specs=[pl.Block...  15.2 us
    ppermute x4, waiting for transfers between devices, dp_gather(): other = lax.ppermute(block, 'dp', [(i, i ^ step) for i in range(count)])  13.4 us
    ppermute x10, starting transfers between devices, swap_heads(): return lax.ppermute(values, 'head', [(0, 1), (1, 0)])  12 us
    ppermute x4, starting transfers between devices, dp_gather(): other = lax.ppermute(block, 'dp', [(i, i ^ step) for i in range(count)])  5.29 us
  transfers between devices with their start and end apart: 19, of which 11 were waited for; matrix products, arithmetic and copies ran while one was open for 34% of the time, Pallas kernels for 21%

profile of v6, /device:TPU:0, one launch (start us, length us, event | category | flops | bytes accessed | tf_op | source)
XLA Modules:
  0.0 241.1 jit_solution(6949587439266112453)
XLA Ops:
  7.2 3.0 %collective-permute-start = (bf16[128,768]{1,0:T(8,128)(2,1)}, bf16[128,768]{1,0:T(8,128)(2,1)S(1)}, u32[]{:S(2)}, u32[]{:S(2)}) collective-permute-start(bf16[128,768]{1,0:T(8,128)(2,1)} %bitcast.116), channel_id=1, source_target_pairs={{0,1},{1,0},{2,3},{3,2},{4,5},{5,4},{6,7},{7,6},{8,9},{9,8},{10,11... | collective-permute-start | bytes 589832 | tf_op jit(solution)/shard_map/ppermute | solution.py:135
  10.4 1.9 collective-permute-start.3
  13.6 15.2 %shard_map.255 = bf16[12,32768]{1,0:T(8,128)(2,1)} custom-call(bf16[32768,256]{1,0:T(8,128)(2,1)} %bitcast.97, f32[1,256]{1,0:T(1,128)} %bitcast.150, bf16[16,256]{1,0:T(8,128)(2,1)} %pad.8.wt_ref), custom_call_target="tpu_custom_call" | custom-call | flops 352321536 | bytes 17563648 | tf_op jit(solution)/shard_map/pallas_call | solution.py:38
  31.3 2.0 copy.110
  34.0 2.1 convolution_reduce_fusion
  38.3 3.8 %copy.86 = bf16[768,3,384]{0,2,1:T(8,128)(2,1)} copy(bf16[768,3,384]{2,0,1:T(8,128)(2,1)} %param.23) | data formatting | bytes 3538944 | tf_op args[7]
  42.1 5.7 %copy.113 = bf16[96,8,2,1536]{3,1,2,0:T(8,128)(2,1)} copy(bf16[96,8,2,1536]{3,2,1,0:T(2,128)(2,1)} %bitcast.103) | data formatting | bytes 9437184
  48.9 2.3 convolution_convert_fusion.3
  51.7 4.0 %fusion.77 = (f32[6,256]{1,0:T(8,128)}, f32[6,256,256]{1,2,0:T(8,128)}) fusion(pred[256]{0:T(512)(128)(4,1)S(1)} %or_and_fusion, bf16[256,6,64]{0,2,1:T(8,128)(2,1)S(1)} %bitcast.131, bf16[256,6,64]{0,2,1:T(8,128)(2,1)S(1)} %bitcast.129, bf16[6,128,256]{1,2,0:T(8,128)(2,1)} %copy.109, bf16[6,128,256]{1,2,0:T(8,128)(2,1)} %collective-permute-done.1, ...), kind=kOutput, calls=%fused_computation.190 | convolution fusion | flops 56230144 | bytes 2758913 | tf_op jit(solution)/shard_map/sub | solution.py:281
  58.2 1.9 collective-permute-start.2
  64.3 2.6 %fusion.75 = (f32[256]{0:T(256)S(1)}, f32[256,768]{1,0:T(8,128)S(1)}, f32[256,768]{1,0:T(8,128)S(1)}) fusion(f32[768]{0:T(1024)S(1)} %get-tuple-element.116, bf16[128,768]{1,0:T(8,128)(2,1)S(1)} %bitcast.120, bf16[128,768]{1,0:T(8,128)(2,1)S(1)} %collective-permute-done, pred[]{:T(512)S(6)} %eq.40, f32[768]{0:T(1024)} %param.27, ...), kind=kOutput, calls=%fused_computation.188 | convolution fusion | flops 311820032 | bytes 3546113 | tf_op jit(solution)/shard_map/dot_general | solution.py:292
  67.1 3.9 %fusion.70 = f32[256,3072]{1,0:T(8,128)S(1)} fusion(bf16[768,3072]{1,0:T(8,128)(2,1)} %bitcast.104, f32[256,768]{1,0:T(8,128)S(1)} %get-tuple-element.80, f32[768]{0:T(1024)S(1)} %copy-done.37, f32[768]{0:T(1024)S(1)} %get-tuple-element.68, f32[256]{0:T(256)S(1)} %add_rsqrt_fusion, f32[256]{0:T(256)S(1)} %broadcast_multiply_fusion.4), kind=kOutput, calls=%fused_computation.186 | convolution fusion | flops 1208942592 | bytes 8658944 | tf_op jit(solution)/shard_map/dot_general | solution.py:298
  71.1 2.3 multiply_convert_fusion.2
  77.8 3.6 %broadcast_in_dim.69 = bf16[768,4992]{1,0:T(8,128)(2,1)} broadcast(bf16[]{:T(256)} %constant.17.clone.1), dimensions={} | broadcast | bytes 7667714 | tf_op jit(solution)/shard_map/broadcast_in_dim | solution.py:337
  81.4 3.7 %fusion.1 = bf16[768,4992]{1,0:T(8,128)(2,1)} fusion(bf16[768,4992]{1,0:T(8,128)(2,1)} %broadcast_in_dim.69, bf16[256,1536]{1,0:T(8,128)(2,1)S(1)} %get-tuple-element.82, bf16[256,1536]{1,0:T(8,128)(2,1)S(1)} %get-tuple-element.81, f32[256,768]{1,0:T(8,128)S(1)} %get-tuple-element.80, f32[768]{0:T(1024)S(1)} %copy-done.37, f32[768]{0:T(1024)S(1)} %get-tuple-element.68, ...), kind=kOutput, calls=%fused_computation.3 | convolution fusion | flops 1214447616 | bytes 7086080 | tf_op jit(solution)/shard_map/dot_general | solution.py:319
  85.1 3.4 %fusion.2 = bf16[768,4992]{1,0:T(8,128)(2,1)} fusion(bf16[768,4992]{1,0:T(8,128)(2,1)} %fusion.1, bf16[256,1536]{1,0:T(8,128)(2,1)S(1)} %get-tuple-element.83, f32[768]{0:T(1024)S(1)} %get-tuple-element.73, bf16[128,768]{1,0:T(8,128)(2,1)} %collective-permute-done.5, bf16[128,768]{1,0:T(8,128)(2,1)S(1)} %bitcast.135, pred[]{:T(512)S(6)} %eq.40), kind=kOutput, calls=%fused_computation.5 | convolution fusion | flops 607518720 | bytes 3542017 | tf_op jit(solution)/shard_map/dot_general | solution.py:310
  90.6 9.7 %collective-permute-done.6 = f32[256,768]{1,0:T(8,128)S(1)} collective-permute-done((f32[256,768]{1,0:T(8,128)S(1)}, f32[256,768]{1,0:T(8,128)S(1)}, u32[]{:S(2)}, u32[]{:S(2)}) %collective-permute-start.6) | collective-permute-done | bytes 786464 | tf_op jit(solution)/shard_map/ppermute | solution.py:135
  101.5 2.2 multiply_reduce_fusion.7
  111.3 2.4 convolution_convert_fusion.5
  119.8 2.6 %collective-permute-done.8 = bf16[6,128,256]{1,2,0:T(8,128)(2,1)} collective-permute-done((bf16[6,128,256]{1,2,0:T(8,128)(2,1)}, bf16[6,128,256]{1,2,0:T(8,128)(2,1)}, u32[]{:S(2)}, u32[]{:S(2)}) %collective-permute-start.8) | collective-permute-done | bytes 393248 | tf_op jit(solution)/shard_map/ppermute | solution.py:135
  127.1 2.8 %fusion.27 = (f32[768]{0:T(1024)S(1)}, f32[768]{0:T(1024)S(1)}, f32[256]{0:T(256)S(1)}, f32[256]{0:T(256)S(1)}, f32[256,768]{1,0:T(8,128)}, /*index=5*/f32[256,768]{1,0:T(8,128)}) fusion(bf16[256,768]{1,0:T(8,128)(2,1)} %collective-permute-done.7, bf16[256,768]{1,0:T(8,128)(2,1)} %convolution_convert_fusion.5, f32[256]{0:T(256)S(1)} %copy-done.34, ...), kind=kLoop, calls=%fused_computation.80 | loop fusion | flops 4323328 | bytes 2765825 | tf_op jit(solution)/shard_map/reduce_sum | solution.py:377
  129.9 34.2 %shard_map.256 = (bf16[32768,256]{1,0:T(8,128)(2,1)}, f32[16,256]{1,0:T(8,128)}, f32[1,256]{1,0:T(1,128)}) custom-call(bf16[32768,256]{1,0:T(8,128)(2,1)} %bitcast.98, bf16[16,32768]{1,0:T(8,128)(2,1)} %pad.9.ds_ref, f32[1,256]{1,0:T(1,128)} %bitcast.151, bf16[16,256]{1,0:T(8,128)(2,1)} %pad.8.wt_ref), custom_call_target="tpu_custom_call" | custom-call | flops 704643072 | bytes 34603008 | tf_op jit(solution)/shard_map/pallas_call | solution.py:85
  166.9 2.5 %convolution_multiply_fusion.2 = f32[1,256]{1,0:T(1,128)} fusion(bf16[256,4608]{1,0:T(8,128)(2,1)S(1)} %copy-done.5, f32[1,4608]{1,0:T(1,128)S(1)} %get-tuple-element.100, f32[1,256]{1,0:T(1,128)S(1)} %copy-done.28), kind=kOutput, calls=%fused_computation.48 | convolution fusion | flops 14157824 | bytes 2379776 | tf_op jit(solution)/shard_map/dot_general | solution.py:409
  169.9 2.4 collective-permute-start.10
  172.3 2.8 %collective-permute-done.10 = f32[1,8960]{1,0:T(1,128)S(1)} collective-permute-done((f32[1,8960]{1,0:T(1,128)S(1)}, f32[1,8960]{1,0:T(1,128)S(1)}, u32[]{:S(2)}, u32[]{:S(2)}) %collective-permute-start.10) | collective-permute-done | bytes 35872 | tf_op jit(solution)/shard_map/ppermute | solution.py:161
  176.9 7.5 %collective-permute-done.11 = f32[2,8960]{1,0:T(2,128)S(1)} collective-permute-done((f32[2,8960]{1,0:T(2,128)S(1)}, f32[2,8960]{1,0:T(2,128)S(1)}, u32[]{:S(2)}, u32[]{:S(2)}) %collective-permute-start.11) | collective-permute-done | bytes 71712 | tf_op jit(solution)/shard_map/ppermute | solution.py:161
  186.7 3.1 %collective-permute-done.12 = f32[4,8960]{1,0:T(4,128)S(1)} collective-permute-done((f32[4,8960]{1,0:T(4,128)S(1)}, f32[4,8960]{1,0:T(4,128)S(1)}, u32[]{:S(2)}, u32[]{:S(2)}) %collective-permute-start.12) | collective-permute-done | bytes 143392 | tf_op jit(solution)/shard_map/ppermute | solution.py:161
  195.8 4.2 %fusion.44 = f32[256,4608]{1,0:T(8,128)} fusion(bf16[16,256]{1,0:T(8,128)(2,1)S(1)} %multiply_convert_fusion.7, f32[16,8960]{1,0:T(8,128)S(1)} %gather_fusion), kind=kOutput, calls=%fused_computation.112 | convolution fusion | flops 226492416 | bytes 5021696 | tf_op jit(solution)/shard_map/dot_general | solution.py:407
  200.0 9.3 %collective-permute-done.15 = bf16[192,1152]{1,0:T(8,128)(2,1)S(1)} collective-permute-done((bf16[192,1152]{1,0:T(8,128)(2,1)S(1)}, bf16[192,1152]{1,0:T(8,128)(2,1)S(1)}, u32[]{:S(2)}, u32[]{:S(2)}) %collective-permute-start.15) | collective-permute-done | bytes 442400 | tf_op jit(solution)/shard_map/ppermute | solution.py:185
  209.6 11.9 %collective-permute-done.16 = bf16[96,1152]{1,0:T(8,128)(2,1)S(1)} collective-permute-done((bf16[96,1152]{1,0:T(8,128)(2,1)S(1)}, bf16[96,1152]{1,0:T(8,128)(2,1)S(1)}, u32[]{:S(2)}, u32[]{:S(2)}) %collective-permute-start.16) | collective-permute-done | bytes 221216 | tf_op jit(solution)/shard_map/ppermute | solution.py:185
  221.6 2.9 %collective-permute-start.17 = (bf16[48,1152]{1,0:T(8,128)(2,1)S(1)}, bf16[48,1152]{1,0:T(8,128)(2,1)S(1)}, u32[]{:S(2)}, u32[]{:S(2)}) collective-permute-start(bf16[48,1152]{1,0:T(8,128)(2,1)S(1)} %fusion.49), channel_id=1, source_target_pairs={{0,16},{2,18},{4,20},{6,22},{8,24},{10,26},{12,28},{14,30},{16,0},... | collective-permute-start | bytes 331784 | tf_op jit(solution)/shard_map/ppermute | solution.py:185
  225.1 4.4 %collective-permute-done.17 = bf16[48,1152]{1,0:T(8,128)(2,1)S(1)} collective-permute-done((bf16[48,1152]{1,0:T(8,128)(2,1)S(1)}, bf16[48,1152]{1,0:T(8,128)(2,1)S(1)}, u32[]{:S(2)}, u32[]{:S(2)}) %collective-permute-start.17) | collective-permute-done | bytes 110624 | tf_op jit(solution)/shard_map/ppermute | solution.py:185
  (214 shorter events, 59.1 us)
Async XLA Ops:
  7.2 63.9 %copy-start = (bf16[1536,768]{1,0:T(8,128)(2,1)S(1)}, bf16[1536,768]{1,0:T(8,128)(2,1)}, u32[]{:S(2)}) copy-start(bf16[1536,768]{1,0:T(8,128)(2,1)} %param.29) | copy-start | bytes 7077892
  7.2 223.1 %reduce-scatter.2.cloned.1.call-start = ((), (), s32[]{:S(2)}) async-start(), calls=%async_computation.1 | async-start | bytes 8146944 | tf_op jit(solution)/shard_map/reduce_scatter | solution.py:341
  7.2 40.6 %collective-permute-start = (bf16[128,768]{1,0:T(8,128)(2,1)}, bf16[128,768]{1,0:T(8,128)(2,1)S(1)}, u32[]{:S(2)}, u32[]{:S(2)}) collective-permute-start(bf16[128,768]{1,0:T(8,128)(2,1)} %bitcast.116), channel_id=1, source_target_pairs={{0,1},{1,0},{2,3},{3,2},{4,5},{5,4},{6,7},{7,6},{8,9},{9,8},{10,11... | collective-permute-start | bytes 589832 | tf_op jit(solution)/shard_map/ppermute | solution.py:135
  10.3 60.8 %collective-permute-start.5 = (bf16[128,768]{1,0:T(8,128)(2,1)}, bf16[128,768]{1,0:T(8,128)(2,1)}, u32[]{:S(2)}, u32[]{:S(2)}) collective-permute-start(bf16[128,768]{1,0:T(8,128)(2,1)} %bitcast.133), channel_id=1, source_target_pairs={{0,1},{1,0},{2,3},{3,2},{4,5},{5,4},{6,7},{7,6},{8,9},{9,8},{10,11... | collective-permute-start | bytes 589832 | tf_op jit(solution)/shard_map/ppermute | solution.py:135
  10.4 52.4 %collective-permute-start.3 = (bf16[384,768]{1,0:T(8,128)(2,1)}, bf16[384,768]{1,0:T(8,128)(2,1)}, u32[]{:S(2)}, u32[]{:S(2)}) collective-permute-start(bf16[384,768]{1,0:T(8,128)(2,1)} %param.26), channel_id=1, source_target_pairs={{0,1},{1,0},{2,3},{3,2},{4,5},{5,4},{6,7},{7,6},{8,9},{9,8},{10,11... | collective-permute-start | bytes 1769480 | tf_op jit(solution)/shard_map/ppermute | solution.py:135
  33.3 18.4 %collective-permute-start.1 = (bf16[6,128,256]{1,2,0:T(8,128)(2,1)}, bf16[6,128,256]{1,2,0:T(8,128)(2,1)}, u32[]{:S(2)}, u32[]{:S(2)}) collective-permute-start(bf16[6,128,256]{1,2,0:T(8,128)(2,1)} %copy.110), channel_id=1, source_target_pairs={{0,1},{1,0},{2,3},{3,2},{4,5},{5,4},{6,7},{7,6},{8,9},{9,8},{10,11... | collective-permute-start | bytes 1179656 | tf_op jit(solution)/shard_map/ppermute | solution.py:135
  37.4 11.0 %copy-start.35 = (f32[768]{0:T(1024)}, f32[768]{0:T(1024)S(1)}, u32[]{:S(2)}) copy-start(f32[768]{0:T(1024)S(1)} %get-tuple-element.70) | copy-start | bytes 9220
  47.9 66.5 %copy-start.12 = (bf16[128,768]{1,0:T(8,128)(2,1)}, bf16[128,768]{1,0:T(8,128)(2,1)S(1)}, u32[]{:S(2)}) copy-start(bf16[128,768]{1,0:T(8,128)(2,1)S(1)} %collective-permute-done) | copy-start | bytes 589828
  58.2 6.0 %collective-permute-start.2 = (bf16[256,384]{1,0:T(8,128)(2,1)}, bf16[256,384]{1,0:T(8,128)(2,1)S(1)}, u32[]{:S(2)}, u32[]{:S(2)}) collective-permute-start(bf16[256,384]{1,0:T(8,128)(2,1)} %copy.94), channel_id=1, source_target_pairs={{0,1},{1,0},{2,3},{3,2},{4,5},{5,4},{6,7},{7,6},{8,9},{9,8},{10,11... | collective-permute-start | bytes 589832 | tf_op jit(solution)/shard_map/ppermute | solution.py:135
  74.2 14.3 %collective-permute-start.4 = (bf16[256,768]{1,0:T(8,128)(2,1)S(1)}, bf16[256,768]{1,0:T(8,128)(2,1)S(1)}, u32[]{:S(2)}, u32[]{:S(2)}) collective-permute-start(bf16[256,768]{1,0:T(8,128)(2,1)S(1)} %convolution_convert_fusion.6), channel_id=1, source_target_pairs={{0,1},{1,0},{2,3},{3,2},{4,5},{5,4},{6,7},{7,6},{8,9},{9,8},{10,11... | collective-permute-start | bytes 1179656 | tf_op jit(solution)/shard_map/ppermute | solution.py:135
  77.5 22.8 %collective-permute-start.6 = (f32[256,768]{1,0:T(8,128)S(1)}, f32[256,768]{1,0:T(8,128)S(1)}, u32[]{:S(2)}, u32[]{:S(2)}) collective-permute-start(f32[256,768]{1,0:T(8,128)S(1)} %fusion.15), channel_id=1, source_target_pairs={{0,1},{1,0},{2,3},{3,2},{4,5},{5,4},{6,7},{7,6},{8,9},{9,8},{10,11... | collective-permute-start | bytes 2359304 | tf_op jit(solution)/shard_map/ppermute | solution.py:135
  110.0 12.3 %collective-permute-start.8 = (bf16[6,128,256]{1,2,0:T(8,128)(2,1)}, bf16[6,128,256]{1,2,0:T(8,128)(2,1)}, u32[]{:S(2)}, u32[]{:S(2)}) collective-permute-start(bf16[6,128,256]{1,2,0:T(8,128)(2,1)} %get-tuple-element.90), channel_id=1, source_target_pairs={{0,1},{1,0},{2,3},{3,2},{4,5},{5,4},{6,7},{7,6},{8,9},{9,8},{10,11... | collective-permute-start | bytes 1179656 | tf_op jit(solution)/shard_map/ppermute | solution.py:135
  113.7 13.4 %collective-permute-start.7 = (bf16[256,768]{1,0:T(8,128)(2,1)}, bf16[256,768]{1,0:T(8,128)(2,1)}, u32[]{:S(2)}, u32[]{:S(2)}) collective-permute-start(bf16[256,768]{1,0:T(8,128)(2,1)} %convolution_convert_fusion.5), channel_id=1, source_target_pairs={{0,1},{1,0},{2,3},{3,2},{4,5},{5,4},{6,7},{7,6},{8,9},{9,8},{10,11... | collective-permute-start | bytes 1179656 | tf_op jit(solution)/shard_map/ppermute | solution.py:135
  116.8 73.2 %collective-permute-start.14 = (bf16[384,1152]{1,0:T(8,128)(2,1)}, bf16[384,1152]{1,0:T(8,128)(2,1)}, u32[]{:S(2)}, u32[]{:S(2)}) collective-permute-start(bf16[384,1152]{1,0:T(8,128)(2,1)} %bitcast.29), channel_id=1, source_target_pairs={{0,2},{2,0},{4,6},{6,4},{8,10},{10,8},{12,14},{14,12},{16,18},{18,... | collective-permute-start | bytes 2654216 | tf_op jit(solution)/shard_map/ppermute | solution.py:185
  129.9 37.0 %copy-start.26 = (f32[768]{0:T(1024)S(1)}, f32[768]{0:T(1024)}, u32[]{:S(2)}) copy-start(f32[768]{0:T(1024)} %get-tuple-element.62) | copy-start | bytes 9220
  129.9 37.0 %copy-start.24 = (f32[768]{0:T(1024)S(1)}, f32[768]{0:T(1024)}, u32[]{:S(2)}) copy-start(f32[768]{0:T(1024)} %get-tuple-element.58) | copy-start | bytes 9220
  129.9 37.0 %copy-start.23 = (f32[768]{0:T(1024)S(1)}, f32[768]{0:T(1024)}, u32[]{:S(2)}) copy-start(f32[768]{0:T(1024)} %get-tuple-element.63) | copy-start | bytes 9220
  129.9 37.0 %copy-start.5 = (bf16[256,4608]{1,0:T(8,128)(2,1)S(1)}, bf16[256,4608]{1,0:T(8,128)(2,1)}, u32[]{:S(2)}) copy-start(bf16[256,4608]{1,0:T(8,128)(2,1)} %param.21) | copy-start | bytes 7077892
  129.9 37.0 %copy-start.28 = (f32[1,256]{1,0:T(1,128)S(1)}, f32[1,256]{1,0:T(1,128)}, u32[]{:S(2)}) copy-start(f32[1,256]{1,0:T(1,128)} %param.18) | copy-start | bytes 3076
  164.2 21.6 %copy-start.4 = (f32[256,768]{1,0:T(8,128)S(1)}, f32[256,768]{1,0:T(8,128)}, u32[]{:S(2)}) copy-start(f32[256,768]{1,0:T(8,128)} %copy-done.2) | copy-start | bytes 2359300
  164.2 21.6 %copy-start.38 = (f32[128]{0:T(128)S(1)}, f32[128]{0:T(128)}, u32[]{:S(2)}) copy-start(f32[128]{0:T(128)} %dynamic-slice.14) | copy-start | bytes 1540
  165.2 20.6 %copy-start.14 = (f32[256,768]{1,0:T(8,128)S(1)}, f32[256,768]{1,0:T(8,128)}, u32[]{:S(2)}) copy-start(f32[256,768]{1,0:T(8,128)} %get-tuple-element.86) | copy-start | bytes 2359300
  165.2 20.6 %copy-start.15 = (f32[256,768]{1,0:T(8,128)S(1)}, f32[256,768]{1,0:T(8,128)}, u32[]{:S(2)}) copy-start(f32[256,768]{1,0:T(8,128)} %get-tuple-element.96) | copy-start | bytes 2359300
  166.0 3.8 %collective-permute-start.9 = (f32[1,3328]{1,0:T(1,128)S(1)}, f32[1,3328]{1,0:T(1,128)S(1)}, u32[]{:S(2)}, u32[]{:S(2)}) collective-permute-start(f32[1,3328]{1,0:T(1,128)S(1)} %broadcast_in_dim.66), channel_id=1, source_target_pairs={{0,1},{1,0},{2,3},{3,2},{4,5},{5,4},{6,7},{7,6},{8,9},{9,8},{10,11... | collective-permute-start | bytes 39944 | tf_op jit(solution)/shard_map/ppermute | solution.py:135
  169.4 20.5 %copy-start.6 = (f32[8,1,48,1152]{3,2,1,0:T(8,128)S(1)}, f32[8,1,48,1152]{3,2,1,0:T(8,128)}, u32[]{:S(2)}) copy-start(f32[8,1,48,1152]{3,2,1,0:T(8,128)} %slice_select_fusion) | copy-start | bytes 5308420
  169.9 5.2 %collective-permute-start.10 = (f32[1,8960]{1,0:T(1,128)S(1)}, f32[1,8960]{1,0:T(1,128)S(1)}, u32[]{:S(2)}, u32[]{:S(2)}) collective-permute-start(f32[1,8960]{1,0:T(1,128)S(1)} %constant_dynamic-update-slice_fusion.6), channel_id=1, source_target_pairs={{0,16},{2,18},{4,20},{6,22},{8,24},{10,26},{12,28},{14,30},{16,0},... | collective-permute-start | bytes 107528 | tf_op jit(solution)/shard_map/ppermute | solution.py:161
  175.1 9.3 %collective-permute-start.11 = (f32[2,8960]{1,0:T(2,128)S(1)}, f32[2,8960]{1,0:T(2,128)S(1)}, u32[]{:S(2)}, u32[]{:S(2)}) collective-permute-start(f32[2,8960]{1,0:T(2,128)S(1)} %maximum_select_fusion.12), channel_id=1, source_target_pairs={{0,8},{2,10},{4,12},{6,14},{8,0},{10,2},{12,4},{14,6},{16,24},{18,... | collective-permute-start | bytes 215048 | tf_op jit(solution)/shard_map/ppermute | solution.py:161
  184.6 5.2 %collective-permute-start.12 = (f32[4,8960]{1,0:T(4,128)S(1)}, f32[4,8960]{1,0:T(4,128)S(1)}, u32[]{:S(2)}, u32[]{:S(2)}) collective-permute-start(f32[4,8960]{1,0:T(4,128)S(1)} %maximum_select_fusion.10), channel_id=1, source_target_pairs={{0,4},{2,6},{4,0},{6,2},{8,12},{10,14},{12,8},{14,10},{16,20},{18,... | collective-permute-start | bytes 430088 | tf_op jit(solution)/shard_map/ppermute | solution.py:161
  189.9 3.0 %collective-permute-start.13 = (f32[8,8960]{1,0:T(8,128)S(1)}, f32[8,8960]{1,0:T(8,128)S(1)}, u32[]{:S(2)}, u32[]{:S(2)}) collective-permute-start(f32[8,8960]{1,0:T(8,128)S(1)} %maximum_select_fusion.9), channel_id=1, source_target_pairs={{0,2},{2,0},{4,6},{6,4},{8,10},{10,8},{12,14},{14,12},{16,18},{18,... | collective-permute-start | bytes 860168 | tf_op jit(solution)/shard_map/ppermute | solution.py:161
  191.6 17.7 %collective-permute-start.15 = (bf16[192,1152]{1,0:T(8,128)(2,1)S(1)}, bf16[192,1152]{1,0:T(8,128)(2,1)S(1)}, u32[]{:S(2)}, u32[]{:S(2)}) collective-permute-start(bf16[192,1152]{1,0:T(8,128)(2,1)S(1)} %bitcast.138), channel_id=1, source_target_pairs={{0,4},{2,6},{4,0},{6,2},{8,12},{10,14},{12,8},{14,10},{16,20},{18,... | collective-permute-start | bytes 1327112 | tf_op jit(solution)/shard_map/ppermute | solution.py:185
  209.4 12.1 %collective-permute-start.16 = (bf16[96,1152]{1,0:T(8,128)(2,1)S(1)}, bf16[96,1152]{1,0:T(8,128)(2,1)S(1)}, u32[]{:S(2)}, u32[]{:S(2)}) collective-permute-start(bf16[96,1152]{1,0:T(8,128)(2,1)S(1)} %bitcast.140), channel_id=1, source_target_pairs={{0,8},{2,10},{4,12},{6,14},{8,0},{10,2},{12,4},{14,6},{16,24},{18,... | collective-permute-start | bytes 663560 | tf_op jit(solution)/shard_map/ppermute | solution.py:185
  221.6 8.0 %collective-permute-start.17 = (bf16[48,1152]{1,0:T(8,128)(2,1)S(1)}, bf16[48,1152]{1,0:T(8,128)(2,1)S(1)}, u32[]{:S(2)}, u32[]{:S(2)}) collective-permute-start(bf16[48,1152]{1,0:T(8,128)(2,1)S(1)} %fusion.49), channel_id=1, source_target_pairs={{0,16},{2,18},{4,20},{6,22},{8,24},{10,26},{12,28},{14,30},{16,0},... | collective-permute-start | bytes 331784 | tf_op jit(solution)/shard_map/ppermute | solution.py:185
  (31 other events, 121.5 us)
Sparse Core Ops, SparseCore 0:
  118.5 102.7 reduce-scatter.1

commit v7 on v3

--- a/solution.py
+++ b/solution.py
@@ -228,9 +228,19 @@
     qkv_w = qkv_weight.reshape(width, 3 * proj)
     gate_up_w = gate_up_weight.reshape(width, 2 * ffn)
 
-    x_rows = whole_rows(layer_input[0], first)
-    g_rows = whole_rows(output_grad[0], first)
-    out_weight_all = whole_rows(out_weight, first)
+    bundle = jnp.concatenate([layer_input[0], output_grad[0], out_weight], axis=0)
+    bundle_other = swap_heads(bundle)
+
+    def joined(start, size):
+        own = bundle[start : start + size]
+        other = bundle_other[start : start + size]
+        return jnp.where(
+            first, jnp.concatenate([own, other], axis=0), jnp.concatenate([other, own], axis=0)
+        )
+
+    x_rows = joined(0, rows)
+    g_rows = joined(rows, rows)
+    out_weight_all = joined(2 * rows, out_weight.shape[0])
 
     positions = jnp.arange(length, dtype=jnp.int32)
     valid = (positions < chain_lengths[0]) & ((residue_mask[0] == 1) | (positions == 0))

time: 221 us -> 224 us (1.014)
  local copies, waits for them, and re-layouts: 38 us -> 41 us
  other arithmetic: 14.9 us -> 17.4 us
    concatenate x0 -> x1, other arithmetic: none -> 2.32 us  [shards(): jnp.concatenate([layer_input[0], output_grad[0], out_weight], axis=0)]
    ppermute x10 -> x8, starting transfers between devices: 9.68 us -> 8.37 us  [swap_heads(): return lax.ppermute(values, 'head', [(0, 1), (1, 0)])]
    ppermute x10 -> x8, waiting for transfers between devices: 15.7 us -> 15.4 us  [swap_heads(): return lax.ppermute(values, 'head', [(0, 1), (1, 0)])]
    unnamed x117 -> x119, local copies, waits for them, and re-layouts: 17.6 us -> 17.5 us
  transfers between devices with their start and end apart: 19 -> 17, of which waited for: 10 -> 8; matrix products, arithmetic and copies ran while one was open for 34% -> 31% of each run, Pallas kernels for 22% -> 22%
where the time goes in v7:
time: 224 us; the launch traced here: 223 us
  Pallas kernels  49.2 us (22%)
  waiting for transfers between devices  41.1 us (18%)
  local copies, waits for them, and re-layouts  41 us (18%)
  matrix products  40.1 us (18%)
  starting transfers between devices  18.2 us (8%)
  other arithmetic  17.4 us (8%)
  between operations  15.5 us (7%)
    pallas_call x1, Pallas kernels, pair_backward(): pl.pallas_call(pair_backward_kernel, grid=(m // tile,), in_specs=[pl.Bloc...  34 us
    unnamed x119, local copies, waits for them, and re-layouts  17.5 us
    ppermute x8, waiting for transfers between devices, swap_heads(): return lax.ppermute(values, 'head', [(0, 1), (1, 0)])  15.4 us
    pallas_call x1, Pallas kernels, pair_forward(): pl.pallas_call(pair_forward_kernel, grid=(m // tile,), in_specs=[pl.Block...  15.2 us
    reduce_scatter x1, waiting for transfers between devices, shards(): lax.psum_scatter(packed, 'dp', scatter_dimension=0, tiled=True)  14.3 us
    ppermute x8, starting transfers between devices, swap_heads(): return lax.ppermute(values, 'head', [(0, 1), (1, 0)])  8.37 us
    ppermute x4, waiting for transfers between devices, dp_gather(): other = lax.ppermute(block, 'dp', [(i, i ^ step) for i in range(count)])  6.05 us
    ppermute x4, waiting for transfers between devices, dp_sum(): other = lax.ppermute(values, 'dp', [(i, i ^ step) for i in range(count)])  5.25 us
  transfers between devices with their start and end apart: 17, of which 8 were waited for; matrix products, arithmetic and copies ran while one was open for 31% of the time, Pallas kernels for 22%

profile of v7, /device:TPU:0, one launch (start us, length us, event | category | flops | bytes accessed | tf_op | source)
XLA Modules:
  0.0 222.5 jit_solution(1877673239679320133)
XLA Ops:
  7.2 2.3 %pad_maximum_fusion.3 = bf16[640,768]{1,0:T(8,128)(2,1)} fusion(bf16[384,768]{1,0:T(8,128)(2,1)} %param.25, bf16[128,768]{1,0:T(8,128)(2,1)} %bitcast.98, bf16[128,768]{1,0:T(8,128)(2,1)} %bitcast.87), kind=kLoop, calls=%fused_computation.48 | loop fusion | flops 2949120 | bytes 1966080 | tf_op jit(solution)/shard_map/concatenate | solution.py:231
  9.6 3.0 %collective-permute-start = (bf16[640,768]{1,0:T(8,128)(2,1)}, bf16[640,768]{1,0:T(8,128)(2,1)}, u32[]{:S(2)}, u32[]{:S(2)}) collective-permute-start(bf16[640,768]{1,0:T(8,128)(2,1)} %pad_maximum_fusion.3), channel_id=1, source_target_pairs={{0,1},{1,0},{2,3},{3,2},{4,5},{5,4},{6,7},{7,6},{8,9},{9,8},{10,11... | collective-permute-start | bytes 2949128 | tf_op jit(solution)/shard_map/ppermute | solution.py:135
  13.1 15.2 %shard_map.246 = bf16[12,32768]{1,0:T(8,128)(2,1)} custom-call(bf16[32768,256]{1,0:T(8,128)(2,1)} %bitcast.80, f32[1,256]{1,0:T(1,128)} %bitcast.122, bf16[16,256]{1,0:T(8,128)(2,1)} %pad.8.wt_ref), custom_call_target="tpu_custom_call" | custom-call | flops 352321536 | bytes 17563648 | tf_op jit(solution)/shard_map/pallas_call | solution.py:38
  30.7 1.9 copy.90
  33.3 2.1 convolution_reduce_fusion
  36.4 3.9 %copy.66 = bf16[768,3,384]{0,2,1:T(8,128)(2,1)} copy(bf16[768,3,384]{2,0,1:T(8,128)(2,1)} %param.22) | data formatting | bytes 3538944 | tf_op args[7]
  43.5 2.3 %convolution_convert_fusion.3 = bf16[256,1152]{1,0:T(8,128)(2,1)S(1)} fusion(bf16[768,1152]{0,1:T(8,128)(2,1)} %bitcast.96, f32[768]{0:T(1024)S(1)} %get-tuple-element.57, f32[768]{0:T(1024)S(1)} %get-tuple-element.58, f32[256]{0:T(256)S(1)} %add_rsqrt_fusion.1, f32[256]{0:T(256)S(1)} %broadcast_multiply_fusion.5, bf16[128,768]{1,0:T(8,128)(2,1)S(1)} %bitcast.90, ...), kind=kOutput, calls=%fused_computation.7 | convolution fusion | flops 456228864 | bytes 2760705 | tf_op jit(solution)/shard_map/dot_general | solution.py:266
  48.7 3.4 %fusion.78 = (f32[6,256]{1,0:T(8,128)S(1)}, f32[6,256,256]{1,2,0:T(8,128)}) fusion(pred[256]{0:T(512)(128)(4,1)} %or_and_fusion, bf16[256,6,64]{0,2,1:T(8,128)(2,1)S(1)} %bitcast.108, bf16[256,6,64]{0,2,1:T(8,128)(2,1)S(1)} %bitcast.106, bf16[6,128,256]{1,2,0:T(8,128)(2,1)} %copy.89, bf16[6,128,256]{1,2,0:T(8,128)(2,1)} %collective-permute-done.1, pred[]{:T(512)S(6)} %eq.44), kind=kOutput, calls=%fused_computation.179 | convolution fusion | flops 56230144 | bytes 2758913 | tf_op jit(solution)/shard_map/sub | solution.py:274
  53.9 2.1 collective-permute-start.2
  56.0 3.6 %copy.93 = bf16[96,8,2,1536]{3,1,2,0:T(8,128)(2,1)S(1)} copy(bf16[96,8,2,1536]{3,2,1,0:T(2,128)(2,1)} %bitcast.82) | data formatting | bytes 9437184
  67.5 4.8 %broadcast_in_dim.64 = bf16[768,6144]{1,0:T(8,128)(2,1)} broadcast(bf16[]{:T(256)} %constant.30.clone.1), dimensions={} | broadcast | bytes 9437186 | tf_op jit(solution)/shard_map/broadcast_in_dim | solution.py:354
  72.2 3.9 %fusion.1 = bf16[768,6144]{1,0:T(8,128)(2,1)} fusion(bf16[768,6144]{1,0:T(8,128)(2,1)} %broadcast_in_dim.64, bf16[256,1536]{1,0:T(8,128)(2,1)S(1)} %get-tuple-element.69, bf16[256,1536]{1,0:T(8,128)(2,1)S(1)} %get-tuple-element.68, f32[256,768]{1,0:T(8,128)S(1)} %get-tuple-element.67, f32[768]{0:T(1024)S(1)} %copy-done.46, f32[768]{0:T(1024)S(1)} %get-tuple-element.55, ...), kind=kOutput, calls=%fused_computation.2 | convolution fusion | flops 1214447616 | bytes 7086080 | tf_op jit(solution)/shard_map/dot_general | solution.py:312
  76.1 2.3 %fusion.2 = bf16[768,6144]{1,0:T(8,128)(2,1)} fusion(bf16[768,6144]{1,0:T(8,128)(2,1)} %fusion.1, bf16[256,1536]{1,0:T(8,128)(2,1)S(1)} %get-tuple-element.70, f32[768]{0:T(1024)S(1)} %get-tuple-element.60, bf16[128,768]{1,0:T(8,128)(2,1)S(1)} %get-tuple-element.74, bf16[128,768]{1,0:T(8,128)(2,1)S(1)} %bitcast.101, pred[]{:T(512)S(6)} %eq.44), kind=kOutput, calls=%fused_computation.5 | convolution fusion | flops 607518720 | bytes 3542017 | tf_op jit(solution)/shard_map/dot_general | solution.py:303
  78.4 6.8 %collective-permute-done.4 = f32[256,768]{1,0:T(8,128)S(1)} collective-permute-done((f32[256,768]{1,0:T(8,128)S(1)}, f32[256,768]{1,0:T(8,128)S(1)}, u32[]{:S(2)}, u32[]{:S(2)}) %collective-permute-start.4) | collective-permute-done | bytes 786464 | tf_op jit(solution)/shard_map/ppermute | solution.py:135
  89.0 1.9 convolution_convert_fusion.7
  95.1 2.2 fusion.3
  97.3 2.7 %convolution_convert_fusion.6 = bf16[256,768]{1,0:T(8,128)(2,1)} fusion(bf16[256,1536]{1,0:T(8,128)(2,1)} %copy-done.51, bf16[1536,768]{1,0:T(8,128)(2,1)S(1)} %copy-done), kind=kOutput, calls=%fused_computation.23 | convolution fusion | flops 604176384 | bytes 3538944 | tf_op jit(solution)/shard_map/dot_general | solution.py:295
  100.9 8.5 %collective-permute-done.3 = bf16[256,768]{1,0:T(8,128)(2,1)} collective-permute-done((bf16[256,768]{1,0:T(8,128)(2,1)}, bf16[256,768]{1,0:T(8,128)(2,1)}, u32[]{:S(2)}, u32[]{:S(2)}) %collective-permute-start.3) | collective-permute-done | bytes 393248 | tf_op jit(solution)/shard_map/ppermute | solution.py:135
  109.4 1.9 fusion.24
  113.3 2.0 copy.80
  116.6 3.4 %convolution_convert_fusion.5 = bf16[256,768]{1,0:T(8,128)(2,1)} fusion(bf16[768,1152]{0,1:T(8,128)(2,1)} %bitcast.97, bf16[256,384]{0,1:T(8,128)(2,1)} %bitcast.128, bf16[256,384]{0,1:T(8,128)(2,1)S(1)} %bitcast.114, bf16[256,384]{0,1:T(8,128)(2,1)} %bitcast.116), kind=kOutput, calls=%fused_computation.22 | convolution fusion | flops 454950912 | bytes 2752512 | tf_op jit(solution)/shard_map/dot_general | solution.py:363
  120.0 1.8 collective-permute-start.5
  121.9 1.9 copy.81
  126.7 34.0 %shard_map.247 = (bf16[32768,256]{1,0:T(8,128)(2,1)}, f32[16,256]{1,0:T(8,128)}, f32[1,256]{1,0:T(1,128)}) custom-call(bf16[32768,256]{1,0:T(8,128)(2,1)} %bitcast.81, bf16[16,32768]{1,0:T(8,128)(2,1)} %pad.9.ds_ref, f32[1,256]{1,0:T(1,128)} %bitcast.123, bf16[16,256]{1,0:T(8,128)(2,1)} %pad.8.wt_ref), custom_call_target="tpu_custom_call" | custom-call | flops 704643072 | bytes 34603008 | tf_op jit(solution)/shard_map/pallas_call | solution.py:85
  162.8 1.7 fusion.28
  164.7 2.5 %convolution_multiply_fusion.2 = f32[1,256]{1,0:T(1,128)} fusion(bf16[256,4608]{1,0:T(8,128)(2,1)S(1)} %copy-done.6, f32[1,4608]{1,0:T(1,128)S(1)} %get-tuple-element.89, f32[1,256]{1,0:T(1,128)S(1)} %copy-done.32), kind=kOutput, calls=%fused_computation.45 | convolution fusion | flops 14157824 | bytes 2379776 | tf_op jit(solution)/shard_map/dot_general | solution.py:402
  170.7 3.7 %collective-permute-done.13 = f32[1,3328]{1,0:T(1,128)S(1)} collective-permute-done((f32[1,3328]{1,0:T(1,128)S(1)}, f32[1,3328]{1,0:T(1,128)S(1)}, u32[]{:S(2)}, u32[]{:S(2)}) %collective-permute-start.13) | collective-permute-done | bytes 13344 | tf_op jit(solution)/shard_map/ppermute | solution.py:168
  178.3 2.3 %collective-permute-start.15 = (f32[1,3328]{1,0:T(1,128)S(1)}, f32[1,3328]{1,0:T(1,128)S(1)}, u32[]{:S(2)}, u32[]{:S(2)}) collective-permute-start(f32[1,3328]{1,0:T(1,128)S(1)} %add.184), channel_id=1, source_target_pairs={{0,16},{2,18},{4,20},{6,22},{8,24},{10,26},{12,28},{14,30},{16,0},... | collective-permute-start | bytes 39944 | tf_op jit(solution)/shard_map/ppermute | solution.py:168
  180.7 2.6 %collective-permute-start.10 = (f32[8,5632]{1,0:T(8,128)S(1)}, f32[8,5632]{1,0:T(8,128)S(1)}, u32[]{:S(2)}, u32[]{:S(2)}) collective-permute-start(f32[8,5632]{1,0:T(8,128)S(1)} %maximum_select_fusion.9), channel_id=1, source_target_pairs={{0,16},{2,18},{4,20},{6,22},{8,24},{10,26},{12,28},{14,30},{16,0},... | collective-permute-start | bytes 540680 | tf_op jit(solution)/shard_map/ppermute | solution.py:153
  185.7 5.4 %collective-permute-done.10 = f32[8,5632]{1,0:T(8,128)S(1)} collective-permute-done((f32[8,5632]{1,0:T(8,128)S(1)}, f32[8,5632]{1,0:T(8,128)S(1)}, u32[]{:S(2)}, u32[]{:S(2)}) %collective-permute-start.10) | collective-permute-done | bytes 180256 | tf_op jit(solution)/shard_map/ppermute | solution.py:153
  192.5 4.2 %fusion.45 = f32[256,4608]{1,0:T(8,128)} fusion(bf16[16,256]{1,0:T(8,128)(2,1)S(1)} %multiply_convert_fusion.7, f32[16,5632]{1,0:T(8,128)S(1)} %maximum_select_fusion.8), kind=kOutput, calls=%fused_computation.103 | convolution fusion | flops 226492416 | bytes 5021696 | tf_op jit(solution)/shard_map/dot_general | solution.py:400
  196.7 14.3 %reduce-scatter.2.cloned.1.call-done = bf16[48,6144]{1,0:T(8,128)(2,1)} async-done(((bf16[768,6144]{1,0:T(8,128)(2,1)}), bf16[48,6144]{1,0:T(8,128)(2,1)}) %reduce-scatter.2.cloned.1.call-update) | async-done | bytes 589840 | tf_op jit(solution)/shard_map/reduce_scatter | solution.py:361
  (218 shorter events, 52.5 us)
Async XLA Ops:
  7.2 56.8 %copy-start = (bf16[1536,768]{1,0:T(8,128)(2,1)S(1)}, bf16[1536,768]{1,0:T(8,128)(2,1)}, u32[]{:S(2)}) copy-start(bf16[1536,768]{1,0:T(8,128)(2,1)} %param.28) | copy-start | bytes 7077892
  7.2 5.4 %copy-start.39 = (bf16[256,12]{0,1:T(8,128)(2,1)S(1)}, bf16[256,12]{0,1:T(8,128)(2,1)}, u32[]{:S(2)}) copy-start(bf16[256,12]{0,1:T(8,128)(2,1)} %param.24) | copy-start | bytes 18436
  7.2 203.8 %reduce-scatter.2.cloned.1.call-start = ((), (), s32[]{:S(2)}) async-start(), calls=%async_computation.1 | async-start | bytes 10027008 | tf_op jit(solution)/shard_map/reduce_scatter | solution.py:361
  9.6 32.4 %collective-permute-start = (bf16[640,768]{1,0:T(8,128)(2,1)}, bf16[640,768]{1,0:T(8,128)(2,1)}, u32[]{:S(2)}, u32[]{:S(2)}) collective-permute-start(bf16[640,768]{1,0:T(8,128)(2,1)} %pad_maximum_fusion.3), channel_id=1, source_target_pairs={{0,1},{1,0},{2,3},{3,2},{4,5},{5,4},{6,7},{7,6},{8,9},{9,8},{10,11... | collective-permute-start | bytes 2949128 | tf_op jit(solution)/shard_map/ppermute | solution.py:135
  32.6 16.0 %collective-permute-start.1 = (bf16[6,128,256]{1,2,0:T(8,128)(2,1)}, bf16[6,128,256]{1,2,0:T(8,128)(2,1)}, u32[]{:S(2)}, u32[]{:S(2)}) collective-permute-start(bf16[6,128,256]{1,2,0:T(8,128)(2,1)} %copy.90), channel_id=1, source_target_pairs={{0,1},{1,0},{2,3},{3,2},{4,5},{5,4},{6,7},{7,6},{8,9},{9,8},{10,11... | collective-permute-start | bytes 1179656 | tf_op jit(solution)/shard_map/ppermute | solution.py:135
  36.4 6.7 %copy-start.8 = (bf16[1,128,768]{2,1,0:T(8,128)(2,1)S(1)}, bf16[1,128,768]{2,1,0:T(8,128)(2,1)}, u32[]{:S(2)}) copy-start(bf16[1,128,768]{2,1,0:T(8,128)(2,1)} %param.15) | copy-start | bytes 589828
  43.0 43.1 %copy-start.10 = (bf16[128,768]{1,0:T(8,128)(2,1)}, bf16[128,768]{1,0:T(8,128)(2,1)S(1)}, u32[]{:S(2)}) copy-start(bf16[128,768]{1,0:T(8,128)(2,1)S(1)} %get-tuple-element.74) | copy-start | bytes 589828
  46.7 5.4 %copy-start.13 = (bf16[256,384]{0,1:T(8,128)(2,1)}, bf16[256,384]{0,1:T(8,128)(2,1)S(1)}, u32[]{:S(2)}) copy-start(bf16[256,384]{0,1:T(8,128)(2,1)S(1)} %copy.69) | copy-start | bytes 589828
  53.8 5.9 %copy-start.17 = (bf16[6,64,256]{2,1,0:T(8,128)(2,1)}, bf16[6,64,256]{2,1,0:T(8,128)(2,1)S(1)}, u32[]{:S(2)}) copy-start(bf16[6,64,256]{2,1,0:T(8,128)(2,1)S(1)} %convolution_convert_fusion.9) | copy-start | bytes 589828
  53.9 7.4 %collective-permute-start.2 = (bf16[256,384]{1,0:T(8,128)(2,1)S(1)}, bf16[256,384]{1,0:T(8,128)(2,1)S(1)}, u32[]{:S(2)}, u32[]{:S(2)}) collective-permute-start(bf16[256,384]{1,0:T(8,128)(2,1)S(1)} %copy.74), channel_id=1, source_target_pairs={{0,1},{1,0},{2,3},{3,2},{4,5},{5,4},{6,7},{7,6},{8,9},{9,8},{10,11... | collective-permute-start | bytes 589832 | tf_op jit(solution)/shard_map/ppermute | solution.py:135
  56.0 5.4 %copy-start.9 = (bf16[384,768]{1,0:T(8,128)(2,1)S(1)}, bf16[384,768]{1,0:T(8,128)(2,1)}, u32[]{:S(2)}) copy-start(bf16[384,768]{1,0:T(8,128)(2,1)} %param.25) | copy-start | bytes 1769476
  56.0 5.4 %copy-start.48 = (f32[768]{0:T(1024)S(1)}, f32[768]{0:T(1024)}, u32[]{:S(2)}) copy-start(f32[768]{0:T(1024)} %param.26) | copy-start | bytes 9220
  62.2 24.0 %copy-start.4 = (f32[256,768]{1,0:T(8,128)}, f32[256,768]{1,0:T(8,128)S(1)}, u32[]{:S(2)}) copy-start(f32[256,768]{1,0:T(8,128)S(1)} %get-tuple-element.67) | copy-start | bytes 2359300
  65.2 10.9 %copy-start.51 = (bf16[256,1536]{1,0:T(8,128)(2,1)}, bf16[256,1536]{1,0:T(8,128)(2,1)S(1)}, u32[]{:S(2)}) copy-start(bf16[256,1536]{1,0:T(8,128)(2,1)S(1)} %get-tuple-element.70) | copy-start | bytes 2359300
  66.7 18.5 %collective-permute-start.4 = (f32[256,768]{1,0:T(8,128)S(1)}, f32[256,768]{1,0:T(8,128)S(1)}, u32[]{:S(2)}, u32[]{:S(2)}) collective-permute-start(f32[256,768]{1,0:T(8,128)S(1)} %fusion.16), channel_id=1, source_target_pairs={{0,1},{1,0},{2,3},{3,2},{4,5},{5,4},{6,7},{7,6},{8,9},{9,8},{10,11... | collective-permute-start | bytes 2359304 | tf_op jit(solution)/shard_map/ppermute | solution.py:135
  97.3 12.1 %copy-start.26 = (f32[768]{0:T(1024)S(1)}, f32[768]{0:T(1024)}, u32[]{:S(2)}) copy-start(f32[768]{0:T(1024)} %get-tuple-element.59) | copy-start | bytes 9220
  100.0 9.5 %collective-permute-start.3 = (bf16[256,768]{1,0:T(8,128)(2,1)}, bf16[256,768]{1,0:T(8,128)(2,1)}, u32[]{:S(2)}, u32[]{:S(2)}) collective-permute-start(bf16[256,768]{1,0:T(8,128)(2,1)} %convolution_convert_fusion.6), channel_id=1, source_target_pairs={{0,1},{1,0},{2,3},{3,2},{4,5},{5,4},{6,7},{7,6},{8,9},{9,8},{10,11... | collective-permute-start | bytes 1179656 | tf_op jit(solution)/shard_map/ppermute | solution.py:135
  112.3 9.5 %collective-permute-start.6 = (bf16[6,128,256]{1,2,0:T(8,128)(2,1)}, bf16[6,128,256]{1,2,0:T(8,128)(2,1)}, u32[]{:S(2)}, u32[]{:S(2)}) collective-permute-start(bf16[6,128,256]{1,2,0:T(8,128)(2,1)} %get-tuple-element.79), channel_id=1, source_target_pairs={{0,1},{1,0},{2,3},{3,2},{4,5},{5,4},{6,7},{7,6},{8,9},{9,8},{10,11... | collective-permute-start | bytes 1179656 | tf_op jit(solution)/shard_map/ppermute | solution.py:135
  120.0 42.8 %collective-permute-start.5 = (bf16[256,768]{1,0:T(8,128)(2,1)}, bf16[256,768]{1,0:T(8,128)(2,1)}, u32[]{:S(2)}, u32[]{:S(2)}) collective-permute-start(bf16[256,768]{1,0:T(8,128)(2,1)} %convolution_convert_fusion.5), channel_id=1, source_target_pairs={{0,1},{1,0},{2,3},{3,2},{4,5},{5,4},{6,7},{7,6},{8,9},{9,8},{10,11... | collective-permute-start | bytes 1179656 | tf_op jit(solution)/shard_map/ppermute | solution.py:135
  126.7 36.1 %copy-start.35 = (f32[256]{0:T(256)S(1)}, f32[256]{0:T(256)}, u32[]{:S(2)}) copy-start(f32[256]{0:T(256)} %copy-done.33) | copy-start | bytes 3076
  126.7 36.1 %copy-start.43 = (f32[256]{0:T(256)S(1)}, f32[256]{0:T(256)}, u32[]{:S(2)}) copy-start(f32[256]{0:T(256)} %copy-done.40) | copy-start | bytes 3076
  162.6 4.7 %collective-permute-start.11 = (f32[1,3328]{1,0:T(1,128)S(1)}, f32[1,3328]{1,0:T(1,128)S(1)}, u32[]{:S(2)}, u32[]{:S(2)}) collective-permute-start(f32[1,3328]{1,0:T(1,128)S(1)} %broadcast_in_dim.65), channel_id=1, source_target_pairs={{0,1},{1,0},{2,3},{3,2},{4,5},{5,4},{6,7},{7,6},{8,9},{9,8},{10,11... | collective-permute-start | bytes 39944 | tf_op jit(solution)/shard_map/ppermute | solution.py:135
  164.7 18.7 %copy-start.3 = (f32[256,768]{1,0:T(8,128)S(1)}, f32[256,768]{1,0:T(8,128)}, u32[]{:S(2)}) copy-start(f32[256,768]{1,0:T(8,128)} %copy-done.1) | copy-start | bytes 2359300
  164.7 18.6 %copy-start.47 = (f32[128]{0:T(128)S(1)}, f32[128]{0:T(128)}, u32[]{:S(2)}) copy-start(f32[128]{0:T(128)} %dynamic-slice.14) | copy-start | bytes 1540
  167.2 1.2 collective-permute-start.7
  167.3 2.9 %collective-permute-start.12 = (f32[1,3328]{1,0:T(1,128)S(1)}, f32[1,3328]{1,0:T(1,128)S(1)}, u32[]{:S(2)}, u32[]{:S(2)}) collective-permute-start(f32[1,3328]{1,0:T(1,128)S(1)} %reshape_add_fusion), channel_id=1, source_target_pairs={{0,2},{2,0},{4,6},{6,4},{8,10},{10,8},{12,14},{14,12},{16,18},{18,... | collective-permute-start | bytes 39944 | tf_op jit(solution)/shard_map/ppermute | solution.py:168
  168.5 7.4 %collective-permute-start.8 = (f32[2,5632]{1,0:T(2,128)S(1)}, f32[2,5632]{1,0:T(2,128)S(1)}, u32[]{:S(2)}, u32[]{:S(2)}) collective-permute-start(f32[2,5632]{1,0:T(2,128)S(1)} %maximum_select_fusion.12), channel_id=1, source_target_pairs={{0,4},{2,6},{4,0},{6,2},{8,12},{10,14},{12,8},{14,10},{16,20},{18,... | collective-permute-start | bytes 135176 | tf_op jit(solution)/shard_map/ppermute | solution.py:153
  170.2 4.2 %collective-permute-start.13 = (f32[1,3328]{1,0:T(1,128)S(1)}, f32[1,3328]{1,0:T(1,128)S(1)}, u32[]{:S(2)}, u32[]{:S(2)}) collective-permute-start(f32[1,3328]{1,0:T(1,128)S(1)} %add.182), channel_id=1, source_target_pairs={{0,4},{2,6},{4,0},{6,2},{8,12},{10,14},{12,8},{14,10},{16,20},{18,... | collective-permute-start | bytes 39944 | tf_op jit(solution)/shard_map/ppermute | solution.py:168
  174.4 3.9 %collective-permute-start.14 = (f32[1,3328]{1,0:T(1,128)S(1)}, f32[1,3328]{1,0:T(1,128)S(1)}, u32[]{:S(2)}, u32[]{:S(2)}) collective-permute-start(f32[1,3328]{1,0:T(1,128)S(1)} %add.183), channel_id=1, source_target_pairs={{0,8},{2,10},{4,12},{6,14},{8,0},{10,2},{12,4},{14,6},{16,24},{18,... | collective-permute-start | bytes 39944 | tf_op jit(solution)/shard_map/ppermute | solution.py:168
  176.0 4.7 %collective-permute-start.9 = (f32[4,5632]{1,0:T(4,128)S(1)}, f32[4,5632]{1,0:T(4,128)S(1)}, u32[]{:S(2)}, u32[]{:S(2)}) collective-permute-start(f32[4,5632]{1,0:T(4,128)S(1)} %maximum_select_fusion.11), channel_id=1, source_target_pairs={{0,8},{2,10},{4,12},{6,14},{8,0},{10,2},{12,4},{14,6},{16,24},{18,... | collective-permute-start | bytes 270344 | tf_op jit(solution)/shard_map/ppermute | solution.py:153
  178.3 5.9 %collective-permute-start.15 = (f32[1,3328]{1,0:T(1,128)S(1)}, f32[1,3328]{1,0:T(1,128)S(1)}, u32[]{:S(2)}, u32[]{:S(2)}) collective-permute-start(f32[1,3328]{1,0:T(1,128)S(1)} %add.184), channel_id=1, source_target_pairs={{0,16},{2,18},{4,20},{6,22},{8,24},{10,26},{12,28},{14,30},{16,0},... | collective-permute-start | bytes 39944 | tf_op jit(solution)/shard_map/ppermute | solution.py:168
  180.7 10.4 %collective-permute-start.10 = (f32[8,5632]{1,0:T(8,128)S(1)}, f32[8,5632]{1,0:T(8,128)S(1)}, u32[]{:S(2)}, u32[]{:S(2)}) collective-permute-start(f32[8,5632]{1,0:T(8,128)S(1)} %maximum_select_fusion.9), channel_id=1, source_target_pairs={{0,16},{2,18},{4,20},{6,22},{8,24},{10,26},{12,28},{14,30},{16,0},... | collective-permute-start | bytes 540680 | tf_op jit(solution)/shard_map/ppermute | solution.py:153
  (37 other events, 94.4 us)
Sparse Core Ops, SparseCore 0:
  97.4 113.5 reduce-scatter.1

commit v8 on v3

--- a/solution.py
+++ b/solution.py
@@ -179,6 +179,11 @@
     return part + swap_heads(part)
 
 
+def head_sum_low(part):
+    low = part.astype(jnp.bfloat16)
+    return low.astype(jnp.float32) + swap_heads(low).astype(jnp.float32)
+
+
 def trade_blocks(values, head, size, axis, mine_axis):
     mine = lax.dynamic_slice_in_dim(values, head * size, size, axis)
     theirs = swap_heads(lax.dynamic_slice_in_dim(values, (1 - head) * size, size, axis))
@@ -305,7 +310,7 @@
     ffn_in_part = lax.dot_general(
         d_gate_up, gate_up_w, (((1,), (1,)), ((), ())), preferred_element_type=jnp.float32
     )
-    d_normed_t = head_sum(ffn_in_part)
+    d_normed_t = head_sum_low(ffn_in_part)
     d_middle = grad_out + norm_back(norm_mid, inv_mid, d_normed_t * (1.0 + scale_t))
     d_scale_t = jnp.sum(d_normed_t * norm_mid, axis=0, keepdims=True)
     d_shift_t = jnp.sum(d_normed_t, axis=0, keepdims=True)

time: 221 us -> 218 us (0.986)
  waiting for transfers between devices: 41.1 us -> 32.9 us
  starting transfers between devices: 19.7 us -> 24 us
    ppermute x10, waiting for transfers between devices: 15.7 us -> 7.69 us  [swap_heads(): return lax.ppermute(values, 'head', [(0, 1), (1, 0)])]
    ppermute x10, starting transfers between devices: 9.68 us -> 13.7 us  [swap_heads(): return lax.ppermute(values, 'head', [(0, 1), (1, 0)])]
    unnamed x117 -> x119, local copies, waits for them, and re-layouts: 17.6 us -> 18.2 us
  transfers between devices with their start and end apart: 19 -> 19, of which waited for: 10 -> 7; matrix products, arithmetic and copies ran while one was open for 34% -> 35% of each run, Pallas kernels for 22% -> 23%
where the time goes in v8:
time: 218 us; the launch traced here: 217 us
  Pallas kernels  49.2 us (23%)
  matrix products  41.8 us (19%)
  local copies, waits for them, and re-layouts  38.6 us (18%)
  waiting for transfers between devices  32.9 us (15%)
  starting transfers between devices  24 us (11%)
  between operations  15.5 us (7%)
  other arithmetic  14.7 us (7%)
    pallas_call x1, Pallas kernels, pair_backward(): pl.pallas_call(pair_backward_kernel, grid=(m // tile,), in_specs=[pl.Bloc...  34 us
    unnamed x119, local copies, waits for them, and re-layouts  18.2 us
    pallas_call x1, Pallas kernels, pair_forward(): pl.pallas_call(pair_forward_kernel, grid=(m // tile,), in_specs=[pl.Block...  15.2 us
    ppermute x10, starting transfers between devices, swap_heads(): return lax.ppermute(values, 'head', [(0, 1), (1, 0)])  13.7 us
    reduce_scatter x1, waiting for transfers between devices, shards(): lax.psum_scatter(packed, 'dp', scatter_dimension=0, tiled=True)  13 us
    ppermute x10, waiting for transfers between devices, swap_heads(): return lax.ppermute(values, 'head', [(0, 1), (1, 0)])  7.69 us
    ppermute x4, waiting for transfers between devices, dp_gather(): other = lax.ppermute(block, 'dp', [(i, i ^ step) for i in range(count)])  7.21 us
    ppermute x4, starting transfers between devices, dp_sum(): other = lax.ppermute(values, 'dp', [(i, i ^ step) for i in range(count)])  5.48 us
  transfers between devices with their start and end apart: 19, of which 7 were waited for; matrix products, arithmetic and copies ran while one was open for 35% of the time, Pallas kernels for 23%

profile of v8, /device:TPU:0, one launch (start us, length us, event | category | flops | bytes accessed | tf_op | source)
XLA Modules:
  0.0 216.6 jit_solution(11527855644128859805)
XLA Ops:
  7.2 3.0 %collective-permute-start = (bf16[128,768]{1,0:T(8,128)(2,1)}, bf16[128,768]{1,0:T(8,128)(2,1)S(1)}, u32[]{:S(2)}, u32[]{:S(2)}) collective-permute-start(bf16[128,768]{1,0:T(8,128)(2,1)} %bitcast.91), channel_id=1, source_target_pairs={{0,1},{1,0},{2,3},{3,2},{4,5},{5,4},{6,7},{7,6},{8,9},{9,8},{10,11... | collective-permute-start | bytes 589832 | tf_op jit(solution)/shard_map/ppermute | solution.py:135
  11.7 15.2 %shard_map.246 = bf16[12,32768]{1,0:T(8,128)(2,1)} custom-call(bf16[32768,256]{1,0:T(8,128)(2,1)} %bitcast.80, f32[1,256]{1,0:T(1,128)} %bitcast.122, bf16[16,256]{1,0:T(8,128)(2,1)} %pad.8.wt_ref), custom_call_target="tpu_custom_call" | custom-call | flops 352321536 | bytes 17563648 | tf_op jit(solution)/shard_map/pallas_call | solution.py:38
  29.3 2.0 copy.90
  31.3 1.9 collective-permute-start.1
  33.9 2.1 convolution_reduce_fusion
  38.2 3.9 %copy.66 = bf16[768,3,384]{0,2,1:T(8,128)(2,1)} copy(bf16[768,3,384]{2,0,1:T(8,128)(2,1)} %param.22) | data formatting | bytes 3538944 | tf_op args[7]
  43.1 2.3 %convolution_convert_fusion.3 = bf16[256,1152]{1,0:T(8,128)(2,1)S(1)} fusion(bf16[768,1152]{0,1:T(8,128)(2,1)} %bitcast.89, f32[768]{0:T(1024)S(1)} %get-tuple-element.57, f32[768]{0:T(1024)S(1)} %get-tuple-element.58, f32[256]{0:T(256)S(1)} %add_rsqrt_fusion.1, f32[256]{0:T(256)S(1)} %broadcast_multiply_fusion.5, bf16[128,768]{1,0:T(8,128)(2,1)S(1)} %bitcast.94, ...), kind=kOutput, calls=%fused_computation.7 | convolution fusion | flops 456228864 | bytes 2760705 | tf_op jit(solution)/shard_map/dot_general | solution.py:261
  45.9 3.3 %fusion.79 = (f32[6,256]{1,0:T(8,128)S(1)}, f32[6,256,256]{1,2,0:T(8,128)}) fusion(pred[256]{0:T(512)(128)(4,1)} %or_and_fusion, bf16[256,6,64]{0,2,1:T(8,128)(2,1)S(1)} %bitcast.103, bf16[256,6,64]{0,2,1:T(8,128)(2,1)S(1)} %bitcast.101, bf16[6,128,256]{1,2,0:T(8,128)(2,1)} %copy.89, bf16[6,128,256]{1,2,0:T(8,128)(2,1)} %collective-permute-done.1, pred[]{:T(512)S(6)} %eq.44), kind=kOutput, calls=%fused_computation.180 | convolution fusion | flops 56230144 | bytes 2758913 | tf_op jit(solution)/shard_map/sub | solution.py:269
  51.9 1.9 collective-permute-start.5
  53.8 3.6 %copy.93 = bf16[96,8,2,1536]{3,1,2,0:T(8,128)(2,1)S(1)} copy(bf16[96,8,2,1536]{3,2,1,0:T(2,128)(2,1)} %bitcast.82) | data formatting | bytes 9437184
  59.8 2.2 %fusion.77 = (f32[256]{0:T(256)S(1)}, f32[256,768]{1,0:T(8,128)S(1)}, f32[256,768]{1,0:T(8,128)S(1)}) fusion(f32[768]{0:T(1024)S(1)} %get-tuple-element.102, bf16[128,768]{1,0:T(8,128)(2,1)S(1)} %bitcast.95, bf16[128,768]{1,0:T(8,128)(2,1)S(1)} %collective-permute-done, pred[]{:T(512)S(6)} %eq.44, f32[768]{0:T(1024)S(1)} %copy-done.48, ...), kind=kOutput, calls=%fused_computation.178 | convolution fusion | flops 311820032 | bytes 3546113 | tf_op jit(solution)/shard_map/dot_general | solution.py:280
  66.7 4.8 %broadcast_in_dim.64 = bf16[768,6144]{1,0:T(8,128)(2,1)} broadcast(bf16[]{:T(256)} %constant.30.clone.1), dimensions={} | broadcast | bytes 9437186 | tf_op jit(solution)/shard_map/broadcast_in_dim | solution.py:349
  71.4 3.9 %fusion.1 = bf16[768,6144]{1,0:T(8,128)(2,1)} fusion(bf16[768,6144]{1,0:T(8,128)(2,1)} %broadcast_in_dim.64, bf16[256,1536]{1,0:T(8,128)(2,1)S(1)} %get-tuple-element.68, bf16[256,1536]{1,0:T(8,128)(2,1)S(1)} %get-tuple-element.67, f32[256,768]{1,0:T(8,128)S(1)} %get-tuple-element.66, f32[768]{0:T(1024)S(1)} %copy-done.46, f32[768]{0:T(1024)S(1)} %get-tuple-element.55, ...), kind=kOutput, calls=%fused_computation.2 | convolution fusion | flops 1214447616 | bytes 7086080 | tf_op jit(solution)/shard_map/dot_general | solution.py:307
  75.3 2.3 %fusion.2 = bf16[768,6144]{1,0:T(8,128)(2,1)} fusion(bf16[768,6144]{1,0:T(8,128)(2,1)} %fusion.1, bf16[256,1536]{1,0:T(8,128)(2,1)S(1)} %get-tuple-element.69, f32[768]{0:T(1024)S(1)} %get-tuple-element.60, bf16[128,768]{1,0:T(8,128)(2,1)S(1)} %collective-permute-done.5, bf16[128,768]{1,0:T(8,128)(2,1)S(1)} %bitcast.109, pred[]{:T(512)S(6)} %eq.44), kind=kOutput, calls=%fused_computation.5 | convolution fusion | flops 607518720 | bytes 3542017 | tf_op jit(solution)/shard_map/dot_general | solution.py:298
  81.4 1.9 convolution_convert_fusion.8
  87.5 2.2 %fusion.3 = bf16[768,6144]{1,0:T(8,128)(2,1)} fusion(bf16[768,6144]{1,0:T(8,128)(2,1)} %fusion.7, bf16[256,384]{0,1:T(8,128)(2,1)S(1)} %bitcast.127, bf16[256,384]{0,1:T(8,128)(2,1)S(1)} %bitcast.113, bf16[256,384]{0,1:T(8,128)(2,1)S(1)} %bitcast.115, f32[768]{0:T(1024)S(1)} %copy-done.45, f32[768]{0:T(1024)S(1)} %get-tuple-element.58, ...), kind=kOutput, calls=%fused_computation.6 | convolution fusion | flops 458588160 | bytes 2760705 | tf_op jit(solution)/shard_map/dot_general | solution.py:345
  91.0 2.7 %convolution_convert_fusion.7 = bf16[256,768]{1,0:T(8,128)(2,1)} fusion(bf16[256,1536]{1,0:T(8,128)(2,1)} %copy-done.51, bf16[1536,768]{1,0:T(8,128)(2,1)S(1)} %copy-done), kind=kOutput, calls=%fused_computation.24 | convolution fusion | flops 604176384 | bytes 3538944 | tf_op jit(solution)/shard_map/dot_general | solution.py:290
  93.7 1.9 collective-permute-start.4
  96.6 1.9 copy.80
  100.0 3.7 %convolution_convert_fusion.5 = bf16[256,768]{1,0:T(8,128)(2,1)} fusion(bf16[768,1152]{0,1:T(8,128)(2,1)} %bitcast.90, bf16[256,384]{0,1:T(8,128)(2,1)} %bitcast.128, bf16[256,384]{0,1:T(8,128)(2,1)} %bitcast.114, bf16[256,384]{0,1:T(8,128)(2,1)} %bitcast.116), kind=kOutput, calls=%fused_computation.22 | convolution fusion | flops 454950912 | bytes 2752512 | tf_op jit(solution)/shard_map/dot_general | solution.py:358
  103.6 1.8 collective-permute-start.7
  107.7 6.0 %collective-permute-done.8 = bf16[6,128,256]{1,2,0:T(8,128)(2,1)} collective-permute-done((bf16[6,128,256]{1,2,0:T(8,128)(2,1)}, bf16[6,128,256]{1,2,0:T(8,128)(2,1)}, u32[]{:S(2)}, u32[]{:S(2)}) %collective-permute-start.8) | collective-permute-done | bytes 393248 | tf_op jit(solution)/shard_map/ppermute | solution.py:135
  113.7 1.9 copy.81
  118.5 34.0 %shard_map.247 = (bf16[32768,256]{1,0:T(8,128)(2,1)}, f32[16,256]{1,0:T(8,128)}, f32[1,256]{1,0:T(1,128)}) custom-call(bf16[32768,256]{1,0:T(8,128)(2,1)} %bitcast.81, bf16[16,32768]{1,0:T(8,128)(2,1)} %pad.9.ds_ref, f32[1,256]{1,0:T(1,128)} %bitcast.123, bf16[16,256]{1,0:T(8,128)(2,1)} %pad.8.wt_ref), custom_call_target="tpu_custom_call" | custom-call | flops 704643072 | bytes 34603008 | tf_op jit(solution)/shard_map/pallas_call | solution.py:85
  154.4 2.5 %collective-permute-start.13 = (f32[1,3328]{1,0:T(1,128)S(1)}, f32[1,3328]{1,0:T(1,128)S(1)}, u32[]{:S(2)}, u32[]{:S(2)}) collective-permute-start(f32[1,3328]{1,0:T(1,128)S(1)} %broadcast_in_dim.65), channel_id=1, source_target_pairs={{0,1},{1,0},{2,3},{3,2},{4,5},{5,4},{6,7},{7,6},{8,9},{9,8},{10,11... | collective-permute-start | bytes 39944 | tf_op jit(solution)/shard_map/ppermute | solution.py:135
  158.8 2.5 %convolution_multiply_fusion.2 = f32[1,256]{1,0:T(1,128)} fusion(bf16[256,4608]{1,0:T(8,128)(2,1)S(1)} %copy-done.6, f32[1,4608]{1,0:T(1,128)S(1)} %get-tuple-element.86, f32[1,256]{1,0:T(1,128)S(1)} %copy-done.33), kind=kOutput, calls=%fused_computation.46 | convolution fusion | flops 14157824 | bytes 2379776 | tf_op jit(solution)/shard_map/dot_general | solution.py:397
  164.8 3.5 %collective-permute-done.15 = f32[1,3328]{1,0:T(1,128)S(1)} collective-permute-done((f32[1,3328]{1,0:T(1,128)S(1)}, f32[1,3328]{1,0:T(1,128)S(1)}, u32[]{:S(2)}, u32[]{:S(2)}) %collective-permute-start.15) | collective-permute-done | bytes 13344 | tf_op jit(solution)/shard_map/ppermute | solution.py:168
  172.1 2.8 %collective-permute-start.17 = (f32[1,3328]{1,0:T(1,128)S(1)}, f32[1,3328]{1,0:T(1,128)S(1)}, u32[]{:S(2)}, u32[]{:S(2)}) collective-permute-start(f32[1,3328]{1,0:T(1,128)S(1)} %add.184), channel_id=1, source_target_pairs={{0,16},{2,18},{4,20},{6,22},{8,24},{10,26},{12,28},{14,30},{16,0},... | collective-permute-start | bytes 39944 | tf_op jit(solution)/shard_map/ppermute | solution.py:168
  175.0 2.6 %collective-permute-start.12 = (f32[8,5632]{1,0:T(8,128)S(1)}, f32[8,5632]{1,0:T(8,128)S(1)}, u32[]{:S(2)}, u32[]{:S(2)}) collective-permute-start(f32[8,5632]{1,0:T(8,128)S(1)} %maximum_select_fusion.9), channel_id=1, source_target_pairs={{0,16},{2,18},{4,20},{6,22},{8,24},{10,26},{12,28},{14,30},{16,0},... | collective-permute-start | bytes 540680 | tf_op jit(solution)/shard_map/ppermute | solution.py:153
  180.0 6.6 %collective-permute-done.12 = f32[8,5632]{1,0:T(8,128)S(1)} collective-permute-done((f32[8,5632]{1,0:T(8,128)S(1)}, f32[8,5632]{1,0:T(8,128)S(1)}, u32[]{:S(2)}, u32[]{:S(2)}) %collective-permute-start.12) | collective-permute-done | bytes 180256 | tf_op jit(solution)/shard_map/ppermute | solution.py:153
  187.9 4.2 %fusion.47 = f32[256,4608]{1,0:T(8,128)} fusion(bf16[16,256]{1,0:T(8,128)(2,1)S(1)} %multiply_convert_fusion.7, f32[16,5632]{1,0:T(8,128)S(1)} %maximum_select_fusion.8), kind=kOutput, calls=%fused_computation.105 | convolution fusion | flops 226492416 | bytes 5021696 | tf_op jit(solution)/shard_map/dot_general | solution.py:395
  192.1 13.0 %reduce-scatter.2.cloned.1.call-done = bf16[48,6144]{1,0:T(8,128)(2,1)} async-done(((bf16[768,6144]{1,0:T(8,128)(2,1)}), bf16[48,6144]{1,0:T(8,128)(2,1)}) %reduce-scatter.2.cloned.1.call-update) | async-done | bytes 589840 | tf_op jit(solution)/shard_map/reduce_scatter | solution.py:356
  (219 shorter events, 53.0 us)
Async XLA Ops:
  7.2 56.6 %copy-start = (bf16[1536,768]{1,0:T(8,128)(2,1)S(1)}, bf16[1536,768]{1,0:T(8,128)(2,1)}, u32[]{:S(2)}) copy-start(bf16[1536,768]{1,0:T(8,128)(2,1)} %param.28) | copy-start | bytes 7077892
  7.2 197.9 %reduce-scatter.2.cloned.1.call-start = ((), (), s32[]{:S(2)}) async-start(), calls=%async_computation.1 | async-start | bytes 10027008 | tf_op jit(solution)/shard_map/reduce_scatter | solution.py:356
  7.2 35.4 %collective-permute-start = (bf16[128,768]{1,0:T(8,128)(2,1)}, bf16[128,768]{1,0:T(8,128)(2,1)S(1)}, u32[]{:S(2)}, u32[]{:S(2)}) collective-permute-start(bf16[128,768]{1,0:T(8,128)(2,1)} %bitcast.91), channel_id=1, source_target_pairs={{0,1},{1,0},{2,3},{3,2},{4,5},{5,4},{6,7},{7,6},{8,9},{9,8},{10,11... | collective-permute-start | bytes 589832 | tf_op jit(solution)/shard_map/ppermute | solution.py:135
  10.3 47.8 %collective-permute-start.3 = (bf16[384,768]{1,0:T(8,128)(2,1)}, bf16[384,768]{1,0:T(8,128)(2,1)}, u32[]{:S(2)}, u32[]{:S(2)}) collective-permute-start(bf16[384,768]{1,0:T(8,128)(2,1)} %param.25), channel_id=1, source_target_pairs={{0,1},{1,0},{2,3},{3,2},{4,5},{5,4},{6,7},{7,6},{8,9},{9,8},{10,11... | collective-permute-start | bytes 1769480 | tf_op jit(solution)/shard_map/ppermute | solution.py:135
  29.3 6.7 %copy-start.24 = (f32[4608]{0:T(1024)S(1)}, f32[4608]{0:T(1024)}, u32[]{:S(2)}) copy-start(f32[4608]{0:T(1024)} %param.21) | copy-start | bytes 55300
  29.3 8.0 %copy-start.9 = (bf16[6,128,256]{2,1,0:T(8,128)(2,1)S(1)}, bf16[6,128,256]{2,1,0:T(8,128)(2,1)}, u32[]{:S(2)}) copy-start(bf16[6,128,256]{2,1,0:T(8,128)(2,1)} %get-tuple-element.77) | copy-start | bytes 1179652
  31.3 14.6 %collective-permute-start.1 = (bf16[6,128,256]{1,2,0:T(8,128)(2,1)}, bf16[6,128,256]{1,2,0:T(8,128)(2,1)}, u32[]{:S(2)}, u32[]{:S(2)}) collective-permute-start(bf16[6,128,256]{1,2,0:T(8,128)(2,1)} %copy.90), channel_id=1, source_target_pairs={{0,1},{1,0},{2,3},{3,2},{4,5},{5,4},{6,7},{7,6},{8,9},{9,8},{10,11... | collective-permute-start | bytes 1179656 | tf_op jit(solution)/shard_map/ppermute | solution.py:135
  51.0 6.5 %copy-start.15 = (bf16[6,64,256]{2,1,0:T(8,128)(2,1)}, bf16[6,64,256]{2,1,0:T(8,128)(2,1)S(1)}, u32[]{:S(2)}) copy-start(bf16[6,64,256]{2,1,0:T(8,128)(2,1)S(1)} %convolution_convert_fusion.10) | copy-start | bytes 589828
  51.8 8.0 %collective-permute-start.2 = (bf16[256,384]{1,0:T(8,128)(2,1)}, bf16[256,384]{1,0:T(8,128)(2,1)S(1)}, u32[]{:S(2)}, u32[]{:S(2)}) collective-permute-start(bf16[256,384]{1,0:T(8,128)(2,1)} %copy.74), channel_id=1, source_target_pairs={{0,1},{1,0},{2,3},{3,2},{4,5},{5,4},{6,7},{7,6},{8,9},{9,8},{10,11... | collective-permute-start | bytes 589832 | tf_op jit(solution)/shard_map/ppermute | solution.py:135
  51.9 11.9 %collective-permute-start.5 = (bf16[128,768]{1,0:T(8,128)(2,1)S(1)}, bf16[128,768]{1,0:T(8,128)(2,1)S(1)}, u32[]{:S(2)}, u32[]{:S(2)}) collective-permute-start(bf16[128,768]{1,0:T(8,128)(2,1)S(1)} %bitcast.107), channel_id=1, source_target_pairs={{0,1},{1,0},{2,3},{3,2},{4,5},{5,4},{6,7},{7,6},{8,9},{9,8},{10,11... | collective-permute-start | bytes 589832 | tf_op jit(solution)/shard_map/ppermute | solution.py:135
  53.8 6.0 %copy-start.21 = (bf16[384,768]{1,0:T(8,128)(2,1)S(1)}, bf16[384,768]{1,0:T(8,128)(2,1)}, u32[]{:S(2)}) copy-start(bf16[384,768]{1,0:T(8,128)(2,1)} %param.25) | copy-start | bytes 1769476
  53.8 6.0 %copy-start.48 = (f32[768]{0:T(1024)S(1)}, f32[768]{0:T(1024)}, u32[]{:S(2)}) copy-start(f32[768]{0:T(1024)} %param.26) | copy-start | bytes 9220
  62.0 16.5 %copy-start.1 = (f32[256,768]{1,0:T(8,128)}, f32[256,768]{1,0:T(8,128)S(1)}, u32[]{:S(2)}) copy-start(f32[256,768]{1,0:T(8,128)S(1)} %get-tuple-element.66) | copy-start | bytes 2359300
  63.8 14.8 %copy-start.19 = (bf16[128,768]{1,0:T(8,128)(2,1)}, bf16[128,768]{1,0:T(8,128)(2,1)S(1)}, u32[]{:S(2)}) copy-start(bf16[128,768]{1,0:T(8,128)(2,1)S(1)} %collective-permute-done.5) | copy-start | bytes 589828
  65.1 10.3 %copy-start.51 = (bf16[256,1536]{1,0:T(8,128)(2,1)}, bf16[256,1536]{1,0:T(8,128)(2,1)S(1)}, u32[]{:S(2)}) copy-start(bf16[256,1536]{1,0:T(8,128)(2,1)S(1)} %get-tuple-element.69) | copy-start | bytes 2359300
  66.5 11.1 %collective-permute-start.6 = (bf16[256,768]{1,0:T(8,128)(2,1)S(1)}, bf16[256,768]{1,0:T(8,128)(2,1)S(1)}, u32[]{:S(2)}, u32[]{:S(2)}) collective-permute-start(bf16[256,768]{1,0:T(8,128)(2,1)S(1)} %convolution_convert_fusion.6), channel_id=1, source_target_pairs={{0,1},{1,0},{2,3},{3,2},{4,5},{5,4},{6,7},{7,6},{8,9},{9,8},{10,11... | collective-permute-start | bytes 1179656 | tf_op jit(solution)/shard_map/ppermute | solution.py:135
  93.7 11.8 %collective-permute-start.4 = (bf16[256,768]{1,0:T(8,128)(2,1)}, bf16[256,768]{1,0:T(8,128)(2,1)}, u32[]{:S(2)}, u32[]{:S(2)}) collective-permute-start(bf16[256,768]{1,0:T(8,128)(2,1)} %convolution_convert_fusion.7), channel_id=1, source_target_pairs={{0,1},{1,0},{2,3},{3,2},{4,5},{5,4},{6,7},{7,6},{8,9},{9,8},{10,11... | collective-permute-start | bytes 1179656 | tf_op jit(solution)/shard_map/ppermute | solution.py:135
  99.8 13.8 %collective-permute-start.8 = (bf16[6,128,256]{1,2,0:T(8,128)(2,1)}, bf16[6,128,256]{1,2,0:T(8,128)(2,1)}, u32[]{:S(2)}, u32[]{:S(2)}) collective-permute-start(bf16[6,128,256]{1,2,0:T(8,128)(2,1)} %get-tuple-element.76), channel_id=1, source_target_pairs={{0,1},{1,0},{2,3},{3,2},{4,5},{5,4},{6,7},{7,6},{8,9},{9,8},{10,11... | collective-permute-start | bytes 1179656 | tf_op jit(solution)/shard_map/ppermute | solution.py:135
  103.6 53.3 %collective-permute-start.7 = (bf16[256,768]{1,0:T(8,128)(2,1)}, bf16[256,768]{1,0:T(8,128)(2,1)}, u32[]{:S(2)}, u32[]{:S(2)}) collective-permute-start(bf16[256,768]{1,0:T(8,128)(2,1)} %convolution_convert_fusion.5), channel_id=1, source_target_pairs={{0,1},{1,0},{2,3},{3,2},{4,5},{5,4},{6,7},{7,6},{8,9},{9,8},{10,11... | collective-permute-start | bytes 1179656 | tf_op jit(solution)/shard_map/ppermute | solution.py:135
  118.5 38.4 %copy-start.36 = (f32[256]{0:T(256)S(1)}, f32[256]{0:T(256)}, u32[]{:S(2)}) copy-start(f32[256]{0:T(256)} %copy-done.34) | copy-start | bytes 3076
  118.5 38.4 %copy-start.43 = (f32[256]{0:T(256)S(1)}, f32[256]{0:T(256)}, u32[]{:S(2)}) copy-start(f32[256]{0:T(256)} %copy-done.40) | copy-start | bytes 3076
  154.4 6.9 %collective-permute-start.13 = (f32[1,3328]{1,0:T(1,128)S(1)}, f32[1,3328]{1,0:T(1,128)S(1)}, u32[]{:S(2)}, u32[]{:S(2)}) collective-permute-start(f32[1,3328]{1,0:T(1,128)S(1)} %broadcast_in_dim.65), channel_id=1, source_target_pairs={{0,1},{1,0},{2,3},{3,2},{4,5},{5,4},{6,7},{7,6},{8,9},{9,8},{10,11... | collective-permute-start | bytes 39944 | tf_op jit(solution)/shard_map/ppermute | solution.py:135
  158.8 18.8 %copy-start.5 = (f32[256,768]{1,0:T(8,128)S(1)}, f32[256,768]{1,0:T(8,128)}, u32[]{:S(2)}) copy-start(f32[256,768]{1,0:T(8,128)} %copy-done.3) | copy-start | bytes 2359300
  158.8 18.8 %copy-start.47 = (f32[128]{0:T(128)S(1)}, f32[128]{0:T(128)}, u32[]{:S(2)}) copy-start(f32[128]{0:T(128)} %dynamic-slice.14) | copy-start | bytes 1540
  161.3 1.2 collective-permute-start.9
  161.4 3.0 %collective-permute-start.14 = (f32[1,3328]{1,0:T(1,128)S(1)}, f32[1,3328]{1,0:T(1,128)S(1)}, u32[]{:S(2)}, u32[]{:S(2)}) collective-permute-start(f32[1,3328]{1,0:T(1,128)S(1)} %reshape_add_fusion), channel_id=1, source_target_pairs={{0,2},{2,0},{4,6},{6,4},{8,10},{10,8},{12,14},{14,12},{16,18},{18,... | collective-permute-start | bytes 39944 | tf_op jit(solution)/shard_map/ppermute | solution.py:168
  162.6 7.4 %collective-permute-start.10 = (f32[2,5632]{1,0:T(2,128)S(1)}, f32[2,5632]{1,0:T(2,128)S(1)}, u32[]{:S(2)}, u32[]{:S(2)}) collective-permute-start(f32[2,5632]{1,0:T(2,128)S(1)} %maximum_select_fusion.12), channel_id=1, source_target_pairs={{0,4},{2,6},{4,0},{6,2},{8,12},{10,14},{12,8},{14,10},{16,20},{18,... | collective-permute-start | bytes 135176 | tf_op jit(solution)/shard_map/ppermute | solution.py:153
  164.4 3.9 %collective-permute-start.15 = (f32[1,3328]{1,0:T(1,128)S(1)}, f32[1,3328]{1,0:T(1,128)S(1)}, u32[]{:S(2)}, u32[]{:S(2)}) collective-permute-start(f32[1,3328]{1,0:T(1,128)S(1)} %add.182), channel_id=1, source_target_pairs={{0,4},{2,6},{4,0},{6,2},{8,12},{10,14},{12,8},{14,10},{16,20},{18,... | collective-permute-start | bytes 39944 | tf_op jit(solution)/shard_map/ppermute | solution.py:168
  168.2 3.9 %collective-permute-start.16 = (f32[1,3328]{1,0:T(1,128)S(1)}, f32[1,3328]{1,0:T(1,128)S(1)}, u32[]{:S(2)}, u32[]{:S(2)}) collective-permute-start(f32[1,3328]{1,0:T(1,128)S(1)} %add.183), channel_id=1, source_target_pairs={{0,8},{2,10},{4,12},{6,14},{8,0},{10,2},{12,4},{14,6},{16,24},{18,... | collective-permute-start | bytes 39944 | tf_op jit(solution)/shard_map/ppermute | solution.py:168
  170.1 4.8 %collective-permute-start.11 = (f32[4,5632]{1,0:T(4,128)S(1)}, f32[4,5632]{1,0:T(4,128)S(1)}, u32[]{:S(2)}, u32[]{:S(2)}) collective-permute-start(f32[4,5632]{1,0:T(4,128)S(1)} %maximum_select_fusion.11), channel_id=1, source_target_pairs={{0,8},{2,10},{4,12},{6,14},{8,0},{10,2},{12,4},{14,6},{16,24},{18,... | collective-permute-start | bytes 270344 | tf_op jit(solution)/shard_map/ppermute | solution.py:153
  172.1 6.4 %collective-permute-start.17 = (f32[1,3328]{1,0:T(1,128)S(1)}, f32[1,3328]{1,0:T(1,128)S(1)}, u32[]{:S(2)}, u32[]{:S(2)}) collective-permute-start(f32[1,3328]{1,0:T(1,128)S(1)} %add.184), channel_id=1, source_target_pairs={{0,16},{2,18},{4,20},{6,22},{8,24},{10,26},{12,28},{14,30},{16,0},... | collective-permute-start | bytes 39944 | tf_op jit(solution)/shard_map/ppermute | solution.py:168
  175.0 11.6 %collective-permute-start.12 = (f32[8,5632]{1,0:T(8,128)S(1)}, f32[8,5632]{1,0:T(8,128)S(1)}, u32[]{:S(2)}, u32[]{:S(2)}) collective-permute-start(f32[8,5632]{1,0:T(8,128)S(1)} %maximum_select_fusion.9), channel_id=1, source_target_pairs={{0,16},{2,18},{4,20},{6,22},{8,24},{10,26},{12,28},{14,30},{16,0},... | collective-permute-start | bytes 540680 | tf_op jit(solution)/shard_map/ppermute | solution.py:153
  (39 other events, 124.1 us)
Sparse Core Ops, SparseCore 0:
  89.9 115.2 reduce-scatter.1

commit v9 on v8

--- a/solution.py
+++ b/solution.py
@@ -3,6 +3,7 @@
 from jax import lax
 from jax.experimental import pallas as pl
 from jax.experimental.pallas import tpu as pltpu
+from jax.experimental.layout import Layout, with_layout_constraint
 from jax.sharding import PartitionSpec as P
 
 DH = 64
@@ -265,6 +266,7 @@
     scores = jnp.einsum("qhe,khe->hqk", queries, keys, preferred_element_type=jnp.float32)
     scores = scores * DH ** (-0.5) + biases.astype(jnp.float32)
     scores = jnp.where(valid[None, None, :], scores, masked_score)
+    scores = with_layout_constraint(scores, Layout(major_to_minor=(0, 1, 2)))
     row_max = jnp.max(scores, axis=-1, keepdims=True)
     exp_scores = jnp.exp(scores - row_max)
     row_total = jnp.sum(exp_scores, axis=-1, keepdims=True)

time: 218 us -> 219 us (level)
  waiting for transfers between devices: 32.9 us -> 44.6 us
  local copies, waits for them, and re-layouts: 38.6 us -> 27.2 us
  matrix products: 41.8 us -> 44.6 us
    ppermute x10, waiting for transfers between devices: 7.69 us -> 15.8 us  [swap_heads(): return lax.ppermute(values, 'head', [(0, 1), (1, 0)])]
    unnamed x119 -> x118, local copies, waits for them, and re-layouts: 18.2 us -> 11.7 us
    reduce_scatter x1, waiting for transfers between devices: 13 us -> 18.4 us  [shards(): lax.psum_scatter(packed, 'dp', scatter_dimension=0, tiled=True)]
    dot_general x1, matrix products: 3.68 us -> 0.71 us  [shards(): lax.dot_general(d_qkv, qkv_w, (((1,), (1,)), ((), ())), preferred_element...]
    dynamic_slice x3 -> x1, local copies, waits for them, and re-layouts: 3.89 us -> 0.94 us  [trade_blocks(): mine = lax.dynamic_slice_in_dim(values, head * size, size, axis)]
  transfers between devices with their start and end apart: 19 -> 19, of which waited for: 7 -> 8; matrix products, arithmetic and copies ran while one was open for 35% -> 28% of each run, Pallas kernels for 23% -> 23%
where the time goes in v9:
time: 219 us; the launch traced here: 218 us
  Pallas kernels  49.3 us (23%)
  matrix products  44.6 us (20%)
  waiting for transfers between devices  44.6 us (20%)
  local copies, waits for them, and re-layouts  27.2 us (12%)
  starting transfers between devices  23.5 us (11%)
  between operations  15.5 us (7%)
  other arithmetic  13.6 us (6%)
    pallas_call x1, Pallas kernels, pair_backward(): pl.pallas_call(pair_backward_kernel, grid=(m // tile,), in_specs=[pl.Bloc...  34.1 us
    reduce_scatter x1, waiting for transfers between devices, shards(): lax.psum_scatter(packed, 'dp', scatter_dimension=0, tiled=True)  18.4 us
    ppermute x10, waiting for transfers between devices, swap_heads(): return lax.ppermute(values, 'head', [(0, 1), (1, 0)])  15.8 us
    pallas_call x1, Pallas kernels, pair_forward(): pl.pallas_call(pair_forward_kernel, grid=(m // tile,), in_specs=[pl.Block...  15.2 us
    ppermute x10, starting transfers between devices, swap_heads(): return lax.ppermute(values, 'head', [(0, 1), (1, 0)])  13.4 us
    unnamed x118, local copies, waits for them, and re-layouts  11.7 us
    ppermute x4, waiting for transfers between devices, dp_gather(): other = lax.ppermute(block, 'dp', [(i, i ^ step) for i in range(count)])  5.48 us
    ppermute x4, starting transfers between devices, dp_sum(): other = lax.ppermute(values, 'dp', [(i, i ^ step) for i in range(count)])  5.45 us
  transfers between devices with their start and end apart: 19, of which 8 were waited for; matrix products, arithmetic and copies ran while one was open for 28% of the time, Pallas kernels for 23%

profile of v9, /device:TPU:0, one launch (start us, length us, event | category | flops | bytes accessed | tf_op | source)
XLA Modules:
  0.0 218.3 jit_solution(7298716889677839724)
XLA Ops:
  7.2 3.0 %collective-permute-start = (bf16[128,768]{1,0:T(8,128)(2,1)}, bf16[128,768]{1,0:T(8,128)(2,1)S(1)}, u32[]{:S(2)}, u32[]{:S(2)}) collective-permute-start(bf16[128,768]{1,0:T(8,128)(2,1)} %bitcast.96), channel_id=1, source_target_pairs={{0,1},{1,0},{2,3},{3,2},{4,5},{5,4},{6,7},{7,6},{8,9},{9,8},{10,11... | collective-permute-start | bytes 589832 | tf_op jit(solution)/shard_map/ppermute | solution.py:136
  11.7 15.2 %shard_map.246 = bf16[12,32768]{1,0:T(8,128)(2,1)} custom-call(bf16[32768,256]{1,0:T(8,128)(2,1)} %bitcast.85, f32[1,256]{1,0:T(1,128)} %bitcast.130, bf16[16,256]{1,0:T(8,128)(2,1)} %pad.8.wt_ref), custom_call_target="tpu_custom_call" | custom-call | flops 352321536 | bytes 17563648 | tf_op jit(solution)/shard_map/pallas_call | solution.py:39
  29.3 1.9 collective-permute-start.1
  32.0 2.1 convolution_reduce_fusion
  35.3 3.9 %copy.54 = bf16[768,3,384]{0,2,1:T(8,128)(2,1)} copy(bf16[768,3,384]{2,0,1:T(8,128)(2,1)} %param.22) | data formatting | bytes 3538944 | tf_op args[7]
  40.2 2.3 %convolution_convert_fusion.3 = bf16[256,1152]{1,0:T(8,128)(2,1)S(1)} fusion(bf16[768,1152]{0,1:T(8,128)(2,1)} %bitcast.94, f32[768]{0:T(1024)S(1)} %get-tuple-element.57, f32[768]{0:T(1024)S(1)} %get-tuple-element.58, f32[256]{0:T(256)S(1)} %add_rsqrt_fusion.1, f32[256]{0:T(256)S(1)} %broadcast_multiply_fusion.5, bf16[128,768]{1,0:T(8,128)(2,1)S(1)} %bitcast.99, ...), kind=kOutput, calls=%fused_computation.7 | convolution fusion | flops 456228864 | bytes 2760705 | tf_op jit(solution)/shard_map/dot_general | solution.py:262
  43.8 3.4 %fusion.79 = (f32[6,256]{1,0:T(8,128)S(1)}, f32[6,256,256]{2,1,0:T(8,128)}) fusion(pred[256]{0:T(512)(128)(4,1)} %or_and_fusion, bf16[256,6,64]{0,2,1:T(8,128)(2,1)S(1)} %bitcast.108, bf16[256,6,64]{0,2,1:T(8,128)(2,1)S(1)} %bitcast.104, bf16[6,128,256]{2,1,0:T(8,128)(2,1)} %get-tuple-element.77, bf16[6,128,256]{2,1,0:T(8,128)(2,1)} %collective-permute-done.1, ...), kind=kOutput, calls=%fused_computation.180 | convolution fusion | flops 56230144 | bytes 2758913 | tf_op jit(solution)/shard_map/sub | solution.py:271
  47.1 2.6 %convolution_convert_fusion.10 = bf16[6,64,256]{2,1,0:T(8,128)(2,1)S(1)} fusion(bf16[256,6,64]{0,2,1:T(8,128)(2,1)} %bitcast.125, f32[6,256]{1,0:T(8,128)S(1)} %get-tuple-element.97, pred[256]{0:T(512)(128)(4,1)} %or_and_fusion, bf16[256,6,64]{0,2,1:T(8,128)(2,1)S(1)} %bitcast.109, bf16[256,6,64]{0,2,1:T(8,128)(2,1)S(1)} %bitcast.105, ...), kind=kOutput, calls=%fused_computation.44 | convolution fusion | flops 107054848 | bytes 1579265 | tf_op jit(solution)/shard_map/hqk,khe->qhe/dot_general | solution.py:275
  50.1 1.9 collective-permute-start.5
  52.0 3.6 %copy.70 = bf16[96,8,2,1536]{3,1,2,0:T(8,128)(2,1)S(1)} copy(bf16[96,8,2,1536]{3,2,1,0:T(2,128)(2,1)} %bitcast.87) | data formatting | bytes 9437184
  57.8 2.0 fusion.77
  64.5 4.8 %broadcast_in_dim.64 = bf16[768,6144]{1,0:T(8,128)(2,1)} broadcast(bf16[]{:T(256)} %constant.30.clone.1), dimensions={} | broadcast | bytes 9437186 | tf_op jit(solution)/shard_map/broadcast_in_dim | solution.py:351
  69.2 3.9 %fusion.1 = bf16[768,6144]{1,0:T(8,128)(2,1)} fusion(bf16[768,6144]{1,0:T(8,128)(2,1)} %broadcast_in_dim.64, bf16[256,1536]{1,0:T(8,128)(2,1)S(1)} %get-tuple-element.68, bf16[256,1536]{1,0:T(8,128)(2,1)S(1)} %get-tuple-element.67, f32[256,768]{1,0:T(8,128)S(1)} %get-tuple-element.66, f32[768]{0:T(1024)S(1)} %copy-done.46, f32[768]{0:T(1024)S(1)} %get-tuple-element.55, ...), kind=kOutput, calls=%fused_computation.2 | convolution fusion | flops 1214447616 | bytes 7086080 | tf_op jit(solution)/shard_map/dot_general | solution.py:309
  73.1 2.3 %fusion.2 = bf16[768,6144]{1,0:T(8,128)(2,1)} fusion(bf16[768,6144]{1,0:T(8,128)(2,1)} %fusion.1, bf16[256,1536]{1,0:T(8,128)(2,1)S(1)} %get-tuple-element.69, f32[768]{0:T(1024)S(1)} %get-tuple-element.60, bf16[128,768]{1,0:T(8,128)(2,1)S(1)} %collective-permute-done.5, bf16[128,768]{1,0:T(8,128)(2,1)S(1)} %bitcast.116, pred[]{:T(512)S(6)} %eq.44), kind=kOutput, calls=%fused_computation.5 | convolution fusion | flops 607518720 | bytes 3542017 | tf_op jit(solution)/shard_map/dot_general | solution.py:300
  79.3 2.2 %multiply_reduce_fusion = (f32[6,256]{1,0:T(8,128)S(1)}, f32[6,256,256]{2,1,0:T(8,128)S(1)}) fusion(f32[6,256,256]{2,1,0:T(8,128)} %get-tuple-element.98, f32[6,256]{1,0:T(8,128)S(1)} %copy-done.40, bf16[256,6,64]{0,2,1:T(8,128)(2,1)S(1)} %bitcast.127, bf16[256,6,64]{0,2,1:T(8,128)(2,1)S(1)} %bitcast.126), kind=kOutput, calls=%fused_computation.11 | convolution fusion | flops 51509760 | bytes 3551232 | tf_op jit(solution)/shard_map/qhe,khe->hqk/dot_general | solution.py:333
  85.8 3.4 %convolution_convert_fusion.8 = bf16[6,64,256]{2,1,0:T(8,128)(2,1)} fusion(bf16[256,6,64]{0,2,1:T(8,128)(2,1)} %bitcast.128, f32[6,256]{1,0:T(8,128)} %copy-done.39, pred[256]{0:T(512)(128)(4,1)} %or_and_fusion, bf16[256,6,64]{0,2,1:T(8,128)(2,1)} %bitcast.110, bf16[256,6,64]{0,2,1:T(8,128)(2,1)} %bitcast.106, ...), kind=kOutput, calls=%fused_computation.42 | convolution fusion | flops 107054848 | bytes 1579265 | tf_op jit(solution)/shard_map/hqk,qhe->khe/dot_general | solution.py:332
  89.2 3.3 %fusion.3 = bf16[768,6144]{1,0:T(8,128)(2,1)} fusion(bf16[768,6144]{1,0:T(8,128)(2,1)} %fusion.7, bf16[256,384]{0,1:T(8,128)(2,1)} %bitcast.135, bf16[256,384]{0,1:T(8,128)(2,1)} %bitcast.121, bf16[256,384]{0,1:T(8,128)(2,1)} %bitcast.123, f32[768]{0:T(1024)} %copy-done.45, f32[768]{0:T(1024)S(1)} %get-tuple-element.58, f32[256]{0:T(256)S(1)} %copy-done.43, ...), kind=kOutput, calls=%fused_computation.6 | convolution fusion | flops 458588160 | bytes 2761729 | tf_op jit(solution)/shard_map/dot_general | solution.py:347
  93.1 1.9 convolution_convert_fusion.7
  95.1 2.0 collective-permute-start.4
  98.3 2.0 collective-permute-start.7
  100.3 6.8 %collective-permute-done.4 = bf16[256,768]{1,0:T(8,128)(2,1)S(1)} collective-permute-done((bf16[256,768]{1,0:T(8,128)(2,1)S(1)}, bf16[256,768]{1,0:T(8,128)(2,1)S(1)}, u32[]{:S(2)}, u32[]{:S(2)}) %collective-permute-start.4) | collective-permute-done | bytes 393248 | tf_op jit(solution)/shard_map/ppermute | solution.py:136
  108.1 7.4 %collective-permute-done.8 = bf16[6,128,256]{2,1,0:T(8,128)(2,1)S(1)} collective-permute-done((bf16[6,128,256]{2,1,0:T(8,128)(2,1)S(1)}, bf16[6,128,256]{2,1,0:T(8,128)(2,1)S(1)}, u32[]{:S(2)}, u32[]{:S(2)}) %collective-permute-start.8) | collective-permute-done | bytes 393248 | tf_op jit(solution)/shard_map/ppermute | solution.py:136
  117.5 34.1 %shard_map.247 = (bf16[32768,256]{1,0:T(8,128)(2,1)}, f32[16,256]{1,0:T(8,128)}, f32[1,256]{1,0:T(1,128)}) custom-call(bf16[32768,256]{1,0:T(8,128)(2,1)} %bitcast.86, bf16[16,32768]{1,0:T(8,128)(2,1)} %pad.9.ds_ref, f32[1,256]{1,0:T(1,128)} %bitcast.131, bf16[16,256]{1,0:T(8,128)(2,1)} %pad.8.wt_ref), custom_call_target="tpu_custom_call" | custom-call | flops 704643072 | bytes 34603008 | tf_op jit(solution)/shard_map/pallas_call | solution.py:86
  153.4 1.9 collective-permute-start.13
  157.0 2.5 %convolution_multiply_fusion.2 = f32[1,256]{1,0:T(1,128)} fusion(bf16[256,4608]{1,0:T(8,128)(2,1)S(1)} %copy-done.6, f32[1,4608]{1,0:T(1,128)S(1)} %get-tuple-element.86, f32[1,256]{1,0:T(1,128)S(1)} %copy-done.35), kind=kOutput, calls=%fused_computation.46 | convolution fusion | flops 14157824 | bytes 2379776 | tf_op jit(solution)/shard_map/dot_general | solution.py:399
  160.8 1.6 collective-permute-start.10
  163.0 3.4 %collective-permute-done.15 = f32[1,3328]{1,0:T(1,128)S(1)} collective-permute-done((f32[1,3328]{1,0:T(1,128)S(1)}, f32[1,3328]{1,0:T(1,128)S(1)}, u32[]{:S(2)}, u32[]{:S(2)}) %collective-permute-start.15) | collective-permute-done | bytes 13344 | tf_op jit(solution)/shard_map/ppermute | solution.py:169
  170.4 2.8 %collective-permute-start.17 = (f32[1,3328]{1,0:T(1,128)S(1)}, f32[1,3328]{1,0:T(1,128)S(1)}, u32[]{:S(2)}, u32[]{:S(2)}) collective-permute-start(f32[1,3328]{1,0:T(1,128)S(1)} %add.184), channel_id=1, source_target_pairs={{0,16},{2,18},{4,20},{6,22},{8,24},{10,26},{12,28},{14,30},{16,0},... | collective-permute-start | bytes 39944 | tf_op jit(solution)/shard_map/ppermute | solution.py:169
  173.3 2.4 %collective-permute-start.12 = (f32[8,5632]{1,0:T(8,128)S(1)}, f32[8,5632]{1,0:T(8,128)S(1)}, u32[]{:S(2)}, u32[]{:S(2)}) collective-permute-start(f32[8,5632]{1,0:T(8,128)S(1)} %maximum_select_fusion.9), channel_id=1, source_target_pairs={{0,16},{2,18},{4,20},{6,22},{8,24},{10,26},{12,28},{14,30},{16,0},... | collective-permute-start | bytes 540680 | tf_op jit(solution)/shard_map/ppermute | solution.py:154
  178.0 4.9 %collective-permute-done.12 = f32[8,5632]{1,0:T(8,128)S(1)} collective-permute-done((f32[8,5632]{1,0:T(8,128)S(1)}, f32[8,5632]{1,0:T(8,128)S(1)}, u32[]{:S(2)}, u32[]{:S(2)}) %collective-permute-start.12) | collective-permute-done | bytes 180256 | tf_op jit(solution)/shard_map/ppermute | solution.py:154
  184.2 4.2 %fusion.47 = f32[256,4608]{1,0:T(8,128)} fusion(bf16[16,256]{1,0:T(8,128)(2,1)S(1)} %multiply_convert_fusion.7, f32[16,5632]{1,0:T(8,128)S(1)} %maximum_select_fusion.8), kind=kOutput, calls=%fused_computation.106 | convolution fusion | flops 226492416 | bytes 5021696 | tf_op jit(solution)/shard_map/dot_general | solution.py:397
  188.4 18.4 %reduce-scatter.2.cloned.1.call-done = bf16[48,6144]{1,0:T(8,128)(2,1)} async-done(((bf16[768,6144]{1,0:T(8,128)(2,1)}), bf16[48,6144]{1,0:T(8,128)(2,1)}) %reduce-scatter.2.cloned.1.call-update) | async-done | bytes 589840 | tf_op jit(solution)/shard_map/reduce_scatter | solution.py:358
  (215 shorter events, 44.7 us)
Async XLA Ops:
  7.2 54.4 %copy-start = (bf16[1536,768]{1,0:T(8,128)(2,1)S(1)}, bf16[1536,768]{1,0:T(8,128)(2,1)}, u32[]{:S(2)}) copy-start(bf16[1536,768]{1,0:T(8,128)(2,1)} %param.28) | copy-start | bytes 7077892
  7.2 199.6 %reduce-scatter.2.cloned.1.call-start = ((), (), s32[]{:S(2)}) async-start(), calls=%async_computation.1 | async-start | bytes 10027008 | tf_op jit(solution)/shard_map/reduce_scatter | solution.py:358
  7.2 32.6 %collective-permute-start = (bf16[128,768]{1,0:T(8,128)(2,1)}, bf16[128,768]{1,0:T(8,128)(2,1)S(1)}, u32[]{:S(2)}, u32[]{:S(2)}) collective-permute-start(bf16[128,768]{1,0:T(8,128)(2,1)} %bitcast.96), channel_id=1, source_target_pairs={{0,1},{1,0},{2,3},{3,2},{4,5},{5,4},{6,7},{7,6},{8,9},{9,8},{10,11... | collective-permute-start | bytes 589832 | tf_op jit(solution)/shard_map/ppermute | solution.py:136
  10.3 46.0 %collective-permute-start.3 = (bf16[384,768]{1,0:T(8,128)(2,1)}, bf16[384,768]{1,0:T(8,128)(2,1)}, u32[]{:S(2)}, u32[]{:S(2)}) collective-permute-start(bf16[384,768]{1,0:T(8,128)(2,1)} %param.25), channel_id=1, source_target_pairs={{0,1},{1,0},{2,3},{3,2},{4,5},{5,4},{6,7},{7,6},{8,9},{9,8},{10,11... | collective-permute-start | bytes 1769480 | tf_op jit(solution)/shard_map/ppermute | solution.py:136
  29.3 14.4 %collective-permute-start.1 = (bf16[6,128,256]{2,1,0:T(8,128)(2,1)}, bf16[6,128,256]{2,1,0:T(8,128)(2,1)}, u32[]{:S(2)}, u32[]{:S(2)}) collective-permute-start(bf16[6,128,256]{2,1,0:T(8,128)(2,1)} %get-tuple-element.78), channel_id=1, source_target_pairs={{0,1},{1,0},{2,3},{3,2},{4,5},{5,4},{6,7},{7,6},{8,9},{9,8},{10,11... | collective-permute-start | bytes 1179656 | tf_op jit(solution)/shard_map/ppermute | solution.py:136
  49.8 5.9 %copy-start.15 = (bf16[6,64,256]{2,1,0:T(8,128)(2,1)}, bf16[6,64,256]{2,1,0:T(8,128)(2,1)S(1)}, u32[]{:S(2)}) copy-start(bf16[6,64,256]{2,1,0:T(8,128)(2,1)S(1)} %convolution_convert_fusion.10) | copy-start | bytes 589828
  49.9 7.8 %collective-permute-start.2 = (bf16[256,384]{1,0:T(8,128)(2,1)S(1)}, bf16[256,384]{1,0:T(8,128)(2,1)S(1)}, u32[]{:S(2)}, u32[]{:S(2)}) collective-permute-start(bf16[256,384]{1,0:T(8,128)(2,1)S(1)} %copy.59), channel_id=1, source_target_pairs={{0,1},{1,0},{2,3},{3,2},{4,5},{5,4},{6,7},{7,6},{8,9},{9,8},{10,11... | collective-permute-start | bytes 589832 | tf_op jit(solution)/shard_map/ppermute | solution.py:136
  50.1 11.5 %collective-permute-start.5 = (bf16[128,768]{1,0:T(8,128)(2,1)S(1)}, bf16[128,768]{1,0:T(8,128)(2,1)S(1)}, u32[]{:S(2)}, u32[]{:S(2)}) collective-permute-start(bf16[128,768]{1,0:T(8,128)(2,1)S(1)} %bitcast.114), channel_id=1, source_target_pairs={{0,1},{1,0},{2,3},{3,2},{4,5},{5,4},{6,7},{7,6},{8,9},{9,8},{10,11... | collective-permute-start | bytes 589832 | tf_op jit(solution)/shard_map/ppermute | solution.py:136
  59.8 16.8 %copy-start.1 = (f32[256,768]{1,0:T(8,128)}, f32[256,768]{1,0:T(8,128)S(1)}, u32[]{:S(2)}) copy-start(f32[256,768]{1,0:T(8,128)S(1)} %get-tuple-element.66) | copy-start | bytes 2359300
  61.6 15.0 %copy-start.19 = (bf16[128,768]{1,0:T(8,128)(2,1)}, bf16[128,768]{1,0:T(8,128)(2,1)S(1)}, u32[]{:S(2)}) copy-start(bf16[128,768]{1,0:T(8,128)(2,1)S(1)} %collective-permute-done.5) | copy-start | bytes 589828
  62.9 10.2 %copy-start.51 = (bf16[256,1536]{1,0:T(8,128)(2,1)}, bf16[256,1536]{1,0:T(8,128)(2,1)S(1)}, u32[]{:S(2)}) copy-start(bf16[256,1536]{1,0:T(8,128)(2,1)S(1)} %get-tuple-element.69) | copy-start | bytes 2359300
  64.3 11.1 %collective-permute-start.6 = (bf16[256,768]{1,0:T(8,128)(2,1)S(1)}, bf16[256,768]{1,0:T(8,128)(2,1)S(1)}, u32[]{:S(2)}, u32[]{:S(2)}) collective-permute-start(bf16[256,768]{1,0:T(8,128)(2,1)S(1)} %convolution_convert_fusion.6), channel_id=1, source_target_pairs={{0,1},{1,0},{2,3},{3,2},{4,5},{5,4},{6,7},{7,6},{8,9},{9,8},{10,11... | collective-permute-start | bytes 1179656 | tf_op jit(solution)/shard_map/ppermute | solution.py:136
  95.1 12.1 %collective-permute-start.4 = (bf16[256,768]{1,0:T(8,128)(2,1)S(1)}, bf16[256,768]{1,0:T(8,128)(2,1)S(1)}, u32[]{:S(2)}, u32[]{:S(2)}) collective-permute-start(bf16[256,768]{1,0:T(8,128)(2,1)S(1)} %convolution_convert_fusion.7), channel_id=1, source_target_pairs={{0,1},{1,0},{2,3},{3,2},{4,5},{5,4},{6,7},{7,6},{8,9},{9,8},{10,11... | collective-permute-start | bytes 1179656 | tf_op jit(solution)/shard_map/ppermute | solution.py:136
  97.4 9.8 %copy-start.18 = (bf16[1,128,768]{2,1,0:T(8,128)(2,1)S(1)}, bf16[1,128,768]{2,1,0:T(8,128)(2,1)}, u32[]{:S(2)}) copy-start(bf16[1,128,768]{2,1,0:T(8,128)(2,1)} %param.29) | copy-start | bytes 589828
  97.4 9.7 %copy-start.20 = (bf16[128,768]{1,0:T(8,128)(2,1)S(1)}, bf16[128,768]{1,0:T(8,128)(2,1)}, u32[]{:S(2)}) copy-start(bf16[128,768]{1,0:T(8,128)(2,1)} %copy-done.19) | copy-start | bytes 589828
  97.4 9.7 %copy-start.29 = (f32[768]{0:T(1024)S(1)}, f32[768]{0:T(1024)}, u32[]{:S(2)}) copy-start(f32[768]{0:T(1024)} %get-tuple-element.59) | copy-start | bytes 9220
  97.4 18.1 %collective-permute-start.8 = (bf16[6,128,256]{2,1,0:T(8,128)(2,1)S(1)}, bf16[6,128,256]{2,1,0:T(8,128)(2,1)S(1)}, u32[]{:S(2)}, u32[]{:S(2)}) collective-permute-start(bf16[6,128,256]{2,1,0:T(8,128)(2,1)S(1)} %get-tuple-element.76), channel_id=1, source_target_pairs={{0,1},{1,0},{2,3},{3,2},{4,5},{5,4},{6,7},{7,6},{8,9},{9,8},{10,11... | collective-permute-start | bytes 1179656 | tf_op jit(solution)/shard_map/ppermute | solution.py:136
  98.3 9.1 %copy-start.2 = (f32[256,768]{1,0:T(8,128)S(1)}, f32[256,768]{1,0:T(8,128)}, u32[]{:S(2)}) copy-start(f32[256,768]{1,0:T(8,128)} %copy-done.1) | copy-start | bytes 2359300
  98.3 57.0 %collective-permute-start.7 = (bf16[256,768]{1,0:T(8,128)(2,1)S(1)}, bf16[256,768]{1,0:T(8,128)(2,1)}, u32[]{:S(2)}, u32[]{:S(2)}) collective-permute-start(bf16[256,768]{1,0:T(8,128)(2,1)S(1)} %convolution_convert_fusion.5), channel_id=1, source_target_pairs={{0,1},{1,0},{2,3},{3,2},{4,5},{5,4},{6,7},{7,6},{8,9},{9,8},{10,11... | collective-permute-start | bytes 1179656 | tf_op jit(solution)/shard_map/ppermute | solution.py:136
  117.5 37.8 %copy-start.38 = (f32[256]{0:T(256)S(1)}, f32[256]{0:T(256)}, u32[]{:S(2)}) copy-start(f32[256]{0:T(256)} %copy-done.36) | copy-start | bytes 3076
  117.5 37.8 %copy-start.44 = (f32[256]{0:T(256)S(1)}, f32[256]{0:T(256)}, u32[]{:S(2)}) copy-start(f32[256]{0:T(256)} %copy-done.42) | copy-start | bytes 3076
  153.4 6.2 %collective-permute-start.13 = (f32[1,3328]{1,0:T(1,128)S(1)}, f32[1,3328]{1,0:T(1,128)S(1)}, u32[]{:S(2)}, u32[]{:S(2)}) collective-permute-start(f32[1,3328]{1,0:T(1,128)S(1)} %broadcast_in_dim.65), channel_id=1, source_target_pairs={{0,1},{1,0},{2,3},{3,2},{4,5},{5,4},{6,7},{7,6},{8,9},{9,8},{10,11... | collective-permute-start | bytes 39944 | tf_op jit(solution)/shard_map/ppermute | solution.py:136
  157.0 18.7 %copy-start.5 = (f32[256,768]{1,0:T(8,128)S(1)}, f32[256,768]{1,0:T(8,128)}, u32[]{:S(2)}) copy-start(f32[256,768]{1,0:T(8,128)} %copy-done.3) | copy-start | bytes 2359300
  157.0 18.7 %copy-start.47 = (f32[128]{0:T(128)S(1)}, f32[128]{0:T(128)}, u32[]{:S(2)}) copy-start(f32[128]{0:T(128)} %dynamic-slice.14) | copy-start | bytes 1540
  159.5 1.2 collective-permute-start.9
  159.6 2.8 %collective-permute-start.14 = (f32[1,3328]{1,0:T(1,128)S(1)}, f32[1,3328]{1,0:T(1,128)S(1)}, u32[]{:S(2)}, u32[]{:S(2)}) collective-permute-start(f32[1,3328]{1,0:T(1,128)S(1)} %reshape_add_fusion), channel_id=1, source_target_pairs={{0,2},{2,0},{4,6},{6,4},{8,10},{10,8},{12,14},{14,12},{16,18},{18,... | collective-permute-start | bytes 39944 | tf_op jit(solution)/shard_map/ppermute | solution.py:169
  160.8 7.1 %collective-permute-start.10 = (f32[2,5632]{1,0:T(2,128)S(1)}, f32[2,5632]{1,0:T(2,128)S(1)}, u32[]{:S(2)}, u32[]{:S(2)}) collective-permute-start(f32[2,5632]{1,0:T(2,128)S(1)} %maximum_select_fusion.12), channel_id=1, source_target_pairs={{0,4},{2,6},{4,0},{6,2},{8,12},{10,14},{12,8},{14,10},{16,20},{18,... | collective-permute-start | bytes 135176 | tf_op jit(solution)/shard_map/ppermute | solution.py:154
  162.4 4.0 %collective-permute-start.15 = (f32[1,3328]{1,0:T(1,128)S(1)}, f32[1,3328]{1,0:T(1,128)S(1)}, u32[]{:S(2)}, u32[]{:S(2)}) collective-permute-start(f32[1,3328]{1,0:T(1,128)S(1)} %add.182), channel_id=1, source_target_pairs={{0,4},{2,6},{4,0},{6,2},{8,12},{10,14},{12,8},{14,10},{16,20},{18,... | collective-permute-start | bytes 39944 | tf_op jit(solution)/shard_map/ppermute | solution.py:169
  166.4 3.9 %collective-permute-start.16 = (f32[1,3328]{1,0:T(1,128)S(1)}, f32[1,3328]{1,0:T(1,128)S(1)}, u32[]{:S(2)}, u32[]{:S(2)}) collective-permute-start(f32[1,3328]{1,0:T(1,128)S(1)} %add.183), channel_id=1, source_target_pairs={{0,8},{2,10},{4,12},{6,14},{8,0},{10,2},{12,4},{14,6},{16,24},{18,... | collective-permute-start | bytes 39944 | tf_op jit(solution)/shard_map/ppermute | solution.py:169
  168.0 5.2 %collective-permute-start.11 = (f32[4,5632]{1,0:T(4,128)S(1)}, f32[4,5632]{1,0:T(4,128)S(1)}, u32[]{:S(2)}, u32[]{:S(2)}) collective-permute-start(f32[4,5632]{1,0:T(4,128)S(1)} %maximum_select_fusion.11), channel_id=1, source_target_pairs={{0,8},{2,10},{4,12},{6,14},{8,0},{10,2},{12,4},{14,6},{16,24},{18,... | collective-permute-start | bytes 270344 | tf_op jit(solution)/shard_map/ppermute | solution.py:154
  170.4 6.2 %collective-permute-start.17 = (f32[1,3328]{1,0:T(1,128)S(1)}, f32[1,3328]{1,0:T(1,128)S(1)}, u32[]{:S(2)}, u32[]{:S(2)}) collective-permute-start(f32[1,3328]{1,0:T(1,128)S(1)} %add.184), channel_id=1, source_target_pairs={{0,16},{2,18},{4,20},{6,22},{8,24},{10,26},{12,28},{14,30},{16,0},... | collective-permute-start | bytes 39944 | tf_op jit(solution)/shard_map/ppermute | solution.py:169
  173.3 9.6 %collective-permute-start.12 = (f32[8,5632]{1,0:T(8,128)S(1)}, f32[8,5632]{1,0:T(8,128)S(1)}, u32[]{:S(2)}, u32[]{:S(2)}) collective-permute-start(f32[8,5632]{1,0:T(8,128)S(1)} %maximum_select_fusion.9), channel_id=1, source_target_pairs={{0,16},{2,18},{4,20},{6,22},{8,24},{10,26},{12,28},{14,30},{16,0},... | collective-permute-start | bytes 540680 | tf_op jit(solution)/shard_map/ppermute | solution.py:154
  (39 other events, 124.1 us)
Sparse Core Ops, SparseCore 0:
  92.6 114.1 reduce-scatter.1

commit v10 on v4

--- a/solution.py
+++ b/solution.py
@@ -191,6 +191,11 @@
     return part + swap_heads(part)
 
 
+def head_sum_low(part):
+    low = part.astype(jnp.bfloat16)
+    return low.astype(jnp.float32) + swap_heads(low).astype(jnp.float32)
+
+
 def trade_blocks(values, head, size, axis, mine_axis):
     mine = lax.dynamic_slice_in_dim(values, head * size, size, axis)
     theirs = swap_heads(lax.dynamic_slice_in_dim(values, (1 - head) * size, size, axis))
@@ -317,7 +322,7 @@
     ffn_in_part = lax.dot_general(
         d_gate_up, gate_up_w, (((1,), (1,)), ((), ())), preferred_element_type=jnp.float32
     )
-    d_normed_t = head_sum(ffn_in_part)
+    d_normed_t = head_sum_low(ffn_in_part)
     d_middle = grad_out + norm_back(norm_mid, inv_mid, d_normed_t * (1.0 + scale_t))
     d_scale_t = jnp.sum(d_normed_t * norm_mid, axis=0, keepdims=True)
     d_shift_t = jnp.sum(d_normed_t, axis=0, keepdims=True)

time: 227 us -> 213 us (0.938)
  waiting for transfers between devices: 43.6 us -> 36.6 us
  matrix products: 47.9 us -> 42 us
  other arithmetic: 17.4 us -> 14.4 us
    ppermute x10, waiting for transfers between devices: 17.8 us -> 11.4 us  [swap_heads(): return lax.ppermute(values, 'head', [(0, 1), (1, 0)])]
    unnamed x141 -> x119, local copies, waits for them, and re-layouts: 17.6 us -> 18.3 us
  transfers between devices with their start and end apart: 19 -> 19, of which waited for: 10 -> 9; matrix products, arithmetic and copies ran while one was open for 32% -> 33% of each run, Pallas kernels for 22% -> 23%
where the time goes in v10:
time: 213 us; the launch traced here: 212 us
  Pallas kernels  49.2 us (23%)
  matrix products  42 us (20%)
  waiting for transfers between devices  36.6 us (17%)
  local copies, waits for them, and re-layouts  33.9 us (16%)
  starting transfers between devices  20.6 us (10%)
  between operations  15.5 us (7%)
  other arithmetic  14.4 us (7%)
    pallas_call x1, Pallas kernels, pair_backward(): pl.pallas_call(pair_backward_kernel, grid=(m // tile,), in_specs=[pl.Bloc...  34 us
    unnamed x119, local copies, waits for them, and re-layouts  18.3 us
    pallas_call x1, Pallas kernels, pair_forward(): pl.pallas_call(pair_forward_kernel, grid=(m // tile,), in_specs=[pl.Block...  15.2 us
    reduce_scatter x1, waiting for transfers between devices, shards(): lax.psum_scatter(packed, 'dp', scatter_dimension=0, tiled=True)  13.3 us
    ppermute x10, waiting for transfers between devices, swap_heads(): return lax.ppermute(values, 'head', [(0, 1), (1, 0)])  11.4 us
    ppermute x10, starting transfers between devices, swap_heads(): return lax.ppermute(values, 'head', [(0, 1), (1, 0)])  10.3 us
    ppermute x4, waiting for transfers between devices, dp_gather(): other = lax.ppermute(block, 'dp', [(i, i ^ step) for i in range(count)])  6.93 us
    ppermute x4, starting transfers between devices, dp_sum(): other = lax.ppermute(values, 'dp', [(i, i ^ step) for i in range(count)])  5.46 us
  transfers between devices with their start and end apart: 19, of which 9 were waited for; matrix products, arithmetic and copies ran while one was open for 33% of the time, Pallas kernels for 23%

profile of v10, /device:TPU:0, one launch (start us, length us, event | category | flops | bytes accessed | tf_op | source)
XLA Modules:
  0.0 212.2 jit_solution(15957615254664481889)
XLA Ops:
  7.2 3.0 %collective-permute-start = (bf16[128,768]{1,0:T(8,128)(2,1)}, bf16[128,768]{1,0:T(8,128)(2,1)S(1)}, u32[]{:S(2)}, u32[]{:S(2)}) collective-permute-start(bf16[128,768]{1,0:T(8,128)(2,1)} %bitcast.91), channel_id=1, source_target_pairs={{0,1},{1,0},{2,3},{3,2},{4,5},{5,4},{6,7},{7,6},{8,9},{9,8},{10,11... | collective-permute-start | bytes 589832 | tf_op jit(solution)/shard_map/ppermute | solution.py:147
  11.7 15.2 %shard_map.246 = bf16[12,32768]{1,0:T(8,128)(2,1)} custom-call(bf16[32768,256]{1,0:T(8,128)(2,1)} %bitcast.80, f32[1,256]{1,0:T(1,128)} %bitcast.122, bf16[16,256]{1,0:T(8,128)(2,1)} %pad.8.wt_ref), custom_call_target="tpu_custom_call" | custom-call | flops 352321536 | bytes 17563648 | tf_op jit(solution)/shard_map/pallas_call | solution.py:50
  29.3 2.0 copy.91
  31.3 1.9 collective-permute-start.1
  33.9 2.1 convolution_reduce_fusion
  38.2 3.9 %copy.67 = bf16[768,3,384]{0,2,1:T(8,128)(2,1)} copy(bf16[768,3,384]{2,0,1:T(8,128)(2,1)} %param.22) | data formatting | bytes 3538944 | tf_op args[7]
  43.1 2.3 %convolution_convert_fusion.3 = bf16[256,1152]{1,0:T(8,128)(2,1)S(1)} fusion(bf16[768,1152]{0,1:T(8,128)(2,1)} %bitcast.89, f32[768]{0:T(1024)S(1)} %get-tuple-element.70, f32[768]{0:T(1024)S(1)} %get-tuple-element.71, f32[256]{0:T(256)S(1)} %add_rsqrt_fusion.1, f32[256]{0:T(256)S(1)} %broadcast_multiply_fusion.5, bf16[128,768]{1,0:T(8,128)(2,1)S(1)} %bitcast.94, ...), kind=kOutput, calls=%fused_computation.7 | convolution fusion | flops 456228864 | bytes 2760705 | tf_op jit(solution)/shard_map/dot_general | solution.py:273
  45.9 3.3 %fusion.79 = (f32[6,256]{1,0:T(8,128)S(1)}, f32[6,256,256]{1,2,0:T(8,128)}) fusion(pred[256]{0:T(512)(128)(4,1)} %or_and_fusion, bf16[256,6,64]{0,2,1:T(8,128)(2,1)S(1)} %bitcast.103, bf16[256,6,64]{0,2,1:T(8,128)(2,1)S(1)} %bitcast.101, bf16[6,128,256]{1,2,0:T(8,128)(2,1)} %copy.90, bf16[6,128,256]{1,2,0:T(8,128)(2,1)} %collective-permute-done.1, pred[]{:T(512)S(6)} %eq.44), kind=kOutput, calls=%fused_computation.180 | convolution fusion | flops 56230144 | bytes 2758913 | tf_op jit(solution)/shard_map/sub | solution.py:281
  51.9 1.9 collective-permute-start.5
  53.8 3.6 %copy.94 = bf16[96,8,2,1536]{3,1,2,0:T(8,128)(2,1)S(1)} copy(bf16[96,8,2,1536]{3,2,1,0:T(2,128)(2,1)} %bitcast.82) | data formatting | bytes 9437184
  58.0 1.8 collective-permute-done.2
  59.9 2.4 %fusion.77 = (f32[256]{0:T(256)S(1)}, f32[256,768]{1,0:T(8,128)S(1)}, f32[256,768]{1,0:T(8,128)S(1)}) fusion(f32[768]{0:T(1024)S(1)} %get-tuple-element.115, bf16[128,768]{1,0:T(8,128)(2,1)S(1)} %bitcast.95, bf16[128,768]{1,0:T(8,128)(2,1)S(1)} %collective-permute-done, pred[]{:T(512)S(6)} %eq.44, f32[768]{0:T(1024)S(1)} %copy-done.48, ...), kind=kOutput, calls=%fused_computation.178 | convolution fusion | flops 311820032 | bytes 3546113 | tf_op jit(solution)/shard_map/dot_general | solution.py:292
  66.9 3.9 %fusion.1 = bf16[768,6144]{1,0:T(8,128)(2,1)} fusion(bf16[768,6144]{1,0:T(8,128)(2,1)} %shard_map.248, bf16[256,1536]{1,0:T(8,128)(2,1)S(1)} %get-tuple-element.81, bf16[256,1536]{1,0:T(8,128)(2,1)S(1)} %get-tuple-element.80, f32[256,768]{1,0:T(8,128)S(1)} %get-tuple-element.79, f32[768]{0:T(1024)S(1)} %copy-done.46, f32[768]{0:T(1024)S(1)} %get-tuple-element.68, ...), kind=kOutput, calls=%fused_computation.2 | convolution fusion | flops 1214447616 | bytes 7086080 | tf_op jit(solution)/shard_map/dot_general | solution.py:319
  70.8 2.3 %fusion.2 = bf16[768,6144]{1,0:T(8,128)(2,1)} fusion(bf16[768,6144]{1,0:T(8,128)(2,1)} %fusion.1, bf16[256,1536]{1,0:T(8,128)(2,1)S(1)} %get-tuple-element.82, f32[768]{0:T(1024)S(1)} %get-tuple-element.73, bf16[128,768]{1,0:T(8,128)(2,1)S(1)} %collective-permute-done.5, bf16[128,768]{1,0:T(8,128)(2,1)S(1)} %bitcast.109, pred[]{:T(512)S(6)} %eq.44), kind=kOutput, calls=%fused_computation.5 | convolution fusion | flops 607518720 | bytes 3542017 | tf_op jit(solution)/shard_map/dot_general | solution.py:310
  78.3 2.1 convolution_convert_fusion.8
  84.6 2.2 %fusion.3 = bf16[768,6144]{1,0:T(8,128)(2,1)} fusion(bf16[768,6144]{1,0:T(8,128)(2,1)} %fusion.7, bf16[256,384]{0,1:T(8,128)(2,1)S(1)} %bitcast.127, bf16[256,384]{0,1:T(8,128)(2,1)S(1)} %bitcast.113, bf16[256,384]{0,1:T(8,128)(2,1)S(1)} %bitcast.115, f32[768]{0:T(1024)S(1)} %copy-done.45, f32[768]{0:T(1024)S(1)} %get-tuple-element.71, ...), kind=kOutput, calls=%fused_computation.6 | convolution fusion | flops 458588160 | bytes 2760705 | tf_op jit(solution)/shard_map/dot_general | solution.py:357
  88.0 2.7 %convolution_convert_fusion.7 = bf16[256,768]{1,0:T(8,128)(2,1)} fusion(bf16[256,1536]{1,0:T(8,128)(2,1)} %copy-done.51, bf16[1536,768]{1,0:T(8,128)(2,1)S(1)} %copy-done), kind=kOutput, calls=%fused_computation.24 | convolution fusion | flops 604176384 | bytes 3538944 | tf_op jit(solution)/shard_map/dot_general | solution.py:302
  92.1 1.9 copy.81
  95.4 1.8 collective-permute-start.8
  97.1 3.5 %convolution_convert_fusion.5 = bf16[256,768]{1,0:T(8,128)(2,1)} fusion(bf16[768,1152]{0,1:T(8,128)(2,1)} %bitcast.90, bf16[256,384]{0,1:T(8,128)(2,1)} %bitcast.128, bf16[256,384]{0,1:T(8,128)(2,1)} %bitcast.114, bf16[256,384]{0,1:T(8,128)(2,1)} %bitcast.116), kind=kOutput, calls=%fused_computation.22 | convolution fusion | flops 454950912 | bytes 2752512 | tf_op jit(solution)/shard_map/dot_general | solution.py:370
  101.0 2.0 collective-permute-done.4
  105.2 6.0 %collective-permute-done.8 = bf16[6,128,256]{1,2,0:T(8,128)(2,1)} collective-permute-done((bf16[6,128,256]{1,2,0:T(8,128)(2,1)}, bf16[6,128,256]{1,2,0:T(8,128)(2,1)}, u32[]{:S(2)}, u32[]{:S(2)}) %collective-permute-start.8) | collective-permute-done | bytes 393248 | tf_op jit(solution)/shard_map/ppermute | solution.py:147
  111.1 1.9 copy.82
  116.0 34.0 %shard_map.247 = (bf16[32768,256]{1,0:T(8,128)(2,1)}, f32[16,256]{1,0:T(8,128)}, f32[1,256]{1,0:T(1,128)}) custom-call(bf16[32768,256]{1,0:T(8,128)(2,1)} %bitcast.81, bf16[16,32768]{1,0:T(8,128)(2,1)} %pad.9.ds_ref, f32[1,256]{1,0:T(1,128)} %bitcast.123, bf16[16,256]{1,0:T(8,128)(2,1)} %pad.8.wt_ref), custom_call_target="tpu_custom_call" | custom-call | flops 704643072 | bytes 34603008 | tf_op jit(solution)/shard_map/pallas_call | solution.py:97
  154.4 2.5 %convolution_multiply_fusion.2 = f32[1,256]{1,0:T(1,128)} fusion(bf16[256,4608]{1,0:T(8,128)(2,1)S(1)} %copy-done.6, f32[1,4608]{1,0:T(1,128)S(1)} %get-tuple-element.99, f32[1,256]{1,0:T(1,128)S(1)} %copy-done.33), kind=kOutput, calls=%fused_computation.46 | convolution fusion | flops 14157824 | bytes 2379776 | tf_op jit(solution)/shard_map/dot_general | solution.py:409
  158.1 1.8 collective-permute-start.10
  160.3 3.5 %collective-permute-done.15 = f32[1,3328]{1,0:T(1,128)S(1)} collective-permute-done((f32[1,3328]{1,0:T(1,128)S(1)}, f32[1,3328]{1,0:T(1,128)S(1)}, u32[]{:S(2)}, u32[]{:S(2)}) %collective-permute-start.15) | collective-permute-done | bytes 13344 | tf_op jit(solution)/shard_map/ppermute | solution.py:180
  167.7 2.8 %collective-permute-start.17 = (f32[1,3328]{1,0:T(1,128)S(1)}, f32[1,3328]{1,0:T(1,128)S(1)}, u32[]{:S(2)}, u32[]{:S(2)}) collective-permute-start(f32[1,3328]{1,0:T(1,128)S(1)} %add.184), channel_id=1, source_target_pairs={{0,16},{2,18},{4,20},{6,22},{8,24},{10,26},{12,28},{14,30},{16,0},... | collective-permute-start | bytes 39944 | tf_op jit(solution)/shard_map/ppermute | solution.py:180
  170.6 2.6 %collective-permute-start.12 = (f32[8,5632]{1,0:T(8,128)S(1)}, f32[8,5632]{1,0:T(8,128)S(1)}, u32[]{:S(2)}, u32[]{:S(2)}) collective-permute-start(f32[8,5632]{1,0:T(8,128)S(1)} %maximum_select_fusion.9), channel_id=1, source_target_pairs={{0,16},{2,18},{4,20},{6,22},{8,24},{10,26},{12,28},{14,30},{16,0},... | collective-permute-start | bytes 540680 | tf_op jit(solution)/shard_map/ppermute | solution.py:165
  175.5 6.3 %collective-permute-done.12 = f32[8,5632]{1,0:T(8,128)S(1)} collective-permute-done((f32[8,5632]{1,0:T(8,128)S(1)}, f32[8,5632]{1,0:T(8,128)S(1)}, u32[]{:S(2)}, u32[]{:S(2)}) %collective-permute-start.12) | collective-permute-done | bytes 180256 | tf_op jit(solution)/shard_map/ppermute | solution.py:165
  183.2 4.2 %fusion.47 = f32[256,4608]{1,0:T(8,128)} fusion(bf16[16,256]{1,0:T(8,128)(2,1)S(1)} %multiply_convert_fusion.7, f32[16,5632]{1,0:T(8,128)S(1)} %maximum_select_fusion.8), kind=kOutput, calls=%fused_computation.105 | convolution fusion | flops 226492416 | bytes 5021696 | tf_op jit(solution)/shard_map/dot_general | solution.py:407
  187.4 13.3 %reduce-scatter.2.cloned.1.call-done = bf16[48,6144]{1,0:T(8,128)(2,1)} async-done(((bf16[768,6144]{1,0:T(8,128)(2,1)}), bf16[48,6144]{1,0:T(8,128)(2,1)}) %reduce-scatter.2.cloned.1.call-update) | async-done | bytes 589840 | tf_op jit(solution)/shard_map/reduce_scatter | solution.py:368
  (219 shorter events, 52.1 us)
Async XLA Ops:
  7.2 56.9 %copy-start = (bf16[1536,768]{1,0:T(8,128)(2,1)S(1)}, bf16[1536,768]{1,0:T(8,128)(2,1)}, u32[]{:S(2)}) copy-start(bf16[1536,768]{1,0:T(8,128)(2,1)} %param.28) | copy-start | bytes 7077892
  7.2 193.5 %reduce-scatter.2.cloned.1.call-start = ((), (), s32[]{:S(2)}) async-start(), calls=%async_computation.1 | async-start | bytes 10027008 | tf_op jit(solution)/shard_map/reduce_scatter | solution.py:368
  7.2 35.4 %collective-permute-start = (bf16[128,768]{1,0:T(8,128)(2,1)}, bf16[128,768]{1,0:T(8,128)(2,1)S(1)}, u32[]{:S(2)}, u32[]{:S(2)}) collective-permute-start(bf16[128,768]{1,0:T(8,128)(2,1)} %bitcast.91), channel_id=1, source_target_pairs={{0,1},{1,0},{2,3},{3,2},{4,5},{5,4},{6,7},{7,6},{8,9},{9,8},{10,11... | collective-permute-start | bytes 589832 | tf_op jit(solution)/shard_map/ppermute | solution.py:147
  10.3 47.8 %collective-permute-start.3 = (bf16[384,768]{1,0:T(8,128)(2,1)}, bf16[384,768]{1,0:T(8,128)(2,1)}, u32[]{:S(2)}, u32[]{:S(2)}) collective-permute-start(bf16[384,768]{1,0:T(8,128)(2,1)} %param.25), channel_id=1, source_target_pairs={{0,1},{1,0},{2,3},{3,2},{4,5},{5,4},{6,7},{7,6},{8,9},{9,8},{10,11... | collective-permute-start | bytes 1769480 | tf_op jit(solution)/shard_map/ppermute | solution.py:147
  29.3 6.7 %copy-start.24 = (f32[4608]{0:T(1024)S(1)}, f32[4608]{0:T(1024)}, u32[]{:S(2)}) copy-start(f32[4608]{0:T(1024)} %param.21) | copy-start | bytes 55300
  29.3 8.0 %copy-start.9 = (bf16[6,128,256]{2,1,0:T(8,128)(2,1)S(1)}, bf16[6,128,256]{2,1,0:T(8,128)(2,1)}, u32[]{:S(2)}) copy-start(bf16[6,128,256]{2,1,0:T(8,128)(2,1)} %get-tuple-element.90) | copy-start | bytes 1179652
  31.3 14.6 %collective-permute-start.1 = (bf16[6,128,256]{1,2,0:T(8,128)(2,1)}, bf16[6,128,256]{1,2,0:T(8,128)(2,1)}, u32[]{:S(2)}, u32[]{:S(2)}) collective-permute-start(bf16[6,128,256]{1,2,0:T(8,128)(2,1)} %copy.91), channel_id=1, source_target_pairs={{0,1},{1,0},{2,3},{3,2},{4,5},{5,4},{6,7},{7,6},{8,9},{9,8},{10,11... | collective-permute-start | bytes 1179656 | tf_op jit(solution)/shard_map/ppermute | solution.py:147
  51.8 8.1 %collective-permute-start.2 = (bf16[256,384]{1,0:T(8,128)(2,1)}, bf16[256,384]{1,0:T(8,128)(2,1)}, u32[]{:S(2)}, u32[]{:S(2)}) collective-permute-start(bf16[256,384]{1,0:T(8,128)(2,1)} %copy.75), channel_id=1, source_target_pairs={{0,1},{1,0},{2,3},{3,2},{4,5},{5,4},{6,7},{7,6},{8,9},{9,8},{10,11... | collective-permute-start | bytes 589832 | tf_op jit(solution)/shard_map/ppermute | solution.py:147
  51.9 12.2 %collective-permute-start.5 = (bf16[128,768]{1,0:T(8,128)(2,1)S(1)}, bf16[128,768]{1,0:T(8,128)(2,1)S(1)}, u32[]{:S(2)}, u32[]{:S(2)}) collective-permute-start(bf16[128,768]{1,0:T(8,128)(2,1)S(1)} %bitcast.107), channel_id=1, source_target_pairs={{0,1},{1,0},{2,3},{3,2},{4,5},{5,4},{6,7},{7,6},{8,9},{9,8},{10,11... | collective-permute-start | bytes 589832 | tf_op jit(solution)/shard_map/ppermute | solution.py:147
  53.8 6.1 %copy-start.21 = (bf16[384,768]{1,0:T(8,128)(2,1)S(1)}, bf16[384,768]{1,0:T(8,128)(2,1)}, u32[]{:S(2)}) copy-start(bf16[384,768]{1,0:T(8,128)(2,1)} %param.25) | copy-start | bytes 1769476
  62.3 13.3 %copy-start.1 = (f32[256,768]{1,0:T(8,128)}, f32[256,768]{1,0:T(8,128)S(1)}, u32[]{:S(2)}) copy-start(f32[256,768]{1,0:T(8,128)S(1)} %get-tuple-element.79) | copy-start | bytes 2359300
  64.0 11.6 %copy-start.19 = (bf16[128,768]{1,0:T(8,128)(2,1)}, bf16[128,768]{1,0:T(8,128)(2,1)S(1)}, u32[]{:S(2)}) copy-start(bf16[128,768]{1,0:T(8,128)(2,1)S(1)} %collective-permute-done.5) | copy-start | bytes 589828
  66.8 7.8 %collective-permute-start.6 = (bf16[256,768]{1,0:T(8,128)(2,1)S(1)}, bf16[256,768]{1,0:T(8,128)(2,1)S(1)}, u32[]{:S(2)}, u32[]{:S(2)}) collective-permute-start(bf16[256,768]{1,0:T(8,128)(2,1)S(1)} %convolution_convert_fusion.6), channel_id=1, source_target_pairs={{0,1},{1,0},{2,3},{3,2},{4,5},{5,4},{6,7},{7,6},{8,9},{9,8},{10,11... | collective-permute-start | bytes 1179656 | tf_op jit(solution)/shard_map/ppermute | solution.py:147
  90.7 12.3 %collective-permute-start.4 = (bf16[256,768]{1,0:T(8,128)(2,1)}, bf16[256,768]{1,0:T(8,128)(2,1)}, u32[]{:S(2)}, u32[]{:S(2)}) collective-permute-start(bf16[256,768]{1,0:T(8,128)(2,1)} %convolution_convert_fusion.7), channel_id=1, source_target_pairs={{0,1},{1,0},{2,3},{3,2},{4,5},{5,4},{6,7},{7,6},{8,9},{9,8},{10,11... | collective-permute-start | bytes 1179656 | tf_op jit(solution)/shard_map/ppermute | solution.py:147
  95.3 7.7 %copy-start.18 = (bf16[1,128,768]{2,1,0:T(8,128)(2,1)S(1)}, bf16[1,128,768]{2,1,0:T(8,128)(2,1)}, u32[]{:S(2)}) copy-start(bf16[1,128,768]{2,1,0:T(8,128)(2,1)} %param.29) | copy-start | bytes 589828
  95.3 7.7 %copy-start.20 = (bf16[128,768]{1,0:T(8,128)(2,1)S(1)}, bf16[128,768]{1,0:T(8,128)(2,1)}, u32[]{:S(2)}) copy-start(bf16[128,768]{1,0:T(8,128)(2,1)} %copy-done.19) | copy-start | bytes 589828
  95.4 7.6 %copy-start.27 = (f32[768]{0:T(1024)S(1)}, f32[768]{0:T(1024)}, u32[]{:S(2)}) copy-start(f32[768]{0:T(1024)} %get-tuple-element.72) | copy-start | bytes 9220
  95.4 15.8 %collective-permute-start.8 = (bf16[6,128,256]{1,2,0:T(8,128)(2,1)}, bf16[6,128,256]{1,2,0:T(8,128)(2,1)}, u32[]{:S(2)}, u32[]{:S(2)}) collective-permute-start(bf16[6,128,256]{1,2,0:T(8,128)(2,1)} %get-tuple-element.89), channel_id=1, source_target_pairs={{0,1},{1,0},{2,3},{3,2},{4,5},{5,4},{6,7},{7,6},{8,9},{9,8},{10,11... | collective-permute-start | bytes 1179656 | tf_op jit(solution)/shard_map/ppermute | solution.py:147
  100.7 51.8 %collective-permute-start.7 = (bf16[256,768]{1,0:T(8,128)(2,1)}, bf16[256,768]{1,0:T(8,128)(2,1)}, u32[]{:S(2)}, u32[]{:S(2)}) collective-permute-start(bf16[256,768]{1,0:T(8,128)(2,1)} %convolution_convert_fusion.5), channel_id=1, source_target_pairs={{0,1},{1,0},{2,3},{3,2},{4,5},{5,4},{6,7},{7,6},{8,9},{9,8},{10,11... | collective-permute-start | bytes 1179656 | tf_op jit(solution)/shard_map/ppermute | solution.py:147
  116.0 36.5 %copy-start.36 = (f32[256]{0:T(256)S(1)}, f32[256]{0:T(256)}, u32[]{:S(2)}) copy-start(f32[256]{0:T(256)} %copy-done.34) | copy-start | bytes 3076
  116.0 36.5 %copy-start.43 = (f32[256]{0:T(256)S(1)}, f32[256]{0:T(256)}, u32[]{:S(2)}) copy-start(f32[256]{0:T(256)} %copy-done.40) | copy-start | bytes 3076
  151.8 5.0 %collective-permute-start.13 = (f32[1,3328]{1,0:T(1,128)S(1)}, f32[1,3328]{1,0:T(1,128)S(1)}, u32[]{:S(2)}, u32[]{:S(2)}) collective-permute-start(f32[1,3328]{1,0:T(1,128)S(1)} %broadcast_in_dim.61), channel_id=1, source_target_pairs={{0,1},{1,0},{2,3},{3,2},{4,5},{5,4},{6,7},{7,6},{8,9},{9,8},{10,11... | collective-permute-start | bytes 39944 | tf_op jit(solution)/shard_map/ppermute | solution.py:147
  154.3 18.9 %copy-start.5 = (f32[256,768]{1,0:T(8,128)S(1)}, f32[256,768]{1,0:T(8,128)}, u32[]{:S(2)}) copy-start(f32[256,768]{1,0:T(8,128)} %copy-done.3) | copy-start | bytes 2359300
  154.3 18.8 %copy-start.47 = (f32[128]{0:T(128)S(1)}, f32[128]{0:T(128)}, u32[]{:S(2)}) copy-start(f32[128]{0:T(128)} %dynamic-slice.14) | copy-start | bytes 1540
  156.9 1.2 collective-permute-start.9
  156.9 3.0 %collective-permute-start.14 = (f32[1,3328]{1,0:T(1,128)S(1)}, f32[1,3328]{1,0:T(1,128)S(1)}, u32[]{:S(2)}, u32[]{:S(2)}) collective-permute-start(f32[1,3328]{1,0:T(1,128)S(1)} %reshape_add_fusion), channel_id=1, source_target_pairs={{0,2},{2,0},{4,6},{6,4},{8,10},{10,8},{12,14},{14,12},{16,18},{18,... | collective-permute-start | bytes 39944 | tf_op jit(solution)/shard_map/ppermute | solution.py:180
  158.1 7.5 %collective-permute-start.10 = (f32[2,5632]{1,0:T(2,128)S(1)}, f32[2,5632]{1,0:T(2,128)S(1)}, u32[]{:S(2)}, u32[]{:S(2)}) collective-permute-start(f32[2,5632]{1,0:T(2,128)S(1)} %maximum_select_fusion.12), channel_id=1, source_target_pairs={{0,4},{2,6},{4,0},{6,2},{8,12},{10,14},{12,8},{14,10},{16,20},{18,... | collective-permute-start | bytes 135176 | tf_op jit(solution)/shard_map/ppermute | solution.py:165
  160.0 3.9 %collective-permute-start.15 = (f32[1,3328]{1,0:T(1,128)S(1)}, f32[1,3328]{1,0:T(1,128)S(1)}, u32[]{:S(2)}, u32[]{:S(2)}) collective-permute-start(f32[1,3328]{1,0:T(1,128)S(1)} %add.182), channel_id=1, source_target_pairs={{0,4},{2,6},{4,0},{6,2},{8,12},{10,14},{12,8},{14,10},{16,20},{18,... | collective-permute-start | bytes 39944 | tf_op jit(solution)/shard_map/ppermute | solution.py:180
  163.9 3.8 %collective-permute-start.16 = (f32[1,3328]{1,0:T(1,128)S(1)}, f32[1,3328]{1,0:T(1,128)S(1)}, u32[]{:S(2)}, u32[]{:S(2)}) collective-permute-start(f32[1,3328]{1,0:T(1,128)S(1)} %add.183), channel_id=1, source_target_pairs={{0,8},{2,10},{4,12},{6,14},{8,0},{10,2},{12,4},{14,6},{16,24},{18,... | collective-permute-start | bytes 39944 | tf_op jit(solution)/shard_map/ppermute | solution.py:180
  165.7 4.9 %collective-permute-start.11 = (f32[4,5632]{1,0:T(4,128)S(1)}, f32[4,5632]{1,0:T(4,128)S(1)}, u32[]{:S(2)}, u32[]{:S(2)}) collective-permute-start(f32[4,5632]{1,0:T(4,128)S(1)} %maximum_select_fusion.11), channel_id=1, source_target_pairs={{0,8},{2,10},{4,12},{6,14},{8,0},{10,2},{12,4},{14,6},{16,24},{18,... | collective-permute-start | bytes 270344 | tf_op jit(solution)/shard_map/ppermute | solution.py:165
  167.7 6.4 %collective-permute-start.17 = (f32[1,3328]{1,0:T(1,128)S(1)}, f32[1,3328]{1,0:T(1,128)S(1)}, u32[]{:S(2)}, u32[]{:S(2)}) collective-permute-start(f32[1,3328]{1,0:T(1,128)S(1)} %add.184), channel_id=1, source_target_pairs={{0,16},{2,18},{4,20},{6,22},{8,24},{10,26},{12,28},{14,30},{16,0},... | collective-permute-start | bytes 39944 | tf_op jit(solution)/shard_map/ppermute | solution.py:180
  170.6 11.2 %collective-permute-start.12 = (f32[8,5632]{1,0:T(8,128)S(1)}, f32[8,5632]{1,0:T(8,128)S(1)}, u32[]{:S(2)}, u32[]{:S(2)}) collective-permute-start(f32[8,5632]{1,0:T(8,128)S(1)} %maximum_select_fusion.9), channel_id=1, source_target_pairs={{0,16},{2,18},{4,20},{6,22},{8,24},{10,26},{12,28},{14,30},{16,0},... | collective-permute-start | bytes 540680 | tf_op jit(solution)/shard_map/ppermute | solution.py:165
  (39 other events, 112.6 us)
Sparse Core Ops, SparseCore 0:
  86.9 113.7 reduce-scatter.1

commit v11 on v10

--- a/solution.py
+++ b/solution.py
@@ -15,6 +15,32 @@
 PAIR_TILE = 4096
 PAIR_BACK_TILE = 2048
 HEAD_PAD = 16
+
+
+def matmul_kernel(a_ref, b_ref, o_ref):
+    o_ref[...] = jnp.dot(a_ref[...], b_ref[...], preferred_element_type=jnp.float32).astype(
+        o_ref.dtype
+    )
+
+
+def matmul(a, b, dtype, cols):
+    m, k = a.shape
+    n = b.shape[1]
+    return pl.pallas_call(
+        matmul_kernel,
+        grid=(n // cols,),
+        in_specs=[
+            pl.BlockSpec((m, k), lambda j: (0, 0)),
+            pl.BlockSpec((k, cols), lambda j: (0, j)),
+        ],
+        out_specs=pl.BlockSpec((m, cols), lambda j: (0, j)),
+        out_shape=jax.ShapeDtypeStruct((m, n), dtype),
+        cost_estimate=pl.CostEstimate(
+            flops=2 * m * k * n,
+            transcendentals=0,
+            bytes_accessed=2 * (m * k + k * n) + m * n * jnp.dtype(dtype).itemsize,
+        ),
+    )(a, b)
 
 
 def blank_kernel(out_ref):
@@ -270,7 +296,7 @@
     residues = x_rows.astype(jnp.float32)
     norm_in, inv_in = layer_norm(residues)
     normed_a = (norm_in * (1.0 + scale_a) + shift_a).astype(jnp.bfloat16)
-    projected = jnp.dot(normed_a, qkv_w, preferred_element_type=jnp.float32).astype(jnp.bfloat16)
+    projected = matmul(normed_a, qkv_w, jnp.bfloat16, proj)
     queries = head_split(projected[:, :proj])
     keys = head_split(projected[:, proj : 2 * proj])
     values = head_split(projected[:, 2 * proj :])
@@ -295,7 +321,7 @@
 
     norm_mid, inv_mid = layer_norm(middle)
     normed_t = (norm_mid * (1.0 + scale_t) + shift_t).astype(jnp.bfloat16)
-    gate_up = jnp.dot(normed_t, gate_up_w, preferred_element_type=jnp.float32)
+    gate_up = matmul(normed_t, gate_up_w, jnp.float32, ffn // 2)
     gate_pre = gate_up[:, :ffn]
     up_pre = gate_up[:, ffn:]
     hidden = (jax.nn.silu(gate_pre) * up_pre).astype(jnp.bfloat16)

time: 213 us -> 233 us (1.094)
  Pallas kernels: 49.2 us -> 58.8 us
  local copies, waits for them, and re-layouts: 33.9 us -> 41.9 us
  other arithmetic: 14.4 us -> 18.9 us
    pallas_call x0 -> x2, Pallas kernels: none -> 9.34 us  [matmul(): pl.pallas_call(matmul_kernel, grid=(n // cols,), in_specs=[pl.BlockSpec((...]
    reshape x0 -> x1, local copies, waits for them, and re-layouts: none -> 3.89 us  [shards(): qkv_w = qkv_weight.reshape(width, 3 * proj)]
    dot_general x2 -> x0, matrix products: 3.75 us -> none  [the longest x1 2.27 us: shards(): jnp.dot(normed_a, qkv_w, preferred_element_type=jnp.float32)]
    ppermute x10, waiting for transfers between devices: 11.4 us -> 8.83 us  [swap_heads(): return lax.ppermute(values, 'head', [(0, 1), (1, 0)])]
    unnamed x119 -> x139, local copies, waits for them, and re-layouts: 18.3 us -> 20.4 us
  transfers between devices with their start and end apart: 19 -> 19, of which waited for: 9 -> 9; matrix products, arithmetic and copies ran while one was open for 33% -> 34% of each run, Pallas kernels for 23% -> 25%
where the time goes in v11:
time: 233 us; the launch traced here: 232 us
  Pallas kernels  58.8 us (25%)
  matrix products  42.7 us (18%)
  local copies, waits for them, and re-layouts  41.9 us (18%)
  waiting for transfers between devices  34.4 us (15%)
  starting transfers between devices  19.7 us (8%)
  other arithmetic  18.9 us (8%)
  between operations  15.4 us (7%)
    pallas_call x1, Pallas kernels, pair_backward(): pl.pallas_call(pair_backward_kernel, grid=(m // tile,), in_specs=[pl.Bloc...  34.2 us
    unnamed x139, local copies, waits for them, and re-layouts  20.4 us
    pallas_call x1, Pallas kernels, pair_forward(): pl.pallas_call(pair_forward_kernel, grid=(m // tile,), in_specs=[pl.Block...  15.2 us
    reduce_scatter x1, waiting for transfers between devices, shards(): lax.psum_scatter(packed, 'dp', scatter_dimension=0, tiled=True)  14.6 us
    ppermute x10, starting transfers between devices, swap_heads(): return lax.ppermute(values, 'head', [(0, 1), (1, 0)])  9.77 us
    pallas_call x2, Pallas kernels, matmul(): pl.pallas_call(matmul_kernel, grid=(n // cols,), in_specs=[pl.BlockSpec((...  9.34 us
    ppermute x10, waiting for transfers between devices, swap_heads(): return lax.ppermute(values, 'head', [(0, 1), (1, 0)])  8.83 us
    ppermute x4, waiting for transfers between devices, dp_gather(): other = lax.ppermute(block, 'dp', [(i, i ^ step) for i in range(count)])  5.68 us
  transfers between devices with their start and end apart: 19, of which 9 were waited for; matrix products, arithmetic and copies ran while one was open for 34% of the time, Pallas kernels for 25%

profile of v11, /device:TPU:0, one launch (start us, length us, event | category | flops | bytes accessed | tf_op | source)
XLA Modules:
  0.0 231.8 jit_solution(10678776226744377358)
XLA Ops:
  7.2 3.0 %collective-permute-start = (bf16[128,768]{1,0:T(8,128)(2,1)}, bf16[128,768]{1,0:T(8,128)(2,1)S(1)}, u32[]{:S(2)}, u32[]{:S(2)}) collective-permute-start(bf16[128,768]{1,0:T(8,128)(2,1)} %bitcast.91), channel_id=1, source_target_pairs={{0,1},{1,0},{2,3},{3,2},{4,5},{5,4},{6,7},{7,6},{8,9},{9,8},{10,11... | collective-permute-start | bytes 589832 | tf_op jit(solution)/shard_map/ppermute | solution.py:173
  11.7 15.2 %shard_map.247 = bf16[12,32768]{1,0:T(8,128)(2,1)} custom-call(bf16[32768,256]{1,0:T(8,128)(2,1)} %bitcast.80, f32[1,256]{1,0:T(1,128)} %bitcast.123, bf16[16,256]{1,0:T(8,128)(2,1)} %pad.8.wt_ref), custom_call_target="tpu_custom_call" | custom-call | flops 352321536 | bytes 17563648 | tf_op jit(solution)/shard_map/pallas_call | solution.py:76
  29.3 2.0 copy.92
  31.3 1.9 collective-permute-start.1
  34.0 2.1 convolution_reduce_fusion
  38.2 3.8 %copy.67 = bf16[768,3,384]{0,2,1:T(8,128)(2,1)} copy(bf16[768,3,384]{2,0,1:T(8,128)(2,1)} %param.22) | data formatting | bytes 3538944 | tf_op args[7]
  42.1 3.9 %copy.68.b_ref = bf16[768,1152]{1,0:T(8,128)(2,1)} copy(bf16[768,1152]{0,1:T(8,128)(2,1)} %bitcast.86) | data formatting | bytes 3538944 | tf_op jit(solution)/shard_map/reshape | solution.py:271
  47.4 3.7 %shard_map.246 = bf16[256,1152]{1,0:T(8,128)(2,1)} custom-call(bf16[256,768]{1,0:T(8,128)(2,1)} %add_convert_fusion.1.a_ref, bf16[768,1152]{1,0:T(8,128)(2,1)} %copy.68.b_ref), custom_call_target="tpu_custom_call" | custom-call | flops 452984832 | bytes 2752512 | tf_op jit(solution)/shard_map/pallas_call | solution.py:29
  53.4 3.5 %fusion.76 = (f32[6,256]{1,0:T(8,128)S(1)}, f32[6,256,256]{1,2,0:T(8,128)}) fusion(pred[256]{0:T(512)(128)(4,1)S(1)} %or_and_fusion, bf16[256,6,64]{0,2,1:T(8,128)(2,1)S(1)} %bitcast.104, bf16[256,6,64]{0,2,1:T(8,128)(2,1)S(1)} %bitcast.102, bf16[6,128,256]{1,2,0:T(8,128)(2,1)} %copy.91, bf16[6,128,256]{1,2,0:T(8,128)(2,1)} %collective-permute-done.1, ...), kind=kOutput, calls=%fused_computation.178 | convolution fusion | flops 56230144 | bytes 2758913 | tf_op jit(solution)/shard_map/sub | solution.py:307
  59.1 1.9 collective-permute-start.5
  61.1 5.8 %copy.95 = bf16[96,8,2,1536]{3,1,2,0:T(8,128)(2,1)} copy(bf16[96,8,2,1536]{3,2,1,0:T(2,128)(2,1)} %bitcast.88) | data formatting | bytes 9437184
  67.5 3.1 %fusion.74 = (f32[256]{0:T(256)S(1)}, f32[256,768]{1,0:T(8,128)S(1)}, f32[256,768]{1,0:T(8,128)}) fusion(f32[768]{0:T(1024)S(1)} %get-tuple-element.115, bf16[128,768]{1,0:T(8,128)(2,1)S(1)} %bitcast.95, bf16[128,768]{1,0:T(8,128)(2,1)S(1)} %collective-permute-done, pred[]{:T(512)S(6)} %eq.44, f32[768]{0:T(1024)S(1)} %copy-done.56, ...), kind=kOutput, calls=%fused_computation.176 | convolution fusion | flops 311820032 | bytes 3546113 | tf_op jit(solution)/shard_map/dot_general | solution.py:318
  71.8 5.6 %shard_map.248 = f32[256,3072]{1,0:T(8,128)} custom-call(bf16[256,768]{1,0:T(8,128)(2,1)} %add_convert_fusion.a_ref, bf16[768,3072]{1,0:T(8,128)(2,1)} %bitcast.82), custom_call_target="tpu_custom_call" | custom-call | flops 1207959552 | bytes 8257536 | tf_op jit(solution)/shard_map/pallas_call | solution.py:29
  77.4 3.4 %multiply_convert_fusion.2 = (bf16[256,1536]{1,0:T(8,128)(2,1)S(1)}, bf16[256,1536]{1,0:T(8,128)(2,1)S(1)}, bf16[256,1536]{1,0:T(8,128)(2,1)S(1)}) fusion(f32[256,3072]{1,0:T(8,128)} %shard_map.248, bf16[1536,768]{1,0:T(8,128)(2,1)S(1)} %copy-done, f32[768]{0:T(1024)S(1)} %get-tuple-element.73, bf16[128,768]{1,0:T(8,128)(2,1)S(1)} %bitcast.109, ...), kind=kOutput, calls=%fused_computation.12 | convolution fusion | flops 612237312 | bytes 8260609 | tf_op jit(solution)/shard_map/dot_general | solution.py:339
  82.5 3.6 %fusion.1 = bf16[768,6144]{1,0:T(8,128)(2,1)} fusion(bf16[768,6144]{1,0:T(8,128)(2,1)} %shard_map.250, bf16[256,768]{1,0:T(8,128)(2,1)S(1)} %copy-done.11, bf16[256,1536]{1,0:T(8,128)(2,1)S(1)} %get-tuple-element.81, bf16[256,1536]{1,0:T(8,128)(2,1)S(1)} %get-tuple-element.80), kind=kOutput, calls=%fused_computation.2 | convolution fusion | flops 1213464576 | bytes 6684672 | tf_op jit(solution)/shard_map/dot_general | solution.py:345
  86.2 3.4 %fusion.2 = bf16[768,6144]{1,0:T(8,128)(2,1)} fusion(bf16[768,6144]{1,0:T(8,128)(2,1)} %fusion.1, bf16[256,1536]{1,0:T(8,128)(2,1)S(1)} %get-tuple-element.82, f32[768]{0:T(1024)S(1)} %get-tuple-element.73, bf16[128,768]{1,0:T(8,128)(2,1)} %collective-permute-done.5, bf16[128,768]{1,0:T(8,128)(2,1)S(1)} %bitcast.110, pred[]{:T(512)S(6)} %eq.44), kind=kOutput, calls=%fused_computation.5 | convolution fusion | flops 607518720 | bytes 3542017 | tf_op jit(solution)/shard_map/dot_general | solution.py:336
  89.6 2.3 %collective-permute-done.6 = bf16[256,768]{1,0:T(8,128)(2,1)S(1)} collective-permute-done((bf16[256,768]{1,0:T(8,128)(2,1)S(1)}, bf16[256,768]{1,0:T(8,128)(2,1)S(1)}, u32[]{:S(2)}, u32[]{:S(2)}) %collective-permute-start.6) | collective-permute-done | bytes 393248 | tf_op jit(solution)/shard_map/ppermute | solution.py:173
  92.9 2.2 multiply_reduce_fusion.7
  105.1 2.0 fusion.3
  108.5 2.7 %convolution_convert_fusion.6 = bf16[256,768]{1,0:T(8,128)(2,1)} fusion(bf16[256,1536]{1,0:T(8,128)(2,1)} %copy-done.59, bf16[1536,768]{1,0:T(8,128)(2,1)S(1)} %copy-done), kind=kOutput, calls=%fused_computation.23 | convolution fusion | flops 604176384 | bytes 3538944 | tf_op jit(solution)/shard_map/dot_general | solution.py:328
  114.5 2.1 copy.96
  118.3 3.5 %convolution_convert_fusion.4 = bf16[256,768]{1,0:T(8,128)(2,1)} fusion(bf16[768,1152]{0,1:T(8,128)(2,1)} %bitcast.87, bf16[256,384]{0,1:T(8,128)(2,1)} %bitcast.129, bf16[256,384]{0,1:T(8,128)(2,1)} %bitcast.115, bf16[256,384]{0,1:T(8,128)(2,1)} %bitcast.117), kind=kOutput, calls=%fused_computation.21 | convolution fusion | flops 454950912 | bytes 2752512 | tf_op jit(solution)/shard_map/dot_general | solution.py:396
  123.2 2.2 fusion.23
  126.1 5.5 %collective-permute-done.8 = bf16[6,128,256]{1,2,0:T(8,128)(2,1)} collective-permute-done((bf16[6,128,256]{1,2,0:T(8,128)(2,1)}, bf16[6,128,256]{1,2,0:T(8,128)(2,1)}, u32[]{:S(2)}, u32[]{:S(2)}) %collective-permute-start.8) | collective-permute-done | bytes 393248 | tf_op jit(solution)/shard_map/ppermute | solution.py:173
  136.0 34.2 %shard_map.249 = (bf16[32768,256]{1,0:T(8,128)(2,1)}, f32[16,256]{1,0:T(8,128)}, f32[1,256]{1,0:T(1,128)}) custom-call(bf16[32768,256]{1,0:T(8,128)(2,1)} %bitcast.81, bf16[16,32768]{1,0:T(8,128)(2,1)} %pad.9.ds_ref, f32[1,256]{1,0:T(1,128)} %bitcast.124, bf16[16,256]{1,0:T(8,128)(2,1)} %pad.8.wt_ref), custom_call_target="tpu_custom_call" | custom-call | flops 704643072 | bytes 34603008 | tf_op jit(solution)/shard_map/pallas_call | solution.py:123
  174.0 2.5 %convolution_multiply_fusion.2 = f32[1,256]{1,0:T(1,128)} fusion(bf16[256,4608]{1,0:T(8,128)(2,1)S(1)} %copy-done.8, f32[1,4608]{1,0:T(1,128)S(1)} %get-tuple-element.99, f32[1,256]{1,0:T(1,128)S(1)} %copy-done.49), kind=kOutput, calls=%fused_computation.45 | convolution fusion | flops 14157824 | bytes 2379776 | tf_op jit(solution)/shard_map/dot_general | solution.py:435
  180.0 3.7 %collective-permute-done.15 = f32[1,3328]{1,0:T(1,128)S(1)} collective-permute-done((f32[1,3328]{1,0:T(1,128)S(1)}, f32[1,3328]{1,0:T(1,128)S(1)}, u32[]{:S(2)}, u32[]{:S(2)}) %collective-permute-start.15) | collective-permute-done | bytes 13344 | tf_op jit(solution)/shard_map/ppermute | solution.py:206
  187.7 2.3 collective-permute-start.17
  190.1 2.7 %collective-permute-start.12 = (f32[8,5632]{1,0:T(8,128)S(1)}, f32[8,5632]{1,0:T(8,128)S(1)}, u32[]{:S(2)}, u32[]{:S(2)}) collective-permute-start(f32[8,5632]{1,0:T(8,128)S(1)} %maximum_select_fusion.9), channel_id=1, source_target_pairs={{0,16},{2,18},{4,20},{6,22},{8,24},{10,26},{12,28},{14,30},{16,0},... | collective-permute-start | bytes 540680 | tf_op jit(solution)/shard_map/ppermute | solution.py:191
  195.2 5.0 %collective-permute-done.12 = f32[8,5632]{1,0:T(8,128)S(1)} collective-permute-done((f32[8,5632]{1,0:T(8,128)S(1)}, f32[8,5632]{1,0:T(8,128)S(1)}, u32[]{:S(2)}, u32[]{:S(2)}) %collective-permute-start.12) | collective-permute-done | bytes 180256 | tf_op jit(solution)/shard_map/ppermute | solution.py:191
  201.5 4.2 %fusion.47 = f32[256,4608]{1,0:T(8,128)} fusion(bf16[16,256]{1,0:T(8,128)(2,1)S(1)} %multiply_convert_fusion.7, f32[16,5632]{1,0:T(8,128)S(1)} %maximum_select_fusion.8), kind=kOutput, calls=%fused_computation.104 | convolution fusion | flops 226492416 | bytes 5021696 | tf_op jit(solution)/shard_map/dot_general | solution.py:433
  205.7 14.6 %reduce-scatter.2.cloned.1.call-done = bf16[48,6144]{1,0:T(8,128)(2,1)} async-done(((bf16[768,6144]{1,0:T(8,128)(2,1)}), bf16[48,6144]{1,0:T(8,128)(2,1)}) %reduce-scatter.2.cloned.1.call-update) | async-done | bytes 589840 | tf_op jit(solution)/shard_map/reduce_scatter | solution.py:394
  (243 shorter events, 58.4 us)
Async XLA Ops:
  7.2 70.2 %copy-start = (bf16[1536,768]{1,0:T(8,128)(2,1)S(1)}, bf16[1536,768]{1,0:T(8,128)(2,1)}, u32[]{:S(2)}) copy-start(bf16[1536,768]{1,0:T(8,128)(2,1)} %param.28) | copy-start | bytes 7077892
  7.2 213.1 %reduce-scatter.2.cloned.1.call-start = ((), (), s32[]{:S(2)}) async-start(), calls=%async_computation.1 | async-start | bytes 10027008 | tf_op jit(solution)/shard_map/reduce_scatter | solution.py:394
  7.2 38.7 %collective-permute-start = (bf16[128,768]{1,0:T(8,128)(2,1)}, bf16[128,768]{1,0:T(8,128)(2,1)S(1)}, u32[]{:S(2)}, u32[]{:S(2)}) collective-permute-start(bf16[128,768]{1,0:T(8,128)(2,1)} %bitcast.91), channel_id=1, source_target_pairs={{0,1},{1,0},{2,3},{3,2},{4,5},{5,4},{6,7},{7,6},{8,9},{9,8},{10,11... | collective-permute-start | bytes 589832 | tf_op jit(solution)/shard_map/ppermute | solution.py:173
  10.3 57.2 %collective-permute-start.3 = (bf16[384,768]{1,0:T(8,128)(2,1)}, bf16[384,768]{1,0:T(8,128)(2,1)}, u32[]{:S(2)}, u32[]{:S(2)}) collective-permute-start(bf16[384,768]{1,0:T(8,128)(2,1)} %param.25), channel_id=1, source_target_pairs={{0,1},{1,0},{2,3},{3,2},{4,5},{5,4},{6,7},{7,6},{8,9},{9,8},{10,11... | collective-permute-start | bytes 1769480 | tf_op jit(solution)/shard_map/ppermute | solution.py:173
  29.3 6.7 %copy-start.33 = (f32[4608]{0:T(1024)S(1)}, f32[4608]{0:T(1024)}, u32[]{:S(2)}) copy-start(f32[4608]{0:T(1024)} %param.21) | copy-start | bytes 55300
  29.3 8.0 %copy-start.12 = (bf16[6,128,256]{2,1,0:T(8,128)(2,1)S(1)}, bf16[6,128,256]{2,1,0:T(8,128)(2,1)}, u32[]{:S(2)}) copy-start(bf16[6,128,256]{2,1,0:T(8,128)(2,1)} %get-tuple-element.90) | copy-start | bytes 1179652
  31.3 22.1 %collective-permute-start.1 = (bf16[6,128,256]{1,2,0:T(8,128)(2,1)}, bf16[6,128,256]{1,2,0:T(8,128)(2,1)}, u32[]{:S(2)}, u32[]{:S(2)}) collective-permute-start(bf16[6,128,256]{1,2,0:T(8,128)(2,1)} %copy.92), channel_id=1, source_target_pairs={{0,1},{1,0},{2,3},{3,2},{4,5},{5,4},{6,7},{7,6},{8,9},{9,8},{10,11... | collective-permute-start | bytes 1179656 | tf_op jit(solution)/shard_map/ppermute | solution.py:173
  58.9 8.5 %collective-permute-start.2 = (bf16[256,384]{1,0:T(8,128)(2,1)S(1)}, bf16[256,384]{1,0:T(8,128)(2,1)}, u32[]{:S(2)}, u32[]{:S(2)}) collective-permute-start(bf16[256,384]{1,0:T(8,128)(2,1)S(1)} %copy.76), channel_id=1, source_target_pairs={{0,1},{1,0},{2,3},{3,2},{4,5},{5,4},{6,7},{7,6},{8,9},{9,8},{10,11... | collective-permute-start | bytes 589832 | tf_op jit(solution)/shard_map/ppermute | solution.py:173
  59.1 18.3 %collective-permute-start.5 = (bf16[128,768]{1,0:T(8,128)(2,1)S(1)}, bf16[128,768]{1,0:T(8,128)(2,1)}, u32[]{:S(2)}, u32[]{:S(2)}) collective-permute-start(bf16[128,768]{1,0:T(8,128)(2,1)S(1)} %bitcast.108), channel_id=1, source_target_pairs={{0,1},{1,0},{2,3},{3,2},{4,5},{5,4},{6,7},{7,6},{8,9},{9,8},{10,11... | collective-permute-start | bytes 589832 | tf_op jit(solution)/shard_map/ppermute | solution.py:173
  61.1 6.4 %copy-start.25 = (bf16[384,768]{1,0:T(8,128)(2,1)S(1)}, bf16[384,768]{1,0:T(8,128)(2,1)}, u32[]{:S(2)}) copy-start(bf16[384,768]{1,0:T(8,128)(2,1)} %param.25) | copy-start | bytes 1769476
  70.6 6.8 %copy-start.31 = (f32[256]{0:T(256)}, f32[256]{0:T(256)S(1)}, u32[]{:S(2)}) copy-start(f32[256]{0:T(256)S(1)} %broadcast_multiply_fusion.4) | copy-start | bytes 3076
  70.8 6.6 %copy-start.44 = (f32[256]{0:T(256)}, f32[256]{0:T(256)S(1)}, u32[]{:S(2)}) copy-start(f32[256]{0:T(256)S(1)} %add_rsqrt_fusion) | copy-start | bytes 3076
  71.8 9.1 %slice-start = ((s8[4718592]{0:T(1024)(128)(4,1)}), s8[524288]{0:T(1024)(128)(4,1)S(1)}, s32[]{:S(2)}) async-start(s8[4718592]{0:T(1024)(128)(4,1)} %bitcast.83), calls=%async_computation.2 | async-start | bytes 1048576
  82.4 9.5 %collective-permute-start.6 = (bf16[256,768]{1,0:T(8,128)(2,1)S(1)}, bf16[256,768]{1,0:T(8,128)(2,1)S(1)}, u32[]{:S(2)}, u32[]{:S(2)}) collective-permute-start(bf16[256,768]{1,0:T(8,128)(2,1)S(1)} %convolution_convert_fusion.5), channel_id=1, source_target_pairs={{0,1},{1,0},{2,3},{3,2},{4,5},{5,4},{6,7},{7,6},{8,9},{9,8},{10,11... | collective-permute-start | bytes 1179656 | tf_op jit(solution)/shard_map/ppermute | solution.py:173
  111.2 12.0 %collective-permute-start.4 = (bf16[256,768]{1,0:T(8,128)(2,1)}, bf16[256,768]{1,0:T(8,128)(2,1)}, u32[]{:S(2)}, u32[]{:S(2)}) collective-permute-start(bf16[256,768]{1,0:T(8,128)(2,1)} %convolution_convert_fusion.6), channel_id=1, source_target_pairs={{0,1},{1,0},{2,3},{3,2},{4,5},{5,4},{6,7},{7,6},{8,9},{9,8},{10,11... | collective-permute-start | bytes 1179656 | tf_op jit(solution)/shard_map/ppermute | solution.py:173
  116.6 6.6 %copy-start.24 = (bf16[1,128,768]{2,1,0:T(8,128)(2,1)S(1)}, bf16[1,128,768]{2,1,0:T(8,128)(2,1)}, u32[]{:S(2)}) copy-start(bf16[1,128,768]{2,1,0:T(8,128)(2,1)} %param.29) | copy-start | bytes 589828
  116.6 6.6 %copy-start.40 = (f32[768]{0:T(1024)S(1)}, f32[768]{0:T(1024)}, u32[]{:S(2)}) copy-start(f32[768]{0:T(1024)} %get-tuple-element.72) | copy-start | bytes 9220
  116.6 15.0 %collective-permute-start.8 = (bf16[6,128,256]{1,2,0:T(8,128)(2,1)}, bf16[6,128,256]{1,2,0:T(8,128)(2,1)}, u32[]{:S(2)}, u32[]{:S(2)}) collective-permute-start(bf16[6,128,256]{1,2,0:T(8,128)(2,1)} %get-tuple-element.89), channel_id=1, source_target_pairs={{0,1},{1,0},{2,3},{3,2},{4,5},{5,4},{6,7},{7,6},{8,9},{9,8},{10,11... | collective-permute-start | bytes 1179656 | tf_op jit(solution)/shard_map/ppermute | solution.py:173
  121.8 50.3 %collective-permute-start.7 = (bf16[256,768]{1,0:T(8,128)(2,1)}, bf16[256,768]{1,0:T(8,128)(2,1)}, u32[]{:S(2)}, u32[]{:S(2)}) collective-permute-start(bf16[256,768]{1,0:T(8,128)(2,1)} %convolution_convert_fusion.4), channel_id=1, source_target_pairs={{0,1},{1,0},{2,3},{3,2},{4,5},{5,4},{6,7},{7,6},{8,9},{9,8},{10,11... | collective-permute-start | bytes 1179656 | tf_op jit(solution)/shard_map/ppermute | solution.py:173
  136.0 36.2 %copy-start.35 = (f32[256]{0:T(256)S(1)}, f32[256]{0:T(256)}, u32[]{:S(2)}) copy-start(f32[256]{0:T(256)} %copy-done.34) | copy-start | bytes 3076
  136.0 36.2 %copy-start.52 = (f32[256]{0:T(256)S(1)}, f32[256]{0:T(256)}, u32[]{:S(2)}) copy-start(f32[256]{0:T(256)} %copy-done.50) | copy-start | bytes 3076
  172.0 4.5 %collective-permute-start.13 = (f32[1,3328]{1,0:T(1,128)S(1)}, f32[1,3328]{1,0:T(1,128)S(1)}, u32[]{:S(2)}, u32[]{:S(2)}) collective-permute-start(f32[1,3328]{1,0:T(1,128)S(1)} %broadcast_in_dim.61), channel_id=1, source_target_pairs={{0,1},{1,0},{2,3},{3,2},{4,5},{5,4},{6,7},{7,6},{8,9},{9,8},{10,11... | collective-permute-start | bytes 39944 | tf_op jit(solution)/shard_map/ppermute | solution.py:173
  174.0 18.8 %copy-start.7 = (f32[256,768]{1,0:T(8,128)S(1)}, f32[256,768]{1,0:T(8,128)}, u32[]{:S(2)}) copy-start(f32[256,768]{1,0:T(8,128)} %copy-done.5) | copy-start | bytes 2359300
  174.0 18.8 %copy-start.55 = (f32[128]{0:T(128)S(1)}, f32[128]{0:T(128)}, u32[]{:S(2)}) copy-start(f32[128]{0:T(128)} %dynamic-slice.14) | copy-start | bytes 1540
  176.5 1.2 collective-permute-start.9
  176.6 3.0 %collective-permute-start.14 = (f32[1,3328]{1,0:T(1,128)S(1)}, f32[1,3328]{1,0:T(1,128)S(1)}, u32[]{:S(2)}, u32[]{:S(2)}) collective-permute-start(f32[1,3328]{1,0:T(1,128)S(1)} %reshape_add_fusion), channel_id=1, source_target_pairs={{0,2},{2,0},{4,6},{6,4},{8,10},{10,8},{12,14},{14,12},{16,18},{18,... | collective-permute-start | bytes 39944 | tf_op jit(solution)/shard_map/ppermute | solution.py:206
  177.8 7.4 %collective-permute-start.10 = (f32[2,5632]{1,0:T(2,128)S(1)}, f32[2,5632]{1,0:T(2,128)S(1)}, u32[]{:S(2)}, u32[]{:S(2)}) collective-permute-start(f32[2,5632]{1,0:T(2,128)S(1)} %maximum_select_fusion.12), channel_id=1, source_target_pairs={{0,4},{2,6},{4,0},{6,2},{8,12},{10,14},{12,8},{14,10},{16,20},{18,... | collective-permute-start | bytes 135176 | tf_op jit(solution)/shard_map/ppermute | solution.py:191
  179.6 4.2 %collective-permute-start.15 = (f32[1,3328]{1,0:T(1,128)S(1)}, f32[1,3328]{1,0:T(1,128)S(1)}, u32[]{:S(2)}, u32[]{:S(2)}) collective-permute-start(f32[1,3328]{1,0:T(1,128)S(1)} %add.182), channel_id=1, source_target_pairs={{0,4},{2,6},{4,0},{6,2},{8,12},{10,14},{12,8},{14,10},{16,20},{18,... | collective-permute-start | bytes 39944 | tf_op jit(solution)/shard_map/ppermute | solution.py:206
  183.7 3.9 %collective-permute-start.16 = (f32[1,3328]{1,0:T(1,128)S(1)}, f32[1,3328]{1,0:T(1,128)S(1)}, u32[]{:S(2)}, u32[]{:S(2)}) collective-permute-start(f32[1,3328]{1,0:T(1,128)S(1)} %add.183), channel_id=1, source_target_pairs={{0,8},{2,10},{4,12},{6,14},{8,0},{10,2},{12,4},{14,6},{16,24},{18,... | collective-permute-start | bytes 39944 | tf_op jit(solution)/shard_map/ppermute | solution.py:206
  185.3 4.7 %collective-permute-start.11 = (f32[4,5632]{1,0:T(4,128)S(1)}, f32[4,5632]{1,0:T(4,128)S(1)}, u32[]{:S(2)}, u32[]{:S(2)}) collective-permute-start(f32[4,5632]{1,0:T(4,128)S(1)} %maximum_select_fusion.11), channel_id=1, source_target_pairs={{0,8},{2,10},{4,12},{6,14},{8,0},{10,2},{12,4},{14,6},{16,24},{18,... | collective-permute-start | bytes 270344 | tf_op jit(solution)/shard_map/ppermute | solution.py:191
  187.7 6.1 %collective-permute-start.17 = (f32[1,3328]{1,0:T(1,128)S(1)}, f32[1,3328]{1,0:T(1,128)S(1)}, u32[]{:S(2)}, u32[]{:S(2)}) collective-permute-start(f32[1,3328]{1,0:T(1,128)S(1)} %add.184), channel_id=1, source_target_pairs={{0,16},{2,18},{4,20},{6,22},{8,24},{10,26},{12,28},{14,30},{16,0},... | collective-permute-start | bytes 39944 | tf_op jit(solution)/shard_map/ppermute | solution.py:206
  190.1 10.1 %collective-permute-start.12 = (f32[8,5632]{1,0:T(8,128)S(1)}, f32[8,5632]{1,0:T(8,128)S(1)}, u32[]{:S(2)}, u32[]{:S(2)}) collective-permute-start(f32[8,5632]{1,0:T(8,128)S(1)} %maximum_select_fusion.9), channel_id=1, source_target_pairs={{0,16},{2,18},{4,20},{6,22},{8,24},{10,26},{12,28},{14,30},{16,0},... | collective-permute-start | bytes 540680 | tf_op jit(solution)/shard_map/ppermute | solution.py:191
  (49 other events, 154.1 us)
Sparse Core Ops, SparseCore 0:
  107.3 112.9 reduce-scatter.1

commit v12 on v10

--- a/solution.py
+++ b/solution.py
@@ -270,7 +270,10 @@
     residues = x_rows.astype(jnp.float32)
     norm_in, inv_in = layer_norm(residues)
     normed_a = (norm_in * (1.0 + scale_a) + shift_a).astype(jnp.bfloat16)
-    projected = jnp.dot(normed_a, qkv_w, preferred_element_type=jnp.float32).astype(jnp.bfloat16)
+    projected = jnp.concatenate(
+        [jnp.dot(normed_a, qkv_weight[:, t, :], preferred_element_type=jnp.float32) for t in range(3)],
+        axis=1,
+    ).astype(jnp.bfloat16)
     queries = head_split(projected[:, :proj])
     keys = head_split(projected[:, proj : 2 * proj])
     values = head_split(projected[:, 2 * proj :])
@@ -367,8 +370,12 @@
     packed = lax.dynamic_update_slice(packed, qkv_grad.astype(jnp.bfloat16), (0, 0))
     reduced = lax.psum_scatter(packed, "dp", scatter_dimension=0, tiled=True).astype(jnp.float32)
 
-    attn_in_part = lax.dot_general(
-        d_qkv, qkv_w, (((1,), (1,)), ((), ())), preferred_element_type=jnp.float32
+    attn_in_part = sum(
+        lax.dot_general(
+            d_qkv[:, t * proj : (t + 1) * proj], qkv_weight[:, t, :], (((1,), (1,)), ((), ())),
+            preferred_element_type=jnp.float32,
+        )
+        for t in range(3)
     ).astype(jnp.bfloat16)
     d_normed_a = attn_in_part.astype(jnp.float32) + swap_heads(attn_in_part).astype(jnp.float32)
     input_grad = own_rows(

time: 213 us -> 218 us (1.023)
  matrix products: 42 us -> 45.1 us
  other arithmetic: 14.4 us -> 16.7 us
    dot_general x2 -> x6, matrix products: 5.82 us -> 9.26 us  [the longest x3 6.03 us: shards(): jnp.dot(normed_a, qkv_weight[:, t, :], preferred_element_type=jnp.float32)]
    unnamed x119 -> x118, local copies, waits for them, and re-layouts: 18.3 us -> 15.4 us
  transfers between devices with their start and end apart: 19 -> 19, of which waited for: 9 -> 10; matrix products, arithmetic and copies ran while one was open for 33% -> 34% of each run, Pallas kernels for 23% -> 23%
where the time goes in v12:
time: 218 us; the launch traced here: 216 us
  Pallas kernels  49.2 us (23%)
  matrix products  45.1 us (21%)
  waiting for transfers between devices  37 us (17%)
  local copies, waits for them, and re-layouts  33 us (15%)
  starting transfers between devices  19.9 us (9%)
  other arithmetic  16.7 us (8%)
  between operations  15.4 us (7%)
    pallas_call x1, Pallas kernels, pair_backward(): pl.pallas_call(pair_backward_kernel, grid=(m // tile,), in_specs=[pl.Bloc...  34 us
    unnamed x118, local copies, waits for them, and re-layouts  15.4 us
    pallas_call x1, Pallas kernels, pair_forward(): pl.pallas_call(pair_forward_kernel, grid=(m // tile,), in_specs=[pl.Block...  15.2 us
    reduce_scatter x1, waiting for transfers between devices, shards(): lax.psum_scatter(packed, 'dp', scatter_dimension=0, tiled=True)  14.5 us
    ppermute x10, waiting for transfers between devices, swap_heads(): return lax.ppermute(values, 'head', [(0, 1), (1, 0)])  11.2 us
    ppermute x10, starting transfers between devices, swap_heads(): return lax.ppermute(values, 'head', [(0, 1), (1, 0)])  10 us
    dot_general x3, matrix products, shards(): jnp.dot(normed_a, qkv_weight[:, t, :], preferred_element_type=jnp.float32)  6.03 us
    ppermute x4, waiting for transfers between devices, dp_gather(): other = lax.ppermute(block, 'dp', [(i, i ^ step) for i in range(count)])  5.85 us
  transfers between devices with their start and end apart: 19, of which 10 were waited for; matrix products, arithmetic and copies ran while one was open for 34% of the time, Pallas kernels for 23%

profile of v12, /device:TPU:0, one launch (start us, length us, event | category | flops | bytes accessed | tf_op | source)
XLA Modules:
  0.0 216.4 jit_solution(15493179229706352253)
XLA Ops:
  7.2 3.0 %collective-permute-start = (bf16[128,768]{1,0:T(8,128)(2,1)}, bf16[128,768]{1,0:T(8,128)(2,1)S(1)}, u32[]{:S(2)}, u32[]{:S(2)}) collective-permute-start(bf16[128,768]{1,0:T(8,128)(2,1)} %bitcast.106), channel_id=1, source_target_pairs={{0,1},{1,0},{2,3},{3,2},{4,5},{5,4},{6,7},{7,6},{8,9},{9,8},{10,11... | collective-permute-start | bytes 589832 | tf_op jit(solution)/shard_map/ppermute | solution.py:147
  11.7 15.2 %shard_map.246 = bf16[12,32768]{1,0:T(8,128)(2,1)} custom-call(bf16[32768,256]{1,0:T(8,128)(2,1)} %bitcast.99, f32[1,256]{1,0:T(1,128)} %bitcast.140, bf16[16,256]{1,0:T(8,128)(2,1)} %pad.8.wt_ref), custom_call_target="tpu_custom_call" | custom-call | flops 352321536 | bytes 17563648 | tf_op jit(solution)/shard_map/pallas_call | solution.py:50
  30.6 2.0 collective-permute-start.1
  33.8 2.1 convolution_reduce_fusion
  43.4 2.3 %convolution_convert_fusion.10 = bf16[256,384]{1,0:T(8,128)(2,1)} fusion(bf16[256,768]{1,0:T(8,128)(2,1)} %copy-done.26, bf16[768,3,384]{2,0,1:T(8,128)(2,1)} %param.22), kind=kOutput, calls=%fused_computation.47 | convolution fusion | flops 151093248 | bytes 1179648 | tf_op jit(solution)/shard_map/dot_general | solution.py:274
  46.7 2.3 %convolution_convert_fusion.11 = bf16[256,384]{1,0:T(8,128)(2,1)} fusion(bf16[256,768]{1,0:T(8,128)(2,1)} %copy-done.26, bf16[768,3,384]{2,0,1:T(8,128)(2,1)} %param.22), kind=kOutput, calls=%fused_computation.48 | convolution fusion | flops 151093248 | bytes 1179648 | tf_op jit(solution)/shard_map/dot_general | solution.py:274
  49.0 1.7 copy.66
  50.8 3.3 %fusion.94 = (f32[6,256]{1,0:T(8,128)S(1)}, f32[6,256,256]{1,2,0:T(8,128)}) fusion(pred[256]{0:T(512)(128)(4,1)S(1)} %copy-done.50, bf16[256,6,64]{0,2,1:T(8,128)(2,1)S(1)} %bitcast.123, bf16[256,6,64]{0,2,1:T(8,128)(2,1)S(1)} %bitcast.121, bf16[6,128,256]{1,2,0:T(8,128)(2,1)} %copy.88, bf16[6,128,256]{1,2,0:T(8,128)(2,1)} %collective-permute-done.1, ...), kind=kOutput, calls=%fused_computation.199 | convolution fusion | flops 56230144 | bytes 2758913 | tf_op jit(solution)/shard_map/sub | solution.py:284
  54.1 1.7 convolution_convert_fusion.8
  56.8 1.9 collective-permute-start.5
  58.7 3.6 %copy.92 = bf16[96,8,2,1536]{3,1,2,0:T(8,128)(2,1)S(1)} copy(bf16[96,8,2,1536]{3,2,1,0:T(2,128)(2,1)} %bitcast.101) | data formatting | bytes 9437184
  63.0 1.8 collective-permute-done.2
  64.8 2.4 %fusion.93 = (f32[256]{0:T(256)S(1)}, f32[256,768]{1,0:T(8,128)S(1)}, f32[256,768]{1,0:T(8,128)S(1)}) fusion(f32[768]{0:T(1024)S(1)} %get-tuple-element.112, bf16[128,768]{1,0:T(8,128)(2,1)S(1)} %bitcast.110, bf16[128,768]{1,0:T(8,128)(2,1)S(1)} %collective-permute-done, pred[]{:T(512)S(6)} %eq.44, f32[768]{0:T(1024)S(1)} %copy-done.48, ...), kind=kOutput, calls=%fused_computation.198 | convolution fusion | flops 311820032 | bytes 3546113 | tf_op jit(solution)/shard_map/dot_general | solution.py:295
  71.8 3.9 %fusion.1 = bf16[768,6144]{1,0:T(8,128)(2,1)} fusion(bf16[768,6144]{1,0:T(8,128)(2,1)} %shard_map.248, bf16[256,1536]{1,0:T(8,128)(2,1)S(1)} %get-tuple-element.81, bf16[256,1536]{1,0:T(8,128)(2,1)S(1)} %get-tuple-element.80, f32[256,768]{1,0:T(8,128)S(1)} %get-tuple-element.79, f32[768]{0:T(1024)S(1)} %copy-done.47, f32[768]{0:T(1024)S(1)} %get-tuple-element.68, ...), kind=kOutput, calls=%fused_computation.2 | convolution fusion | flops 1214447616 | bytes 7086080 | tf_op jit(solution)/shard_map/dot_general | solution.py:322
  75.7 2.3 %fusion.2 = bf16[768,6144]{1,0:T(8,128)(2,1)} fusion(bf16[768,6144]{1,0:T(8,128)(2,1)} %fusion.1, bf16[256,1536]{1,0:T(8,128)(2,1)S(1)} %get-tuple-element.82, f32[768]{0:T(1024)S(1)} %get-tuple-element.73, bf16[128,768]{1,0:T(8,128)(2,1)S(1)} %collective-permute-done.5, bf16[128,768]{1,0:T(8,128)(2,1)S(1)} %bitcast.129, pred[]{:T(512)S(6)} %eq.44), kind=kOutput, calls=%fused_computation.5 | convolution fusion | flops 607518720 | bytes 3542017 | tf_op jit(solution)/shard_map/dot_general | solution.py:313
  83.3 1.9 convolution_convert_fusion.6
  89.4 2.0 fusion.3
  92.2 2.7 %convolution_convert_fusion.5 = bf16[256,768]{1,0:T(8,128)(2,1)} fusion(bf16[256,1536]{1,0:T(8,128)(2,1)} %copy-done.51, bf16[1536,768]{1,0:T(8,128)(2,1)S(1)} %copy-done), kind=kOutput, calls=%fused_computation.25 | convolution fusion | flops 604176384 | bytes 3538944 | tf_op jit(solution)/shard_map/dot_general | solution.py:305
  96.2 2.0 copy.79
  101.3 1.7 fusion.40
  109.3 6.1 %collective-permute-done.8 = bf16[6,128,256]{1,2,0:T(8,128)(2,1)} collective-permute-done((bf16[6,128,256]{1,2,0:T(8,128)(2,1)}, bf16[6,128,256]{1,2,0:T(8,128)(2,1)}, u32[]{:S(2)}, u32[]{:S(2)}) %collective-permute-start.8) | collective-permute-done | bytes 393248 | tf_op jit(solution)/shard_map/ppermute | solution.py:147
  115.5 1.9 copy.80
  120.3 34.0 %shard_map.247 = (bf16[32768,256]{1,0:T(8,128)(2,1)}, f32[16,256]{1,0:T(8,128)}, f32[1,256]{1,0:T(1,128)}) custom-call(bf16[32768,256]{1,0:T(8,128)(2,1)} %bitcast.100, bf16[16,32768]{1,0:T(8,128)(2,1)} %pad.9.ds_ref, f32[1,256]{1,0:T(1,128)} %bitcast.141, bf16[16,256]{1,0:T(8,128)(2,1)} %pad.8.wt_ref), custom_call_target="tpu_custom_call" | custom-call | flops 704643072 | bytes 34603008 | tf_op jit(solution)/shard_map/pallas_call | solution.py:97
  156.5 1.7 fusion.30
  158.4 2.5 %convolution_multiply_fusion.2 = f32[1,256]{1,0:T(1,128)} fusion(bf16[256,4608]{1,0:T(8,128)(2,1)S(1)} %copy-done.6, f32[1,4608]{1,0:T(1,128)S(1)} %get-tuple-element.96, f32[1,256]{1,0:T(1,128)S(1)} %copy-done.41), kind=kOutput, calls=%fused_computation.50 | convolution fusion | flops 14157824 | bytes 2379776 | tf_op jit(solution)/shard_map/dot_general | solution.py:416
  162.1 1.9 collective-permute-start.10
  164.3 3.9 %collective-permute-done.15 = f32[1,3328]{1,0:T(1,128)S(1)} collective-permute-done((f32[1,3328]{1,0:T(1,128)S(1)}, f32[1,3328]{1,0:T(1,128)S(1)}, u32[]{:S(2)}, u32[]{:S(2)}) %collective-permute-start.15) | collective-permute-done | bytes 13344 | tf_op jit(solution)/shard_map/ppermute | solution.py:180
  172.2 2.2 %collective-permute-start.17 = (f32[1,3328]{1,0:T(1,128)S(1)}, f32[1,3328]{1,0:T(1,128)S(1)}, u32[]{:S(2)}, u32[]{:S(2)}) collective-permute-start(f32[1,3328]{1,0:T(1,128)S(1)} %add.192), channel_id=1, source_target_pairs={{0,16},{2,18},{4,20},{6,22},{8,24},{10,26},{12,28},{14,30},{16,0},... | collective-permute-start | bytes 39944 | tf_op jit(solution)/shard_map/ppermute | solution.py:180
  174.7 2.7 %collective-permute-start.12 = (f32[8,5632]{1,0:T(8,128)S(1)}, f32[8,5632]{1,0:T(8,128)S(1)}, u32[]{:S(2)}, u32[]{:S(2)}) collective-permute-start(f32[8,5632]{1,0:T(8,128)S(1)} %maximum_select_fusion.9), channel_id=1, source_target_pairs={{0,16},{2,18},{4,20},{6,22},{8,24},{10,26},{12,28},{14,30},{16,0},... | collective-permute-start | bytes 540680 | tf_op jit(solution)/shard_map/ppermute | solution.py:165
  179.7 5.1 %collective-permute-done.12 = f32[8,5632]{1,0:T(8,128)S(1)} collective-permute-done((f32[8,5632]{1,0:T(8,128)S(1)}, f32[8,5632]{1,0:T(8,128)S(1)}, u32[]{:S(2)}, u32[]{:S(2)}) %collective-permute-start.12) | collective-permute-done | bytes 180256 | tf_op jit(solution)/shard_map/ppermute | solution.py:165
  186.1 4.2 %fusion.66 = f32[256,4608]{1,0:T(8,128)} fusion(bf16[16,256]{1,0:T(8,128)(2,1)S(1)} %multiply_convert_fusion.7, f32[16,5632]{1,0:T(8,128)S(1)} %maximum_select_fusion.8), kind=kOutput, calls=%fused_computation.126 | convolution fusion | flops 226492416 | bytes 5021696 | tf_op jit(solution)/shard_map/dot_general | solution.py:414
  190.3 14.5 %reduce-scatter.2.cloned.1.call-done = bf16[48,6144]{1,0:T(8,128)(2,1)} async-done(((bf16[768,6144]{1,0:T(8,128)(2,1)}), bf16[48,6144]{1,0:T(8,128)(2,1)}) %reduce-scatter.2.cloned.1.call-update) | async-done | bytes 589840 | tf_op jit(solution)/shard_map/reduce_scatter | solution.py:371
  (222 shorter events, 60.2 us)
Async XLA Ops:
  7.2 61.8 %copy-start = (bf16[1536,768]{1,0:T(8,128)(2,1)S(1)}, bf16[1536,768]{1,0:T(8,128)(2,1)}, u32[]{:S(2)}) copy-start(bf16[1536,768]{1,0:T(8,128)(2,1)} %param.28) | copy-start | bytes 7077892
  7.2 197.7 %reduce-scatter.2.cloned.1.call-start = ((), (), s32[]{:S(2)}) async-start(), calls=%async_computation.1 | async-start | bytes 10027008 | tf_op jit(solution)/shard_map/reduce_scatter | solution.py:371
  7.2 32.8 %collective-permute-start = (bf16[128,768]{1,0:T(8,128)(2,1)}, bf16[128,768]{1,0:T(8,128)(2,1)S(1)}, u32[]{:S(2)}, u32[]{:S(2)}) collective-permute-start(bf16[128,768]{1,0:T(8,128)(2,1)} %bitcast.106), channel_id=1, source_target_pairs={{0,1},{1,0},{2,3},{3,2},{4,5},{5,4},{6,7},{7,6},{8,9},{9,8},{10,11... | collective-permute-start | bytes 589832 | tf_op jit(solution)/shard_map/ppermute | solution.py:147
  10.3 52.7 %collective-permute-start.3 = (bf16[384,768]{1,0:T(8,128)(2,1)}, bf16[384,768]{1,0:T(8,128)(2,1)}, u32[]{:S(2)}, u32[]{:S(2)}) collective-permute-start(bf16[384,768]{1,0:T(8,128)(2,1)} %param.25), channel_id=1, source_target_pairs={{0,1},{1,0},{2,3},{3,2},{4,5},{5,4},{6,7},{7,6},{8,9},{9,8},{10,11... | collective-permute-start | bytes 1769480 | tf_op jit(solution)/shard_map/ppermute | solution.py:147
  29.3 8.6 %copy-start.10 = (bf16[6,128,256]{2,1,0:T(8,128)(2,1)S(1)}, bf16[6,128,256]{2,1,0:T(8,128)(2,1)}, u32[]{:S(2)}) copy-start(bf16[6,128,256]{2,1,0:T(8,128)(2,1)} %get-tuple-element.90) | copy-start | bytes 1179652
  30.6 20.2 %collective-permute-start.1 = (bf16[6,128,256]{1,2,0:T(8,128)(2,1)S(1)}, bf16[6,128,256]{1,2,0:T(8,128)(2,1)}, u32[]{:S(2)}, u32[]{:S(2)}) collective-permute-start(bf16[6,128,256]{1,2,0:T(8,128)(2,1)S(1)} %copy.89), channel_id=1, source_target_pairs={{0,1},{1,0},{2,3},{3,2},{4,5},{5,4},{6,7},{7,6},{8,9},{9,8},{10,11... | collective-permute-start | bytes 1179656 | tf_op jit(solution)/shard_map/ppermute | solution.py:147
  33.8 6.2 %copy-start.8 = (bf16[1,128,768]{2,1,0:T(8,128)(2,1)S(1)}, bf16[1,128,768]{2,1,0:T(8,128)(2,1)}, u32[]{:S(2)}) copy-start(bf16[1,128,768]{2,1,0:T(8,128)(2,1)} %param.15) | copy-start | bytes 589828
  43.3 7.5 %copy-start.15 = (bf16[256,384]{0,1:T(8,128)(2,1)}, bf16[256,384]{0,1:T(8,128)(2,1)S(1)}, u32[]{:S(2)}) copy-start(bf16[256,384]{0,1:T(8,128)(2,1)S(1)} %copy.68) | copy-start | bytes 589828
  43.3 7.4 %copy-start.50 = (pred[256]{0:T(512)(128)(4,1)S(1)}, pred[256]{0:T(512)(128)(4,1)}, u32[]{:S(2)}) copy-start(pred[256]{0:T(512)(128)(4,1)} %or_and_fusion) | copy-start | bytes 772
  46.7 7.4 %copy-start.17 = (bf16[256,384]{0,1:T(8,128)(2,1)}, bf16[256,384]{0,1:T(8,128)(2,1)S(1)}, u32[]{:S(2)}) copy-start(bf16[256,384]{0,1:T(8,128)(2,1)S(1)} %copy.67) | copy-start | bytes 589828
  56.7 8.1 %collective-permute-start.2 = (bf16[256,384]{1,0:T(8,128)(2,1)}, bf16[256,384]{1,0:T(8,128)(2,1)}, u32[]{:S(2)}, u32[]{:S(2)}) collective-permute-start(bf16[256,384]{1,0:T(8,128)(2,1)} %copy.73), channel_id=1, source_target_pairs={{0,1},{1,0},{2,3},{3,2},{4,5},{5,4},{6,7},{7,6},{8,9},{9,8},{10,11... | collective-permute-start | bytes 589832 | tf_op jit(solution)/shard_map/ppermute | solution.py:147
  56.8 12.2 %collective-permute-start.5 = (bf16[128,768]{1,0:T(8,128)(2,1)S(1)}, bf16[128,768]{1,0:T(8,128)(2,1)S(1)}, u32[]{:S(2)}, u32[]{:S(2)}) collective-permute-start(bf16[128,768]{1,0:T(8,128)(2,1)S(1)} %bitcast.127), channel_id=1, source_target_pairs={{0,1},{1,0},{2,3},{3,2},{4,5},{5,4},{6,7},{7,6},{8,9},{9,8},{10,11... | collective-permute-start | bytes 589832 | tf_op jit(solution)/shard_map/ppermute | solution.py:147
  58.7 6.1 %copy-start.25 = (bf16[384,768]{1,0:T(8,128)(2,1)S(1)}, bf16[384,768]{1,0:T(8,128)(2,1)}, u32[]{:S(2)}) copy-start(bf16[384,768]{1,0:T(8,128)(2,1)} %param.25) | copy-start | bytes 1769476
  58.7 6.1 %copy-start.48 = (f32[768]{0:T(1024)S(1)}, f32[768]{0:T(1024)}, u32[]{:S(2)}) copy-start(f32[768]{0:T(1024)} %param.26) | copy-start | bytes 9220
  67.2 13.5 %copy-start.1 = (f32[256,768]{1,0:T(8,128)}, f32[256,768]{1,0:T(8,128)S(1)}, u32[]{:S(2)}) copy-start(f32[256,768]{1,0:T(8,128)S(1)} %get-tuple-element.79) | copy-start | bytes 2359300
  68.9 11.7 %copy-start.23 = (bf16[128,768]{1,0:T(8,128)(2,1)}, bf16[128,768]{1,0:T(8,128)(2,1)S(1)}, u32[]{:S(2)}) copy-start(bf16[128,768]{1,0:T(8,128)(2,1)S(1)} %collective-permute-done.5) | copy-start | bytes 589828
  71.7 7.8 %collective-permute-start.6 = (bf16[256,768]{1,0:T(8,128)(2,1)S(1)}, bf16[256,768]{1,0:T(8,128)(2,1)S(1)}, u32[]{:S(2)}, u32[]{:S(2)}) collective-permute-start(bf16[256,768]{1,0:T(8,128)(2,1)S(1)} %convolution_convert_fusion.4), channel_id=1, source_target_pairs={{0,1},{1,0},{2,3},{3,2},{4,5},{5,4},{6,7},{7,6},{8,9},{9,8},{10,11... | collective-permute-start | bytes 1179656 | tf_op jit(solution)/shard_map/ppermute | solution.py:147
  94.9 12.3 %collective-permute-start.4 = (bf16[256,768]{1,0:T(8,128)(2,1)}, bf16[256,768]{1,0:T(8,128)(2,1)}, u32[]{:S(2)}, u32[]{:S(2)}) collective-permute-start(bf16[256,768]{1,0:T(8,128)(2,1)} %convolution_convert_fusion.5), channel_id=1, source_target_pairs={{0,1},{1,0},{2,3},{3,2},{4,5},{5,4},{6,7},{7,6},{8,9},{9,8},{10,11... | collective-permute-start | bytes 1179656 | tf_op jit(solution)/shard_map/ppermute | solution.py:147
  96.2 6.7 %copy-start.13 = (bf16[6,64,256]{2,1,0:T(8,128)(2,1)S(1)}, bf16[6,64,256]{2,1,0:T(8,128)(2,1)}, u32[]{:S(2)}) copy-start(bf16[6,64,256]{2,1,0:T(8,128)(2,1)} %copy-done.12) | copy-start | bytes 589828
  99.6 15.8 %collective-permute-start.8 = (bf16[6,128,256]{1,2,0:T(8,128)(2,1)}, bf16[6,128,256]{1,2,0:T(8,128)(2,1)}, u32[]{:S(2)}, u32[]{:S(2)}) collective-permute-start(bf16[6,128,256]{1,2,0:T(8,128)(2,1)} %get-tuple-element.89), channel_id=1, source_target_pairs={{0,1},{1,0},{2,3},{3,2},{4,5},{5,4},{6,7},{7,6},{8,9},{9,8},{10,11... | collective-permute-start | bytes 1179656 | tf_op jit(solution)/shard_map/ppermute | solution.py:147
  105.1 51.4 %collective-permute-start.7 = (bf16[256,768]{1,0:T(8,128)(2,1)}, bf16[256,768]{1,0:T(8,128)(2,1)}, u32[]{:S(2)}, u32[]{:S(2)}) collective-permute-start(bf16[256,768]{1,0:T(8,128)(2,1)} %fusion.8), channel_id=1, source_target_pairs={{0,1},{1,0},{2,3},{3,2},{4,5},{5,4},{6,7},{7,6},{8,9},{9,8},{10,11... | collective-permute-start | bytes 1179656 | tf_op jit(solution)/shard_map/ppermute | solution.py:147
  120.3 36.2 %copy-start.32 = (f32[256]{0:T(256)S(1)}, f32[256]{0:T(256)}, u32[]{:S(2)}) copy-start(f32[256]{0:T(256)} %copy-done.31) | copy-start | bytes 3076
  156.2 4.7 %collective-permute-start.13 = (f32[1,3328]{1,0:T(1,128)S(1)}, f32[1,3328]{1,0:T(1,128)S(1)}, u32[]{:S(2)}, u32[]{:S(2)}) collective-permute-start(f32[1,3328]{1,0:T(1,128)S(1)} %broadcast_in_dim.61), channel_id=1, source_target_pairs={{0,1},{1,0},{2,3},{3,2},{4,5},{5,4},{6,7},{7,6},{8,9},{9,8},{10,11... | collective-permute-start | bytes 39944 | tf_op jit(solution)/shard_map/ppermute | solution.py:147
  158.3 19.0 %copy-start.5 = (f32[256,768]{1,0:T(8,128)S(1)}, f32[256,768]{1,0:T(8,128)}, u32[]{:S(2)}) copy-start(f32[256,768]{1,0:T(8,128)} %copy-done.3) | copy-start | bytes 2359300
  160.9 1.2 collective-permute-start.9
  160.9 3.1 %collective-permute-start.14 = (f32[1,3328]{1,0:T(1,128)S(1)}, f32[1,3328]{1,0:T(1,128)S(1)}, u32[]{:S(2)}, u32[]{:S(2)}) collective-permute-start(f32[1,3328]{1,0:T(1,128)S(1)} %reshape_add_fusion), channel_id=1, source_target_pairs={{0,2},{2,0},{4,6},{6,4},{8,10},{10,8},{12,14},{14,12},{16,18},{18,... | collective-permute-start | bytes 39944 | tf_op jit(solution)/shard_map/ppermute | solution.py:180
  162.1 7.7 %collective-permute-start.10 = (f32[2,5632]{1,0:T(2,128)S(1)}, f32[2,5632]{1,0:T(2,128)S(1)}, u32[]{:S(2)}, u32[]{:S(2)}) collective-permute-start(f32[2,5632]{1,0:T(2,128)S(1)} %maximum_select_fusion.12), channel_id=1, source_target_pairs={{0,4},{2,6},{4,0},{6,2},{8,12},{10,14},{12,8},{14,10},{16,20},{18,... | collective-permute-start | bytes 135176 | tf_op jit(solution)/shard_map/ppermute | solution.py:165
  164.1 4.2 %collective-permute-start.15 = (f32[1,3328]{1,0:T(1,128)S(1)}, f32[1,3328]{1,0:T(1,128)S(1)}, u32[]{:S(2)}, u32[]{:S(2)}) collective-permute-start(f32[1,3328]{1,0:T(1,128)S(1)} %add.190), channel_id=1, source_target_pairs={{0,4},{2,6},{4,0},{6,2},{8,12},{10,14},{12,8},{14,10},{16,20},{18,... | collective-permute-start | bytes 39944 | tf_op jit(solution)/shard_map/ppermute | solution.py:180
  168.3 3.9 %collective-permute-start.16 = (f32[1,3328]{1,0:T(1,128)S(1)}, f32[1,3328]{1,0:T(1,128)S(1)}, u32[]{:S(2)}, u32[]{:S(2)}) collective-permute-start(f32[1,3328]{1,0:T(1,128)S(1)} %add.191), channel_id=1, source_target_pairs={{0,8},{2,10},{4,12},{6,14},{8,0},{10,2},{12,4},{14,6},{16,24},{18,... | collective-permute-start | bytes 39944 | tf_op jit(solution)/shard_map/ppermute | solution.py:180
  169.9 4.7 %collective-permute-start.11 = (f32[4,5632]{1,0:T(4,128)S(1)}, f32[4,5632]{1,0:T(4,128)S(1)}, u32[]{:S(2)}, u32[]{:S(2)}) collective-permute-start(f32[4,5632]{1,0:T(4,128)S(1)} %maximum_select_fusion.11), channel_id=1, source_target_pairs={{0,8},{2,10},{4,12},{6,14},{8,0},{10,2},{12,4},{14,6},{16,24},{18,... | collective-permute-start | bytes 270344 | tf_op jit(solution)/shard_map/ppermute | solution.py:165
  172.2 6.1 %collective-permute-start.17 = (f32[1,3328]{1,0:T(1,128)S(1)}, f32[1,3328]{1,0:T(1,128)S(1)}, u32[]{:S(2)}, u32[]{:S(2)}) collective-permute-start(f32[1,3328]{1,0:T(1,128)S(1)} %add.192), channel_id=1, source_target_pairs={{0,16},{2,18},{4,20},{6,22},{8,24},{10,26},{12,28},{14,30},{16,0},... | collective-permute-start | bytes 39944 | tf_op jit(solution)/shard_map/ppermute | solution.py:180
  174.7 10.2 %collective-permute-start.12 = (f32[8,5632]{1,0:T(8,128)S(1)}, f32[8,5632]{1,0:T(8,128)S(1)}, u32[]{:S(2)}, u32[]{:S(2)}) collective-permute-start(f32[8,5632]{1,0:T(8,128)S(1)} %maximum_select_fusion.9), channel_id=1, source_target_pairs={{0,16},{2,18},{4,20},{6,22},{8,24},{10,26},{12,28},{14,30},{16,0},... | collective-permute-start | bytes 540680 | tf_op jit(solution)/shard_map/ppermute | solution.py:165
  (39 other events, 104.2 us)
Sparse Core Ops, SparseCore 0:
  91.6 113.2 reduce-scatter.1

commit v13 on v10

--- a/solution.py
+++ b/solution.py
@@ -39,9 +39,9 @@
     normed, _ = pair_stats(x_ref[...].astype(jnp.float32))
     scaled = (normed * gain_ref[...]).astype(jnp.bfloat16)
     bias = lax.dot_general(
-        wt_ref[...], scaled, (((1,), (1,)), ((), ())), preferred_element_type=jnp.float32
-    )
-    bias_ref[...] = bias[: bias_ref.shape[0]].astype(bias_ref.dtype)
+        wt_ref[...], scaled, (((0,), (1,)), ((), ())), preferred_element_type=jnp.float32
+    )
+    bias_ref[...] = bias.astype(bias_ref.dtype)
 
 
 def pair_forward(flat, gain, wt, heads):
@@ -262,7 +262,7 @@
     pair_flat = pair_input.reshape(-1, pair_width)
     pair_wt = jnp.pad(pair_weight.T, ((0, HEAD_PAD - heads_all), (0, 0)))
     pair_gain_row = pair_gain.reshape(1, pair_width)
-    bias_flat = pair_forward(pair_flat, pair_gain_row, pair_wt, heads_all)
+    bias_flat = pair_forward(pair_flat, pair_gain_row, pair_weight, heads_all)
     bias_rows = bias_flat.reshape(heads_all, rows, length)
     heads_own = proj // DH
     biases = trade_blocks(bias_rows, head, heads_own, 0, 1)

time: 213 us -> 214 us (level)
    unnamed x119 -> x124, local copies, waits for them, and re-layouts: 18.3 us -> 19.7 us
where the time goes in v13:
time: 214 us; the launch traced here: 213 us
  Pallas kernels  49.4 us (23%)
  matrix products  42 us (20%)
  waiting for transfers between devices  36.7 us (17%)
  local copies, waits for them, and re-layouts  34.1 us (16%)
  starting transfers between devices  20.5 us (10%)
  between operations  15.5 us (7%)
  other arithmetic  14.4 us (7%)
    pallas_call x1, Pallas kernels, pair_backward(): pl.pallas_call(pair_backward_kernel, grid=(m // tile,), in_specs=[pl.Bloc...  34 us
    unnamed x124, local copies, waits for them, and re-layouts  19.7 us
    pallas_call x1, Pallas kernels, pair_forward(): pl.pallas_call(pair_forward_kernel, grid=(m // tile,), in_specs=[pl.Block...  15.4 us
    reduce_scatter x1, waiting for transfers between devices, shards(): lax.psum_scatter(packed, 'dp', scatter_dimension=0, tiled=True)  13.1 us
    ppermute x10, waiting for transfers between devices, swap_heads(): return lax.ppermute(values, 'head', [(0, 1), (1, 0)])  11.4 us
    ppermute x10, starting transfers between devices, swap_heads(): return lax.ppermute(values, 'head', [(0, 1), (1, 0)])  10.3 us
    ppermute x4, waiting for transfers between devices, dp_gather(): other = lax.ppermute(block, 'dp', [(i, i ^ step) for i in range(count)])  7.09 us
    ppermute x4, starting transfers between devices, dp_sum(): other = lax.ppermute(values, 'dp', [(i, i ^ step) for i in range(count)])  5.32 us
  transfers between devices with their start and end apart: 19, of which 9 were waited for; matrix products, arithmetic and copies ran while one was open for 33% of the time, Pallas kernels for 23%

profile of v13, /device:TPU:0, one launch (start us, length us, event | category | flops | bytes accessed | tf_op | source)
XLA Modules:
  0.0 212.7 jit_solution(17228534488500075292)
XLA Ops:
  7.2 3.0 %collective-permute-start = (bf16[128,768]{1,0:T(8,128)(2,1)}, bf16[128,768]{1,0:T(8,128)(2,1)S(1)}, u32[]{:S(2)}, u32[]{:S(2)}) collective-permute-start(bf16[128,768]{1,0:T(8,128)(2,1)} %bitcast.91), channel_id=1, source_target_pairs={{0,1},{1,0},{2,3},{3,2},{4,5},{5,4},{6,7},{7,6},{8,9},{9,8},{10,11... | collective-permute-start | bytes 589832 | tf_op jit(solution)/shard_map/ppermute | solution.py:147
  11.8 15.4 %shard_map.246 = bf16[12,32768]{1,0:T(8,128)(2,1)} custom-call(bf16[32768,256]{1,0:T(8,128)(2,1)} %bitcast.80, f32[1,256]{1,0:T(1,128)} %bitcast.122, bf16[256,12]{1,0:T(8,128)(2,1)} %copy.73.wt_ref), custom_call_target="tpu_custom_call" | custom-call | flops 352321536 | bytes 17563648 | tf_op jit(solution)/shard_map/pallas_call | solution.py:50
  29.7 2.0 copy.94
  31.6 1.9 collective-permute-start.1
  34.3 2.1 convolution_reduce_fusion
  38.5 3.9 %copy.69 = bf16[768,3,384]{0,2,1:T(8,128)(2,1)} copy(bf16[768,3,384]{2,0,1:T(8,128)(2,1)} %param.22) | data formatting | bytes 3538944 | tf_op args[7]
  43.4 2.3 %convolution_convert_fusion.3 = bf16[256,1152]{1,0:T(8,128)(2,1)S(1)} fusion(bf16[768,1152]{0,1:T(8,128)(2,1)} %bitcast.89, f32[768]{0:T(1024)S(1)} %get-tuple-element.70, f32[768]{0:T(1024)S(1)} %get-tuple-element.71, f32[256]{0:T(256)S(1)} %add_rsqrt_fusion.1, f32[256]{0:T(256)S(1)} %broadcast_multiply_fusion.5, bf16[128,768]{1,0:T(8,128)(2,1)S(1)} %bitcast.94, ...), kind=kOutput, calls=%fused_computation.7 | convolution fusion | flops 456228864 | bytes 2760705 | tf_op jit(solution)/shard_map/dot_general | solution.py:273
  46.2 3.3 %fusion.79 = (f32[6,256]{1,0:T(8,128)S(1)}, f32[6,256,256]{1,2,0:T(8,128)}) fusion(pred[256]{0:T(512)(128)(4,1)} %or_and_fusion, bf16[256,6,64]{0,2,1:T(8,128)(2,1)S(1)} %bitcast.103, bf16[256,6,64]{0,2,1:T(8,128)(2,1)S(1)} %bitcast.101, bf16[6,128,256]{1,2,0:T(8,128)(2,1)} %copy.93, bf16[6,128,256]{1,2,0:T(8,128)(2,1)} %collective-permute-done.1, pred[]{:T(512)S(6)} %eq.44), kind=kOutput, calls=%fused_computation.180 | convolution fusion | flops 56230144 | bytes 2758913 | tf_op jit(solution)/shard_map/sub | solution.py:281
  52.2 1.9 collective-permute-start.5
  54.2 3.6 %copy.97 = bf16[96,8,2,1536]{3,1,2,0:T(8,128)(2,1)S(1)} copy(bf16[96,8,2,1536]{3,2,1,0:T(2,128)(2,1)} %bitcast.82) | data formatting | bytes 9437184
  58.4 1.8 collective-permute-done.2
  60.2 2.4 %fusion.77 = (f32[256]{0:T(256)S(1)}, f32[256,768]{1,0:T(8,128)S(1)}, f32[256,768]{1,0:T(8,128)S(1)}) fusion(f32[768]{0:T(1024)S(1)} %get-tuple-element.115, bf16[128,768]{1,0:T(8,128)(2,1)S(1)} %bitcast.95, bf16[128,768]{1,0:T(8,128)(2,1)S(1)} %collective-permute-done, pred[]{:T(512)S(6)} %eq.44, f32[768]{0:T(1024)S(1)} %copy-done.50, ...), kind=kOutput, calls=%fused_computation.178 | convolution fusion | flops 311820032 | bytes 3546113 | tf_op jit(solution)/shard_map/dot_general | solution.py:292
  67.2 3.9 %fusion.1 = bf16[768,6144]{1,0:T(8,128)(2,1)} fusion(bf16[768,6144]{1,0:T(8,128)(2,1)} %shard_map.248, bf16[256,1536]{1,0:T(8,128)(2,1)S(1)} %get-tuple-element.81, bf16[256,1536]{1,0:T(8,128)(2,1)S(1)} %get-tuple-element.80, f32[256,768]{1,0:T(8,128)S(1)} %get-tuple-element.79, f32[768]{0:T(1024)S(1)} %copy-done.49, f32[768]{0:T(1024)S(1)} %get-tuple-element.68, ...), kind=kOutput, calls=%fused_computation.2 | convolution fusion | flops 1214447616 | bytes 7086080 | tf_op jit(solution)/shard_map/dot_general | solution.py:319
  71.1 2.3 %fusion.2 = bf16[768,6144]{1,0:T(8,128)(2,1)} fusion(bf16[768,6144]{1,0:T(8,128)(2,1)} %fusion.1, bf16[256,1536]{1,0:T(8,128)(2,1)S(1)} %get-tuple-element.82, f32[768]{0:T(1024)S(1)} %get-tuple-element.73, bf16[128,768]{1,0:T(8,128)(2,1)S(1)} %collective-permute-done.5, bf16[128,768]{1,0:T(8,128)(2,1)S(1)} %bitcast.109, pred[]{:T(512)S(6)} %eq.44), kind=kOutput, calls=%fused_computation.5 | convolution fusion | flops 607518720 | bytes 3542017 | tf_op jit(solution)/shard_map/dot_general | solution.py:310
  78.6 2.1 convolution_convert_fusion.8
  84.9 2.2 %fusion.3 = bf16[768,6144]{1,0:T(8,128)(2,1)} fusion(bf16[768,6144]{1,0:T(8,128)(2,1)} %fusion.7, bf16[256,384]{0,1:T(8,128)(2,1)S(1)} %bitcast.127, bf16[256,384]{0,1:T(8,128)(2,1)S(1)} %bitcast.113, bf16[256,384]{0,1:T(8,128)(2,1)S(1)} %bitcast.115, f32[768]{0:T(1024)S(1)} %copy-done.48, f32[768]{0:T(1024)S(1)} %get-tuple-element.71, ...), kind=kOutput, calls=%fused_computation.6 | convolution fusion | flops 458588160 | bytes 2760705 | tf_op jit(solution)/shard_map/dot_general | solution.py:357
  88.5 2.7 %convolution_convert_fusion.7 = bf16[256,768]{1,0:T(8,128)(2,1)} fusion(bf16[256,1536]{1,0:T(8,128)(2,1)} %copy-done.53, bf16[1536,768]{1,0:T(8,128)(2,1)S(1)} %copy-done), kind=kOutput, calls=%fused_computation.24 | convolution fusion | flops 604176384 | bytes 3538944 | tf_op jit(solution)/shard_map/dot_general | solution.py:302
  92.5 1.9 copy.84
  97.5 3.5 %convolution_convert_fusion.5 = bf16[256,768]{1,0:T(8,128)(2,1)} fusion(bf16[768,1152]{0,1:T(8,128)(2,1)} %bitcast.90, bf16[256,384]{0,1:T(8,128)(2,1)} %bitcast.128, bf16[256,384]{0,1:T(8,128)(2,1)} %bitcast.114, bf16[256,384]{0,1:T(8,128)(2,1)} %bitcast.116), kind=kOutput, calls=%fused_computation.22 | convolution fusion | flops 454950912 | bytes 2752512 | tf_op jit(solution)/shard_map/dot_general | solution.py:370
  101.4 2.0 collective-permute-done.4
  105.6 6.0 %collective-permute-done.8 = bf16[6,128,256]{1,2,0:T(8,128)(2,1)} collective-permute-done((bf16[6,128,256]{1,2,0:T(8,128)(2,1)}, bf16[6,128,256]{1,2,0:T(8,128)(2,1)}, u32[]{:S(2)}, u32[]{:S(2)}) %collective-permute-start.8) | collective-permute-done | bytes 393248 | tf_op jit(solution)/shard_map/ppermute | solution.py:147
  111.6 1.9 copy.85
  116.4 34.0 %shard_map.247 = (bf16[32768,256]{1,0:T(8,128)(2,1)}, f32[16,256]{1,0:T(8,128)}, f32[1,256]{1,0:T(1,128)}) custom-call(bf16[32768,256]{1,0:T(8,128)(2,1)} %bitcast.81, bf16[16,32768]{1,0:T(8,128)(2,1)} %pad.8.ds_ref, f32[1,256]{1,0:T(1,128)} %bitcast.123, bf16[16,256]{1,0:T(8,128)(2,1)} %pad.9.wt_ref), custom_call_target="tpu_custom_call" | custom-call | flops 704643072 | bytes 34603008 | tf_op jit(solution)/shard_map/pallas_call | solution.py:97
  154.8 2.5 %convolution_multiply_fusion.2 = f32[1,256]{1,0:T(1,128)} fusion(bf16[256,4608]{1,0:T(8,128)(2,1)S(1)} %copy-done.6, f32[1,4608]{1,0:T(1,128)S(1)} %get-tuple-element.99, f32[1,256]{1,0:T(1,128)S(1)} %copy-done.36), kind=kOutput, calls=%fused_computation.46 | convolution fusion | flops 14157824 | bytes 2379776 | tf_op jit(solution)/shard_map/dot_general | solution.py:409
  158.6 1.8 collective-permute-start.10
  160.7 3.5 %collective-permute-done.15 = f32[1,3328]{1,0:T(1,128)S(1)} collective-permute-done((f32[1,3328]{1,0:T(1,128)S(1)}, f32[1,3328]{1,0:T(1,128)S(1)}, u32[]{:S(2)}, u32[]{:S(2)}) %collective-permute-start.15) | collective-permute-done | bytes 13344 | tf_op jit(solution)/shard_map/ppermute | solution.py:180
  164.3 1.7 collective-permute-start.16
  168.2 2.7 %collective-permute-start.17 = (f32[1,3328]{1,0:T(1,128)S(1)}, f32[1,3328]{1,0:T(1,128)S(1)}, u32[]{:S(2)}, u32[]{:S(2)}) collective-permute-start(f32[1,3328]{1,0:T(1,128)S(1)} %add.184), channel_id=1, source_target_pairs={{0,16},{2,18},{4,20},{6,22},{8,24},{10,26},{12,28},{14,30},{16,0},... | collective-permute-start | bytes 39944 | tf_op jit(solution)/shard_map/ppermute | solution.py:180
  171.0 2.7 %collective-permute-start.12 = (f32[8,5632]{1,0:T(8,128)S(1)}, f32[8,5632]{1,0:T(8,128)S(1)}, u32[]{:S(2)}, u32[]{:S(2)}) collective-permute-start(f32[8,5632]{1,0:T(8,128)S(1)} %maximum_select_fusion.9), channel_id=1, source_target_pairs={{0,16},{2,18},{4,20},{6,22},{8,24},{10,26},{12,28},{14,30},{16,0},... | collective-permute-start | bytes 540680 | tf_op jit(solution)/shard_map/ppermute | solution.py:165
  176.0 6.5 %collective-permute-done.12 = f32[8,5632]{1,0:T(8,128)S(1)} collective-permute-done((f32[8,5632]{1,0:T(8,128)S(1)}, f32[8,5632]{1,0:T(8,128)S(1)}, u32[]{:S(2)}, u32[]{:S(2)}) %collective-permute-start.12) | collective-permute-done | bytes 180256 | tf_op jit(solution)/shard_map/ppermute | solution.py:165
  183.8 4.2 %fusion.47 = f32[256,4608]{1,0:T(8,128)} fusion(bf16[16,256]{1,0:T(8,128)(2,1)S(1)} %multiply_convert_fusion.7, f32[16,5632]{1,0:T(8,128)S(1)} %maximum_select_fusion.8), kind=kOutput, calls=%fused_computation.105 | convolution fusion | flops 226492416 | bytes 5021696 | tf_op jit(solution)/shard_map/dot_general | solution.py:407
  188.0 13.1 %reduce-scatter.2.cloned.1.call-done = bf16[48,6144]{1,0:T(8,128)(2,1)} async-done(((bf16[768,6144]{1,0:T(8,128)(2,1)}), bf16[48,6144]{1,0:T(8,128)(2,1)}) %reduce-scatter.2.cloned.1.call-update) | async-done | bytes 589840 | tf_op jit(solution)/shard_map/reduce_scatter | solution.py:368
  (224 shorter events, 52.4 us)
Async XLA Ops:
  7.2 57.2 %copy-start = (bf16[1536,768]{1,0:T(8,128)(2,1)S(1)}, bf16[1536,768]{1,0:T(8,128)(2,1)}, u32[]{:S(2)}) copy-start(bf16[1536,768]{1,0:T(8,128)(2,1)} %param.28) | copy-start | bytes 7077892
  7.2 194.0 %reduce-scatter.2.cloned.1.call-start = ((), (), s32[]{:S(2)}) async-start(), calls=%async_computation.1 | async-start | bytes 10027008 | tf_op jit(solution)/shard_map/reduce_scatter | solution.py:368
  7.2 35.7 %collective-permute-start = (bf16[128,768]{1,0:T(8,128)(2,1)}, bf16[128,768]{1,0:T(8,128)(2,1)S(1)}, u32[]{:S(2)}, u32[]{:S(2)}) collective-permute-start(bf16[128,768]{1,0:T(8,128)(2,1)} %bitcast.91), channel_id=1, source_target_pairs={{0,1},{1,0},{2,3},{3,2},{4,5},{5,4},{6,7},{7,6},{8,9},{9,8},{10,11... | collective-permute-start | bytes 589832 | tf_op jit(solution)/shard_map/ppermute | solution.py:147
  10.3 48.1 %collective-permute-start.3 = (bf16[384,768]{1,0:T(8,128)(2,1)}, bf16[384,768]{1,0:T(8,128)(2,1)}, u32[]{:S(2)}, u32[]{:S(2)}) collective-permute-start(bf16[384,768]{1,0:T(8,128)(2,1)} %param.25), channel_id=1, source_target_pairs={{0,1},{1,0},{2,3},{3,2},{4,5},{5,4},{6,7},{7,6},{8,9},{9,8},{10,11... | collective-permute-start | bytes 1769480 | tf_op jit(solution)/shard_map/ppermute | solution.py:147
  29.7 6.7 %copy-start.25 = (f32[4608]{0:T(1024)S(1)}, f32[4608]{0:T(1024)}, u32[]{:S(2)}) copy-start(f32[4608]{0:T(1024)} %param.21) | copy-start | bytes 55300
  29.7 8.0 %copy-start.9 = (bf16[6,128,256]{2,1,0:T(8,128)(2,1)S(1)}, bf16[6,128,256]{2,1,0:T(8,128)(2,1)}, u32[]{:S(2)}) copy-start(bf16[6,128,256]{2,1,0:T(8,128)(2,1)} %get-tuple-element.90) | copy-start | bytes 1179652
  31.6 14.6 %collective-permute-start.1 = (bf16[6,128,256]{1,2,0:T(8,128)(2,1)}, bf16[6,128,256]{1,2,0:T(8,128)(2,1)}, u32[]{:S(2)}, u32[]{:S(2)}) collective-permute-start(bf16[6,128,256]{1,2,0:T(8,128)(2,1)} %copy.94), channel_id=1, source_target_pairs={{0,1},{1,0},{2,3},{3,2},{4,5},{5,4},{6,7},{7,6},{8,9},{9,8},{10,11... | collective-permute-start | bytes 1179656 | tf_op jit(solution)/shard_map/ppermute | solution.py:147
  37.6 47.2 %copy-start.26 = (f32[768]{0:T(1024)}, f32[768]{0:T(1024)S(1)}, u32[]{:S(2)}) copy-start(f32[768]{0:T(1024)S(1)} %get-tuple-element.71) | copy-start | bytes 9220
  52.1 8.1 %collective-permute-start.2 = (bf16[256,384]{1,0:T(8,128)(2,1)}, bf16[256,384]{1,0:T(8,128)(2,1)}, u32[]{:S(2)}, u32[]{:S(2)}) collective-permute-start(bf16[256,384]{1,0:T(8,128)(2,1)} %copy.78), channel_id=1, source_target_pairs={{0,1},{1,0},{2,3},{3,2},{4,5},{5,4},{6,7},{7,6},{8,9},{9,8},{10,11... | collective-permute-start | bytes 589832 | tf_op jit(solution)/shard_map/ppermute | solution.py:147
  52.2 12.2 %collective-permute-start.5 = (bf16[128,768]{1,0:T(8,128)(2,1)S(1)}, bf16[128,768]{1,0:T(8,128)(2,1)S(1)}, u32[]{:S(2)}, u32[]{:S(2)}) collective-permute-start(bf16[128,768]{1,0:T(8,128)(2,1)S(1)} %bitcast.107), channel_id=1, source_target_pairs={{0,1},{1,0},{2,3},{3,2},{4,5},{5,4},{6,7},{7,6},{8,9},{9,8},{10,11... | collective-permute-start | bytes 589832 | tf_op jit(solution)/shard_map/ppermute | solution.py:147
  62.6 13.3 %copy-start.1 = (f32[256,768]{1,0:T(8,128)}, f32[256,768]{1,0:T(8,128)S(1)}, u32[]{:S(2)}) copy-start(f32[256,768]{1,0:T(8,128)S(1)} %get-tuple-element.79) | copy-start | bytes 2359300
  64.4 11.6 %copy-start.19 = (bf16[128,768]{1,0:T(8,128)(2,1)}, bf16[128,768]{1,0:T(8,128)(2,1)S(1)}, u32[]{:S(2)}) copy-start(bf16[128,768]{1,0:T(8,128)(2,1)S(1)} %collective-permute-done.5) | copy-start | bytes 589828
  67.1 7.8 %collective-permute-start.6 = (bf16[256,768]{1,0:T(8,128)(2,1)S(1)}, bf16[256,768]{1,0:T(8,128)(2,1)S(1)}, u32[]{:S(2)}, u32[]{:S(2)}) collective-permute-start(bf16[256,768]{1,0:T(8,128)(2,1)S(1)} %convolution_convert_fusion.6), channel_id=1, source_target_pairs={{0,1},{1,0},{2,3},{3,2},{4,5},{5,4},{6,7},{7,6},{8,9},{9,8},{10,11... | collective-permute-start | bytes 1179656 | tf_op jit(solution)/shard_map/ppermute | solution.py:147
  91.1 12.3 %collective-permute-start.4 = (bf16[256,768]{1,0:T(8,128)(2,1)}, bf16[256,768]{1,0:T(8,128)(2,1)}, u32[]{:S(2)}, u32[]{:S(2)}) collective-permute-start(bf16[256,768]{1,0:T(8,128)(2,1)} %convolution_convert_fusion.7), channel_id=1, source_target_pairs={{0,1},{1,0},{2,3},{3,2},{4,5},{5,4},{6,7},{7,6},{8,9},{9,8},{10,11... | collective-permute-start | bytes 1179656 | tf_op jit(solution)/shard_map/ppermute | solution.py:147
  95.8 7.7 %copy-start.18 = (bf16[1,128,768]{2,1,0:T(8,128)(2,1)S(1)}, bf16[1,128,768]{2,1,0:T(8,128)(2,1)}, u32[]{:S(2)}) copy-start(bf16[1,128,768]{2,1,0:T(8,128)(2,1)} %param.29) | copy-start | bytes 589828
  95.8 7.7 %copy-start.20 = (bf16[128,768]{1,0:T(8,128)(2,1)S(1)}, bf16[128,768]{1,0:T(8,128)(2,1)}, u32[]{:S(2)}) copy-start(bf16[128,768]{1,0:T(8,128)(2,1)} %copy-done.19) | copy-start | bytes 589828
  95.8 7.6 %copy-start.30 = (f32[768]{0:T(1024)S(1)}, f32[768]{0:T(1024)}, u32[]{:S(2)}) copy-start(f32[768]{0:T(1024)} %get-tuple-element.72) | copy-start | bytes 9220
  95.8 15.8 %collective-permute-start.8 = (bf16[6,128,256]{1,2,0:T(8,128)(2,1)}, bf16[6,128,256]{1,2,0:T(8,128)(2,1)}, u32[]{:S(2)}, u32[]{:S(2)}) collective-permute-start(bf16[6,128,256]{1,2,0:T(8,128)(2,1)} %get-tuple-element.89), channel_id=1, source_target_pairs={{0,1},{1,0},{2,3},{3,2},{4,5},{5,4},{6,7},{7,6},{8,9},{9,8},{10,11... | collective-permute-start | bytes 1179656 | tf_op jit(solution)/shard_map/ppermute | solution.py:147
  101.0 51.9 %collective-permute-start.7 = (bf16[256,768]{1,0:T(8,128)(2,1)}, bf16[256,768]{1,0:T(8,128)(2,1)}, u32[]{:S(2)}, u32[]{:S(2)}) collective-permute-start(bf16[256,768]{1,0:T(8,128)(2,1)} %convolution_convert_fusion.5), channel_id=1, source_target_pairs={{0,1},{1,0},{2,3},{3,2},{4,5},{5,4},{6,7},{7,6},{8,9},{9,8},{10,11... | collective-permute-start | bytes 1179656 | tf_op jit(solution)/shard_map/ppermute | solution.py:147
  116.4 36.5 %copy-start.27 = (f32[768]{0:T(1024)S(1)}, f32[768]{0:T(1024)}, u32[]{:S(2)}) copy-start(f32[768]{0:T(1024)} %copy-done.26) | copy-start | bytes 9220
  116.4 36.5 %copy-start.39 = (f32[256]{0:T(256)S(1)}, f32[256]{0:T(256)}, u32[]{:S(2)}) copy-start(f32[256]{0:T(256)} %copy-done.37) | copy-start | bytes 3076
  116.4 36.5 %copy-start.46 = (f32[256]{0:T(256)S(1)}, f32[256]{0:T(256)}, u32[]{:S(2)}) copy-start(f32[256]{0:T(256)} %copy-done.43) | copy-start | bytes 3076
  152.3 5.0 %collective-permute-start.13 = (f32[1,3328]{1,0:T(1,128)S(1)}, f32[1,3328]{1,0:T(1,128)S(1)}, u32[]{:S(2)}, u32[]{:S(2)}) collective-permute-start(f32[1,3328]{1,0:T(1,128)S(1)} %broadcast_in_dim.61), channel_id=1, source_target_pairs={{0,1},{1,0},{2,3},{3,2},{4,5},{5,4},{6,7},{7,6},{8,9},{9,8},{10,11... | collective-permute-start | bytes 39944 | tf_op jit(solution)/shard_map/ppermute | solution.py:147
  154.8 18.9 %copy-start.5 = (f32[256,768]{1,0:T(8,128)S(1)}, f32[256,768]{1,0:T(8,128)}, u32[]{:S(2)}) copy-start(f32[256,768]{1,0:T(8,128)} %copy-done.3) | copy-start | bytes 2359300
  157.3 1.2 collective-permute-start.9
  157.3 3.0 %collective-permute-start.14 = (f32[1,3328]{1,0:T(1,128)S(1)}, f32[1,3328]{1,0:T(1,128)S(1)}, u32[]{:S(2)}, u32[]{:S(2)}) collective-permute-start(f32[1,3328]{1,0:T(1,128)S(1)} %reshape_add_fusion), channel_id=1, source_target_pairs={{0,2},{2,0},{4,6},{6,4},{8,10},{10,8},{12,14},{14,12},{16,18},{18,... | collective-permute-start | bytes 39944 | tf_op jit(solution)/shard_map/ppermute | solution.py:180
  158.6 7.5 %collective-permute-start.10 = (f32[2,5632]{1,0:T(2,128)S(1)}, f32[2,5632]{1,0:T(2,128)S(1)}, u32[]{:S(2)}, u32[]{:S(2)}) collective-permute-start(f32[2,5632]{1,0:T(2,128)S(1)} %maximum_select_fusion.12), channel_id=1, source_target_pairs={{0,4},{2,6},{4,0},{6,2},{8,12},{10,14},{12,8},{14,10},{16,20},{18,... | collective-permute-start | bytes 135176 | tf_op jit(solution)/shard_map/ppermute | solution.py:165
  160.4 3.9 %collective-permute-start.15 = (f32[1,3328]{1,0:T(1,128)S(1)}, f32[1,3328]{1,0:T(1,128)S(1)}, u32[]{:S(2)}, u32[]{:S(2)}) collective-permute-start(f32[1,3328]{1,0:T(1,128)S(1)} %add.182), channel_id=1, source_target_pairs={{0,4},{2,6},{4,0},{6,2},{8,12},{10,14},{12,8},{14,10},{16,20},{18,... | collective-permute-start | bytes 39944 | tf_op jit(solution)/shard_map/ppermute | solution.py:180
  164.3 3.9 %collective-permute-start.16 = (f32[1,3328]{1,0:T(1,128)S(1)}, f32[1,3328]{1,0:T(1,128)S(1)}, u32[]{:S(2)}, u32[]{:S(2)}) collective-permute-start(f32[1,3328]{1,0:T(1,128)S(1)} %add.183), channel_id=1, source_target_pairs={{0,8},{2,10},{4,12},{6,14},{8,0},{10,2},{12,4},{14,6},{16,24},{18,... | collective-permute-start | bytes 39944 | tf_op jit(solution)/shard_map/ppermute | solution.py:180
  166.1 4.8 %collective-permute-start.11 = (f32[4,5632]{1,0:T(4,128)S(1)}, f32[4,5632]{1,0:T(4,128)S(1)}, u32[]{:S(2)}, u32[]{:S(2)}) collective-permute-start(f32[4,5632]{1,0:T(4,128)S(1)} %maximum_select_fusion.11), channel_id=1, source_target_pairs={{0,8},{2,10},{4,12},{6,14},{8,0},{10,2},{12,4},{14,6},{16,24},{18,... | collective-permute-start | bytes 270344 | tf_op jit(solution)/shard_map/ppermute | solution.py:165
  168.2 6.3 %collective-permute-start.17 = (f32[1,3328]{1,0:T(1,128)S(1)}, f32[1,3328]{1,0:T(1,128)S(1)}, u32[]{:S(2)}, u32[]{:S(2)}) collective-permute-start(f32[1,3328]{1,0:T(1,128)S(1)} %add.184), channel_id=1, source_target_pairs={{0,16},{2,18},{4,20},{6,22},{8,24},{10,26},{12,28},{14,30},{16,0},... | collective-permute-start | bytes 39944 | tf_op jit(solution)/shard_map/ppermute | solution.py:180
  171.0 11.5 %collective-permute-start.12 = (f32[8,5632]{1,0:T(8,128)S(1)}, f32[8,5632]{1,0:T(8,128)S(1)}, u32[]{:S(2)}, u32[]{:S(2)}) collective-permute-start(f32[8,5632]{1,0:T(8,128)S(1)} %maximum_select_fusion.9), channel_id=1, source_target_pairs={{0,16},{2,18},{4,20},{6,22},{8,24},{10,26},{12,28},{14,30},{16,0},... | collective-permute-start | bytes 540680 | tf_op jit(solution)/shard_map/ppermute | solution.py:165
  (41 other events, 120.1 us)
Sparse Core Ops, SparseCore 0:
  87.2 113.8 reduce-scatter.1

commit v14 on v13

--- a/solution.py
+++ b/solution.py
@@ -306,7 +306,6 @@
 
     grad_out = g_rows.astype(jnp.float32)
     d_ffn = (grad_out * sig_t).astype(jnp.bfloat16)
-    d_gate_t = jnp.sum(grad_out * ffn_branch * sig_t * (1.0 - sig_t), axis=0, keepdims=True)
     down_grad_t = lax.dot_general(
         d_ffn, hidden, (((0,), (0,)), ((), ())), preferred_element_type=jnp.float32
     )
@@ -324,11 +323,7 @@
     )
     d_normed_t = head_sum_low(ffn_in_part)
     d_middle = grad_out + norm_back(norm_mid, inv_mid, d_normed_t * (1.0 + scale_t))
-    d_scale_t = jnp.sum(d_normed_t * norm_mid, axis=0, keepdims=True)
-    d_shift_t = jnp.sum(d_normed_t, axis=0, keepdims=True)
     d_attn = d_middle * sig_a
-    d_gate_a = jnp.sum(d_middle * attn_branch * sig_a * (1.0 - sig_a), axis=0, keepdims=True)
-    d_out_bias = jnp.sum(d_attn, axis=0, keepdims=True)
     d_attn_low = d_attn.astype(jnp.bfloat16)
 
     out_weight_grad_t = lax.dot_general(
@@ -357,6 +352,15 @@
     qkv_grad = lax.dot_general(
         normed_a, d_qkv, (((0,), (0,)), ((), ())), preferred_element_type=jnp.float32
     )
+
+    late_dnt, late_nm, late_dm, late_ab, late_go, late_ffn, _ = lax.optimization_barrier(
+        (d_normed_t, norm_mid, d_middle, attn_branch, grad_out, ffn_branch, qkv_grad)
+    )
+    d_gate_t = jnp.sum(late_go * late_ffn * sig_t * (1.0 - sig_t), axis=0, keepdims=True)
+    d_scale_t = jnp.sum(late_dnt * late_nm, axis=0, keepdims=True)
+    d_shift_t = jnp.sum(late_dnt, axis=0, keepdims=True)
+    d_gate_a = jnp.sum(late_dm * late_ab * sig_a * (1.0 - sig_a), axis=0, keepdims=True)
+    d_out_bias = jnp.sum(late_dm * sig_a, axis=0, keepdims=True)
 
     packed = blank((width, 4 * proj + 3 * ffn), jnp.bfloat16)
     packed = lax.dynamic_update_slice(packed, gate_up_grad.astype(jnp.bfloat16), (0, 4 * proj))

time: 214 us -> 219 us (1.023)
  other arithmetic: 14.4 us -> 19.5 us
  waiting for transfers between devices: 36.7 us -> 32.5 us
  local copies, waits for them, and re-layouts: 34.1 us -> 37.2 us
    reduce_scatter x1, waiting for transfers between devices: 13.1 us -> 5.85 us  [shards(): lax.psum_scatter(packed, 'dp', scatter_dimension=0, tiled=True)]
    ppermute x4, waiting for transfers between devices: 7.09 us -> 12.5 us  [dp_gather(): other = lax.ppermute(block, 'dp', [(i, i ^ step) for i in range(count)])]
    ppermute x10, waiting for transfers between devices: 11.4 us -> 8.32 us  [swap_heads(): return lax.ppermute(values, 'head', [(0, 1), (1, 0)])]
    unnamed x124 -> x134, local copies, waits for them, and re-layouts: 19.7 us -> 19 us
  transfers between devices with their start and end apart: 19 -> 19, of which waited for: 9 -> 10; matrix products, arithmetic and copies ran while one was open for 33% -> 37% of each run, Pallas kernels for 23% -> 23%
where the time goes in v14:
time: 219 us; the launch traced here: 217 us
  Pallas kernels  49.4 us (23%)
  matrix products  43.4 us (20%)
  local copies, waits for them, and re-layouts  37.2 us (17%)
  waiting for transfers between devices  32.5 us (15%)
  starting transfers between devices  19.7 us (9%)
  other arithmetic  19.5 us (9%)
  between operations  15.5 us (7%)
    pallas_call x1, Pallas kernels, pair_backward(): pl.pallas_call(pair_backward_kernel, grid=(m // tile,), in_specs=[pl.Bloc...  34 us
    unnamed x134, local copies, waits for them, and re-layouts  19 us
    pallas_call x1, Pallas kernels, pair_forward(): pl.pallas_call(pair_forward_kernel, grid=(m // tile,), in_specs=[pl.Block...  15.4 us
    ppermute x4, waiting for transfers between devices, dp_gather(): other = lax.ppermute(block, 'dp', [(i, i ^ step) for i in range(count)])  12.5 us
    ppermute x10, starting transfers between devices, swap_heads(): return lax.ppermute(values, 'head', [(0, 1), (1, 0)])  9.75 us
    ppermute x10, waiting for transfers between devices, swap_heads(): return lax.ppermute(values, 'head', [(0, 1), (1, 0)])  8.32 us
    reduce_scatter x1, waiting for transfers between devices, shards(): lax.psum_scatter(packed, 'dp', scatter_dimension=0, tiled=True)  5.85 us
    ppermute x4, waiting for transfers between devices, dp_sum(): other = lax.ppermute(values, 'dp', [(i, i ^ step) for i in range(count)])  5.83 us
  transfers between devices with their start and end apart: 19, of which 10 were waited for; matrix products, arithmetic and copies ran while one was open for 37% of the time, Pallas kernels for 23%

profile of v14, /device:TPU:0, one launch (start us, length us, event | category | flops | bytes accessed | tf_op | source)
XLA Modules:
  0.0 217.2 jit_solution(200778091140200683)
XLA Ops:
  7.2 3.0 %collective-permute-start = (bf16[128,768]{1,0:T(8,128)(2,1)}, bf16[128,768]{1,0:T(8,128)(2,1)S(1)}, u32[]{:S(2)}, u32[]{:S(2)}) collective-permute-start(bf16[128,768]{1,0:T(8,128)(2,1)} %bitcast.91), channel_id=1, source_target_pairs={{0,1},{1,0},{2,3},{3,2},{4,5},{5,4},{6,7},{7,6},{8,9},{9,8},{10,11... | collective-permute-start | bytes 589832 | tf_op jit(solution)/shard_map/ppermute | solution.py:147
  11.8 15.4 %shard_map.246 = bf16[12,32768]{1,0:T(8,128)(2,1)} custom-call(bf16[32768,256]{1,0:T(8,128)(2,1)} %bitcast.80, f32[1,256]{1,0:T(1,128)} %bitcast.122, bf16[256,12]{1,0:T(8,128)(2,1)} %copy.73.wt_ref), custom_call_target="tpu_custom_call" | custom-call | flops 352321536 | bytes 17563648 | tf_op jit(solution)/shard_map/pallas_call | solution.py:50
  29.7 2.0 copy.94
  31.6 1.9 collective-permute-start.1
  34.3 2.1 convolution_reduce_fusion
  38.5 3.9 %copy.69 = bf16[768,3,384]{0,2,1:T(8,128)(2,1)} copy(bf16[768,3,384]{2,0,1:T(8,128)(2,1)} %param.22) | data formatting | bytes 3538944 | tf_op args[7]
  43.4 2.3 %convolution_convert_fusion.2 = bf16[256,1152]{1,0:T(8,128)(2,1)S(1)} fusion(bf16[768,1152]{0,1:T(8,128)(2,1)} %bitcast.89, f32[768]{0:T(1024)S(1)} %get-tuple-element.82, f32[768]{0:T(1024)S(1)} %get-tuple-element.83, f32[256]{0:T(256)S(1)} %add_rsqrt_fusion.1, f32[256]{0:T(256)S(1)} %broadcast_multiply_fusion.5, bf16[128,768]{1,0:T(8,128)(2,1)S(1)} %bitcast.94, ...), kind=kOutput, calls=%fused_computation.5 | convolution fusion | flops 456228864 | bytes 2760705 | tf_op jit(solution)/shard_map/dot_general | solution.py:273
  46.2 3.4 %fusion.74 = (f32[6,256]{1,0:T(8,128)S(1)}, f32[6,256,256]{1,2,0:T(8,128)}) fusion(pred[256]{0:T(512)(128)(4,1)} %or_and_fusion, bf16[256,6,64]{0,2,1:T(8,128)(2,1)S(1)} %bitcast.103, bf16[256,6,64]{0,2,1:T(8,128)(2,1)S(1)} %bitcast.101, bf16[6,128,256]{1,2,0:T(8,128)(2,1)} %copy.93, bf16[6,128,256]{1,2,0:T(8,128)(2,1)} %collective-permute-done.1, pred[]{:T(512)S(6)} %eq.44), kind=kOutput, calls=%fused_computation.176 | convolution fusion | flops 56230144 | bytes 2758913 | tf_op jit(solution)/shard_map/sub | solution.py:281
  51.7 1.9 collective-permute-start.5
  53.7 3.6 %copy.97 = bf16[96,8,2,1536]{3,1,2,0:T(8,128)(2,1)S(1)} copy(bf16[96,8,2,1536]{3,2,1,0:T(2,128)(2,1)} %bitcast.82) | data formatting | bytes 9437184
  59.5 3.0 %fusion.72 = (f32[256]{0:T(256)S(1)}, f32[256,768]{1,0:T(8,128)S(1)}, f32[256,768]{1,0:T(8,128)}) fusion(f32[768]{0:T(1024)S(1)} %get-tuple-element.127, bf16[128,768]{1,0:T(8,128)(2,1)S(1)} %bitcast.95, bf16[128,768]{1,0:T(8,128)(2,1)S(1)} %collective-permute-done, pred[]{:T(512)S(6)} %eq.44, f32[768]{0:T(1024)S(1)} %copy-done.55, ...), kind=kOutput, calls=%fused_computation.174 | convolution fusion | flops 311820032 | bytes 3546113 | tf_op jit(solution)/shard_map/dot_general | solution.py:292
  67.5 3.7 %fusion.1 = bf16[768,6144]{1,0:T(8,128)(2,1)} fusion(bf16[768,6144]{1,0:T(8,128)(2,1)} %shard_map.248, bf16[256,1536]{1,0:T(8,128)(2,1)S(1)} %get-tuple-element.92, bf16[256,1536]{1,0:T(8,128)(2,1)S(1)} %get-tuple-element.91, f32[256,768]{1,0:T(8,128)S(1)} %subtract_multiply_fusion, f32[768]{0:T(1024)S(1)} %copy-done.53, f32[768]{0:T(1024)S(1)} %get-tuple-element.80), kind=kOutput, calls=%fused_computation.2 | convolution fusion | flops 1214054400 | bytes 7084032 | tf_op jit(solution)/shard_map/dot_general | solution.py:318
  71.2 2.3 %fusion.2 = bf16[768,6144]{1,0:T(8,128)(2,1)} fusion(bf16[768,6144]{1,0:T(8,128)(2,1)} %fusion.1, bf16[256,1536]{1,0:T(8,128)(2,1)S(1)} %get-tuple-element.93, f32[768]{0:T(1024)S(1)} %get-tuple-element.85, bf16[128,768]{1,0:T(8,128)(2,1)S(1)} %collective-permute-done.5, bf16[128,768]{1,0:T(8,128)(2,1)S(1)} %bitcast.110, pred[]{:T(512)S(6)} %eq.44), kind=kOutput, calls=%fused_computation.4 | convolution fusion | flops 607518720 | bytes 3542017 | tf_op jit(solution)/shard_map/dot_general | solution.py:309
  73.6 1.8 collective-permute-done.6
  79.8 1.9 convolution_convert_fusion.7
  85.9 2.2 %convert_dynamic-update-slice_fusion = bf16[768,6144]{1,0:T(8,128)(2,1)} fusion(bf16[768,6144]{1,0:T(8,128)(2,1)} %fusion.6, bf16[256,384]{0,1:T(8,128)(2,1)S(1)} %bitcast.127, bf16[256,384]{0,1:T(8,128)(2,1)S(1)} %bitcast.113, bf16[256,384]{0,1:T(8,128)(2,1)S(1)} %bitcast.115, f32[768]{0:T(1024)S(1)} %copy-done.52, f32[768]{0:T(1024)S(1)} %get-tuple-element.83, ...), kind=kOutput, calls=%fused_computation.6 | convolution fusion | flops 457703424 | bytes 2760705 | tf_op jit(solution)/shard_map/dot_general | solution.py:352
  90.1 2.2 %fusion.33 = f32[256,768]{1,0:T(8,128)} fusion(bf16[128,768]{1,0:T(8,128)(2,1)} %copy-done.23, bf16[128,768]{1,0:T(8,128)(2,1)} %bitcast.107, pred[]{:T(512)S(6)} %eq.44), kind=kLoop, calls=%fused_computation.91 | loop fusion | flops 1966080 | bytes 1179649 | tf_op jit(solution)/shard_map/convert_element_type | solution.py:307
  92.3 2.7 %convolution_convert_fusion.6 = bf16[256,768]{1,0:T(8,128)(2,1)} fusion(bf16[256,1536]{1,0:T(8,128)(2,1)} %copy-done.58, bf16[1536,768]{1,0:T(8,128)(2,1)S(1)} %copy-done), kind=kOutput, calls=%fused_computation.23 | convolution fusion | flops 604176384 | bytes 3538944 | tf_op jit(solution)/shard_map/dot_general | solution.py:302
  96.4 2.0 copy.84
  98.4 2.0 copy.98
  102.1 3.5 %convolution_convert_fusion.4 = bf16[256,768]{1,0:T(8,128)(2,1)} fusion(bf16[768,1152]{0,1:T(8,128)(2,1)} %bitcast.90, bf16[256,384]{0,1:T(8,128)(2,1)} %bitcast.128, bf16[256,384]{0,1:T(8,128)(2,1)} %bitcast.114, bf16[256,384]{0,1:T(8,128)(2,1)} %bitcast.116), kind=kOutput, calls=%fused_computation.21 | convolution fusion | flops 454950912 | bytes 2752512 | tf_op jit(solution)/shard_map/dot_general | solution.py:374
  111.1 4.1 %collective-permute-done.8 = bf16[6,128,256]{1,2,0:T(8,128)(2,1)} collective-permute-done((bf16[6,128,256]{1,2,0:T(8,128)(2,1)}, bf16[6,128,256]{1,2,0:T(8,128)(2,1)}, u32[]{:S(2)}, u32[]{:S(2)}) %collective-permute-start.8) | collective-permute-done | bytes 393248 | tf_op jit(solution)/shard_map/ppermute | solution.py:147
  115.3 1.9 copy.85
  118.4 1.9 maximum_select_fusion.2
  121.3 34.0 %shard_map.247 = (bf16[32768,256]{1,0:T(8,128)(2,1)}, f32[16,256]{1,0:T(8,128)}, f32[1,256]{1,0:T(1,128)}) custom-call(bf16[32768,256]{1,0:T(8,128)(2,1)} %bitcast.81, bf16[16,32768]{1,0:T(8,128)(2,1)} %pad.8.ds_ref, f32[1,256]{1,0:T(1,128)} %bitcast.123, bf16[16,256]{1,0:T(8,128)(2,1)} %pad.9.wt_ref), custom_call_target="tpu_custom_call" | custom-call | flops 704643072 | bytes 34603008 | tf_op jit(solution)/shard_map/pallas_call | solution.py:97
  160.8 2.5 %convolution_multiply_fusion.2 = f32[1,256]{1,0:T(1,128)} fusion(bf16[256,4608]{1,0:T(8,128)(2,1)S(1)} %copy-done.5, f32[1,4608]{1,0:T(1,128)S(1)} %get-tuple-element.109, f32[1,256]{1,0:T(1,128)S(1)} %copy-done.43), kind=kOutput, calls=%fused_computation.42 | convolution fusion | flops 14157824 | bytes 2379776 | tf_op jit(solution)/shard_map/dot_general | solution.py:413
  166.7 3.2 %collective-permute-done.15 = f32[1,3328]{1,0:T(1,128)S(1)} collective-permute-done((f32[1,3328]{1,0:T(1,128)S(1)}, f32[1,3328]{1,0:T(1,128)S(1)}, u32[]{:S(2)}, u32[]{:S(2)}) %collective-permute-start.15) | collective-permute-done | bytes 13344 | tf_op jit(solution)/shard_map/ppermute | solution.py:180
  173.8 2.7 %collective-permute-start.17 = (f32[1,3328]{1,0:T(1,128)S(1)}, f32[1,3328]{1,0:T(1,128)S(1)}, u32[]{:S(2)}, u32[]{:S(2)}) collective-permute-start(f32[1,3328]{1,0:T(1,128)S(1)} %add.184), channel_id=1, source_target_pairs={{0,16},{2,18},{4,20},{6,22},{8,24},{10,26},{12,28},{14,30},{16,0},... | collective-permute-start | bytes 39944 | tf_op jit(solution)/shard_map/ppermute | solution.py:180
  176.6 2.3 %collective-permute-start.12 = (f32[8,5632]{1,0:T(8,128)S(1)}, f32[8,5632]{1,0:T(8,128)S(1)}, u32[]{:S(2)}, u32[]{:S(2)}) collective-permute-start(f32[8,5632]{1,0:T(8,128)S(1)} %maximum_select_fusion.9), channel_id=1, source_target_pairs={{0,16},{2,18},{4,20},{6,22},{8,24},{10,26},{12,28},{14,30},{16,0},... | collective-permute-start | bytes 540680 | tf_op jit(solution)/shard_map/ppermute | solution.py:165
  182.4 11.9 %collective-permute-done.12 = f32[8,5632]{1,0:T(8,128)S(1)} collective-permute-done((f32[8,5632]{1,0:T(8,128)S(1)}, f32[8,5632]{1,0:T(8,128)S(1)}, u32[]{:S(2)}, u32[]{:S(2)}) %collective-permute-start.12) | collective-permute-done | bytes 180256 | tf_op jit(solution)/shard_map/ppermute | solution.py:165
  195.6 4.2 %fusion.37 = f32[256,4608]{1,0:T(8,128)} fusion(bf16[16,256]{1,0:T(8,128)(2,1)S(1)} %multiply_convert_fusion.10, f32[16,5632]{1,0:T(8,128)S(1)} %maximum_select_fusion.8), kind=kOutput, calls=%fused_computation.98 | convolution fusion | flops 226492416 | bytes 5021696 | tf_op jit(solution)/shard_map/dot_general | solution.py:411
  199.8 5.8 %reduce-scatter.2.cloned.1.call-done = bf16[48,6144]{1,0:T(8,128)(2,1)} async-done(((bf16[768,6144]{1,0:T(8,128)(2,1)}), bf16[48,6144]{1,0:T(8,128)(2,1)}) %reduce-scatter.2.cloned.1.call-update) | async-done | bytes 589840 | tf_op jit(solution)/shard_map/reduce_scatter | solution.py:372
  (239 shorter events, 60.2 us)
Async XLA Ops:
  7.2 57.5 %copy-start = (bf16[1536,768]{1,0:T(8,128)(2,1)S(1)}, bf16[1536,768]{1,0:T(8,128)(2,1)}, u32[]{:S(2)}) copy-start(bf16[1536,768]{1,0:T(8,128)(2,1)} %param.28) | copy-start | bytes 7077892
  7.2 198.5 %reduce-scatter.2.cloned.1.call-start = ((), (), s32[]{:S(2)}) async-start(), calls=%async_computation.1 | async-start | bytes 10027008 | tf_op jit(solution)/shard_map/reduce_scatter | solution.py:372
  7.2 35.7 %collective-permute-start = (bf16[128,768]{1,0:T(8,128)(2,1)}, bf16[128,768]{1,0:T(8,128)(2,1)S(1)}, u32[]{:S(2)}, u32[]{:S(2)}) collective-permute-start(bf16[128,768]{1,0:T(8,128)(2,1)} %bitcast.91), channel_id=1, source_target_pairs={{0,1},{1,0},{2,3},{3,2},{4,5},{5,4},{6,7},{7,6},{8,9},{9,8},{10,11... | collective-permute-start | bytes 589832 | tf_op jit(solution)/shard_map/ppermute | solution.py:147
  10.3 47.6 %collective-permute-start.3 = (bf16[384,768]{1,0:T(8,128)(2,1)}, bf16[384,768]{1,0:T(8,128)(2,1)}, u32[]{:S(2)}, u32[]{:S(2)}) collective-permute-start(bf16[384,768]{1,0:T(8,128)(2,1)} %param.25), channel_id=1, source_target_pairs={{0,1},{1,0},{2,3},{3,2},{4,5},{5,4},{6,7},{7,6},{8,9},{9,8},{10,11... | collective-permute-start | bytes 1769480 | tf_op jit(solution)/shard_map/ppermute | solution.py:147
  28.7 5.6 %copy-start.42 = (f32[1,256]{1,0:T(1,128)S(1)}, f32[1,256]{1,0:T(1,128)}, u32[]{:S(2)}) copy-start(f32[1,256]{1,0:T(1,128)} %param.17) | copy-start | bytes 3076
  29.7 6.7 %copy-start.31 = (f32[4608]{0:T(1024)S(1)}, f32[4608]{0:T(1024)}, u32[]{:S(2)}) copy-start(f32[4608]{0:T(1024)} %param.21) | copy-start | bytes 55300
  29.7 8.0 %copy-start.12 = (bf16[6,128,256]{2,1,0:T(8,128)(2,1)S(1)}, bf16[6,128,256]{2,1,0:T(8,128)(2,1)}, u32[]{:S(2)}) copy-start(bf16[6,128,256]{2,1,0:T(8,128)(2,1)} %get-tuple-element.100) | copy-start | bytes 1179652
  31.6 14.6 %collective-permute-start.1 = (bf16[6,128,256]{1,2,0:T(8,128)(2,1)}, bf16[6,128,256]{1,2,0:T(8,128)(2,1)}, u32[]{:S(2)}, u32[]{:S(2)}) collective-permute-start(bf16[6,128,256]{1,2,0:T(8,128)(2,1)} %copy.94), channel_id=1, source_target_pairs={{0,1},{1,0},{2,3},{3,2},{4,5},{5,4},{6,7},{7,6},{8,9},{9,8},{10,11... | collective-permute-start | bytes 1179656 | tf_op jit(solution)/shard_map/ppermute | solution.py:147
  37.6 5.8 %copy-start.51 = (f32[768]{0:T(1024)}, f32[768]{0:T(1024)S(1)}, u32[]{:S(2)}) copy-start(f32[768]{0:T(1024)S(1)} %get-tuple-element.82) | copy-start | bytes 9220
  37.6 48.2 %copy-start.32 = (f32[768]{0:T(1024)}, f32[768]{0:T(1024)S(1)}, u32[]{:S(2)}) copy-start(f32[768]{0:T(1024)S(1)} %get-tuple-element.83) | copy-start | bytes 9220
  51.5 7.9 %collective-permute-start.2 = (bf16[256,384]{1,0:T(8,128)(2,1)S(1)}, bf16[256,384]{1,0:T(8,128)(2,1)}, u32[]{:S(2)}, u32[]{:S(2)}) collective-permute-start(bf16[256,384]{1,0:T(8,128)(2,1)S(1)} %copy.78), channel_id=1, source_target_pairs={{0,1},{1,0},{2,3},{3,2},{4,5},{5,4},{6,7},{7,6},{8,9},{9,8},{10,11... | collective-permute-start | bytes 589832 | tf_op jit(solution)/shard_map/ppermute | solution.py:147
  51.7 13.0 %collective-permute-start.5 = (bf16[128,768]{1,0:T(8,128)(2,1)S(1)}, bf16[128,768]{1,0:T(8,128)(2,1)S(1)}, u32[]{:S(2)}, u32[]{:S(2)}) collective-permute-start(bf16[128,768]{1,0:T(8,128)(2,1)S(1)} %bitcast.108), channel_id=1, source_target_pairs={{0,1},{1,0},{2,3},{3,2},{4,5},{5,4},{6,7},{7,6},{8,9},{9,8},{10,11... | collective-permute-start | bytes 589832 | tf_op jit(solution)/shard_map/ppermute | solution.py:147
  53.6 5.8 %copy-start.25 = (bf16[384,768]{1,0:T(8,128)(2,1)S(1)}, bf16[384,768]{1,0:T(8,128)(2,1)}, u32[]{:S(2)}) copy-start(bf16[384,768]{1,0:T(8,128)(2,1)} %param.25) | copy-start | bytes 1769476
  53.6 5.8 %copy-start.55 = (f32[768]{0:T(1024)S(1)}, f32[768]{0:T(1024)}, u32[]{:S(2)}) copy-start(f32[768]{0:T(1024)} %param.26) | copy-start | bytes 9220
  62.5 14.0 %copy-start.1 = (f32[256,768]{1,0:T(8,128)}, f32[256,768]{1,0:T(8,128)S(1)}, u32[]{:S(2)}) copy-start(f32[256,768]{1,0:T(8,128)S(1)} %get-tuple-element.90) | copy-start | bytes 2359300
  64.7 6.6 %copy-start.23 = (bf16[128,768]{1,0:T(8,128)(2,1)}, bf16[128,768]{1,0:T(8,128)(2,1)S(1)}, u32[]{:S(2)}) copy-start(bf16[128,768]{1,0:T(8,128)(2,1)S(1)} %collective-permute-done.5) | copy-start | bytes 589828
  67.4 8.0 %collective-permute-start.6 = (bf16[256,768]{1,0:T(8,128)(2,1)S(1)}, bf16[256,768]{1,0:T(8,128)(2,1)S(1)}, u32[]{:S(2)}, u32[]{:S(2)}) collective-permute-start(bf16[256,768]{1,0:T(8,128)(2,1)S(1)} %convolution_convert_fusion.5), channel_id=1, source_target_pairs={{0,1},{1,0},{2,3},{3,2},{4,5},{5,4},{6,7},{7,6},{8,9},{9,8},{10,11... | collective-permute-start | bytes 1179656 | tf_op jit(solution)/shard_map/ppermute | solution.py:147
  95.0 11.8 %collective-permute-start.4 = (bf16[256,768]{1,0:T(8,128)(2,1)}, bf16[256,768]{1,0:T(8,128)(2,1)}, u32[]{:S(2)}, u32[]{:S(2)}) collective-permute-start(bf16[256,768]{1,0:T(8,128)(2,1)} %convolution_convert_fusion.6), channel_id=1, source_target_pairs={{0,1},{1,0},{2,3},{3,2},{4,5},{5,4},{6,7},{7,6},{8,9},{9,8},{10,11... | collective-permute-start | bytes 1179656 | tf_op jit(solution)/shard_map/ppermute | solution.py:147
  100.4 7.7 %copy-start.9 = (f32[256,768]{1,0:T(8,128)S(1)}, f32[256,768]{1,0:T(8,128)}, u32[]{:S(2)}) copy-start(f32[256,768]{1,0:T(8,128)} %fusion.33) | copy-start | bytes 2359300
  100.4 7.7 %copy-start.39 = (f32[768]{0:T(1024)S(1)}, f32[768]{0:T(1024)}, u32[]{:S(2)}) copy-start(f32[768]{0:T(1024)} %get-tuple-element.84) | copy-start | bytes 9220
  100.4 14.8 %collective-permute-start.8 = (bf16[6,128,256]{1,2,0:T(8,128)(2,1)}, bf16[6,128,256]{1,2,0:T(8,128)(2,1)}, u32[]{:S(2)}, u32[]{:S(2)}) collective-permute-start(bf16[6,128,256]{1,2,0:T(8,128)(2,1)} %get-tuple-element.99), channel_id=1, source_target_pairs={{0,1},{1,0},{2,3},{3,2},{4,5},{5,4},{6,7},{7,6},{8,9},{9,8},{10,11... | collective-permute-start | bytes 1179656 | tf_op jit(solution)/shard_map/ppermute | solution.py:147
  105.6 53.3 %collective-permute-start.7 = (bf16[256,768]{1,0:T(8,128)(2,1)}, bf16[256,768]{1,0:T(8,128)(2,1)}, u32[]{:S(2)}, u32[]{:S(2)}) collective-permute-start(bf16[256,768]{1,0:T(8,128)(2,1)} %convolution_convert_fusion.4), channel_id=1, source_target_pairs={{0,1},{1,0},{2,3},{3,2},{4,5},{5,4},{6,7},{7,6},{8,9},{9,8},{10,11... | collective-permute-start | bytes 1179656 | tf_op jit(solution)/shard_map/ppermute | solution.py:147
  158.8 4.5 %collective-permute-start.13 = (f32[1,3328]{1,0:T(1,128)S(1)}, f32[1,3328]{1,0:T(1,128)S(1)}, u32[]{:S(2)}, u32[]{:S(2)}) collective-permute-start(f32[1,3328]{1,0:T(1,128)S(1)} %broadcast_in_dim.61), channel_id=1, source_target_pairs={{0,1},{1,0},{2,3},{3,2},{4,5},{5,4},{6,7},{7,6},{8,9},{9,8},{10,11... | collective-permute-start | bytes 39944 | tf_op jit(solution)/shard_map/ppermute | solution.py:147
  160.7 18.2 %copy-start.54 = (f32[128]{0:T(128)S(1)}, f32[128]{0:T(128)}, u32[]{:S(2)}) copy-start(f32[128]{0:T(128)} %dynamic-slice.14) | copy-start | bytes 1540
  163.3 1.2 collective-permute-start.9
  163.3 2.8 %collective-permute-start.14 = (f32[1,3328]{1,0:T(1,128)S(1)}, f32[1,3328]{1,0:T(1,128)S(1)}, u32[]{:S(2)}, u32[]{:S(2)}) collective-permute-start(f32[1,3328]{1,0:T(1,128)S(1)} %reshape_add_fusion), channel_id=1, source_target_pairs={{0,2},{2,0},{4,6},{6,4},{8,10},{10,8},{12,14},{14,12},{16,18},{18,... | collective-permute-start | bytes 39944 | tf_op jit(solution)/shard_map/ppermute | solution.py:180
  164.5 7.0 %collective-permute-start.10 = (f32[2,5632]{1,0:T(2,128)S(1)}, f32[2,5632]{1,0:T(2,128)S(1)}, u32[]{:S(2)}, u32[]{:S(2)}) collective-permute-start(f32[2,5632]{1,0:T(2,128)S(1)} %maximum_select_fusion.12), channel_id=1, source_target_pairs={{0,4},{2,6},{4,0},{6,2},{8,12},{10,14},{12,8},{14,10},{16,20},{18,... | collective-permute-start | bytes 135176 | tf_op jit(solution)/shard_map/ppermute | solution.py:165
  166.1 3.8 %collective-permute-start.15 = (f32[1,3328]{1,0:T(1,128)S(1)}, f32[1,3328]{1,0:T(1,128)S(1)}, u32[]{:S(2)}, u32[]{:S(2)}) collective-permute-start(f32[1,3328]{1,0:T(1,128)S(1)} %add.182), channel_id=1, source_target_pairs={{0,4},{2,6},{4,0},{6,2},{8,12},{10,14},{12,8},{14,10},{16,20},{18,... | collective-permute-start | bytes 39944 | tf_op jit(solution)/shard_map/ppermute | solution.py:180
  169.9 3.9 %collective-permute-start.16 = (f32[1,3328]{1,0:T(1,128)S(1)}, f32[1,3328]{1,0:T(1,128)S(1)}, u32[]{:S(2)}, u32[]{:S(2)}) collective-permute-start(f32[1,3328]{1,0:T(1,128)S(1)} %add.183), channel_id=1, source_target_pairs={{0,8},{2,10},{4,12},{6,14},{8,0},{10,2},{12,4},{14,6},{16,24},{18,... | collective-permute-start | bytes 39944 | tf_op jit(solution)/shard_map/ppermute | solution.py:180
  171.7 4.9 %collective-permute-start.11 = (f32[4,5632]{1,0:T(4,128)S(1)}, f32[4,5632]{1,0:T(4,128)S(1)}, u32[]{:S(2)}, u32[]{:S(2)}) collective-permute-start(f32[4,5632]{1,0:T(4,128)S(1)} %maximum_select_fusion.11), channel_id=1, source_target_pairs={{0,8},{2,10},{4,12},{6,14},{8,0},{10,2},{12,4},{14,6},{16,24},{18,... | collective-permute-start | bytes 270344 | tf_op jit(solution)/shard_map/ppermute | solution.py:165
  173.8 7.1 %collective-permute-start.17 = (f32[1,3328]{1,0:T(1,128)S(1)}, f32[1,3328]{1,0:T(1,128)S(1)}, u32[]{:S(2)}, u32[]{:S(2)}) collective-permute-start(f32[1,3328]{1,0:T(1,128)S(1)} %add.184), channel_id=1, source_target_pairs={{0,16},{2,18},{4,20},{6,22},{8,24},{10,26},{12,28},{14,30},{16,0},... | collective-permute-start | bytes 39944 | tf_op jit(solution)/shard_map/ppermute | solution.py:180
  176.6 17.7 %collective-permute-start.12 = (f32[8,5632]{1,0:T(8,128)S(1)}, f32[8,5632]{1,0:T(8,128)S(1)}, u32[]{:S(2)}, u32[]{:S(2)}) collective-permute-start(f32[8,5632]{1,0:T(8,128)S(1)} %maximum_select_fusion.9), channel_id=1, source_target_pairs={{0,16},{2,18},{4,20},{6,22},{8,24},{10,26},{12,28},{14,30},{16,0},... | collective-permute-start | bytes 540680 | tf_op jit(solution)/shard_map/ppermute | solution.py:165
  (46 other events, 121.3 us)
Sparse Core Ops, SparseCore 0:
  88.2 117.3 reduce-scatter.1

commit v15 on v13

--- a/solution.py
+++ b/solution.py
@@ -35,9 +35,9 @@
     return centred * inv_std, inv_std
 
 
-def pair_forward_kernel(x_ref, gain_ref, wt_ref, bias_ref):
+def pair_forward_kernel(x_ref, wt_ref, bias_ref):
     normed, _ = pair_stats(x_ref[...].astype(jnp.float32))
-    scaled = (normed * gain_ref[...]).astype(jnp.bfloat16)
+    scaled = normed.astype(jnp.bfloat16)
     bias = lax.dot_general(
         wt_ref[...], scaled, (((0,), (1,)), ((), ())), preferred_element_type=jnp.float32
     )
@@ -47,12 +47,12 @@
 def pair_forward(flat, gain, wt, heads):
     m, width = flat.shape
     tile = min(PAIR_TILE, m)
+    wt = (wt.astype(jnp.float32) * gain.reshape(-1, 1)).astype(jnp.bfloat16)
     return pl.pallas_call(
         pair_forward_kernel,
         grid=(m // tile,),
         in_specs=[
             pl.BlockSpec((tile, width), lambda i: (i, 0)),
-            pl.BlockSpec((1, width), lambda i: (0, 0)),
             pl.BlockSpec(wt.shape, lambda i: (0, 0)),
         ],
         out_specs=pl.BlockSpec((heads, tile), lambda i: (0, i)),
@@ -62,7 +62,7 @@
             transcendentals=m,
             bytes_accessed=m * width * 2 + heads * m * 2,
         ),
-    )(flat, gain, wt)
+    )(flat, wt)
 
 
 def pair_backward_kernel(x_ref, ds_ref, gain_ref, wt_ref, grad_ref, wg_ref, gg_ref):

time: 214 us -> 213 us (level)
    unnamed x124 -> x123, local copies, waits for them, and re-layouts: 19.7 us -> 18.3 us
where the time goes in v15:
time: 213 us; the launch traced here: 212 us
  Pallas kernels  48.9 us (23%)
  matrix products  42 us (20%)
  waiting for transfers between devices  36.7 us (17%)
  local copies, waits for them, and re-layouts  33.4 us (16%)
  starting transfers between devices  20.6 us (10%)
  between operations  15.5 us (7%)
  other arithmetic  15.1 us (7%)
    pallas_call x1, Pallas kernels, pair_backward(): pl.pallas_call(pair_backward_kernel, grid=(m // tile,), in_specs=[pl.Bloc...  34 us
    unnamed x123, local copies, waits for them, and re-layouts  18.3 us
    pallas_call x1, Pallas kernels, pair_forward(): pl.pallas_call(pair_forward_kernel, grid=(m // tile,), in_specs=[pl.Block...  14.9 us
    reduce_scatter x1, waiting for transfers between devices, shards(): lax.psum_scatter(packed, 'dp', scatter_dimension=0, tiled=True)  12.8 us
    ppermute x10, waiting for transfers between devices, swap_heads(): return lax.ppermute(values, 'head', [(0, 1), (1, 0)])  11.4 us
    ppermute x10, starting transfers between devices, swap_heads(): return lax.ppermute(values, 'head', [(0, 1), (1, 0)])  10.3 us
    ppermute x4, waiting for transfers between devices, dp_gather(): other = lax.ppermute(block, 'dp', [(i, i ^ step) for i in range(count)])  7.4 us
    ppermute x4, starting transfers between devices, dp_sum(): other = lax.ppermute(values, 'dp', [(i, i ^ step) for i in range(count)])  5.39 us
  transfers between devices with their start and end apart: 19, of which 9 were waited for; matrix products, arithmetic and copies ran while one was open for 33% of the time, Pallas kernels for 23%

profile of v15, /device:TPU:0, one launch (start us, length us, event | category | flops | bytes accessed | tf_op | source)
XLA Modules:
  0.0 212.2 jit_solution(15892777436594263445)
XLA Ops:
  7.2 3.0 %collective-permute-start = (bf16[128,768]{1,0:T(8,128)(2,1)}, bf16[128,768]{1,0:T(8,128)(2,1)S(1)}, u32[]{:S(2)}, u32[]{:S(2)}) collective-permute-start(bf16[128,768]{1,0:T(8,128)(2,1)} %bitcast.91), channel_id=1, source_target_pairs={{0,1},{1,0},{2,3},{3,2},{4,5},{5,4},{6,7},{7,6},{8,9},{9,8},{10,11... | collective-permute-start | bytes 589832 | tf_op jit(solution)/shard_map/ppermute | solution.py:147
  11.8 14.9 %shard_map.246 = bf16[12,32768]{1,0:T(8,128)(2,1)} custom-call(bf16[32768,256]{1,0:T(8,128)(2,1)} %bitcast.80, bf16[256,12]{1,0:T(8,128)(2,1)} %copy.96.wt_ref), custom_call_target="tpu_custom_call" | custom-call | flops 352321536 | bytes 17563648 | tf_op jit(solution)/shard_map/pallas_call | solution.py:51
  29.2 2.0 copy.117
  31.2 1.9 collective-permute-start.1
  33.8 2.1 convolution_reduce_fusion
  38.1 3.9 %copy.92 = bf16[768,3,384]{0,2,1:T(8,128)(2,1)} copy(bf16[768,3,384]{2,0,1:T(8,128)(2,1)} %param.22) | data formatting | bytes 3538944 | tf_op args[7]
  42.9 2.3 %convolution_convert_fusion.3 = bf16[256,1152]{1,0:T(8,128)(2,1)S(1)} fusion(bf16[768,1152]{0,1:T(8,128)(2,1)} %bitcast.89, f32[768]{0:T(1024)S(1)} %get-tuple-element.83, f32[768]{0:T(1024)S(1)} %get-tuple-element.84, f32[256]{0:T(256)S(1)} %add_rsqrt_fusion.1, f32[256]{0:T(256)S(1)} %broadcast_multiply_fusion.5, bf16[128,768]{1,0:T(8,128)(2,1)S(1)} %bitcast.94, ...), kind=kOutput, calls=%fused_computation.7 | convolution fusion | flops 456228864 | bytes 2760705 | tf_op jit(solution)/shard_map/dot_general | solution.py:273
  45.8 3.3 %fusion.79 = (f32[6,256]{1,0:T(8,128)S(1)}, f32[6,256,256]{1,2,0:T(8,128)}) fusion(pred[256]{0:T(512)(128)(4,1)} %or_and_fusion, bf16[256,6,64]{0,2,1:T(8,128)(2,1)S(1)} %bitcast.103, bf16[256,6,64]{0,2,1:T(8,128)(2,1)S(1)} %bitcast.101, bf16[6,128,256]{1,2,0:T(8,128)(2,1)} %copy.116, bf16[6,128,256]{1,2,0:T(8,128)(2,1)} %collective-permute-done.1, ...), kind=kOutput, calls=%fused_computation.181 | convolution fusion | flops 56230144 | bytes 2758913 | tf_op jit(solution)/shard_map/sub | solution.py:281
  51.7 1.9 collective-permute-start.5
  53.7 3.6 %copy.120 = bf16[96,8,2,1536]{3,1,2,0:T(8,128)(2,1)S(1)} copy(bf16[96,8,2,1536]{3,2,1,0:T(2,128)(2,1)} %bitcast.82) | data formatting | bytes 9437184
  57.9 1.8 collective-permute-done.2
  59.7 2.4 %fusion.77 = (f32[256]{0:T(256)S(1)}, f32[256,768]{1,0:T(8,128)S(1)}, f32[256,768]{1,0:T(8,128)S(1)}) fusion(f32[768]{0:T(1024)S(1)} %get-tuple-element.128, bf16[128,768]{1,0:T(8,128)(2,1)S(1)} %bitcast.95, bf16[128,768]{1,0:T(8,128)(2,1)S(1)} %collective-permute-done, pred[]{:T(512)S(6)} %eq.44, f32[768]{0:T(1024)S(1)} %copy-done.50, ...), kind=kOutput, calls=%fused_computation.179 | convolution fusion | flops 311820032 | bytes 3546113 | tf_op jit(solution)/shard_map/dot_general | solution.py:292
  66.7 3.9 %fusion.1 = bf16[768,6144]{1,0:T(8,128)(2,1)} fusion(bf16[768,6144]{1,0:T(8,128)(2,1)} %shard_map.248, bf16[256,1536]{1,0:T(8,128)(2,1)S(1)} %get-tuple-element.94, bf16[256,1536]{1,0:T(8,128)(2,1)S(1)} %get-tuple-element.93, f32[256,768]{1,0:T(8,128)S(1)} %get-tuple-element.92, f32[768]{0:T(1024)S(1)} %copy-done.49, f32[768]{0:T(1024)S(1)} %get-tuple-element.81, ...), kind=kOutput, calls=%fused_computation.2 | convolution fusion | flops 1214447616 | bytes 7086080 | tf_op jit(solution)/shard_map/dot_general | solution.py:319
  70.6 2.3 %fusion.2 = bf16[768,6144]{1,0:T(8,128)(2,1)} fusion(bf16[768,6144]{1,0:T(8,128)(2,1)} %fusion.1, bf16[256,1536]{1,0:T(8,128)(2,1)S(1)} %get-tuple-element.95, f32[768]{0:T(1024)S(1)} %get-tuple-element.86, bf16[128,768]{1,0:T(8,128)(2,1)S(1)} %collective-permute-done.5, bf16[128,768]{1,0:T(8,128)(2,1)S(1)} %bitcast.109, pred[]{:T(512)S(6)} %eq.44), kind=kOutput, calls=%fused_computation.5 | convolution fusion | flops 607518720 | bytes 3542017 | tf_op jit(solution)/shard_map/dot_general | solution.py:310
  78.1 2.1 convolution_convert_fusion.8
  84.4 2.2 %fusion.3 = bf16[768,6144]{1,0:T(8,128)(2,1)} fusion(bf16[768,6144]{1,0:T(8,128)(2,1)} %fusion.7, bf16[256,384]{0,1:T(8,128)(2,1)S(1)} %bitcast.126, bf16[256,384]{0,1:T(8,128)(2,1)S(1)} %bitcast.113, bf16[256,384]{0,1:T(8,128)(2,1)S(1)} %bitcast.115, f32[768]{0:T(1024)S(1)} %copy-done.48, f32[768]{0:T(1024)S(1)} %get-tuple-element.84, ...), kind=kOutput, calls=%fused_computation.6 | convolution fusion | flops 458588160 | bytes 2760705 | tf_op jit(solution)/shard_map/dot_general | solution.py:357
  88.0 2.7 %convolution_convert_fusion.7 = bf16[256,768]{1,0:T(8,128)(2,1)} fusion(bf16[256,1536]{1,0:T(8,128)(2,1)} %copy-done.53, bf16[1536,768]{1,0:T(8,128)(2,1)S(1)} %copy-done), kind=kOutput, calls=%fused_computation.24 | convolution fusion | flops 604176384 | bytes 3538944 | tf_op jit(solution)/shard_map/dot_general | solution.py:302
  92.0 1.9 copy.107
  97.0 3.5 %convolution_convert_fusion.5 = bf16[256,768]{1,0:T(8,128)(2,1)} fusion(bf16[768,1152]{0,1:T(8,128)(2,1)} %bitcast.90, bf16[256,384]{0,1:T(8,128)(2,1)} %bitcast.127, bf16[256,384]{0,1:T(8,128)(2,1)} %bitcast.114, bf16[256,384]{0,1:T(8,128)(2,1)} %bitcast.116), kind=kOutput, calls=%fused_computation.22 | convolution fusion | flops 454950912 | bytes 2752512 | tf_op jit(solution)/shard_map/dot_general | solution.py:370
  100.9 2.0 collective-permute-done.4
  105.1 6.0 %collective-permute-done.8 = bf16[6,128,256]{1,2,0:T(8,128)(2,1)} collective-permute-done((bf16[6,128,256]{1,2,0:T(8,128)(2,1)}, bf16[6,128,256]{1,2,0:T(8,128)(2,1)}, u32[]{:S(2)}, u32[]{:S(2)}) %collective-permute-start.8) | collective-permute-done | bytes 393248 | tf_op jit(solution)/shard_map/ppermute | solution.py:147
  111.1 1.9 copy.108
  116.0 34.0 %shard_map.247 = (bf16[32768,256]{1,0:T(8,128)(2,1)}, f32[16,256]{1,0:T(8,128)}, f32[1,256]{1,0:T(1,128)}) custom-call(bf16[32768,256]{1,0:T(8,128)(2,1)} %bitcast.81, bf16[16,32768]{1,0:T(8,128)(2,1)} %pad.8.ds_ref, f32[1,256]{1,0:T(1,128)} %bitcast.122, bf16[16,256]{1,0:T(8,128)(2,1)} %pad.9.wt_ref), custom_call_target="tpu_custom_call" | custom-call | flops 704643072 | bytes 34603008 | tf_op jit(solution)/shard_map/pallas_call | solution.py:97
  154.3 2.5 %convolution_multiply_fusion.2 = f32[1,256]{1,0:T(1,128)} fusion(bf16[256,4608]{1,0:T(8,128)(2,1)S(1)} %copy-done.6, f32[1,4608]{1,0:T(1,128)S(1)} %get-tuple-element.112, f32[1,256]{1,0:T(1,128)S(1)} %copy-done.36), kind=kOutput, calls=%fused_computation.46 | convolution fusion | flops 14157824 | bytes 2379776 | tf_op jit(solution)/shard_map/dot_general | solution.py:409
  158.1 1.8 collective-permute-start.10
  160.3 3.6 %collective-permute-done.15 = f32[1,3328]{1,0:T(1,128)S(1)} collective-permute-done((f32[1,3328]{1,0:T(1,128)S(1)}, f32[1,3328]{1,0:T(1,128)S(1)}, u32[]{:S(2)}, u32[]{:S(2)}) %collective-permute-start.15) | collective-permute-done | bytes 13344 | tf_op jit(solution)/shard_map/ppermute | solution.py:180
  163.8 1.8 collective-permute-start.16
  167.7 2.7 %collective-permute-start.17 = (f32[1,3328]{1,0:T(1,128)S(1)}, f32[1,3328]{1,0:T(1,128)S(1)}, u32[]{:S(2)}, u32[]{:S(2)}) collective-permute-start(f32[1,3328]{1,0:T(1,128)S(1)} %add.184), channel_id=1, source_target_pairs={{0,16},{2,18},{4,20},{6,22},{8,24},{10,26},{12,28},{14,30},{16,0},... | collective-permute-start | bytes 39944 | tf_op jit(solution)/shard_map/ppermute | solution.py:180
  170.5 2.7 %collective-permute-start.12 = (f32[8,5632]{1,0:T(8,128)S(1)}, f32[8,5632]{1,0:T(8,128)S(1)}, u32[]{:S(2)}, u32[]{:S(2)}) collective-permute-start(f32[8,5632]{1,0:T(8,128)S(1)} %maximum_select_fusion.9), channel_id=1, source_target_pairs={{0,16},{2,18},{4,20},{6,22},{8,24},{10,26},{12,28},{14,30},{16,0},... | collective-permute-start | bytes 540680 | tf_op jit(solution)/shard_map/ppermute | solution.py:165
  175.6 6.8 %collective-permute-done.12 = f32[8,5632]{1,0:T(8,128)S(1)} collective-permute-done((f32[8,5632]{1,0:T(8,128)S(1)}, f32[8,5632]{1,0:T(8,128)S(1)}, u32[]{:S(2)}, u32[]{:S(2)}) %collective-permute-start.12) | collective-permute-done | bytes 180256 | tf_op jit(solution)/shard_map/ppermute | solution.py:165
  183.7 4.2 %fusion.47 = f32[256,4608]{1,0:T(8,128)} fusion(bf16[16,256]{1,0:T(8,128)(2,1)S(1)} %multiply_convert_fusion.7, f32[16,5632]{1,0:T(8,128)S(1)} %maximum_select_fusion.8), kind=kOutput, calls=%fused_computation.105 | convolution fusion | flops 226492416 | bytes 5021696 | tf_op jit(solution)/shard_map/dot_general | solution.py:407
  187.9 12.8 %reduce-scatter.2.cloned.1.call-done = bf16[48,6144]{1,0:T(8,128)(2,1)} async-done(((bf16[768,6144]{1,0:T(8,128)(2,1)}), bf16[48,6144]{1,0:T(8,128)(2,1)}) %reduce-scatter.2.cloned.1.call-update) | async-done | bytes 589840 | tf_op jit(solution)/shard_map/reduce_scatter | solution.py:368
  (225 shorter events, 52.3 us)
Async XLA Ops:
  7.2 56.7 %copy-start = (bf16[1536,768]{1,0:T(8,128)(2,1)S(1)}, bf16[1536,768]{1,0:T(8,128)(2,1)}, u32[]{:S(2)}) copy-start(bf16[1536,768]{1,0:T(8,128)(2,1)} %param.28) | copy-start | bytes 7077892
  7.2 193.5 %reduce-scatter.2.cloned.1.call-start = ((), (), s32[]{:S(2)}) async-start(), calls=%async_computation.1 | async-start | bytes 10027008 | tf_op jit(solution)/shard_map/reduce_scatter | solution.py:368
  7.2 35.2 %collective-permute-start = (bf16[128,768]{1,0:T(8,128)(2,1)}, bf16[128,768]{1,0:T(8,128)(2,1)S(1)}, u32[]{:S(2)}, u32[]{:S(2)}) collective-permute-start(bf16[128,768]{1,0:T(8,128)(2,1)} %bitcast.91), channel_id=1, source_target_pairs={{0,1},{1,0},{2,3},{3,2},{4,5},{5,4},{6,7},{7,6},{8,9},{9,8},{10,11... | collective-permute-start | bytes 589832 | tf_op jit(solution)/shard_map/ppermute | solution.py:147
  10.3 47.6 %collective-permute-start.3 = (bf16[384,768]{1,0:T(8,128)(2,1)}, bf16[384,768]{1,0:T(8,128)(2,1)}, u32[]{:S(2)}, u32[]{:S(2)}) collective-permute-start(bf16[384,768]{1,0:T(8,128)(2,1)} %param.25), channel_id=1, source_target_pairs={{0,1},{1,0},{2,3},{3,2},{4,5},{5,4},{6,7},{7,6},{8,9},{9,8},{10,11... | collective-permute-start | bytes 1769480 | tf_op jit(solution)/shard_map/ppermute | solution.py:147
  29.2 6.7 %copy-start.25 = (f32[4608]{0:T(1024)S(1)}, f32[4608]{0:T(1024)}, u32[]{:S(2)}) copy-start(f32[4608]{0:T(1024)} %param.21) | copy-start | bytes 55300
  29.2 8.0 %copy-start.9 = (bf16[6,128,256]{2,1,0:T(8,128)(2,1)S(1)}, bf16[6,128,256]{2,1,0:T(8,128)(2,1)}, u32[]{:S(2)}) copy-start(bf16[6,128,256]{2,1,0:T(8,128)(2,1)} %get-tuple-element.103) | copy-start | bytes 1179652
  31.2 14.6 %collective-permute-start.1 = (bf16[6,128,256]{1,2,0:T(8,128)(2,1)}, bf16[6,128,256]{1,2,0:T(8,128)(2,1)}, u32[]{:S(2)}, u32[]{:S(2)}) collective-permute-start(bf16[6,128,256]{1,2,0:T(8,128)(2,1)} %copy.117), channel_id=1, source_target_pairs={{0,1},{1,0},{2,3},{3,2},{4,5},{5,4},{6,7},{7,6},{8,9},{9,8},{10,11... | collective-permute-start | bytes 1179656 | tf_op jit(solution)/shard_map/ppermute | solution.py:147
  37.2 47.2 %copy-start.26 = (f32[768]{0:T(1024)}, f32[768]{0:T(1024)S(1)}, u32[]{:S(2)}) copy-start(f32[768]{0:T(1024)S(1)} %get-tuple-element.84) | copy-start | bytes 9220
  51.6 8.1 %collective-permute-start.2 = (bf16[256,384]{1,0:T(8,128)(2,1)}, bf16[256,384]{1,0:T(8,128)(2,1)}, u32[]{:S(2)}, u32[]{:S(2)}) collective-permute-start(bf16[256,384]{1,0:T(8,128)(2,1)} %copy.101), channel_id=1, source_target_pairs={{0,1},{1,0},{2,3},{3,2},{4,5},{5,4},{6,7},{7,6},{8,9},{9,8},{10,11... | collective-permute-start | bytes 589832 | tf_op jit(solution)/shard_map/ppermute | solution.py:147
  51.7 12.2 %collective-permute-start.5 = (bf16[128,768]{1,0:T(8,128)(2,1)S(1)}, bf16[128,768]{1,0:T(8,128)(2,1)S(1)}, u32[]{:S(2)}, u32[]{:S(2)}) collective-permute-start(bf16[128,768]{1,0:T(8,128)(2,1)S(1)} %bitcast.107), channel_id=1, source_target_pairs={{0,1},{1,0},{2,3},{3,2},{4,5},{5,4},{6,7},{7,6},{8,9},{9,8},{10,11... | collective-permute-start | bytes 589832 | tf_op jit(solution)/shard_map/ppermute | solution.py:147
  62.1 13.3 %copy-start.1 = (f32[256,768]{1,0:T(8,128)}, f32[256,768]{1,0:T(8,128)S(1)}, u32[]{:S(2)}) copy-start(f32[256,768]{1,0:T(8,128)S(1)} %get-tuple-element.92) | copy-start | bytes 2359300
  63.9 11.5 %copy-start.19 = (bf16[128,768]{1,0:T(8,128)(2,1)}, bf16[128,768]{1,0:T(8,128)(2,1)S(1)}, u32[]{:S(2)}) copy-start(bf16[128,768]{1,0:T(8,128)(2,1)S(1)} %collective-permute-done.5) | copy-start | bytes 589828
  66.6 7.8 %collective-permute-start.6 = (bf16[256,768]{1,0:T(8,128)(2,1)S(1)}, bf16[256,768]{1,0:T(8,128)(2,1)S(1)}, u32[]{:S(2)}, u32[]{:S(2)}) collective-permute-start(bf16[256,768]{1,0:T(8,128)(2,1)S(1)} %convolution_convert_fusion.6), channel_id=1, source_target_pairs={{0,1},{1,0},{2,3},{3,2},{4,5},{5,4},{6,7},{7,6},{8,9},{9,8},{10,11... | collective-permute-start | bytes 1179656 | tf_op jit(solution)/shard_map/ppermute | solution.py:147
  90.6 12.3 %collective-permute-start.4 = (bf16[256,768]{1,0:T(8,128)(2,1)}, bf16[256,768]{1,0:T(8,128)(2,1)}, u32[]{:S(2)}, u32[]{:S(2)}) collective-permute-start(bf16[256,768]{1,0:T(8,128)(2,1)} %convolution_convert_fusion.7), channel_id=1, source_target_pairs={{0,1},{1,0},{2,3},{3,2},{4,5},{5,4},{6,7},{7,6},{8,9},{9,8},{10,11... | collective-permute-start | bytes 1179656 | tf_op jit(solution)/shard_map/ppermute | solution.py:147
  95.3 7.7 %copy-start.18 = (bf16[1,128,768]{2,1,0:T(8,128)(2,1)S(1)}, bf16[1,128,768]{2,1,0:T(8,128)(2,1)}, u32[]{:S(2)}) copy-start(bf16[1,128,768]{2,1,0:T(8,128)(2,1)} %param.29) | copy-start | bytes 589828
  95.3 7.7 %copy-start.20 = (bf16[128,768]{1,0:T(8,128)(2,1)S(1)}, bf16[128,768]{1,0:T(8,128)(2,1)}, u32[]{:S(2)}) copy-start(bf16[128,768]{1,0:T(8,128)(2,1)} %copy-done.19) | copy-start | bytes 589828
  95.3 7.6 %copy-start.30 = (f32[768]{0:T(1024)S(1)}, f32[768]{0:T(1024)}, u32[]{:S(2)}) copy-start(f32[768]{0:T(1024)} %get-tuple-element.85) | copy-start | bytes 9220
  95.3 15.8 %collective-permute-start.8 = (bf16[6,128,256]{1,2,0:T(8,128)(2,1)}, bf16[6,128,256]{1,2,0:T(8,128)(2,1)}, u32[]{:S(2)}, u32[]{:S(2)}) collective-permute-start(bf16[6,128,256]{1,2,0:T(8,128)(2,1)} %get-tuple-element.102), channel_id=1, source_target_pairs={{0,1},{1,0},{2,3},{3,2},{4,5},{5,4},{6,7},{7,6},{8,9},{9,8},{10,11... | collective-permute-start | bytes 1179656 | tf_op jit(solution)/shard_map/ppermute | solution.py:147
  100.6 51.9 %collective-permute-start.7 = (bf16[256,768]{1,0:T(8,128)(2,1)}, bf16[256,768]{1,0:T(8,128)(2,1)}, u32[]{:S(2)}, u32[]{:S(2)}) collective-permute-start(bf16[256,768]{1,0:T(8,128)(2,1)} %convolution_convert_fusion.5), channel_id=1, source_target_pairs={{0,1},{1,0},{2,3},{3,2},{4,5},{5,4},{6,7},{7,6},{8,9},{9,8},{10,11... | collective-permute-start | bytes 1179656 | tf_op jit(solution)/shard_map/ppermute | solution.py:147
  116.0 36.5 %copy-start.27 = (f32[768]{0:T(1024)S(1)}, f32[768]{0:T(1024)}, u32[]{:S(2)}) copy-start(f32[768]{0:T(1024)} %copy-done.26) | copy-start | bytes 9220
  116.0 36.5 %copy-start.39 = (f32[256]{0:T(256)S(1)}, f32[256]{0:T(256)}, u32[]{:S(2)}) copy-start(f32[256]{0:T(256)} %copy-done.37) | copy-start | bytes 3076
  116.0 36.5 %copy-start.46 = (f32[256]{0:T(256)S(1)}, f32[256]{0:T(256)}, u32[]{:S(2)}) copy-start(f32[256]{0:T(256)} %copy-done.43) | copy-start | bytes 3076
  151.8 5.0 %collective-permute-start.13 = (f32[1,3328]{1,0:T(1,128)S(1)}, f32[1,3328]{1,0:T(1,128)S(1)}, u32[]{:S(2)}, u32[]{:S(2)}) collective-permute-start(f32[1,3328]{1,0:T(1,128)S(1)} %broadcast_in_dim.61), channel_id=1, source_target_pairs={{0,1},{1,0},{2,3},{3,2},{4,5},{5,4},{6,7},{7,6},{8,9},{9,8},{10,11... | collective-permute-start | bytes 39944 | tf_op jit(solution)/shard_map/ppermute | solution.py:147
  154.3 18.9 %copy-start.5 = (f32[256,768]{1,0:T(8,128)S(1)}, f32[256,768]{1,0:T(8,128)}, u32[]{:S(2)}) copy-start(f32[256,768]{1,0:T(8,128)} %copy-done.3) | copy-start | bytes 2359300
  156.8 1.2 collective-permute-start.9
  156.8 3.0 %collective-permute-start.14 = (f32[1,3328]{1,0:T(1,128)S(1)}, f32[1,3328]{1,0:T(1,128)S(1)}, u32[]{:S(2)}, u32[]{:S(2)}) collective-permute-start(f32[1,3328]{1,0:T(1,128)S(1)} %reshape_add_fusion), channel_id=1, source_target_pairs={{0,2},{2,0},{4,6},{6,4},{8,10},{10,8},{12,14},{14,12},{16,18},{18,... | collective-permute-start | bytes 39944 | tf_op jit(solution)/shard_map/ppermute | solution.py:180
  158.1 7.5 %collective-permute-start.10 = (f32[2,5632]{1,0:T(2,128)S(1)}, f32[2,5632]{1,0:T(2,128)S(1)}, u32[]{:S(2)}, u32[]{:S(2)}) collective-permute-start(f32[2,5632]{1,0:T(2,128)S(1)} %maximum_select_fusion.12), channel_id=1, source_target_pairs={{0,4},{2,6},{4,0},{6,2},{8,12},{10,14},{12,8},{14,10},{16,20},{18,... | collective-permute-start | bytes 135176 | tf_op jit(solution)/shard_map/ppermute | solution.py:165
  159.9 3.9 %collective-permute-start.15 = (f32[1,3328]{1,0:T(1,128)S(1)}, f32[1,3328]{1,0:T(1,128)S(1)}, u32[]{:S(2)}, u32[]{:S(2)}) collective-permute-start(f32[1,3328]{1,0:T(1,128)S(1)} %add.182), channel_id=1, source_target_pairs={{0,4},{2,6},{4,0},{6,2},{8,12},{10,14},{12,8},{14,10},{16,20},{18,... | collective-permute-start | bytes 39944 | tf_op jit(solution)/shard_map/ppermute | solution.py:180
  163.8 3.9 %collective-permute-start.16 = (f32[1,3328]{1,0:T(1,128)S(1)}, f32[1,3328]{1,0:T(1,128)S(1)}, u32[]{:S(2)}, u32[]{:S(2)}) collective-permute-start(f32[1,3328]{1,0:T(1,128)S(1)} %add.183), channel_id=1, source_target_pairs={{0,8},{2,10},{4,12},{6,14},{8,0},{10,2},{12,4},{14,6},{16,24},{18,... | collective-permute-start | bytes 39944 | tf_op jit(solution)/shard_map/ppermute | solution.py:180
  165.7 4.8 %collective-permute-start.11 = (f32[4,5632]{1,0:T(4,128)S(1)}, f32[4,5632]{1,0:T(4,128)S(1)}, u32[]{:S(2)}, u32[]{:S(2)}) collective-permute-start(f32[4,5632]{1,0:T(4,128)S(1)} %maximum_select_fusion.11), channel_id=1, source_target_pairs={{0,8},{2,10},{4,12},{6,14},{8,0},{10,2},{12,4},{14,6},{16,24},{18,... | collective-permute-start | bytes 270344 | tf_op jit(solution)/shard_map/ppermute | solution.py:165
  167.7 6.4 %collective-permute-start.17 = (f32[1,3328]{1,0:T(1,128)S(1)}, f32[1,3328]{1,0:T(1,128)S(1)}, u32[]{:S(2)}, u32[]{:S(2)}) collective-permute-start(f32[1,3328]{1,0:T(1,128)S(1)} %add.184), channel_id=1, source_target_pairs={{0,16},{2,18},{4,20},{6,22},{8,24},{10,26},{12,28},{14,30},{16,0},... | collective-permute-start | bytes 39944 | tf_op jit(solution)/shard_map/ppermute | solution.py:180
  170.5 11.8 %collective-permute-start.12 = (f32[8,5632]{1,0:T(8,128)S(1)}, f32[8,5632]{1,0:T(8,128)S(1)}, u32[]{:S(2)}, u32[]{:S(2)}) collective-permute-start(f32[8,5632]{1,0:T(8,128)S(1)} %maximum_select_fusion.9), channel_id=1, source_target_pairs={{0,16},{2,18},{4,20},{6,22},{8,24},{10,26},{12,28},{14,30},{16,0},... | collective-permute-start | bytes 540680 | tf_op jit(solution)/shard_map/ppermute | solution.py:165
  (41 other events, 120.0 us)
Sparse Core Ops, SparseCore 0:
  86.7 113.8 reduce-scatter.1

commit v16 on v13

--- a/solution.py
+++ b/solution.py
@@ -156,20 +156,28 @@
     )
 
 
+def bit_reverse(value, bits):
+    out = 0
+    for bit in range(bits):
+        out |= ((value >> bit) & 1) << (bits - 1 - bit)
+    return out
+
+
 def dp_gather(values):
     count = lax.axis_size("dp")
     index = lax.axis_index("dp")
+    bits = count.bit_length() - 1
     block = values
-    step = 1
-    while step < count:
+    step = count // 2
+    while step >= 1:
         other = lax.ppermute(block, "dp", [(i, i ^ step) for i in range(count)])
         block = jnp.where(
             (index & step) == 0,
             jnp.concatenate([block, other], axis=0),
             jnp.concatenate([other, block], axis=0),
         )
-        step *= 2
-    return block
+        step //= 2
+    return block[jnp.array([bit_reverse(i, bits) for i in range(count)])]
 
 
 def dp_sum(values):

time: 214 us -> 214 us (level)
  waiting for transfers between devices: 36.7 us -> 34.5 us
    ppermute x4, waiting for transfers between devices: 7.09 us -> 1.8 us  [dp_gather(): other = lax.ppermute(block, 'dp', [(i, i ^ step) for i in range(count)])]
    reduce_scatter x1, waiting for transfers between devices: 13.1 us -> 16.4 us  [shards(): lax.psum_scatter(packed, 'dp', scatter_dimension=0, tiled=True)]
  transfers between devices with their start and end apart: 19 -> 19, of which waited for: 9 -> 9; matrix products, arithmetic and copies ran while one was open for 33% -> 34% of each run, Pallas kernels for 23% -> 23%
where the time goes in v16:
time: 214 us; the launch traced here: 213 us
  Pallas kernels  49.4 us (23%)
  matrix products  42 us (20%)
  local copies, waits for them, and re-layouts  34.7 us (16%)
  waiting for transfers between devices  34.5 us (16%)
  starting transfers between devices  21.4 us (10%)
  between operations  15.5 us (7%)
  other arithmetic  15.1 us (7%)
    pallas_call x1, Pallas kernels, pair_backward(): pl.pallas_call(pair_backward_kernel, grid=(m // tile,), in_specs=[pl.Bloc...  34 us
    unnamed x124, local copies, waits for them, and re-layouts  19.7 us
    reduce_scatter x1, waiting for transfers between devices, shards(): lax.psum_scatter(packed, 'dp', scatter_dimension=0, tiled=True)  16.4 us
    pallas_call x1, Pallas kernels, pair_forward(): pl.pallas_call(pair_forward_kernel, grid=(m // tile,), in_specs=[pl.Block...  15.4 us
    ppermute x10, waiting for transfers between devices, swap_heads(): return lax.ppermute(values, 'head', [(0, 1), (1, 0)])  11.4 us
    ppermute x10, starting transfers between devices, swap_heads(): return lax.ppermute(values, 'head', [(0, 1), (1, 0)])  10.3 us
    ppermute x4, starting transfers between devices, dp_gather(): other = lax.ppermute(block, 'dp', [(i, i ^ step) for i in range(count)])  6.77 us
    ppermute x4, waiting for transfers between devices, dp_sum(): other = lax.ppermute(values, 'dp', [(i, i ^ step) for i in range(count)])  4.9 us
  transfers between devices with their start and end apart: 19, of which 9 were waited for; matrix products, arithmetic and copies ran while one was open for 34% of the time, Pallas kernels for 23%

profile of v16, /device:TPU:0, one launch (start us, length us, event | category | flops | bytes accessed | tf_op | source)
XLA Modules:
  0.0 212.7 jit_solution(661552667622744647)
XLA Ops:
  7.2 3.0 %collective-permute-start = (bf16[128,768]{1,0:T(8,128)(2,1)}, bf16[128,768]{1,0:T(8,128)(2,1)S(1)}, u32[]{:S(2)}, u32[]{:S(2)}) collective-permute-start(bf16[128,768]{1,0:T(8,128)(2,1)} %bitcast.91), channel_id=1, source_target_pairs={{0,1},{1,0},{2,3},{3,2},{4,5},{5,4},{6,7},{7,6},{8,9},{9,8},{10,11... | collective-permute-start | bytes 589832 | tf_op jit(solution)/shard_map/ppermute | solution.py:147
  11.8 15.4 %shard_map.255 = bf16[12,32768]{1,0:T(8,128)(2,1)} custom-call(bf16[32768,256]{1,0:T(8,128)(2,1)} %bitcast.80, f32[1,256]{1,0:T(1,128)} %bitcast.122, bf16[256,12]{1,0:T(8,128)(2,1)} %copy.54.wt_ref), custom_call_target="tpu_custom_call" | custom-call | flops 352321536 | bytes 17563648 | tf_op jit(solution)/shard_map/pallas_call | solution.py:50
  29.7 2.0 copy.75
  31.6 1.9 collective-permute-start.1
  34.3 2.1 convolution_reduce_fusion
  38.5 3.9 %copy.50 = bf16[768,3,384]{0,2,1:T(8,128)(2,1)} copy(bf16[768,3,384]{2,0,1:T(8,128)(2,1)} %param.23) | data formatting | bytes 3538944 | tf_op args[7]
  43.4 2.3 %convolution_convert_fusion.3 = bf16[256,1152]{1,0:T(8,128)(2,1)S(1)} fusion(bf16[768,1152]{0,1:T(8,128)(2,1)} %bitcast.89, f32[768]{0:T(1024)S(1)} %get-tuple-element.57, f32[768]{0:T(1024)S(1)} %get-tuple-element.58, f32[256]{0:T(256)S(1)} %add_rsqrt_fusion.1, f32[256]{0:T(256)S(1)} %broadcast_multiply_fusion.5, bf16[128,768]{1,0:T(8,128)(2,1)S(1)} %bitcast.94, ...), kind=kOutput, calls=%fused_computation.8 | convolution fusion | flops 456228864 | bytes 2760705 | tf_op jit(solution)/shard_map/dot_general | solution.py:281
  46.2 3.3 %fusion.79 = (f32[6,256]{1,0:T(8,128)S(1)}, f32[6,256,256]{1,2,0:T(8,128)}) fusion(pred[256]{0:T(512)(128)(4,1)} %or_and_fusion, bf16[256,6,64]{0,2,1:T(8,128)(2,1)S(1)} %bitcast.103, bf16[256,6,64]{0,2,1:T(8,128)(2,1)S(1)} %bitcast.101, bf16[6,128,256]{1,2,0:T(8,128)(2,1)} %copy.74, bf16[6,128,256]{1,2,0:T(8,128)(2,1)} %collective-permute-done.1, pred[]{:T(512)S(6)} %eq.44), kind=kOutput, calls=%fused_computation.182 | convolution fusion | flops 56230144 | bytes 2758913 | tf_op jit(solution)/shard_map/sub | solution.py:289
  52.2 1.9 collective-permute-start.5
  54.2 3.6 %copy.78 = bf16[96,8,2,1536]{3,1,2,0:T(8,128)(2,1)S(1)} copy(bf16[96,8,2,1536]{3,2,1,0:T(2,128)(2,1)} %bitcast.82) | data formatting | bytes 9437184
  58.4 1.8 collective-permute-done.2
  60.2 2.4 %fusion.77 = (f32[256]{0:T(256)S(1)}, f32[256,768]{1,0:T(8,128)S(1)}, f32[256,768]{1,0:T(8,128)S(1)}) fusion(f32[768]{0:T(1024)S(1)} %get-tuple-element.102, bf16[128,768]{1,0:T(8,128)(2,1)S(1)} %bitcast.95, bf16[128,768]{1,0:T(8,128)(2,1)S(1)} %collective-permute-done, pred[]{:T(512)S(6)} %eq.44, f32[768]{0:T(1024)S(1)} %copy-done.50, ...), kind=kOutput, calls=%fused_computation.180 | convolution fusion | flops 311820032 | bytes 3546113 | tf_op jit(solution)/shard_map/dot_general | solution.py:300
  67.2 3.9 %fusion.1 = bf16[768,6144]{1,0:T(8,128)(2,1)} fusion(bf16[768,6144]{1,0:T(8,128)(2,1)} %shard_map.257, bf16[256,1536]{1,0:T(8,128)(2,1)S(1)} %get-tuple-element.68, bf16[256,1536]{1,0:T(8,128)(2,1)S(1)} %get-tuple-element.67, f32[256,768]{1,0:T(8,128)S(1)} %get-tuple-element.66, f32[768]{0:T(1024)S(1)} %copy-done.49, f32[768]{0:T(1024)S(1)} %get-tuple-element.55, ...), kind=kOutput, calls=%fused_computation.3 | convolution fusion | flops 1214447616 | bytes 7086080 | tf_op jit(solution)/shard_map/dot_general | solution.py:327
  71.1 2.3 %fusion.2 = bf16[768,6144]{1,0:T(8,128)(2,1)} fusion(bf16[768,6144]{1,0:T(8,128)(2,1)} %fusion.1, bf16[256,1536]{1,0:T(8,128)(2,1)S(1)} %get-tuple-element.69, f32[768]{0:T(1024)S(1)} %get-tuple-element.60, bf16[128,768]{1,0:T(8,128)(2,1)S(1)} %collective-permute-done.5, bf16[128,768]{1,0:T(8,128)(2,1)S(1)} %bitcast.109, pred[]{:T(512)S(6)} %eq.44), kind=kOutput, calls=%fused_computation.6 | convolution fusion | flops 607518720 | bytes 3542017 | tf_op jit(solution)/shard_map/dot_general | solution.py:318
  78.6 2.1 convolution_convert_fusion.8
  84.9 2.2 %fusion.3 = bf16[768,6144]{1,0:T(8,128)(2,1)} fusion(bf16[768,6144]{1,0:T(8,128)(2,1)} %fusion.7, bf16[256,384]{0,1:T(8,128)(2,1)S(1)} %bitcast.127, bf16[256,384]{0,1:T(8,128)(2,1)S(1)} %bitcast.113, bf16[256,384]{0,1:T(8,128)(2,1)S(1)} %bitcast.115, f32[768]{0:T(1024)S(1)} %copy-done.48, f32[768]{0:T(1024)S(1)} %get-tuple-element.58, ...), kind=kOutput, calls=%fused_computation.7 | convolution fusion | flops 458588160 | bytes 2760705 | tf_op jit(solution)/shard_map/dot_general | solution.py:365
  89.1 2.7 %convolution_convert_fusion.7 = bf16[256,768]{1,0:T(8,128)(2,1)} fusion(bf16[256,1536]{1,0:T(8,128)(2,1)} %copy-done.53, bf16[1536,768]{1,0:T(8,128)(2,1)S(1)} %copy-done), kind=kOutput, calls=%fused_computation.25 | convolution fusion | flops 604176384 | bytes 3538944 | tf_op jit(solution)/shard_map/dot_general | solution.py:310
  93.2 1.9 copy.65
  98.1 3.5 %convolution_convert_fusion.5 = bf16[256,768]{1,0:T(8,128)(2,1)} fusion(bf16[768,1152]{0,1:T(8,128)(2,1)} %bitcast.90, bf16[256,384]{0,1:T(8,128)(2,1)} %bitcast.128, bf16[256,384]{0,1:T(8,128)(2,1)} %bitcast.114, bf16[256,384]{0,1:T(8,128)(2,1)} %bitcast.116), kind=kOutput, calls=%fused_computation.23 | convolution fusion | flops 454950912 | bytes 2752512 | tf_op jit(solution)/shard_map/dot_general | solution.py:378
  102.0 2.1 collective-permute-done.4
  106.3 5.9 %collective-permute-done.8 = bf16[6,128,256]{1,2,0:T(8,128)(2,1)} collective-permute-done((bf16[6,128,256]{1,2,0:T(8,128)(2,1)}, bf16[6,128,256]{1,2,0:T(8,128)(2,1)}, u32[]{:S(2)}, u32[]{:S(2)}) %collective-permute-start.8) | collective-permute-done | bytes 393248 | tf_op jit(solution)/shard_map/ppermute | solution.py:147
  112.2 1.9 copy.66
  117.1 34.0 %shard_map.256 = (bf16[32768,256]{1,0:T(8,128)(2,1)}, f32[16,256]{1,0:T(8,128)}, f32[1,256]{1,0:T(1,128)}) custom-call(bf16[32768,256]{1,0:T(8,128)(2,1)} %bitcast.81, bf16[16,32768]{1,0:T(8,128)(2,1)} %pad.8.ds_ref, f32[1,256]{1,0:T(1,128)} %bitcast.123, bf16[16,256]{1,0:T(8,128)(2,1)} %pad.9.wt_ref), custom_call_target="tpu_custom_call" | custom-call | flops 704643072 | bytes 34603008 | tf_op jit(solution)/shard_map/pallas_call | solution.py:97
  155.4 2.5 %convolution_multiply_fusion.2 = f32[1,256]{1,0:T(1,128)} fusion(bf16[256,4608]{1,0:T(8,128)(2,1)S(1)} %copy-done.6, f32[1,4608]{1,0:T(1,128)S(1)} %get-tuple-element.86, f32[1,256]{1,0:T(1,128)S(1)} %copy-done.36), kind=kOutput, calls=%fused_computation.47 | convolution fusion | flops 14157824 | bytes 2379776 | tf_op jit(solution)/shard_map/dot_general | solution.py:417
  157.9 2.8 %collective-permute-start.9 = (f32[1,5632]{1,0:T(1,128)S(1)}, f32[1,5632]{1,0:T(1,128)S(1)}, u32[]{:S(2)}, u32[]{:S(2)}) collective-permute-start(f32[1,5632]{1,0:T(1,128)S(1)} %constant_dynamic-update-slice_fusion.6), channel_id=1, source_target_pairs={{0,16},{2,18},{4,20},{6,22},{8,24},{10,26},{12,28},{14,30},{16,0},... | collective-permute-start | bytes 67592 | tf_op jit(solution)/shard_map/ppermute | solution.py:173
  160.8 1.8 collective-permute-done.9
  162.7 2.1 collective-permute-start.10
  166.3 2.3 %collective-permute-done.15 = f32[1,3328]{1,0:T(1,128)S(1)} collective-permute-done((f32[1,3328]{1,0:T(1,128)S(1)}, f32[1,3328]{1,0:T(1,128)S(1)}, u32[]{:S(2)}, u32[]{:S(2)}) %collective-permute-start.15) | collective-permute-done | bytes 13344 | tf_op jit(solution)/shard_map/ppermute | solution.py:188
  168.8 1.8 collective-permute-start.11
  172.4 2.7 %collective-permute-start.17 = (f32[1,3328]{1,0:T(1,128)S(1)}, f32[1,3328]{1,0:T(1,128)S(1)}, u32[]{:S(2)}, u32[]{:S(2)}) collective-permute-start(f32[1,3328]{1,0:T(1,128)S(1)} %add.188), channel_id=1, source_target_pairs={{0,16},{2,18},{4,20},{6,22},{8,24},{10,26},{12,28},{14,30},{16,0},... | collective-permute-start | bytes 39944 | tf_op jit(solution)/shard_map/ppermute | solution.py:188
  180.5 4.2 %fusion.47 = f32[256,4608]{1,0:T(8,128)} fusion(bf16[16,256]{1,0:T(8,128)(2,1)S(1)} %multiply_convert_fusion.7, f32[16,5632]{1,0:T(8,128)S(1)} %gather_fusion), kind=kOutput, calls=%fused_computation.106 | convolution fusion | flops 226492416 | bytes 5021696 | tf_op jit(solution)/shard_map/dot_general | solution.py:415
  184.8 16.4 %reduce-scatter.2.cloned.1.call-done = bf16[48,6144]{1,0:T(8,128)(2,1)} async-done(((bf16[768,6144]{1,0:T(8,128)(2,1)}), bf16[48,6144]{1,0:T(8,128)(2,1)}) %reduce-scatter.2.cloned.1.call-update) | async-done | bytes 589840 | tf_op jit(solution)/shard_map/reduce_scatter | solution.py:376
  (226 shorter events, 54.6 us)
Async XLA Ops:
  7.2 57.2 %copy-start = (bf16[1536,768]{1,0:T(8,128)(2,1)S(1)}, bf16[1536,768]{1,0:T(8,128)(2,1)}, u32[]{:S(2)}) copy-start(bf16[1536,768]{1,0:T(8,128)(2,1)} %param.29) | copy-start | bytes 7077892
  7.2 194.0 %reduce-scatter.2.cloned.1.call-start = ((), (), s32[]{:S(2)}) async-start(), calls=%async_computation.1 | async-start | bytes 10027008 | tf_op jit(solution)/shard_map/reduce_scatter | solution.py:376
  7.2 35.7 %collective-permute-start = (bf16[128,768]{1,0:T(8,128)(2,1)}, bf16[128,768]{1,0:T(8,128)(2,1)S(1)}, u32[]{:S(2)}, u32[]{:S(2)}) collective-permute-start(bf16[128,768]{1,0:T(8,128)(2,1)} %bitcast.91), channel_id=1, source_target_pairs={{0,1},{1,0},{2,3},{3,2},{4,5},{5,4},{6,7},{7,6},{8,9},{9,8},{10,11... | collective-permute-start | bytes 589832 | tf_op jit(solution)/shard_map/ppermute | solution.py:147
  10.3 48.1 %collective-permute-start.3 = (bf16[384,768]{1,0:T(8,128)(2,1)}, bf16[384,768]{1,0:T(8,128)(2,1)}, u32[]{:S(2)}, u32[]{:S(2)}) collective-permute-start(bf16[384,768]{1,0:T(8,128)(2,1)} %param.26), channel_id=1, source_target_pairs={{0,1},{1,0},{2,3},{3,2},{4,5},{5,4},{6,7},{7,6},{8,9},{9,8},{10,11... | collective-permute-start | bytes 1769480 | tf_op jit(solution)/shard_map/ppermute | solution.py:147
  29.7 6.7 %copy-start.25 = (f32[4608]{0:T(1024)S(1)}, f32[4608]{0:T(1024)}, u32[]{:S(2)}) copy-start(f32[4608]{0:T(1024)} %param.22) | copy-start | bytes 55300
  29.7 8.0 %copy-start.9 = (bf16[6,128,256]{2,1,0:T(8,128)(2,1)S(1)}, bf16[6,128,256]{2,1,0:T(8,128)(2,1)}, u32[]{:S(2)}) copy-start(bf16[6,128,256]{2,1,0:T(8,128)(2,1)} %get-tuple-element.77) | copy-start | bytes 1179652
  31.6 14.6 %collective-permute-start.1 = (bf16[6,128,256]{1,2,0:T(8,128)(2,1)}, bf16[6,128,256]{1,2,0:T(8,128)(2,1)}, u32[]{:S(2)}, u32[]{:S(2)}) collective-permute-start(bf16[6,128,256]{1,2,0:T(8,128)(2,1)} %copy.75), channel_id=1, source_target_pairs={{0,1},{1,0},{2,3},{3,2},{4,5},{5,4},{6,7},{7,6},{8,9},{9,8},{10,11... | collective-permute-start | bytes 1179656 | tf_op jit(solution)/shard_map/ppermute | solution.py:147
  37.6 47.2 %copy-start.26 = (f32[768]{0:T(1024)}, f32[768]{0:T(1024)S(1)}, u32[]{:S(2)}) copy-start(f32[768]{0:T(1024)S(1)} %get-tuple-element.58) | copy-start | bytes 9220
  52.1 8.1 %collective-permute-start.2 = (bf16[256,384]{1,0:T(8,128)(2,1)}, bf16[256,384]{1,0:T(8,128)(2,1)}, u32[]{:S(2)}, u32[]{:S(2)}) collective-permute-start(bf16[256,384]{1,0:T(8,128)(2,1)} %copy.59), channel_id=1, source_target_pairs={{0,1},{1,0},{2,3},{3,2},{4,5},{5,4},{6,7},{7,6},{8,9},{9,8},{10,11... | collective-permute-start | bytes 589832 | tf_op jit(solution)/shard_map/ppermute | solution.py:147
  52.2 12.2 %collective-permute-start.5 = (bf16[128,768]{1,0:T(8,128)(2,1)S(1)}, bf16[128,768]{1,0:T(8,128)(2,1)S(1)}, u32[]{:S(2)}, u32[]{:S(2)}) collective-permute-start(bf16[128,768]{1,0:T(8,128)(2,1)S(1)} %bitcast.107), channel_id=1, source_target_pairs={{0,1},{1,0},{2,3},{3,2},{4,5},{5,4},{6,7},{7,6},{8,9},{9,8},{10,11... | collective-permute-start | bytes 589832 | tf_op jit(solution)/shard_map/ppermute | solution.py:147
  62.6 13.3 %copy-start.1 = (f32[256,768]{1,0:T(8,128)}, f32[256,768]{1,0:T(8,128)S(1)}, u32[]{:S(2)}) copy-start(f32[256,768]{1,0:T(8,128)S(1)} %get-tuple-element.66) | copy-start | bytes 2359300
  64.4 11.6 %copy-start.19 = (bf16[128,768]{1,0:T(8,128)(2,1)}, bf16[128,768]{1,0:T(8,128)(2,1)S(1)}, u32[]{:S(2)}) copy-start(bf16[128,768]{1,0:T(8,128)(2,1)S(1)} %collective-permute-done.5) | copy-start | bytes 589828
  67.1 7.8 %collective-permute-start.6 = (bf16[256,768]{1,0:T(8,128)(2,1)S(1)}, bf16[256,768]{1,0:T(8,128)(2,1)S(1)}, u32[]{:S(2)}, u32[]{:S(2)}) collective-permute-start(bf16[256,768]{1,0:T(8,128)(2,1)S(1)} %convolution_convert_fusion.6), channel_id=1, source_target_pairs={{0,1},{1,0},{2,3},{3,2},{4,5},{5,4},{6,7},{7,6},{8,9},{9,8},{10,11... | collective-permute-start | bytes 1179656 | tf_op jit(solution)/shard_map/ppermute | solution.py:147
  91.8 12.3 %collective-permute-start.4 = (bf16[256,768]{1,0:T(8,128)(2,1)}, bf16[256,768]{1,0:T(8,128)(2,1)}, u32[]{:S(2)}, u32[]{:S(2)}) collective-permute-start(bf16[256,768]{1,0:T(8,128)(2,1)} %convolution_convert_fusion.7), channel_id=1, source_target_pairs={{0,1},{1,0},{2,3},{3,2},{4,5},{5,4},{6,7},{7,6},{8,9},{9,8},{10,11... | collective-permute-start | bytes 1179656 | tf_op jit(solution)/shard_map/ppermute | solution.py:147
  96.4 7.7 %copy-start.18 = (bf16[1,128,768]{2,1,0:T(8,128)(2,1)S(1)}, bf16[1,128,768]{2,1,0:T(8,128)(2,1)}, u32[]{:S(2)}) copy-start(bf16[1,128,768]{2,1,0:T(8,128)(2,1)} %param.30) | copy-start | bytes 589828
  96.4 7.7 %copy-start.20 = (bf16[128,768]{1,0:T(8,128)(2,1)S(1)}, bf16[128,768]{1,0:T(8,128)(2,1)}, u32[]{:S(2)}) copy-start(bf16[128,768]{1,0:T(8,128)(2,1)} %copy-done.19) | copy-start | bytes 589828
  96.4 7.7 %copy-start.30 = (f32[768]{0:T(1024)S(1)}, f32[768]{0:T(1024)}, u32[]{:S(2)}) copy-start(f32[768]{0:T(1024)} %get-tuple-element.59) | copy-start | bytes 9220
  96.4 15.8 %collective-permute-start.8 = (bf16[6,128,256]{1,2,0:T(8,128)(2,1)}, bf16[6,128,256]{1,2,0:T(8,128)(2,1)}, u32[]{:S(2)}, u32[]{:S(2)}) collective-permute-start(bf16[6,128,256]{1,2,0:T(8,128)(2,1)} %get-tuple-element.76), channel_id=1, source_target_pairs={{0,1},{1,0},{2,3},{3,2},{4,5},{5,4},{6,7},{7,6},{8,9},{9,8},{10,11... | collective-permute-start | bytes 1179656 | tf_op jit(solution)/shard_map/ppermute | solution.py:147
  101.7 51.9 %collective-permute-start.7 = (bf16[256,768]{1,0:T(8,128)(2,1)}, bf16[256,768]{1,0:T(8,128)(2,1)}, u32[]{:S(2)}, u32[]{:S(2)}) collective-permute-start(bf16[256,768]{1,0:T(8,128)(2,1)} %convolution_convert_fusion.5), channel_id=1, source_target_pairs={{0,1},{1,0},{2,3},{3,2},{4,5},{5,4},{6,7},{7,6},{8,9},{9,8},{10,11... | collective-permute-start | bytes 1179656 | tf_op jit(solution)/shard_map/ppermute | solution.py:147
  117.1 36.5 %copy-start.27 = (f32[768]{0:T(1024)S(1)}, f32[768]{0:T(1024)}, u32[]{:S(2)}) copy-start(f32[768]{0:T(1024)} %copy-done.26) | copy-start | bytes 9220
  117.1 36.5 %copy-start.39 = (f32[256]{0:T(256)S(1)}, f32[256]{0:T(256)}, u32[]{:S(2)}) copy-start(f32[256]{0:T(256)} %copy-done.37) | copy-start | bytes 3076
  117.1 36.5 %copy-start.46 = (f32[256]{0:T(256)S(1)}, f32[256]{0:T(256)}, u32[]{:S(2)}) copy-start(f32[256]{0:T(256)} %copy-done.43) | copy-start | bytes 3076
  152.9 7.8 %collective-permute-start.13 = (f32[1,3328]{1,0:T(1,128)S(1)}, f32[1,3328]{1,0:T(1,128)S(1)}, u32[]{:S(2)}, u32[]{:S(2)}) collective-permute-start(f32[1,3328]{1,0:T(1,128)S(1)} %broadcast_in_dim.65), channel_id=1, source_target_pairs={{0,1},{1,0},{2,3},{3,2},{4,5},{5,4},{6,7},{7,6},{8,9},{9,8},{10,11... | collective-permute-start | bytes 39944 | tf_op jit(solution)/shard_map/ppermute | solution.py:147
  155.4 19.8 %copy-start.5 = (f32[256,768]{1,0:T(8,128)S(1)}, f32[256,768]{1,0:T(8,128)}, u32[]{:S(2)}) copy-start(f32[256,768]{1,0:T(8,128)} %copy-done.3) | copy-start | bytes 2359300
  157.9 4.7 %collective-permute-start.9 = (f32[1,5632]{1,0:T(1,128)S(1)}, f32[1,5632]{1,0:T(1,128)S(1)}, u32[]{:S(2)}, u32[]{:S(2)}) collective-permute-start(f32[1,5632]{1,0:T(1,128)S(1)} %constant_dynamic-update-slice_fusion.6), channel_id=1, source_target_pairs={{0,16},{2,18},{4,20},{6,22},{8,24},{10,26},{12,28},{14,30},{16,0},... | collective-permute-start | bytes 67592 | tf_op jit(solution)/shard_map/ppermute | solution.py:173
  160.8 4.0 %collective-permute-start.14 = (f32[1,3328]{1,0:T(1,128)S(1)}, f32[1,3328]{1,0:T(1,128)S(1)}, u32[]{:S(2)}, u32[]{:S(2)}) collective-permute-start(f32[1,3328]{1,0:T(1,128)S(1)} %reshape_add_fusion), channel_id=1, source_target_pairs={{0,2},{2,0},{4,6},{6,4},{8,10},{10,8},{12,14},{14,12},{16,18},{18,... | collective-permute-start | bytes 39944 | tf_op jit(solution)/shard_map/ppermute | solution.py:188
  162.7 6.0 %collective-permute-start.10 = (f32[2,5632]{1,0:T(2,128)S(1)}, f32[2,5632]{1,0:T(2,128)S(1)}, u32[]{:S(2)}, u32[]{:S(2)}) collective-permute-start(f32[2,5632]{1,0:T(2,128)S(1)} %maximum_select_fusion.12), channel_id=1, source_target_pairs={{0,8},{2,10},{4,12},{6,14},{8,0},{10,2},{12,4},{14,6},{16,24},{18,... | collective-permute-start | bytes 135176 | tf_op jit(solution)/shard_map/ppermute | solution.py:173
  164.8 3.8 %collective-permute-start.15 = (f32[1,3328]{1,0:T(1,128)S(1)}, f32[1,3328]{1,0:T(1,128)S(1)}, u32[]{:S(2)}, u32[]{:S(2)}) collective-permute-start(f32[1,3328]{1,0:T(1,128)S(1)} %add.186), channel_id=1, source_target_pairs={{0,4},{2,6},{4,0},{6,2},{8,12},{10,14},{12,8},{14,10},{16,20},{18,... | collective-permute-start | bytes 39944 | tf_op jit(solution)/shard_map/ppermute | solution.py:188
  168.6 3.8 %collective-permute-start.16 = (f32[1,3328]{1,0:T(1,128)S(1)}, f32[1,3328]{1,0:T(1,128)S(1)}, u32[]{:S(2)}, u32[]{:S(2)}) collective-permute-start(f32[1,3328]{1,0:T(1,128)S(1)} %add.187), channel_id=1, source_target_pairs={{0,8},{2,10},{4,12},{6,14},{8,0},{10,2},{12,4},{14,6},{16,24},{18,... | collective-permute-start | bytes 39944 | tf_op jit(solution)/shard_map/ppermute | solution.py:188
  168.8 6.3 %collective-permute-start.11 = (f32[4,5632]{1,0:T(4,128)S(1)}, f32[4,5632]{1,0:T(4,128)S(1)}, u32[]{:S(2)}, u32[]{:S(2)}) collective-permute-start(f32[4,5632]{1,0:T(4,128)S(1)} %maximum_select_fusion.11), channel_id=1, source_target_pairs={{0,4},{2,6},{4,0},{6,2},{8,12},{10,14},{12,8},{14,10},{16,20},{18,... | collective-permute-start | bytes 270344 | tf_op jit(solution)/shard_map/ppermute | solution.py:173
  172.4 4.7 %collective-permute-start.17 = (f32[1,3328]{1,0:T(1,128)S(1)}, f32[1,3328]{1,0:T(1,128)S(1)}, u32[]{:S(2)}, u32[]{:S(2)}) collective-permute-start(f32[1,3328]{1,0:T(1,128)S(1)} %add.188), channel_id=1, source_target_pairs={{0,16},{2,18},{4,20},{6,22},{8,24},{10,26},{12,28},{14,30},{16,0},... | collective-permute-start | bytes 39944 | tf_op jit(solution)/shard_map/ppermute | solution.py:188
  175.2 3.4 %collective-permute-start.12 = (f32[8,5632]{1,0:T(8,128)S(1)}, f32[8,5632]{1,0:T(8,128)S(1)}, u32[]{:S(2)}, u32[]{:S(2)}) collective-permute-start(f32[8,5632]{1,0:T(8,128)S(1)} %maximum_select_fusion.9), channel_id=1, source_target_pairs={{0,2},{2,0},{4,6},{6,4},{8,10},{10,8},{12,14},{14,12},{16,18},{18,... | collective-permute-start | bytes 540680 | tf_op jit(solution)/shard_map/ppermute | solution.py:173
  (41 other events, 120.7 us)
Sparse Core Ops, SparseCore 0:
  87.2 113.8 reduce-scatter.1
